TPU v7x, 32 devices: a whole 2x2x4 slice. The times are simulated.
32 devices in a mesh: pair: 4 (over z), src: 2 (over x), tgt: 4 (over y, core).
Axes of the slice: x: 2, y: 2, z: 4, core: 2. Of those that a mesh axis runs over, the one named last changes fastest.
Arguments:
- src_cells: float32 [4, 30, 4096], P('pair', None, 'src'), may hold values from -17 to 17
- final_cells: float32 [30, 4096], P(None, 'tgt'), may hold values from -17 to 17
- growth: float32 [4, 4096], P('pair', 'src'), may hold values from 0.5 to 2
- live: int32 [5], replicated, may hold values from 1024 to 4096, as said below
- final_fates: float32 [40, 4096], P(None, 'tgt'), may hold values from 0 to 1
Outputs:
- fate_maps: float32 [4, 40, 4096], P('pair', None, ('src', 'tgt'))
- potentials: float32 [4, 4096], P('pair', 'src')
Inputs may be any that keep to these rules, and one draw needn't show every extreme that they name: `live`: every count is at least 1024 and one snapshot fills all 4096 slots.
All inputs are finite; a program needn't handle non-finite values.
Results may differ from a plain program's by a relative error of at most 0.0049.
Values may be sent and summed in bfloat16 or wider, within the bound.
No kernel may reach another device: no remote copies, remote signals or barrier semaphores. Data moves between devices by JAX's collectives and lax.ppermute only.
A program may use at most 64 MiB of HBM per device.

v0:
```python
import jax
import jax.numpy as jnp
from jax import lax
from jax.sharding import PartitionSpec as P
import functools
from jax.experimental import pallas as pl
from jax.experimental.pallas import tpu as pltpu

ITERS = 8


EPS = 0.1
LAM = 1.0
NEG = -1e30


GROUP = 16
WIDTH = 512


def sweep_kernel(do_row, do_col, emit_w, shrink, c_ref, b_ref, la_ref, *rest):
    rest = list(rest)
    f_ref = rest.pop(0) if do_row else None
    lse_ref = rest.pop(0) if do_col else None
    w_ref = rest.pop(0) if emit_w else None
    a_ref = rest.pop(0)
    rows, cols = c_ref.shape
    groups = rows // GROUP
    chunks = cols // WIDTH

    if do_row:
        def row_group(r, carry):
            rs = pl.ds(pl.multiple_of(r * GROUP, GROUP), GROUP)
            m = jnp.full((GROUP, WIDTH), -jnp.inf, jnp.float32)
            for j in range(chunks):
                cs = slice(j * WIDTH, (j + 1) * WIDTH)
                m = jnp.maximum(m, b_ref[:, cs] - c_ref[rs, cs])
            peak = jnp.max(m, axis=1, keepdims=True)
            s = jnp.zeros((GROUP, WIDTH), jnp.float32)
            for j in range(chunks):
                cs = slice(j * WIDTH, (j + 1) * WIDTH)
                s = s + jnp.exp(b_ref[:, cs] - c_ref[rs, cs] - peak)
            total = jnp.sum(s, axis=1, keepdims=True)
            pot = -shrink * EPS * (peak + jnp.log(total))
            f_ref[rs, :] = pot
            a_ref[rs, :] = pot * (1.0 / EPS) + la_ref[rs, :]
            if emit_w:
                for j in range(chunks):
                    cs = slice(j * WIDTH, (j + 1) * WIDTH)
                    e = jnp.exp(b_ref[:, cs] - c_ref[rs, cs] - peak)
                    w_ref[rs, cs] = (e / total).astype(w_ref.dtype)
            return carry
        lax.fori_loop(0, groups, row_group, 0)
    else:
        a_ref[...] = la_ref[...]

    if do_col:
        def col_chunk(j, carry):
            cs = pl.ds(pl.multiple_of(j * WIDTH, WIDTH), WIDTH)

            def peak_group(r, m):
                rs = pl.ds(pl.multiple_of(r * GROUP, GROUP), GROUP)
                return jnp.maximum(m, a_ref[rs, :] - c_ref[rs, cs])
            m = lax.fori_loop(0, groups, peak_group,
                              jnp.full((GROUP, WIDTH), -jnp.inf, jnp.float32))
            peak = jnp.max(m, axis=0, keepdims=True)

            def sum_group(r, s):
                rs = pl.ds(pl.multiple_of(r * GROUP, GROUP), GROUP)
                return s + jnp.exp(a_ref[rs, :] - c_ref[rs, cs] - peak)
            s = lax.fori_loop(0, groups, sum_group, jnp.zeros((GROUP, WIDTH), jnp.float32))
            lse_ref[:, cs] = peak + jnp.log(jnp.sum(s, axis=0, keepdims=True))
            return carry
        lax.fori_loop(0, chunks, col_chunk, 0)


def sweep(scaled_cost, col_shift, log_a, shrink, do_row, do_col, emit_w):
    rows, cols = scaled_cost.shape
    outs = []
    if do_row:
        outs.append(jax.ShapeDtypeStruct((rows, 1), jnp.float32))
    if do_col:
        outs.append(jax.ShapeDtypeStruct((1, cols), jnp.float32))
    if emit_w:
        outs.append(jax.ShapeDtypeStruct((rows, cols), jnp.bfloat16))
    passes = (2 if do_row else 0) + (2 if do_col else 0) + (1 if emit_w else 0)
    vmem = pl.BlockSpec(memory_space=pltpu.VMEM)
    return pl.pallas_call(
        functools.partial(sweep_kernel, do_row, do_col, emit_w, shrink),
        out_shape=tuple(outs),
        in_specs=[vmem] * 3,
        out_specs=tuple([vmem] * len(outs)),
        scratch_shapes=[pltpu.VMEM((rows, 1), jnp.float32)],
        compiler_params=pltpu.CompilerParams(vmem_limit_bytes=48 * 1024 * 1024),
        cost_estimate=pl.CostEstimate(
            flops=4 * passes * rows * cols,
            transcendentals=passes * rows * cols // 2,
            bytes_accessed=4 * rows * cols + (2 * rows * cols if emit_w else 0),
        ),
    )(scaled_cost, col_shift[None, :], log_a[:, None])


def shifted(shard, axis, by):
    devices = lax.axis_size(axis)
    pairs = [(i, i + by) for i in range(devices) if 0 <= i + by < devices]
    return lax.ppermute(shard, axis, pairs)


def local(src_cells, final_cells, growth, live, final_fates):
    pair_count = lax.axis_size("pair")
    tgt_count = lax.axis_size("tgt")
    pair_rank = lax.axis_index("pair")
    src_rank = lax.axis_index("src")
    tgt_rank = lax.axis_index("tgt")
    shrink = LAM / (LAM + EPS)
    source_all = src_cells[0]
    dims = source_all.shape[0]
    src_width = source_all.shape[1]
    rows = src_width // tgt_count
    row_off = tgt_rank * rows
    is_last = pair_rank == pair_count - 1
    source_pos = lax.dynamic_slice_in_dim(source_all, row_off, rows, 1)
    arrived = lax.all_gather(shifted(source_all, "pair", -1), "src", axis=1, tiled=True)
    final_all = lax.all_gather(final_cells, "tgt", axis=1, tiled=True)
    target_pos = jnp.where(is_last, final_all, arrived)
    cols = target_pos.shape[1]
    cross = lax.dot_general(
        source_pos,
        target_pos,
        (((0,), (0,)), ((), ())),
        precision=lax.Precision.HIGHEST,
        preferred_element_type=jnp.float32,
    )
    src_sq = jnp.sum(source_pos * source_pos, axis=0)
    tgt_sq = jnp.sum(target_pos * target_pos, axis=0)
    cost_tile = (src_sq[:, None] + tgt_sq[None, :] - 2.0 * cross) / (2.0 * dims)
    live_now = lax.dynamic_index_in_dim(live, pair_rank, keepdims=False)
    live_next = lax.dynamic_index_in_dim(live, pair_rank + 1, keepdims=False)
    row_index = src_rank * src_width + row_off + jnp.arange(rows, dtype=jnp.int32)
    col_index = jnp.arange(cols, dtype=jnp.int32)
    live_src = row_index < live_now
    live_tgt = col_index < live_next
    growth_rows = lax.dynamic_slice_in_dim(growth[0], row_off, rows, 0)
    log_mass_a = jnp.where(
        live_src, jnp.log(growth_rows) - jnp.log(live_now.astype(jnp.float32)), NEG
    )
    log_mass_b = jnp.where(
        live_tgt, -jnp.log(live_next.astype(jnp.float32)) * jnp.ones((cols,), jnp.float32), NEG
    )
    scaled_cost = cost_tile * (1.0 / EPS)
    (part_lse,) = sweep(scaled_cost, log_mass_b, log_mass_a, shrink, False, True, False)
    for step_num in range(ITERS):
        every = lax.all_gather(part_lse[0], ("src", "tgt"))
        every_peak = jnp.max(every, axis=0)
        col_lse = every_peak + jnp.log(jnp.sum(jnp.exp(every - every_peak[None, :]), axis=0))
        pot_tgt = -shrink * EPS * col_lse
        col_shift = pot_tgt * (1.0 / EPS) + log_mass_b
        if step_num + 1 < ITERS:
            pot_col, part_lse = sweep(scaled_cost, col_shift, log_mass_a, shrink, True, True, False)
        else:
            pot_col, weights = sweep(scaled_cost, col_shift, log_mass_a, shrink, True, False, True)
    pot_src = pot_col[:, 0]
    final_handed = lax.all_gather(final_fates.astype(jnp.bfloat16), "tgt", axis=1, tiled=True)
    handed = jnp.where(is_last, final_handed, jnp.zeros(final_handed.shape, jnp.bfloat16))
    fate_maps = jnp.zeros((final_fates.shape[0], rows), jnp.float32)
    for section_num in range(pair_count):
        active = pair_count - 1 - section_num
        pulled = lax.dot_general(
            handed, weights, (((1,), (1,)), ((), ())), preferred_element_type=jnp.float32
        )
        pulled = jnp.where(live_src[None, :], pulled, 0.0)
        fate_maps = jnp.where(pair_rank == active, pulled, fate_maps)
        if section_num + 1 < pair_count:
            passed = shifted(pulled.astype(jnp.bfloat16), "pair", -1)
            fresh = lax.all_gather(passed, ("src", "tgt"), axis=1, tiled=True)
            handed = jnp.where(pair_rank == active - 1, fresh, handed)
    pot_all = lax.all_gather(pot_src, "tgt", axis=0, tiled=True)
    return (fate_maps[None], pot_all[None])


def solution(mesh):
    placed = (P("pair", None, "src"), P(None, "tgt"), P("pair", "src"), P(), P(None, "tgt"))
    return jax.shard_map(
        local,
        mesh=mesh,
        in_specs=placed,
        out_specs=(P("pair", None, ("src", "tgt")), P("pair", "src")),
        check_vma=False,
    )
```

profile of v0, /device:TPU:0, one launch (start us, length us, event | category | flops | bytes accessed | tf_op | source)
XLA Modules:
  0.0 604.0 jit_solution(1039985135171300789)
XLA Ops:
  0.6 1.0 copy.33
  1.7 1.3 collective-permute-start
  3.0 1.3 fusion.34
  6.4 0.8 constant_dynamic-slice_fusion
  7.2 8.9 %all_gather.46 = f32[30,4096]{1,0:T(8,128)S(1)} all-gather(f32[30,1024]{1,0:T(8,128)} %param.6), channel_id=1, replica_groups=mesh['pair'=4,'src'=2,'tgt'=4] {'tgt'}, dimensions={1}, use_global_device_ids=true | all-gather | bytes 614400 | tf_op jit(solution)/shard_map/all_gather | solution.py:124
  16.1 0.9 convert_element_type.18
  17.0 6.2 %all_gather.45 = bf16[40,4096]{1,0:T(8,128)(2,1)S(1)} all-gather(bf16[40,1024]{1,0:T(8,128)(2,1)S(1)} %convert_element_type.18), channel_id=1, replica_groups=mesh['pair'=4,'src'=2,'tgt'=4] {'tgt'}, dimensions={1}, use_global_device_ids=true | all-gather | bytes 409600 | tf_op jit(solution)/shard_map/all_gather | solution.py:163
  23.2 0.7 subtract_bitcast_fusion
  24.8 0.7 fusion.4.la_ref
  25.5 9.2 %all_gather.47 = f32[30,4096]{1,0:T(8,128)S(1)} all-gather(f32[30,2048]{1,0:T(8,128)S(1)} %collective-permute-done), channel_id=1, replica_groups=mesh['pair'=4,'src'=2,'tgt'=4] {'src'}, dimensions={1}, use_global_device_ids=true | all-gather | bytes 737280 | tf_op jit(solution)/shard_map/all_gather | solution.py:123
  34.8 9.7 %subtract_multiply_fusion.c_ref = f32[512,4096]{1,0:T(8,128)} fusion(f32[4096]{0:T(1024)S(1)} %multiply_reduce_fusion, f32[512]{0:T(512)S(1)} %fusion.23, f32[30,4096]{1,0:T(8,128)S(1)} %all_gather.46, f32[30,4096]{1,0:T(8,128)S(1)} %all_gather.47, pred[]{:T(512)S(6)} %eq.19, f32[1,30,512]{2,0,1:T(1,128)S(1)} %constant_dynamic-slice_fusion), kind=kOutput, calls=%fused_computation | convolution fusion | flops 763486208 | bytes 9451521 | tf_op jit(solution)/shard_map/dot_general | solution.py:127
  44.5 43.8 %shard_map.68 = f32[1,4096]{1,0:T(1,128)S(1)} custom-call(f32[512,4096]{1,0:T(8,128)} %subtract_multiply_fusion.c_ref, f32[1,4096]{1,0:T(1,128)S(1)} %compare_select_fusion.b_ref, f32[512,1]{1,0:T(8,128)S(1)} %fusion.4.la_ref), custom_call_target="tpu_custom_call" | custom-call | flops 16777216 | bytes 8388608 | tf_op jit(solution)/shard_map/pallas_call | solution.py:88
  88.3 9.2 %all-gather.1 = f32[8,1,4096]{2,1,0:T(1,128)S(1)} all-gather(f32[1,1,4096]{2,1,0:T(1,128)S(1)} %bitcast.85), channel_id=1, replica_groups=mesh['pair'=4,'src'=2,'tgt'=4] {'src','tgt'}, dimensions={0}, use_global_device_ids=true | all-gather | bytes 147456 | tf_op jit(solution)/shard_map/all_gather | solution.py:153
  97.7 0.7 fusion.33.b_ref
  98.4 51.6 %shard_map.69 = (f32[512,1]{1,0:T(8,128)}, f32[1,4096]{1,0:T(1,128)S(1)}) custom-call(f32[512,4096]{1,0:T(8,128)} %subtract_multiply_fusion.c_ref, f32[1,4096]{1,0:T(1,128)S(1)} %fusion.33.b_ref, f32[512,1]{1,0:T(8,128)S(1)} %fusion.4.la_ref), custom_call_target="tpu_custom_call" | custom-call | flops 33554432 | bytes 8388608 | tf_op jit(solution)/shard_map/pallas_call | solution.py:88
  150.0 8.8 %all-gather.2 = f32[8,1,4096]{2,1,0:T(1,128)S(1)} all-gather(f32[1,1,4096]{2,1,0:T(1,128)S(1)} %bitcast.86), channel_id=1, replica_groups=mesh['pair'=4,'src'=2,'tgt'=4] {'src','tgt'}, dimensions={0}, use_global_device_ids=true | all-gather | bytes 147456 | tf_op jit(solution)/shard_map/all_gather | solution.py:153
  159.0 0.7 fusion.32.b_ref
  159.6 51.6 %shard_map.70 = (f32[512,1]{1,0:T(8,128)}, f32[1,4096]{1,0:T(1,128)S(1)}) custom-call(f32[512,4096]{1,0:T(8,128)} %subtract_multiply_fusion.c_ref, f32[1,4096]{1,0:T(1,128)S(1)} %fusion.32.b_ref, f32[512,1]{1,0:T(8,128)S(1)} %fusion.4.la_ref), custom_call_target="tpu_custom_call" | custom-call | flops 33554432 | bytes 8388608 | tf_op jit(solution)/shard_map/pallas_call | solution.py:88
  211.2 8.6 %all-gather.3 = f32[8,1,4096]{2,1,0:T(1,128)S(1)} all-gather(f32[1,1,4096]{2,1,0:T(1,128)S(1)} %bitcast.87), channel_id=1, replica_groups=mesh['pair'=4,'src'=2,'tgt'=4] {'src','tgt'}, dimensions={0}, use_global_device_ids=true | all-gather | bytes 147456 | tf_op jit(solution)/shard_map/all_gather | solution.py:153
  220.1 0.7 fusion.31.b_ref
  220.8 51.6 %shard_map.71 = (f32[512,1]{1,0:T(8,128)}, f32[1,4096]{1,0:T(1,128)S(1)}) custom-call(f32[512,4096]{1,0:T(8,128)} %subtract_multiply_fusion.c_ref, f32[1,4096]{1,0:T(1,128)S(1)} %fusion.31.b_ref, f32[512,1]{1,0:T(8,128)S(1)} %fusion.4.la_ref), custom_call_target="tpu_custom_call" | custom-call | flops 33554432 | bytes 8388608 | tf_op jit(solution)/shard_map/pallas_call | solution.py:88
  272.4 8.8 %all-gather.4 = f32[8,1,4096]{2,1,0:T(1,128)S(1)} all-gather(f32[1,1,4096]{2,1,0:T(1,128)S(1)} %bitcast.88), channel_id=1, replica_groups=mesh['pair'=4,'src'=2,'tgt'=4] {'src','tgt'}, dimensions={0}, use_global_device_ids=true | all-gather | bytes 147456 | tf_op jit(solution)/shard_map/all_gather | solution.py:153
  281.4 0.7 fusion.30.b_ref
  282.0 51.6 %shard_map.72 = (f32[512,1]{1,0:T(8,128)}, f32[1,4096]{1,0:T(1,128)S(1)}) custom-call(f32[512,4096]{1,0:T(8,128)} %subtract_multiply_fusion.c_ref, f32[1,4096]{1,0:T(1,128)S(1)} %fusion.30.b_ref, f32[512,1]{1,0:T(8,128)S(1)} %fusion.4.la_ref), custom_call_target="tpu_custom_call" | custom-call | flops 33554432 | bytes 8388608 | tf_op jit(solution)/shard_map/pallas_call | solution.py:88
  333.6 8.6 %all-gather.5 = f32[8,1,4096]{2,1,0:T(1,128)S(1)} all-gather(f32[1,1,4096]{2,1,0:T(1,128)S(1)} %bitcast.89), channel_id=1, replica_groups=mesh['pair'=4,'src'=2,'tgt'=4] {'src','tgt'}, dimensions={0}, use_global_device_ids=true | all-gather | bytes 147456 | tf_op jit(solution)/shard_map/all_gather | solution.py:153
  342.5 0.7 fusion.29.b_ref
  343.2 51.6 %shard_map.73 = (f32[512,1]{1,0:T(8,128)}, f32[1,4096]{1,0:T(1,128)S(1)}) custom-call(f32[512,4096]{1,0:T(8,128)} %subtract_multiply_fusion.c_ref, f32[1,4096]{1,0:T(1,128)S(1)} %fusion.29.b_ref, f32[512,1]{1,0:T(8,128)S(1)} %fusion.4.la_ref), custom_call_target="tpu_custom_call" | custom-call | flops 33554432 | bytes 8388608 | tf_op jit(solution)/shard_map/pallas_call | solution.py:88
  394.8 8.8 %all-gather.6 = f32[8,1,4096]{2,1,0:T(1,128)S(1)} all-gather(f32[1,1,4096]{2,1,0:T(1,128)S(1)} %bitcast.90), channel_id=1, replica_groups=mesh['pair'=4,'src'=2,'tgt'=4] {'src','tgt'}, dimensions={0}, use_global_device_ids=true | all-gather | bytes 147456 | tf_op jit(solution)/shard_map/all_gather | solution.py:153
  404.5 51.6 %shard_map.74 = (f32[512,1]{1,0:T(8,128)}, f32[1,4096]{1,0:T(1,128)S(1)}) custom-call(f32[512,4096]{1,0:T(8,128)} %subtract_multiply_fusion.c_ref, f32[1,4096]{1,0:T(1,128)S(1)} %fusion.28.b_ref, f32[512,1]{1,0:T(8,128)S(1)} %fusion.4.la_ref), custom_call_target="tpu_custom_call" | custom-call | flops 33554432 | bytes 8388608 | tf_op jit(solution)/shard_map/pallas_call | solution.py:88
  456.0 8.8 %all-gather.7 = f32[8,1,4096]{2,1,0:T(1,128)S(1)} all-gather(f32[1,1,4096]{2,1,0:T(1,128)S(1)} %bitcast.91), channel_id=1, replica_groups=mesh['pair'=4,'src'=2,'tgt'=4] {'src','tgt'}, dimensions={0}, use_global_device_ids=true | all-gather | bytes 147456 | tf_op jit(solution)/shard_map/all_gather | solution.py:153
  465.8 51.6 %shard_map.75 = (f32[512,1]{1,0:T(8,128)}, f32[1,4096]{1,0:T(1,128)S(1)}) custom-call(f32[512,4096]{1,0:T(8,128)} %subtract_multiply_fusion.c_ref, f32[1,4096]{1,0:T(1,128)S(1)} %fusion.27.b_ref, f32[512,1]{1,0:T(8,128)S(1)} %fusion.4.la_ref), custom_call_target="tpu_custom_call" | custom-call | flops 33554432 | bytes 8388608 | tf_op jit(solution)/shard_map/pallas_call | solution.py:88
  517.3 8.8 %all-gather.8 = f32[8,1,4096]{2,1,0:T(1,128)S(1)} all-gather(f32[1,1,4096]{2,1,0:T(1,128)S(1)} %bitcast.92), channel_id=1, replica_groups=mesh['pair'=4,'src'=2,'tgt'=4] {'src','tgt'}, dimensions={0}, use_global_device_ids=true | all-gather | bytes 147456 | tf_op jit(solution)/shard_map/all_gather | solution.py:153
  527.0 10.7 %shard_map.76 = (f32[512,1]{1,0:T(8,128)S(1)}, bf16[512,4096]{1,0:T(8,128)(2,1)S(1)}) custom-call(f32[512,4096]{1,0:T(8,128)} %subtract_multiply_fusion.c_ref, f32[1,4096]{1,0:T(1,128)S(1)} %fusion.26.b_ref, f32[512,1]{1,0:T(8,128)S(1)} %fusion.4.la_ref), custom_call_target="tpu_custom_call" | custom-call | flops 25165824 | bytes 12582912 | tf_op jit(solution)/shard_map/pallas_call | solution.py:88
  537.7 1.9 copy-done
  539.6 1.4 fusion.35
  541.0 1.3 collective-permute-start.1
  542.3 5.1 collective-permute-done.1
  547.4 9.1 %all_gather.56 = bf16[40,4096]{1,0:T(8,128)(2,1)S(1)} all-gather(bf16[40,512]{1,0:T(8,128)(2,1)S(1)} %collective-permute-done.1), channel_id=1, replica_groups=mesh['pair'=4,'src'=2,'tgt'=4] {'src','tgt'}, dimensions={1}, use_global_device_ids=true | all-gather | bytes 368640 | tf_op jit(solution)/shard_map/all_gather | solution.py:175
  556.6 3.6 fusion.36
  560.1 1.3 collective-permute-start.2
  561.4 4.6 collective-permute-done.2
  566.0 8.7 %all_gather.57 = bf16[40,4096]{1,0:T(8,128)(2,1)S(1)} all-gather(bf16[40,512]{1,0:T(8,128)(2,1)S(1)} %collective-permute-done.2), channel_id=1, replica_groups=mesh['pair'=4,'src'=2,'tgt'=4] {'src','tgt'}, dimensions={1}, use_global_device_ids=true | all-gather | bytes 368640 | tf_op jit(solution)/shard_map/all_gather | solution.py:175
  574.7 3.6 fusion.37
  578.3 1.3 collective-permute-start.3
  579.6 10.1 %all-gather = f32[2048,1]{1,0:T(8,128)S(1)} all-gather(f32[512,1]{1,0:T(8,128)S(1)} %get-tuple-element.19), channel_id=2, replica_groups=mesh['pair'=4,'src'=2,'tgt'=4] {'tgt'}, dimensions={0}, use_global_device_ids=true | all-gather | bytes 10240 | tf_op jit(solution)/shard_map/all_gather | solution.py:177
  589.8 0.9 reduce.8
  590.7 9.1 %all_gather.58 = bf16[40,4096]{1,0:T(8,128)(2,1)S(1)} all-gather(bf16[40,512]{1,0:T(8,128)(2,1)S(1)} %collective-permute-done.3), channel_id=1, replica_groups=mesh['pair'=4,'src'=2,'tgt'=4] {'src','tgt'}, dimensions={1}, use_global_device_ids=true | all-gather | bytes 368640 | tf_op jit(solution)/shard_map/all_gather | solution.py:175
  599.8 4.2 fusion.1
  (36 shorter events, 5.4 us)
Async XLA Ops:
  1.7 23.8 %collective-permute-start = (f32[30,2048]{1,0:T(8,128)S(1)}, f32[30,2048]{1,0:T(8,128)S(1)}, u32[]{:S(2)}, u32[]{:S(2)}) collective-permute-start(f32[30,2048]{1,0:T(8,128)S(1)} %bitcast.93), channel_id=1, source_target_pairs={{8,0},{16,8},{24,16},{9,1},{17,9},{25,17},{10,2},{18,10},{26,18},{... | collective-permute-start | bytes 737288 | tf_op jit(solution)/shard_map/ppermute | solution.py:106
  537.7 1.9 copy-start
  541.0 6.4 %collective-permute-start.1 = (bf16[40,512]{1,0:T(8,128)(2,1)S(1)}, bf16[40,512]{1,0:T(8,128)(2,1)S(1)}, u32[]{:S(2)}, u32[]{:S(2)}) collective-permute-start(bf16[40,512]{1,0:T(8,128)(2,1)S(1)} %get-tuple-element.22), channel_id=1, source_target_pairs={{8,0},{16,8},{24,16},{9,1},{17,9},{25,17},{10,2},{18,10},{26,18},{... | collective-permute-start | bytes 122888 | tf_op jit(solution)/shard_map/ppermute | solution.py:106
  560.1 5.9 collective-permute-start.2
  578.3 12.4 %collective-permute-start.3 = (bf16[40,512]{1,0:T(8,128)(2,1)S(1)}, bf16[40,512]{1,0:T(8,128)(2,1)S(1)}, u32[]{:S(2)}, u32[]{:S(2)}) collective-permute-start(bf16[40,512]{1,0:T(8,128)(2,1)S(1)} %get-tuple-element.26), channel_id=1, source_target_pairs={{8,0},{16,8},{24,16},{9,1},{17,9},{25,17},{10,2},{18,10},{26,18},{... | collective-permute-start | bytes 122888 | tf_op jit(solution)/shard_map/ppermute | solution.py:106
where the time goes:
time: 605 us; the launch traced here: 604 us
  Pallas kernels  416 us (69%)
  blocking collectives  132 us (22%)
  matrix products  22.4 us (4%)
  other arithmetic  11.9 us (2%)
  waiting for transfers between devices  9.65 us (2%)
    pallas_call x9, Pallas kernels, sweep(): pl.pallas_call(functools.partial(sweep_kernel, do_row, do_col, emit_w, sh...  416 us
    all_gather x8, blocking collectives, local(): every = lax.all_gather(part_lse[0], ('src', 'tgt'))  70.3 us
    all_gather x3, blocking collectives, local(): fresh = lax.all_gather(passed, ('src', 'tgt'), axis=1, tiled=True)  27 us
    dot_general x4, matrix products, local(): lax.dot_general(handed, weights, (((1,), (1,)), ((), ())), preferred_elem...  12.7 us
  transfers between devices with their start and end apart: 4, of which 2 were waited for; matrix products, arithmetic and copies ran while one was open for 1% of the time, Pallas kernels for 0%

commit v1 on v0

--- a/solution.py
+++ b/solution.py
@@ -15,6 +15,7 @@
 
 
 GROUP = 16
+ROW_GROUP = 32
 WIDTH = 512
 
 
@@ -29,47 +30,46 @@
     chunks = cols // WIDTH
 
     if do_row:
+        rg = ROW_GROUP if rows % ROW_GROUP == 0 else GROUP
+
         def row_group(r, carry):
-            rs = pl.ds(pl.multiple_of(r * GROUP, GROUP), GROUP)
-            m = jnp.full((GROUP, WIDTH), -jnp.inf, jnp.float32)
+            rs = pl.ds(pl.multiple_of(r * rg, rg), rg)
+            m = jnp.full((rg, WIDTH), -jnp.inf, jnp.float32)
             for j in range(chunks):
                 cs = slice(j * WIDTH, (j + 1) * WIDTH)
                 m = jnp.maximum(m, b_ref[:, cs] - c_ref[rs, cs])
             peak = jnp.max(m, axis=1, keepdims=True)
-            s = jnp.zeros((GROUP, WIDTH), jnp.float32)
+            s = jnp.zeros((rg, WIDTH), jnp.float32)
             for j in range(chunks):
                 cs = slice(j * WIDTH, (j + 1) * WIDTH)
                 s = s + jnp.exp(b_ref[:, cs] - c_ref[rs, cs] - peak)
             total = jnp.sum(s, axis=1, keepdims=True)
             pot = -shrink * EPS * (peak + jnp.log(total))
             f_ref[rs, :] = pot
-            a_ref[rs, :] = pot * (1.0 / EPS) + la_ref[rs, :]
+            a_ref[rs, :] = jnp.broadcast_to(pot * (1.0 / EPS) + la_ref[rs, :], (rg, 128))
             if emit_w:
                 for j in range(chunks):
                     cs = slice(j * WIDTH, (j + 1) * WIDTH)
                     e = jnp.exp(b_ref[:, cs] - c_ref[rs, cs] - peak)
                     w_ref[rs, cs] = (e / total).astype(w_ref.dtype)
             return carry
-        lax.fori_loop(0, groups, row_group, 0)
+        lax.fori_loop(0, rows // rg, row_group, 0)
     else:
-        a_ref[...] = la_ref[...]
+        a_ref[...] = jnp.broadcast_to(la_ref[...], a_ref.shape)
 
     if do_col:
         def col_chunk(j, carry):
             cs = pl.ds(pl.multiple_of(j * WIDTH, WIDTH), WIDTH)
-
-            def peak_group(r, m):
-                rs = pl.ds(pl.multiple_of(r * GROUP, GROUP), GROUP)
-                return jnp.maximum(m, a_ref[rs, :] - c_ref[rs, cs])
-            m = lax.fori_loop(0, groups, peak_group,
-                              jnp.full((GROUP, WIDTH), -jnp.inf, jnp.float32))
-            peak = jnp.max(m, axis=0, keepdims=True)
-
-            def sum_group(r, s):
-                rs = pl.ds(pl.multiple_of(r * GROUP, GROUP), GROUP)
-                return s + jnp.exp(a_ref[rs, :] - c_ref[rs, cs] - peak)
-            s = lax.fori_loop(0, groups, sum_group, jnp.zeros((GROUP, WIDTH), jnp.float32))
-            lse_ref[:, cs] = peak + jnp.log(jnp.sum(s, axis=0, keepdims=True))
+            shifts = [jnp.tile(a_ref[r * GROUP:(r + 1) * GROUP, :], (1, WIDTH // 128))
+                      for r in range(groups)]
+            m = [jnp.full((GROUP, WIDTH), -jnp.inf, jnp.float32) for _ in range(2)]
+            for r in range(groups):
+                m[r % 2] = jnp.maximum(m[r % 2], shifts[r] - c_ref[r * GROUP:(r + 1) * GROUP, cs])
+            peak = jnp.max(jnp.maximum(m[0], m[1]), axis=0, keepdims=True)
+            s = [jnp.zeros((GROUP, WIDTH), jnp.float32) for _ in range(2)]
+            for r in range(groups):
+                s[r % 2] = s[r % 2] + jnp.exp(shifts[r] - c_ref[r * GROUP:(r + 1) * GROUP, cs] - peak)
+            lse_ref[:, cs] = peak + jnp.log(jnp.sum(s[0] + s[1], axis=0, keepdims=True))
             return carry
         lax.fori_loop(0, chunks, col_chunk, 0)
 
@@ -90,8 +90,8 @@
         out_shape=tuple(outs),
         in_specs=[vmem] * 3,
         out_specs=tuple([vmem] * len(outs)),
-        scratch_shapes=[pltpu.VMEM((rows, 1), jnp.float32)],
-        compiler_params=pltpu.CompilerParams(vmem_limit_bytes=48 * 1024 * 1024),
+        scratch_shapes=[pltpu.VMEM((rows, 128), jnp.float32)],
+        compiler_params=pltpu.CompilerParams(vmem_limit_bytes=24 * 1024 * 1024),
         cost_estimate=pl.CostEstimate(
             flops=4 * passes * rows * cols,
             transcendentals=passes * rows * cols // 2,

time: 605 us -> 279 us (0.46)
  Pallas kernels: 416 us -> 63 us
  local copies, waits for them, and re-layouts: 5.26 us -> 33.3 us
    pallas_call x9, Pallas kernels: 416 us -> 63 us  [sweep(): pl.pallas_call(functools.partial(sweep_kernel, do_row, do_col, emit_w, sh...]
    unnamed x3 -> x21, local copies, waits for them, and re-layouts: 2.94 us -> 31 us
  transfers between devices with their start and end apart: 4 -> 4, of which waited for: 2 -> 2; matrix products, arithmetic and copies ran while one was open for 1% -> 2% of each run, Pallas kernels for 0% -> 0%
where the time goes in v1:
time: 279 us; the launch traced here: 278 us
  blocking collectives  132 us (47%)
  Pallas kernels  63 us (23%)
  local copies, waits for them, and re-layouts  33.3 us (12%)
  matrix products  20.1 us (7%)
  other arithmetic  11.9 us (4%)
  waiting for transfers between devices  9.65 us (3%)
  starting transfers between devices  5.17 us (2%)
    all_gather x8, blocking collectives, local(): every = lax.all_gather(part_lse[0], ('src', 'tgt'))  70.3 us
    pallas_call x9, Pallas kernels, sweep(): pl.pallas_call(functools.partial(sweep_kernel, do_row, do_col, emit_w, sh...  63 us
    unnamed x21, local copies, waits for them, and re-layouts  31 us
    all_gather x3, blocking collectives, local(): fresh = lax.all_gather(passed, ('src', 'tgt'), axis=1, tiled=True)  27.2 us
    dot_general x4, matrix products, local(): lax.dot_general(handed, weights, (((1,), (1,)), ((), ())), preferred_elem...  12.7 us
    all_gather x1, blocking collectives, local(): pot_all = lax.all_gather(pot_src, 'tgt', axis=0, tiled=True)  10.1 us
    ppermute x4, waiting for transfers between devices, shifted(): return lax.ppermute(shard, axis, pairs)  9.65 us
    all_gather x1, blocking collectives, local(): lax.all_gather(shifted(source_all, 'pair', -1), 'src', axis=1, tiled=True)  9.22 us
  transfers between devices with their start and end apart: 4, of which 2 were waited for; matrix products, arithmetic and copies ran while one was open for 2% of the time, Pallas kernels for 0%

profile of v1, /device:TPU:0, one launch (start us, length us, event | category | flops | bytes accessed | tf_op | source)
XLA Modules:
  0.0 277.6 jit_solution(11476828971170365439)
XLA Ops:
  0.6 1.0 copy.33
  1.7 1.3 collective-permute-start
  3.0 1.3 fusion.34
  7.2 8.9 %all_gather.46 = f32[30,4096]{1,0:T(8,128)S(1)} all-gather(f32[30,1024]{1,0:T(8,128)} %param.6), channel_id=1, replica_groups=mesh['pair'=4,'src'=2,'tgt'=4] {'tgt'}, dimensions={1}, use_global_device_ids=true | all-gather | bytes 614400 | tf_op jit(solution)/shard_map/all_gather | solution.py:124
  17.0 6.2 %all_gather.45 = bf16[40,4096]{1,0:T(8,128)(2,1)S(1)} all-gather(bf16[40,1024]{1,0:T(8,128)(2,1)S(1)} %convert_element_type.18), channel_id=1, replica_groups=mesh['pair'=4,'src'=2,'tgt'=4] {'tgt'}, dimensions={1}, use_global_device_ids=true | all-gather | bytes 409600 | tf_op jit(solution)/shard_map/all_gather | solution.py:163
  25.5 9.2 %all_gather.47 = f32[30,4096]{1,0:T(8,128)S(1)} all-gather(f32[30,2048]{1,0:T(8,128)S(1)} %collective-permute-done), channel_id=1, replica_groups=mesh['pair'=4,'src'=2,'tgt'=4] {'src'}, dimensions={1}, use_global_device_ids=true | all-gather | bytes 737280 | tf_op jit(solution)/shard_map/all_gather | solution.py:123
  34.8 7.4 %subtract_multiply_fusion.c_ref = f32[512,4096]{1,0:T(8,128)S(1)} fusion(f32[4096]{0:T(1024)S(1)} %multiply_reduce_fusion, f32[512]{0:T(512)S(1)} %fusion.23, f32[30,4096]{1,0:T(8,128)S(1)} %all_gather.46, f32[30,4096]{1,0:T(8,128)S(1)} %all_gather.47, pred[]{:T(512)S(6)} %eq.19, f32[1,30,512]{2,0,1:T(1,128)S(1)} %constant_dynamic-slice_fusion), kind=kOutput, calls=%fused_computation | convolution fusion | flops 763486208 | bytes 9451521 | tf_op jit(solution)/shard_map/dot_general | solution.py:127
  42.2 2.2 shard_map.68
  44.4 1.0 copy-done
  45.4 9.2 %all-gather.1 = f32[8,1,4096]{2,1,0:T(1,128)S(1)} all-gather(f32[1,1,4096]{2,1,0:T(1,128)S(1)} %bitcast.85), channel_id=1, replica_groups=mesh['pair'=4,'src'=2,'tgt'=4] {'src','tgt'}, dimensions={0}, use_global_device_ids=true | all-gather | bytes 147456 | tf_op jit(solution)/shard_map/all_gather | solution.py:153
  55.5 3.4 %copy-done.1 = f32[512,4096]{1,0:T(8,128)S(1)} copy-done((f32[512,4096]{1,0:T(8,128)S(1)}, f32[512,4096]{1,0:T(8,128)}, u32[]{:S(2)}) %copy-start.1) | copy-done | bytes 8388632
  58.9 7.9 %shard_map.69 = (f32[512,1]{1,0:T(8,128)}, f32[1,4096]{1,0:T(1,128)S(1)}) custom-call(f32[512,4096]{1,0:T(8,128)S(1)} %copy-done.1, f32[1,4096]{1,0:T(1,128)S(1)} %fusion.33.b_ref, f32[512,1]{1,0:T(8,128)S(1)} %fusion.4.la_ref), custom_call_target="tpu_custom_call" | custom-call | flops 33554432 | bytes 8388608 | tf_op jit(solution)/shard_map/pallas_call | solution.py:88
  66.8 8.8 %all-gather.2 = f32[8,1,4096]{2,1,0:T(1,128)S(1)} all-gather(f32[1,1,4096]{2,1,0:T(1,128)S(1)} %bitcast.86), channel_id=1, replica_groups=mesh['pair'=4,'src'=2,'tgt'=4] {'src','tgt'}, dimensions={0}, use_global_device_ids=true | all-gather | bytes 147456 | tf_op jit(solution)/shard_map/all_gather | solution.py:153
  76.5 3.4 %copy-done.2 = f32[512,4096]{1,0:T(8,128)S(1)} copy-done((f32[512,4096]{1,0:T(8,128)S(1)}, f32[512,4096]{1,0:T(8,128)}, u32[]{:S(2)}) %copy-start.2) | copy-done | bytes 8388632
  79.9 7.9 %shard_map.70 = (f32[512,1]{1,0:T(8,128)}, f32[1,4096]{1,0:T(1,128)S(1)}) custom-call(f32[512,4096]{1,0:T(8,128)S(1)} %copy-done.2, f32[1,4096]{1,0:T(1,128)S(1)} %fusion.32.b_ref, f32[512,1]{1,0:T(8,128)S(1)} %fusion.4.la_ref), custom_call_target="tpu_custom_call" | custom-call | flops 33554432 | bytes 8388608 | tf_op jit(solution)/shard_map/pallas_call | solution.py:88
  87.8 8.8 %all-gather.3 = f32[8,1,4096]{2,1,0:T(1,128)S(1)} all-gather(f32[1,1,4096]{2,1,0:T(1,128)S(1)} %bitcast.87), channel_id=1, replica_groups=mesh['pair'=4,'src'=2,'tgt'=4] {'src','tgt'}, dimensions={0}, use_global_device_ids=true | all-gather | bytes 147456 | tf_op jit(solution)/shard_map/all_gather | solution.py:153
  97.6 3.4 %copy-done.3 = f32[512,4096]{1,0:T(8,128)S(1)} copy-done((f32[512,4096]{1,0:T(8,128)S(1)}, f32[512,4096]{1,0:T(8,128)}, u32[]{:S(2)}) %copy-start.3) | copy-done | bytes 8388632
  100.9 7.9 %shard_map.71 = (f32[512,1]{1,0:T(8,128)}, f32[1,4096]{1,0:T(1,128)S(1)}) custom-call(f32[512,4096]{1,0:T(8,128)S(1)} %copy-done.3, f32[1,4096]{1,0:T(1,128)S(1)} %fusion.31.b_ref, f32[512,1]{1,0:T(8,128)S(1)} %fusion.4.la_ref), custom_call_target="tpu_custom_call" | custom-call | flops 33554432 | bytes 8388608 | tf_op jit(solution)/shard_map/pallas_call | solution.py:88
  108.9 8.8 %all-gather.4 = f32[8,1,4096]{2,1,0:T(1,128)S(1)} all-gather(f32[1,1,4096]{2,1,0:T(1,128)S(1)} %bitcast.88), channel_id=1, replica_groups=mesh['pair'=4,'src'=2,'tgt'=4] {'src','tgt'}, dimensions={0}, use_global_device_ids=true | all-gather | bytes 147456 | tf_op jit(solution)/shard_map/all_gather | solution.py:153
  118.6 3.4 %copy-done.4 = f32[512,4096]{1,0:T(8,128)S(1)} copy-done((f32[512,4096]{1,0:T(8,128)S(1)}, f32[512,4096]{1,0:T(8,128)}, u32[]{:S(2)}) %copy-start.4) | copy-done | bytes 8388632
  121.9 7.9 %shard_map.72 = (f32[512,1]{1,0:T(8,128)}, f32[1,4096]{1,0:T(1,128)S(1)}) custom-call(f32[512,4096]{1,0:T(8,128)S(1)} %copy-done.4, f32[1,4096]{1,0:T(1,128)S(1)} %fusion.30.b_ref, f32[512,1]{1,0:T(8,128)S(1)} %fusion.4.la_ref), custom_call_target="tpu_custom_call" | custom-call | flops 33554432 | bytes 8388608 | tf_op jit(solution)/shard_map/pallas_call | solution.py:88
  129.9 8.6 %all-gather.5 = f32[8,1,4096]{2,1,0:T(1,128)S(1)} all-gather(f32[1,1,4096]{2,1,0:T(1,128)S(1)} %bitcast.89), channel_id=1, replica_groups=mesh['pair'=4,'src'=2,'tgt'=4] {'src','tgt'}, dimensions={0}, use_global_device_ids=true | all-gather | bytes 147456 | tf_op jit(solution)/shard_map/all_gather | solution.py:153
  139.4 3.4 %copy-done.5 = f32[512,4096]{1,0:T(8,128)S(1)} copy-done((f32[512,4096]{1,0:T(8,128)S(1)}, f32[512,4096]{1,0:T(8,128)}, u32[]{:S(2)}) %copy-start.5) | copy-done | bytes 8388632
  142.8 7.9 %shard_map.73 = (f32[512,1]{1,0:T(8,128)}, f32[1,4096]{1,0:T(1,128)S(1)}) custom-call(f32[512,4096]{1,0:T(8,128)S(1)} %copy-done.5, f32[1,4096]{1,0:T(1,128)S(1)} %fusion.29.b_ref, f32[512,1]{1,0:T(8,128)S(1)} %fusion.4.la_ref), custom_call_target="tpu_custom_call" | custom-call | flops 33554432 | bytes 8388608 | tf_op jit(solution)/shard_map/pallas_call | solution.py:88
  150.7 8.8 %all-gather.6 = f32[8,1,4096]{2,1,0:T(1,128)S(1)} all-gather(f32[1,1,4096]{2,1,0:T(1,128)S(1)} %bitcast.90), channel_id=1, replica_groups=mesh['pair'=4,'src'=2,'tgt'=4] {'src','tgt'}, dimensions={0}, use_global_device_ids=true | all-gather | bytes 147456 | tf_op jit(solution)/shard_map/all_gather | solution.py:153
  160.4 3.4 %copy-done.6 = f32[512,4096]{1,0:T(8,128)S(1)} copy-done((f32[512,4096]{1,0:T(8,128)S(1)}, f32[512,4096]{1,0:T(8,128)}, u32[]{:S(2)}) %copy-start.6) | copy-done | bytes 8388632
  163.8 7.9 %shard_map.74 = (f32[512,1]{1,0:T(8,128)}, f32[1,4096]{1,0:T(1,128)S(1)}) custom-call(f32[512,4096]{1,0:T(8,128)S(1)} %copy-done.6, f32[1,4096]{1,0:T(1,128)S(1)} %fusion.28.b_ref, f32[512,1]{1,0:T(8,128)S(1)} %fusion.4.la_ref), custom_call_target="tpu_custom_call" | custom-call | flops 33554432 | bytes 8388608 | tf_op jit(solution)/shard_map/pallas_call | solution.py:88
  171.7 8.6 %all-gather.7 = f32[8,1,4096]{2,1,0:T(1,128)S(1)} all-gather(f32[1,1,4096]{2,1,0:T(1,128)S(1)} %bitcast.91), channel_id=1, replica_groups=mesh['pair'=4,'src'=2,'tgt'=4] {'src','tgt'}, dimensions={0}, use_global_device_ids=true | all-gather | bytes 147456 | tf_op jit(solution)/shard_map/all_gather | solution.py:153
  181.3 3.4 %copy-done.7 = f32[512,4096]{1,0:T(8,128)S(1)} copy-done((f32[512,4096]{1,0:T(8,128)S(1)}, f32[512,4096]{1,0:T(8,128)}, u32[]{:S(2)}) %copy-start.7) | copy-done | bytes 8388632
  184.7 7.9 %shard_map.75 = (f32[512,1]{1,0:T(8,128)}, f32[1,4096]{1,0:T(1,128)S(1)}) custom-call(f32[512,4096]{1,0:T(8,128)S(1)} %copy-done.7, f32[1,4096]{1,0:T(1,128)S(1)} %fusion.27.b_ref, f32[512,1]{1,0:T(8,128)S(1)} %fusion.4.la_ref), custom_call_target="tpu_custom_call" | custom-call | flops 33554432 | bytes 8388608 | tf_op jit(solution)/shard_map/pallas_call | solution.py:88
  192.6 8.8 %all-gather.8 = f32[8,1,4096]{2,1,0:T(1,128)S(1)} all-gather(f32[1,1,4096]{2,1,0:T(1,128)S(1)} %bitcast.92), channel_id=1, replica_groups=mesh['pair'=4,'src'=2,'tgt'=4] {'src','tgt'}, dimensions={0}, use_global_device_ids=true | all-gather | bytes 147456 | tf_op jit(solution)/shard_map/all_gather | solution.py:153
  202.3 3.4 %copy-done.8 = f32[512,4096]{1,0:T(8,128)S(1)} copy-done((f32[512,4096]{1,0:T(8,128)S(1)}, f32[512,4096]{1,0:T(8,128)}, u32[]{:S(2)}) %copy-start.8) | copy-done | bytes 8388632
  205.7 5.3 %shard_map.76 = (f32[512,1]{1,0:T(8,128)S(1)}, bf16[512,4096]{1,0:T(8,128)(2,1)S(1)}) custom-call(f32[512,4096]{1,0:T(8,128)S(1)} %copy-done.8, f32[1,4096]{1,0:T(1,128)S(1)} %fusion.26.b_ref, f32[512,1]{1,0:T(8,128)S(1)} %fusion.4.la_ref), custom_call_target="tpu_custom_call" | custom-call | flops 25165824 | bytes 12582912 | tf_op jit(solution)/shard_map/pallas_call | solution.py:88
  211.0 2.0 copy-done.9
  213.0 1.4 fusion.35
  214.3 1.3 collective-permute-start.1
  215.7 5.1 %collective-permute-done.1 = bf16[40,512]{1,0:T(8,128)(2,1)S(1)} collective-permute-done((bf16[40,512]{1,0:T(8,128)(2,1)S(1)}, bf16[40,512]{1,0:T(8,128)(2,1)S(1)}, u32[]{:S(2)}, u32[]{:S(2)}) %collective-permute-start.1) | collective-permute-done | bytes 40992 | tf_op jit(solution)/shard_map/ppermute | solution.py:106
  220.7 9.1 %all_gather.56 = bf16[40,4096]{1,0:T(8,128)(2,1)S(1)} all-gather(bf16[40,512]{1,0:T(8,128)(2,1)S(1)} %collective-permute-done.1), channel_id=1, replica_groups=mesh['pair'=4,'src'=2,'tgt'=4] {'src','tgt'}, dimensions={1}, use_global_device_ids=true | all-gather | bytes 368640 | tf_op jit(solution)/shard_map/all_gather | solution.py:175
  229.9 3.6 %fusion.36 = (bf16[40,512]{1,0:T(8,128)(2,1)S(1)}, f32[40,512]{1,0:T(8,128)S(1)}) fusion(bf16[40,4096]{1,0:T(8,128)(2,1)S(1)} %broadcast_select_fusion.1, bf16[512,4096]{1,0:T(8,128)(2,1)} %copy-done.9, pred[512]{0:T(512)(128)(4,1)S(1)} %add_compare_fusion.1), kind=kOutput, calls=%fused_computation.69 | convolution fusion | flops 167813120 | bytes 4645376 | tf_op jit(solution)/shard_map/dot_general | solution.py:168
  233.4 1.3 collective-permute-start.2
  234.8 4.6 %collective-permute-done.2 = bf16[40,512]{1,0:T(8,128)(2,1)S(1)} collective-permute-done((bf16[40,512]{1,0:T(8,128)(2,1)S(1)}, bf16[40,512]{1,0:T(8,128)(2,1)S(1)}, u32[]{:S(2)}, u32[]{:S(2)}) %collective-permute-start.2) | collective-permute-done | bytes 40992 | tf_op jit(solution)/shard_map/ppermute | solution.py:106
  239.3 9.0 %all_gather.57 = bf16[40,4096]{1,0:T(8,128)(2,1)S(1)} all-gather(bf16[40,512]{1,0:T(8,128)(2,1)S(1)} %collective-permute-done.2), channel_id=1, replica_groups=mesh['pair'=4,'src'=2,'tgt'=4] {'src','tgt'}, dimensions={1}, use_global_device_ids=true | all-gather | bytes 368640 | tf_op jit(solution)/shard_map/all_gather | solution.py:175
  248.3 3.6 %fusion.37 = (bf16[40,512]{1,0:T(8,128)(2,1)S(1)}, f32[40,512]{1,0:T(8,128)S(1)}) fusion(bf16[512,4096]{1,0:T(8,128)(2,1)} %copy-done.9, bf16[40,4096]{1,0:T(8,128)(2,1)S(1)} %all_gather.57, bf16[40,4096]{1,0:T(8,128)(2,1)S(1)} %broadcast_select_fusion.1, pred[]{:T(512)S(6)} %eq.17, pred[512]{0:T(512)(128)(4,1)S(1)} %add_compare_fusion.1), kind=kOutput, calls=%fused_computation.70 | convolution fusion | flops 167976960 | bytes 4973057 | tf_op jit(solution)/shard_map/dot_general | solution.py:168
  251.9 1.3 collective-permute-start.3
  253.2 10.1 %all-gather = f32[2048,1]{1,0:T(8,128)S(1)} all-gather(f32[512,1]{1,0:T(8,128)S(1)} %get-tuple-element.19), channel_id=2, replica_groups=mesh['pair'=4,'src'=2,'tgt'=4] {'tgt'}, dimensions={0}, use_global_device_ids=true | all-gather | bytes 10240 | tf_op jit(solution)/shard_map/all_gather | solution.py:177
  263.3 0.9 reduce.8
  264.3 9.1 %all_gather.58 = bf16[40,4096]{1,0:T(8,128)(2,1)S(1)} all-gather(bf16[40,512]{1,0:T(8,128)(2,1)S(1)} %collective-permute-done.3), channel_id=1, replica_groups=mesh['pair'=4,'src'=2,'tgt'=4] {'src','tgt'}, dimensions={1}, use_global_device_ids=true | all-gather | bytes 368640 | tf_op jit(solution)/shard_map/all_gather | solution.py:175
  273.4 4.2 %fusion.1 = f32[1,40,512]{2,1,0:T(8,128)} fusion(bf16[512,4096]{1,0:T(8,128)(2,1)} %copy-done.9, bf16[40,4096]{1,0:T(8,128)(2,1)S(1)} %all_gather.58, pred[]{:T(512)S(6)} %eq.16, bf16[40,4096]{1,0:T(8,128)(2,1)S(1)} %all_gather.57, bf16[40,4096]{1,0:T(8,128)(2,1)S(1)} %broadcast_select_fusion.1, pred[]{:T(512)S(6)} %eq.17, ...), kind=kOutput, calls=%fused_computation.6 | convolution fusion | flops 168202240 | bytes 5505540 | tf_op jit(solution)/shard_map/dot_general | solution.py:168
  (54 shorter events, 12.0 us)
Async XLA Ops:
  1.7 23.8 %collective-permute-start = (f32[30,2048]{1,0:T(8,128)S(1)}, f32[30,2048]{1,0:T(8,128)S(1)}, u32[]{:S(2)}, u32[]{:S(2)}) collective-permute-start(f32[30,2048]{1,0:T(8,128)S(1)} %bitcast.93), channel_id=1, source_target_pairs={{8,0},{16,8},{24,16},{9,1},{17,9},{25,17},{10,2},{18,10},{26,18},{... | collective-permute-start | bytes 737288 | tf_op jit(solution)/shard_map/ppermute | solution.py:106
  42.2 3.2 %copy-start = (f32[512,4096]{1,0:T(8,128)}, f32[512,4096]{1,0:T(8,128)S(1)}, u32[]{:S(2)}) copy-start(f32[512,4096]{1,0:T(8,128)S(1)} %subtract_multiply_fusion.c_ref) | copy-start | bytes 25165828
  55.5 3.4 %copy-start.1 = (f32[512,4096]{1,0:T(8,128)S(1)}, f32[512,4096]{1,0:T(8,128)}, u32[]{:S(2)}) copy-start(f32[512,4096]{1,0:T(8,128)} %copy-done) | copy-start | bytes 25165828
  76.5 3.4 %copy-start.2 = (f32[512,4096]{1,0:T(8,128)S(1)}, f32[512,4096]{1,0:T(8,128)}, u32[]{:S(2)}) copy-start(f32[512,4096]{1,0:T(8,128)} %copy-done) | copy-start | bytes 25165828
  97.5 3.4 %copy-start.3 = (f32[512,4096]{1,0:T(8,128)S(1)}, f32[512,4096]{1,0:T(8,128)}, u32[]{:S(2)}) copy-start(f32[512,4096]{1,0:T(8,128)} %copy-done) | copy-start | bytes 25165828
  118.5 3.4 %copy-start.4 = (f32[512,4096]{1,0:T(8,128)S(1)}, f32[512,4096]{1,0:T(8,128)}, u32[]{:S(2)}) copy-start(f32[512,4096]{1,0:T(8,128)} %copy-done) | copy-start | bytes 25165828
  139.4 3.4 %copy-start.5 = (f32[512,4096]{1,0:T(8,128)S(1)}, f32[512,4096]{1,0:T(8,128)}, u32[]{:S(2)}) copy-start(f32[512,4096]{1,0:T(8,128)} %copy-done) | copy-start | bytes 25165828
  160.4 3.4 %copy-start.6 = (f32[512,4096]{1,0:T(8,128)S(1)}, f32[512,4096]{1,0:T(8,128)}, u32[]{:S(2)}) copy-start(f32[512,4096]{1,0:T(8,128)} %copy-done) | copy-start | bytes 25165828
  181.3 3.4 %copy-start.7 = (f32[512,4096]{1,0:T(8,128)S(1)}, f32[512,4096]{1,0:T(8,128)}, u32[]{:S(2)}) copy-start(f32[512,4096]{1,0:T(8,128)} %copy-done) | copy-start | bytes 25165828
  202.3 3.4 %copy-start.8 = (f32[512,4096]{1,0:T(8,128)S(1)}, f32[512,4096]{1,0:T(8,128)}, u32[]{:S(2)}) copy-start(f32[512,4096]{1,0:T(8,128)} %copy-done) | copy-start | bytes 25165828
  211.0 2.0 copy-start.9
  214.3 6.4 %collective-permute-start.1 = (bf16[40,512]{1,0:T(8,128)(2,1)S(1)}, bf16[40,512]{1,0:T(8,128)(2,1)S(1)}, u32[]{:S(2)}, u32[]{:S(2)}) collective-permute-start(bf16[40,512]{1,0:T(8,128)(2,1)S(1)} %get-tuple-element.22), channel_id=1, source_target_pairs={{8,0},{16,8},{24,16},{9,1},{17,9},{25,17},{10,2},{18,10},{26,18},{... | collective-permute-start | bytes 122888 | tf_op jit(solution)/shard_map/ppermute | solution.py:106
  233.4 5.9 %collective-permute-start.2 = (bf16[40,512]{1,0:T(8,128)(2,1)S(1)}, bf16[40,512]{1,0:T(8,128)(2,1)S(1)}, u32[]{:S(2)}, u32[]{:S(2)}) collective-permute-start(bf16[40,512]{1,0:T(8,128)(2,1)S(1)} %get-tuple-element.24), channel_id=1, source_target_pairs={{8,0},{16,8},{24,16},{9,1},{17,9},{25,17},{10,2},{18,10},{26,18},{... | collective-permute-start | bytes 122888 | tf_op jit(solution)/shard_map/ppermute | solution.py:106
  251.9 12.4 %collective-permute-start.3 = (bf16[40,512]{1,0:T(8,128)(2,1)S(1)}, bf16[40,512]{1,0:T(8,128)(2,1)S(1)}, u32[]{:S(2)}, u32[]{:S(2)}) collective-permute-start(bf16[40,512]{1,0:T(8,128)(2,1)S(1)} %get-tuple-element.26), channel_id=1, source_target_pairs={{8,0},{16,8},{24,16},{9,1},{17,9},{25,17},{10,2},{18,10},{26,18},{... | collective-permute-start | bytes 122888 | tf_op jit(solution)/shard_map/ppermute | solution.py:106

commit v2 on v1

--- a/solution.py
+++ b/solution.py
@@ -106,12 +106,33 @@
     return lax.ppermute(shard, axis, pairs)
 
 
+def blocks_from_group(block, axes, group, lead=None):
+    lead_count = 1 if lead is None else lax.axis_size(lead)
+    names = axes if lead is None else (lead,) + tuple(axes)
+    received = []
+    for k in range(group):
+        if lead is None and k == 0:
+            received.append(block)
+            continue
+        pairs = []
+        for up in range(lead_count):
+            down = up if lead is None else up - 1
+            if down < 0:
+                continue
+            for member in range(group):
+                pairs.append((up * group + member, down * group + (member + k) % group))
+        received.append(lax.ppermute(block, names, pairs))
+    return received
+
+
 def local(src_cells, final_cells, growth, live, final_fates):
     pair_count = lax.axis_size("pair")
     tgt_count = lax.axis_size("tgt")
     pair_rank = lax.axis_index("pair")
     src_rank = lax.axis_index("src")
     tgt_rank = lax.axis_index("tgt")
+    group = lax.axis_size("src") * tgt_count
+    member_rank = src_rank * tgt_count + tgt_rank
     shrink = LAM / (LAM + EPS)
     source_all = src_cells[0]
     dims = source_all.shape[0]
@@ -171,8 +192,14 @@
         pulled = jnp.where(live_src[None, :], pulled, 0.0)
         fate_maps = jnp.where(pair_rank == active, pulled, fate_maps)
         if section_num + 1 < pair_count:
-            passed = shifted(pulled.astype(jnp.bfloat16), "pair", -1)
-            fresh = lax.all_gather(passed, ("src", "tgt"), axis=1, tiled=True)
+            passed = pulled.astype(jnp.bfloat16)
+            if group <= 8:
+                got = jnp.stack(blocks_from_group(passed, ("src", "tgt"), group, lead="pair"))
+                order = (member_rank - jnp.arange(group, dtype=jnp.int32)) % group
+                got = jnp.take(got, order, axis=0)
+                fresh = jnp.transpose(got, (1, 0, 2)).reshape(passed.shape[0], group * rows)
+            else:
+                fresh = lax.all_gather(shifted(passed, "pair", -1), ("src", "tgt"), axis=1, tiled=True)
             handed = jnp.where(pair_rank == active - 1, fresh, handed)
     pot_all = lax.all_gather(pot_src, "tgt", axis=0, tiled=True)
     return (fate_maps[None], pot_all[None])

time: 279 us -> 303 us (1.086)
  starting transfers between devices: 5.17 us -> 32.4 us
  blocking collectives: 132 us -> 105 us
  waiting for transfers between devices: 9.65 us -> 29.1 us
    ppermute x0 -> x24, starting transfers between devices: none -> 31.1 us  [blocks_from_group(): received.append(lax.ppermute(block, names, pairs))]
    ppermute x0 -> x24, waiting for transfers between devices: none -> 29.1 us  [blocks_from_group(): received.append(lax.ppermute(block, names, pairs))]
    all_gather x3 -> x0, blocking collectives: 27.2 us -> none  [local(): fresh = lax.all_gather(passed, ('src', 'tgt'), axis=1, tiled=True)]
    ppermute x4 -> x1, waiting for transfers between devices: 9.65 us -> 0.01 us  [shifted(): return lax.ppermute(shard, axis, pairs)]
    ppermute x4 -> x1, starting transfers between devices: 5.17 us -> 1.29 us  [shifted(): return lax.ppermute(shard, axis, pairs)]
    unnamed x21 -> x42, local copies, waits for them, and re-layouts: 31 us -> 31.1 us
  transfers between devices with their start and end apart: 4 -> 25, of which waited for: 2 -> 18; matrix products, arithmetic and copies ran while one was open for 2% -> 2% of each run, Pallas kernels for 0% -> 0%
where the time goes in v2:
time: 303 us; the launch traced here: 299 us
  blocking collectives  105 us (35%)
  Pallas kernels  63 us (21%)
  local copies, waits for them, and re-layouts  35.2 us (12%)
  starting transfers between devices  32.4 us (11%)
  waiting for transfers between devices  29.1 us (10%)
  matrix products  20.1 us (7%)
  other arithmetic  12.2 us (4%)
    all_gather x8, blocking collectives, local(): every = lax.all_gather(part_lse[0], ('src', 'tgt'))  70.3 us
    pallas_call x9, Pallas kernels, sweep(): pl.pallas_call(functools.partial(sweep_kernel, do_row, do_col, emit_w, sh...  63 us
    ppermute x24, starting transfers between devices, blocks_from_group(): received.append(lax.ppermute(block, names, pairs))  31.1 us
    unnamed x42, local copies, waits for them, and re-layouts  31.1 us
    ppermute x24, waiting for transfers between devices, blocks_from_group(): received.append(lax.ppermute(block, names, pairs))  29.1 us
    dot_general x4, matrix products, local(): lax.dot_general(handed, weights, (((1,), (1,)), ((), ())), preferred_elem...  12.7 us
    all_gather x1, blocking collectives, local(): pot_all = lax.all_gather(pot_src, 'tgt', axis=0, tiled=True)  9.95 us
    all_gather x1, blocking collectives, local(): lax.all_gather(shifted(source_all, 'pair', -1), 'src', axis=1, tiled=True)  9.23 us
  transfers between devices with their start and end apart: 25, of which 18 were waited for; matrix products, arithmetic and copies ran while one was open for 2% of the time, Pallas kernels for 0%

profile of v2, /device:TPU:0, one launch (start us, length us, event | category | flops | bytes accessed | tf_op | source)
XLA Modules:
  0.0 299.5 jit_solution(1767786906762823018)
XLA Ops:
  7.2 8.9 %all_gather.37 = f32[30,4096]{1,0:T(8,128)S(1)} all-gather(f32[30,1024]{1,0:T(8,128)} %param.8), channel_id=1, replica_groups=mesh['pair'=4,'src'=2,'tgt'=4] {'tgt'}, dimensions={1}, use_global_device_ids=true | all-gather | bytes 614400 | tf_op jit(solution)/shard_map/all_gather | solution.py:145
  17.0 6.2 %all_gather.36 = bf16[40,4096]{1,0:T(8,128)(2,1)S(1)} all-gather(bf16[40,1024]{1,0:T(8,128)(2,1)S(1)} %convert_element_type.18), channel_id=1, replica_groups=mesh['pair'=4,'src'=2,'tgt'=4] {'tgt'}, dimensions={1}, use_global_device_ids=true | all-gather | bytes 409600 | tf_op jit(solution)/shard_map/all_gather | solution.py:184
  25.5 9.2 %all_gather.38 = f32[30,4096]{1,0:T(8,128)S(1)} all-gather(f32[30,2048]{1,0:T(8,128)S(1)} %collective-permute-done), channel_id=1, replica_groups=mesh['pair'=4,'src'=2,'tgt'=4] {'src'}, dimensions={1}, use_global_device_ids=true | all-gather | bytes 737280 | tf_op jit(solution)/shard_map/all_gather | solution.py:144
  34.8 7.4 %subtract_multiply_fusion.c_ref = f32[512,4096]{1,0:T(8,128)S(1)} fusion(f32[4096]{0:T(1024)S(1)} %multiply_reduce_fusion, f32[512]{0:T(512)S(1)} %fusion.23, f32[30,4096]{1,0:T(8,128)S(1)} %all_gather.37, f32[30,4096]{1,0:T(8,128)S(1)} %all_gather.38, pred[]{:T(512)S(6)} %eq.23, f32[1,30,512]{2,0,1:T(1,128)S(1)} %constant_dynamic-slice_fusion), kind=kOutput, calls=%fused_computation.3 | convolution fusion | flops 763486208 | bytes 9451521 | tf_op jit(solution)/shard_map/dot_general | solution.py:148
  42.2 2.2 shard_map.68
  45.4 9.2 %all-gather.1 = f32[8,1,4096]{2,1,0:T(1,128)S(1)} all-gather(f32[1,1,4096]{2,1,0:T(1,128)S(1)} %bitcast.145), channel_id=1, replica_groups=mesh['pair'=4,'src'=2,'tgt'=4] {'src','tgt'}, dimensions={0}, use_global_device_ids=true | all-gather | bytes 147456 | tf_op jit(solution)/shard_map/all_gather | solution.py:174
  55.5 3.4 %copy-done.1 = f32[512,4096]{1,0:T(8,128)S(1)} copy-done((f32[512,4096]{1,0:T(8,128)S(1)}, f32[512,4096]{1,0:T(8,128)}, u32[]{:S(2)}) %copy-start.1) | copy-done | bytes 8388632
  58.9 7.9 %shard_map.69 = (f32[512,1]{1,0:T(8,128)}, f32[1,4096]{1,0:T(1,128)S(1)}) custom-call(f32[512,4096]{1,0:T(8,128)S(1)} %copy-done.1, f32[1,4096]{1,0:T(1,128)S(1)} %fusion.34.b_ref, f32[512,1]{1,0:T(8,128)S(1)} %fusion.4.la_ref), custom_call_target="tpu_custom_call" | custom-call | flops 33554432 | bytes 8388608 | tf_op jit(solution)/shard_map/pallas_call | solution.py:88
  66.8 8.8 %all-gather.2 = f32[8,1,4096]{2,1,0:T(1,128)S(1)} all-gather(f32[1,1,4096]{2,1,0:T(1,128)S(1)} %bitcast.146), channel_id=1, replica_groups=mesh['pair'=4,'src'=2,'tgt'=4] {'src','tgt'}, dimensions={0}, use_global_device_ids=true | all-gather | bytes 147456 | tf_op jit(solution)/shard_map/all_gather | solution.py:174
  76.5 3.4 %copy-done.2 = f32[512,4096]{1,0:T(8,128)S(1)} copy-done((f32[512,4096]{1,0:T(8,128)S(1)}, f32[512,4096]{1,0:T(8,128)}, u32[]{:S(2)}) %copy-start.2) | copy-done | bytes 8388632
  79.9 7.9 %shard_map.70 = (f32[512,1]{1,0:T(8,128)}, f32[1,4096]{1,0:T(1,128)S(1)}) custom-call(f32[512,4096]{1,0:T(8,128)S(1)} %copy-done.2, f32[1,4096]{1,0:T(1,128)S(1)} %fusion.33.b_ref, f32[512,1]{1,0:T(8,128)S(1)} %fusion.4.la_ref), custom_call_target="tpu_custom_call" | custom-call | flops 33554432 | bytes 8388608 | tf_op jit(solution)/shard_map/pallas_call | solution.py:88
  87.9 8.8 %all-gather.3 = f32[8,1,4096]{2,1,0:T(1,128)S(1)} all-gather(f32[1,1,4096]{2,1,0:T(1,128)S(1)} %bitcast.147), channel_id=1, replica_groups=mesh['pair'=4,'src'=2,'tgt'=4] {'src','tgt'}, dimensions={0}, use_global_device_ids=true | all-gather | bytes 147456 | tf_op jit(solution)/shard_map/all_gather | solution.py:174
  97.6 3.4 %copy-done.3 = f32[512,4096]{1,0:T(8,128)S(1)} copy-done((f32[512,4096]{1,0:T(8,128)S(1)}, f32[512,4096]{1,0:T(8,128)}, u32[]{:S(2)}) %copy-start.3) | copy-done | bytes 8388632
  101.0 7.9 %shard_map.71 = (f32[512,1]{1,0:T(8,128)}, f32[1,4096]{1,0:T(1,128)S(1)}) custom-call(f32[512,4096]{1,0:T(8,128)S(1)} %copy-done.3, f32[1,4096]{1,0:T(1,128)S(1)} %fusion.32.b_ref, f32[512,1]{1,0:T(8,128)S(1)} %fusion.4.la_ref), custom_call_target="tpu_custom_call" | custom-call | flops 33554432 | bytes 8388608 | tf_op jit(solution)/shard_map/pallas_call | solution.py:88
  108.9 8.8 %all-gather.4 = f32[8,1,4096]{2,1,0:T(1,128)S(1)} all-gather(f32[1,1,4096]{2,1,0:T(1,128)S(1)} %bitcast.148), channel_id=1, replica_groups=mesh['pair'=4,'src'=2,'tgt'=4] {'src','tgt'}, dimensions={0}, use_global_device_ids=true | all-gather | bytes 147456 | tf_op jit(solution)/shard_map/all_gather | solution.py:174
  118.6 3.4 %copy-done.4 = f32[512,4096]{1,0:T(8,128)S(1)} copy-done((f32[512,4096]{1,0:T(8,128)S(1)}, f32[512,4096]{1,0:T(8,128)}, u32[]{:S(2)}) %copy-start.4) | copy-done | bytes 8388632
  122.0 7.9 %shard_map.72 = (f32[512,1]{1,0:T(8,128)}, f32[1,4096]{1,0:T(1,128)S(1)}) custom-call(f32[512,4096]{1,0:T(8,128)S(1)} %copy-done.4, f32[1,4096]{1,0:T(1,128)S(1)} %fusion.31.b_ref, f32[512,1]{1,0:T(8,128)S(1)} %fusion.4.la_ref), custom_call_target="tpu_custom_call" | custom-call | flops 33554432 | bytes 8388608 | tf_op jit(solution)/shard_map/pallas_call | solution.py:88
  129.9 8.6 %all-gather.5 = f32[8,1,4096]{2,1,0:T(1,128)S(1)} all-gather(f32[1,1,4096]{2,1,0:T(1,128)S(1)} %bitcast.149), channel_id=1, replica_groups=mesh['pair'=4,'src'=2,'tgt'=4] {'src','tgt'}, dimensions={0}, use_global_device_ids=true | all-gather | bytes 147456 | tf_op jit(solution)/shard_map/all_gather | solution.py:174
  139.4 3.4 %copy-done.5 = f32[512,4096]{1,0:T(8,128)S(1)} copy-done((f32[512,4096]{1,0:T(8,128)S(1)}, f32[512,4096]{1,0:T(8,128)}, u32[]{:S(2)}) %copy-start.5) | copy-done | bytes 8388632
  142.8 7.9 %shard_map.73 = (f32[512,1]{1,0:T(8,128)}, f32[1,4096]{1,0:T(1,128)S(1)}) custom-call(f32[512,4096]{1,0:T(8,128)S(1)} %copy-done.5, f32[1,4096]{1,0:T(1,128)S(1)} %fusion.30.b_ref, f32[512,1]{1,0:T(8,128)S(1)} %fusion.4.la_ref), custom_call_target="tpu_custom_call" | custom-call | flops 33554432 | bytes 8388608 | tf_op jit(solution)/shard_map/pallas_call | solution.py:88
  150.8 8.8 %all-gather.6 = f32[8,1,4096]{2,1,0:T(1,128)S(1)} all-gather(f32[1,1,4096]{2,1,0:T(1,128)S(1)} %bitcast.150), channel_id=1, replica_groups=mesh['pair'=4,'src'=2,'tgt'=4] {'src','tgt'}, dimensions={0}, use_global_device_ids=true | all-gather | bytes 147456 | tf_op jit(solution)/shard_map/all_gather | solution.py:174
  160.5 3.4 %copy-done.6 = f32[512,4096]{1,0:T(8,128)S(1)} copy-done((f32[512,4096]{1,0:T(8,128)S(1)}, f32[512,4096]{1,0:T(8,128)}, u32[]{:S(2)}) %copy-start.6) | copy-done | bytes 8388632
  163.8 7.9 %shard_map.74 = (f32[512,1]{1,0:T(8,128)}, f32[1,4096]{1,0:T(1,128)S(1)}) custom-call(f32[512,4096]{1,0:T(8,128)S(1)} %copy-done.6, f32[1,4096]{1,0:T(1,128)S(1)} %fusion.29.b_ref, f32[512,1]{1,0:T(8,128)S(1)} %fusion.4.la_ref), custom_call_target="tpu_custom_call" | custom-call | flops 33554432 | bytes 8388608 | tf_op jit(solution)/shard_map/pallas_call | solution.py:88
  171.8 8.6 %all-gather.7 = f32[8,1,4096]{2,1,0:T(1,128)S(1)} all-gather(f32[1,1,4096]{2,1,0:T(1,128)S(1)} %bitcast.151), channel_id=1, replica_groups=mesh['pair'=4,'src'=2,'tgt'=4] {'src','tgt'}, dimensions={0}, use_global_device_ids=true | all-gather | bytes 147456 | tf_op jit(solution)/shard_map/all_gather | solution.py:174
  181.3 3.4 %copy-done.7 = f32[512,4096]{1,0:T(8,128)S(1)} copy-done((f32[512,4096]{1,0:T(8,128)S(1)}, f32[512,4096]{1,0:T(8,128)}, u32[]{:S(2)}) %copy-start.7) | copy-done | bytes 8388632
  184.7 7.9 %shard_map.75 = (f32[512,1]{1,0:T(8,128)}, f32[1,4096]{1,0:T(1,128)S(1)}) custom-call(f32[512,4096]{1,0:T(8,128)S(1)} %copy-done.7, f32[1,4096]{1,0:T(1,128)S(1)} %fusion.28.b_ref, f32[512,1]{1,0:T(8,128)S(1)} %fusion.4.la_ref), custom_call_target="tpu_custom_call" | custom-call | flops 33554432 | bytes 8388608 | tf_op jit(solution)/shard_map/pallas_call | solution.py:88
  192.6 8.8 %all-gather.8 = f32[8,1,4096]{2,1,0:T(1,128)S(1)} all-gather(f32[1,1,4096]{2,1,0:T(1,128)S(1)} %bitcast.152), channel_id=1, replica_groups=mesh['pair'=4,'src'=2,'tgt'=4] {'src','tgt'}, dimensions={0}, use_global_device_ids=true | all-gather | bytes 147456 | tf_op jit(solution)/shard_map/all_gather | solution.py:174
  202.3 3.4 %copy-done.8 = f32[512,4096]{1,0:T(8,128)S(1)} copy-done((f32[512,4096]{1,0:T(8,128)S(1)}, f32[512,4096]{1,0:T(8,128)}, u32[]{:S(2)}) %copy-start.8) | copy-done | bytes 8388632
  205.7 5.3 %shard_map.76 = (f32[512,1]{1,0:T(8,128)S(1)}, bf16[512,4096]{1,0:T(8,128)(2,1)S(1)}) custom-call(f32[512,4096]{1,0:T(8,128)S(1)} %copy-done.8, f32[1,4096]{1,0:T(1,128)S(1)} %fusion.27.b_ref, f32[512,1]{1,0:T(8,128)S(1)} %fusion.4.la_ref), custom_call_target="tpu_custom_call" | custom-call | flops 25165824 | bytes 12582912 | tf_op jit(solution)/shard_map/pallas_call | solution.py:88
  211.0 2.0 copy-done.9
  213.0 1.4 fusion.36
  226.9 2.3 collective-permute-done.5
  229.1 1.6 collective-permute-done.6
  230.7 2.3 collective-permute-done.7
  234.8 3.6 %fusion.37 = (bf16[40,512]{1,0:T(8,128)(2,1)S(1)}, f32[40,512]{1,0:T(8,128)S(1)}) fusion(bf16[40,4096]{1,0:T(8,128)(2,1)S(1)} %broadcast_select_fusion.1, bf16[512,4096]{1,0:T(8,128)(2,1)} %copy-done.9, pred[512]{0:T(512)(128)(4,1)S(1)} %add_compare_fusion.1), kind=kOutput, calls=%fused_computation.106 | convolution fusion | flops 167813120 | bytes 4645376 | tf_op jit(solution)/shard_map/dot_general | solution.py:189
  246.2 2.0 collective-permute-done.10
  249.5 1.5 collective-permute-start.16
  251.6 2.0 collective-permute-done.13
  253.5 2.1 collective-permute-done.14
  255.7 1.4 collective-permute-done.15
  257.0 1.7 collective-permute-done.16
  259.5 3.6 %fusion.38 = (bf16[40,512]{1,0:T(8,128)(2,1)S(1)}, f32[40,512]{1,0:T(8,128)S(1)}) fusion(bf16[512,4096]{1,0:T(8,128)(2,1)} %copy-done.9, bf16[40,4096]{1,0:T(8,128)(2,1)S(1)} %bitcast.153, bf16[40,4096]{1,0:T(8,128)(2,1)S(1)} %broadcast_select_fusion.1, pred[]{:T(512)S(6)} %eq.21, pred[512]{0:T(512)(128)(4,1)S(1)} %add_compare_fusion.1), kind=kOutput, calls=%fused_computation.107 | convolution fusion | flops 167976960 | bytes 4973057 | tf_op jit(solution)/shard_map/dot_general | solution.py:189
  264.4 9.9 %all-gather = f32[2048,1]{1,0:T(8,128)S(1)} all-gather(f32[512,1]{1,0:T(8,128)S(1)} %get-tuple-element.20), channel_id=2, replica_groups=mesh['pair'=4,'src'=2,'tgt'=4] {'tgt'}, dimensions={0}, use_global_device_ids=true | all-gather | bytes 10240 | tf_op jit(solution)/shard_map/all_gather | solution.py:204
  281.8 2.1 collective-permute-done.18
  287.5 1.9 collective-permute-done.21
  289.4 2.4 collective-permute-done.22
  291.8 2.3 collective-permute-done.23
  295.3 4.2 %fusion.1 = f32[1,40,512]{2,1,0:T(8,128)} fusion(bf16[512,4096]{1,0:T(8,128)(2,1)} %copy-done.9, bf16[40,4096]{1,0:T(8,128)(2,1)S(1)} %bitcast.155, pred[]{:T(512)S(6)} %eq.20, bf16[40,4096]{1,0:T(8,128)(2,1)S(1)} %bitcast.154, bf16[40,4096]{1,0:T(8,128)(2,1)S(1)} %broadcast_select_fusion.1, pred[]{:T(512)S(6)} %eq.21, f32[40,512]{1,0:T(8,128)S(1)} %get-tuple-element.28, ...), kind=kOutput, calls=%fused_computation.9 | convolution fusion | flops 168202240 | bytes 5505540 | tf_op jit(solution)/shard_map/dot_general | solution.py:189
  (129 shorter events, 54.4 us)
Async XLA Ops:
  1.7 23.8 %collective-permute-start = (f32[30,2048]{1,0:T(8,128)S(1)}, f32[30,2048]{1,0:T(8,128)S(1)}, u32[]{:S(2)}, u32[]{:S(2)}) collective-permute-start(f32[30,2048]{1,0:T(8,128)S(1)} %bitcast.157), channel_id=1, source_target_pairs={{8,0},{16,8},{24,16},{9,1},{17,9},{25,17},{10,2},{18,10},{26,18},{... | collective-permute-start | bytes 737288 | tf_op jit(solution)/shard_map/ppermute | solution.py:106
  42.2 3.2 %copy-start = (f32[512,4096]{1,0:T(8,128)}, f32[512,4096]{1,0:T(8,128)S(1)}, u32[]{:S(2)}) copy-start(f32[512,4096]{1,0:T(8,128)S(1)} %subtract_multiply_fusion.c_ref) | copy-start | bytes 25165828
  55.5 3.4 %copy-start.1 = (f32[512,4096]{1,0:T(8,128)S(1)}, f32[512,4096]{1,0:T(8,128)}, u32[]{:S(2)}) copy-start(f32[512,4096]{1,0:T(8,128)} %copy-done) | copy-start | bytes 25165828
  76.5 3.4 %copy-start.2 = (f32[512,4096]{1,0:T(8,128)S(1)}, f32[512,4096]{1,0:T(8,128)}, u32[]{:S(2)}) copy-start(f32[512,4096]{1,0:T(8,128)} %copy-done) | copy-start | bytes 25165828
  97.6 3.4 %copy-start.3 = (f32[512,4096]{1,0:T(8,128)S(1)}, f32[512,4096]{1,0:T(8,128)}, u32[]{:S(2)}) copy-start(f32[512,4096]{1,0:T(8,128)} %copy-done) | copy-start | bytes 25165828
  118.6 3.4 %copy-start.4 = (f32[512,4096]{1,0:T(8,128)S(1)}, f32[512,4096]{1,0:T(8,128)}, u32[]{:S(2)}) copy-start(f32[512,4096]{1,0:T(8,128)} %copy-done) | copy-start | bytes 25165828
  139.4 3.4 %copy-start.5 = (f32[512,4096]{1,0:T(8,128)S(1)}, f32[512,4096]{1,0:T(8,128)}, u32[]{:S(2)}) copy-start(f32[512,4096]{1,0:T(8,128)} %copy-done) | copy-start | bytes 25165828
  160.4 3.4 %copy-start.6 = (f32[512,4096]{1,0:T(8,128)S(1)}, f32[512,4096]{1,0:T(8,128)}, u32[]{:S(2)}) copy-start(f32[512,4096]{1,0:T(8,128)} %copy-done) | copy-start | bytes 25165828
  181.3 3.4 %copy-start.7 = (f32[512,4096]{1,0:T(8,128)S(1)}, f32[512,4096]{1,0:T(8,128)}, u32[]{:S(2)}) copy-start(f32[512,4096]{1,0:T(8,128)} %copy-done) | copy-start | bytes 25165828
  202.3 3.4 %copy-start.8 = (f32[512,4096]{1,0:T(8,128)S(1)}, f32[512,4096]{1,0:T(8,128)}, u32[]{:S(2)}) copy-start(f32[512,4096]{1,0:T(8,128)} %copy-done) | copy-start | bytes 25165828
  211.0 2.0 copy-start.9
  214.4 6.5 %collective-permute-start.1 = (bf16[40,512]{1,0:T(8,128)(2,1)S(1)}, bf16[40,512]{1,0:T(8,128)(2,1)S(1)}, u32[]{:S(2)}, u32[]{:S(2)}) collective-permute-start(bf16[40,512]{1,0:T(8,128)(2,1)S(1)} %get-tuple-element.23), channel_id=1, source_target_pairs={{8,0},{9,1},{10,2},{11,3},{12,4},{13,5},{14,6},{15,7},{16,8},{17,9... | collective-permute-start | bytes 122888 | tf_op jit(solution)/shard_map/ppermute | solution.py:124
  215.7 7.5 %collective-permute-start.2 = (bf16[40,512]{1,0:T(8,128)(2,1)S(1)}, bf16[40,512]{1,0:T(8,128)(2,1)S(1)}, u32[]{:S(2)}, u32[]{:S(2)}) collective-permute-start(bf16[40,512]{1,0:T(8,128)(2,1)S(1)} %get-tuple-element.23), channel_id=1, source_target_pairs={{8,1},{9,2},{10,3},{11,4},{12,5},{13,6},{14,7},{15,0},{16,9},{17,1... | collective-permute-start | bytes 122888 | tf_op jit(solution)/shard_map/ppermute | solution.py:124
  217.0 8.5 %collective-permute-start.3 = (bf16[40,512]{1,0:T(8,128)(2,1)S(1)}, bf16[40,512]{1,0:T(8,128)(2,1)S(1)}, u32[]{:S(2)}, u32[]{:S(2)}) collective-permute-start(bf16[40,512]{1,0:T(8,128)(2,1)S(1)} %get-tuple-element.23), channel_id=1, source_target_pairs={{8,2},{9,3},{10,4},{11,5},{12,6},{13,7},{14,0},{15,1},{16,10},{17,... | collective-permute-start | bytes 122888 | tf_op jit(solution)/shard_map/ppermute | solution.py:124
  218.3 8.6 %collective-permute-start.4 = (bf16[40,512]{1,0:T(8,128)(2,1)S(1)}, bf16[40,512]{1,0:T(8,128)(2,1)S(1)}, u32[]{:S(2)}, u32[]{:S(2)}) collective-permute-start(bf16[40,512]{1,0:T(8,128)(2,1)S(1)} %get-tuple-element.23), channel_id=1, source_target_pairs={{8,3},{9,4},{10,5},{11,6},{12,7},{13,0},{14,1},{15,2},{16,11},{17,... | collective-permute-start | bytes 122888 | tf_op jit(solution)/shard_map/ppermute | solution.py:124
  219.6 9.5 %collective-permute-start.5 = (bf16[40,512]{1,0:T(8,128)(2,1)S(1)}, bf16[40,512]{1,0:T(8,128)(2,1)S(1)}, u32[]{:S(2)}, u32[]{:S(2)}) collective-permute-start(bf16[40,512]{1,0:T(8,128)(2,1)S(1)} %get-tuple-element.23), channel_id=1, source_target_pairs={{8,4},{9,5},{10,6},{11,7},{12,0},{13,1},{14,2},{15,3},{16,12},{17,... | collective-permute-start | bytes 122888 | tf_op jit(solution)/shard_map/ppermute | solution.py:124
  220.9 9.8 %collective-permute-start.6 = (bf16[40,512]{1,0:T(8,128)(2,1)S(1)}, bf16[40,512]{1,0:T(8,128)(2,1)S(1)}, u32[]{:S(2)}, u32[]{:S(2)}) collective-permute-start(bf16[40,512]{1,0:T(8,128)(2,1)S(1)} %get-tuple-element.23), channel_id=1, source_target_pairs={{8,5},{9,6},{10,7},{11,0},{12,1},{13,2},{14,3},{15,4},{16,13},{17,... | collective-permute-start | bytes 122888 | tf_op jit(solution)/shard_map/ppermute | solution.py:124
  223.3 9.8 %collective-permute-start.7 = (bf16[40,512]{1,0:T(8,128)(2,1)S(1)}, bf16[40,512]{1,0:T(8,128)(2,1)S(1)}, u32[]{:S(2)}, u32[]{:S(2)}) collective-permute-start(bf16[40,512]{1,0:T(8,128)(2,1)S(1)} %get-tuple-element.23), channel_id=1, source_target_pairs={{8,6},{9,7},{10,0},{11,1},{12,2},{13,3},{14,4},{15,5},{16,14},{17,... | collective-permute-start | bytes 122888 | tf_op jit(solution)/shard_map/ppermute | solution.py:124
  225.5 8.5 %collective-permute-start.8 = (bf16[40,512]{1,0:T(8,128)(2,1)S(1)}, bf16[40,512]{1,0:T(8,128)(2,1)S(1)}, u32[]{:S(2)}, u32[]{:S(2)}) collective-permute-start(bf16[40,512]{1,0:T(8,128)(2,1)S(1)} %get-tuple-element.23), channel_id=1, source_target_pairs={{8,7},{9,0},{10,1},{11,2},{12,3},{13,4},{14,5},{15,6},{16,15},{17,... | collective-permute-start | bytes 122888 | tf_op jit(solution)/shard_map/ppermute | solution.py:124
  238.3 6.6 %collective-permute-start.9 = (bf16[40,512]{1,0:T(8,128)(2,1)S(1)}, bf16[40,512]{1,0:T(8,128)(2,1)S(1)}, u32[]{:S(2)}, u32[]{:S(2)}) collective-permute-start(bf16[40,512]{1,0:T(8,128)(2,1)S(1)} %get-tuple-element.25), channel_id=1, source_target_pairs={{8,0},{9,1},{10,2},{11,3},{12,4},{13,5},{14,6},{15,7},{16,8},{17,9... | collective-permute-start | bytes 122888 | tf_op jit(solution)/shard_map/ppermute | solution.py:124
  239.6 8.6 %collective-permute-start.10 = (bf16[40,512]{1,0:T(8,128)(2,1)S(1)}, bf16[40,512]{1,0:T(8,128)(2,1)S(1)}, u32[]{:S(2)}, u32[]{:S(2)}) collective-permute-start(bf16[40,512]{1,0:T(8,128)(2,1)S(1)} %get-tuple-element.25), channel_id=1, source_target_pairs={{8,1},{9,2},{10,3},{11,4},{12,5},{13,6},{14,7},{15,0},{16,9},{17,1... | collective-permute-start | bytes 122888 | tf_op jit(solution)/shard_map/ppermute | solution.py:124
  240.9 8.6 %collective-permute-start.11 = (bf16[40,512]{1,0:T(8,128)(2,1)S(1)}, bf16[40,512]{1,0:T(8,128)(2,1)S(1)}, u32[]{:S(2)}, u32[]{:S(2)}) collective-permute-start(bf16[40,512]{1,0:T(8,128)(2,1)S(1)} %get-tuple-element.25), channel_id=1, source_target_pairs={{8,2},{9,3},{10,4},{11,5},{12,6},{13,7},{14,0},{15,1},{16,10},{17,... | collective-permute-start | bytes 122888 | tf_op jit(solution)/shard_map/ppermute | solution.py:124
  242.2 9.4 %collective-permute-start.12 = (bf16[40,512]{1,0:T(8,128)(2,1)S(1)}, bf16[40,512]{1,0:T(8,128)(2,1)S(1)}, u32[]{:S(2)}, u32[]{:S(2)}) collective-permute-start(bf16[40,512]{1,0:T(8,128)(2,1)S(1)} %get-tuple-element.25), channel_id=1, source_target_pairs={{8,3},{9,4},{10,5},{11,6},{12,7},{13,0},{14,1},{15,2},{16,11},{17,... | collective-permute-start | bytes 122888 | tf_op jit(solution)/shard_map/ppermute | solution.py:124
  243.5 10.0 %collective-permute-start.13 = (bf16[40,512]{1,0:T(8,128)(2,1)S(1)}, bf16[40,512]{1,0:T(8,128)(2,1)S(1)}, u32[]{:S(2)}, u32[]{:S(2)}) collective-permute-start(bf16[40,512]{1,0:T(8,128)(2,1)S(1)} %get-tuple-element.25), channel_id=1, source_target_pairs={{8,4},{9,5},{10,6},{11,7},{12,0},{13,1},{14,2},{15,3},{16,12},{17,... | collective-permute-start | bytes 122888 | tf_op jit(solution)/shard_map/ppermute | solution.py:124
  244.9 10.8 %collective-permute-start.14 = (bf16[40,512]{1,0:T(8,128)(2,1)S(1)}, bf16[40,512]{1,0:T(8,128)(2,1)S(1)}, u32[]{:S(2)}, u32[]{:S(2)}) collective-permute-start(bf16[40,512]{1,0:T(8,128)(2,1)S(1)} %get-tuple-element.25), channel_id=1, source_target_pairs={{8,5},{9,6},{10,7},{11,0},{12,1},{13,2},{14,3},{15,4},{16,13},{17,... | collective-permute-start | bytes 122888 | tf_op jit(solution)/shard_map/ppermute | solution.py:124
  248.2 8.8 %collective-permute-start.15 = (bf16[40,512]{1,0:T(8,128)(2,1)S(1)}, bf16[40,512]{1,0:T(8,128)(2,1)S(1)}, u32[]{:S(2)}, u32[]{:S(2)}) collective-permute-start(bf16[40,512]{1,0:T(8,128)(2,1)S(1)} %get-tuple-element.25), channel_id=1, source_target_pairs={{8,6},{9,7},{10,0},{11,1},{12,2},{13,3},{14,4},{15,5},{16,14},{17,... | collective-permute-start | bytes 122888 | tf_op jit(solution)/shard_map/ppermute | solution.py:124
  249.5 9.2 %collective-permute-start.16 = (bf16[40,512]{1,0:T(8,128)(2,1)S(1)}, bf16[40,512]{1,0:T(8,128)(2,1)S(1)}, u32[]{:S(2)}, u32[]{:S(2)}) collective-permute-start(bf16[40,512]{1,0:T(8,128)(2,1)S(1)} %get-tuple-element.25), channel_id=1, source_target_pairs={{8,7},{9,0},{10,1},{11,2},{12,3},{13,4},{14,5},{15,6},{16,15},{17,... | collective-permute-start | bytes 122888 | tf_op jit(solution)/shard_map/ppermute | solution.py:124
  263.1 17.4 %collective-permute-start.17 = (bf16[40,512]{1,0:T(8,128)(2,1)S(1)}, bf16[40,512]{1,0:T(8,128)(2,1)S(1)}, u32[]{:S(2)}, u32[]{:S(2)}) collective-permute-start(bf16[40,512]{1,0:T(8,128)(2,1)S(1)} %get-tuple-element.27), channel_id=1, source_target_pairs={{8,0},{9,1},{10,2},{11,3},{12,4},{13,5},{14,6},{15,7},{16,8},{17,9... | collective-permute-start | bytes 122888 | tf_op jit(solution)/shard_map/ppermute | solution.py:124
  275.3 8.7 %collective-permute-start.18 = (bf16[40,512]{1,0:T(8,128)(2,1)S(1)}, bf16[40,512]{1,0:T(8,128)(2,1)S(1)}, u32[]{:S(2)}, u32[]{:S(2)}) collective-permute-start(bf16[40,512]{1,0:T(8,128)(2,1)S(1)} %get-tuple-element.27), channel_id=1, source_target_pairs={{8,1},{9,2},{10,3},{11,4},{12,5},{13,6},{14,7},{15,0},{16,9},{17,1... | collective-permute-start | bytes 122888 | tf_op jit(solution)/shard_map/ppermute | solution.py:124
  276.6 9.6 %collective-permute-start.19 = (bf16[40,512]{1,0:T(8,128)(2,1)S(1)}, bf16[40,512]{1,0:T(8,128)(2,1)S(1)}, u32[]{:S(2)}, u32[]{:S(2)}) collective-permute-start(bf16[40,512]{1,0:T(8,128)(2,1)S(1)} %get-tuple-element.27), channel_id=1, source_target_pairs={{8,2},{9,3},{10,4},{11,5},{12,6},{13,7},{14,0},{15,1},{16,10},{17,... | collective-permute-start | bytes 122888 | tf_op jit(solution)/shard_map/ppermute | solution.py:124
  277.9 9.6 %collective-permute-start.20 = (bf16[40,512]{1,0:T(8,128)(2,1)S(1)}, bf16[40,512]{1,0:T(8,128)(2,1)S(1)}, u32[]{:S(2)}, u32[]{:S(2)}) collective-permute-start(bf16[40,512]{1,0:T(8,128)(2,1)S(1)} %get-tuple-element.27), channel_id=1, source_target_pairs={{8,3},{9,4},{10,5},{11,6},{12,7},{13,0},{14,1},{15,2},{16,11},{17,... | collective-permute-start | bytes 122888 | tf_op jit(solution)/shard_map/ppermute | solution.py:124
  279.2 10.3 %collective-permute-start.21 = (bf16[40,512]{1,0:T(8,128)(2,1)S(1)}, bf16[40,512]{1,0:T(8,128)(2,1)S(1)}, u32[]{:S(2)}, u32[]{:S(2)}) collective-permute-start(bf16[40,512]{1,0:T(8,128)(2,1)S(1)} %get-tuple-element.27), channel_id=1, source_target_pairs={{8,4},{9,5},{10,6},{11,7},{12,0},{13,1},{14,2},{15,3},{16,12},{17,... | collective-permute-start | bytes 122888 | tf_op jit(solution)/shard_map/ppermute | solution.py:124
  280.5 11.4 %collective-permute-start.22 = (bf16[40,512]{1,0:T(8,128)(2,1)S(1)}, bf16[40,512]{1,0:T(8,128)(2,1)S(1)}, u32[]{:S(2)}, u32[]{:S(2)}) collective-permute-start(bf16[40,512]{1,0:T(8,128)(2,1)S(1)} %get-tuple-element.27), channel_id=1, source_target_pairs={{8,5},{9,6},{10,7},{11,0},{12,1},{13,2},{14,3},{15,4},{16,13},{17,... | collective-permute-start | bytes 122888 | tf_op jit(solution)/shard_map/ppermute | solution.py:124
  283.9 10.2 %collective-permute-start.23 = (bf16[40,512]{1,0:T(8,128)(2,1)S(1)}, bf16[40,512]{1,0:T(8,128)(2,1)S(1)}, u32[]{:S(2)}, u32[]{:S(2)}) collective-permute-start(bf16[40,512]{1,0:T(8,128)(2,1)S(1)} %get-tuple-element.27), channel_id=1, source_target_pairs={{8,6},{9,7},{10,0},{11,1},{12,2},{13,3},{14,4},{15,5},{16,14},{17,... | collective-permute-start | bytes 122888 | tf_op jit(solution)/shard_map/ppermute | solution.py:124
  286.2 8.4 %collective-permute-start.24 = (bf16[40,512]{1,0:T(8,128)(2,1)S(1)}, bf16[40,512]{1,0:T(8,128)(2,1)S(1)}, u32[]{:S(2)}, u32[]{:S(2)}) collective-permute-start(bf16[40,512]{1,0:T(8,128)(2,1)S(1)} %get-tuple-element.27), channel_id=1, source_target_pairs={{8,7},{9,0},{10,1},{11,2},{12,3},{13,4},{14,5},{15,6},{16,15},{17,... | collective-permute-start | bytes 122888 | tf_op jit(solution)/shard_map/ppermute | solution.py:124

commit v3 on v1

--- a/solution.py
+++ b/solution.py
@@ -120,9 +120,27 @@
     row_off = tgt_rank * rows
     is_last = pair_rank == pair_count - 1
     source_pos = lax.dynamic_slice_in_dim(source_all, row_off, rows, 1)
-    arrived = lax.all_gather(shifted(source_all, "pair", -1), "src", axis=1, tiled=True)
-    final_all = lax.all_gather(final_cells, "tgt", axis=1, tiled=True)
-    target_pos = jnp.where(is_last, final_all, arrived)
+    group = lax.axis_size("src") * tgt_count
+    src_count = lax.axis_size("src")
+    arrived = shifted(source_all, "pair", -1)
+    mine_next = lax.dynamic_slice_in_dim(arrived, row_off, rows, 1)
+    fin_width = final_cells.shape[1]
+    mine_final = lax.dynamic_slice_in_dim(final_cells, (src_rank * rows) % fin_width, rows, 1)
+    piece = jnp.where(is_last, mine_final, mine_next)
+    pieces = lax.all_gather(piece, ("src", "tgt"))
+    per_fin = fin_width // rows
+    final_order = [
+        (b % per_fin) * tgt_count + b // per_fin if per_fin == src_count else b for b in range(group)
+    ]
+    if per_fin == src_count:
+        final_pieces = pieces[jnp.array(final_order, dtype=jnp.int32)]
+        pieces = jnp.where(is_last, final_pieces, pieces)
+        target_pos = jnp.transpose(pieces, (1, 0, 2)).reshape(dims, group * rows)
+    else:
+        final_all = lax.all_gather(final_cells, "tgt", axis=1, tiled=True)
+        target_pos = jnp.where(
+            is_last, final_all, jnp.transpose(pieces, (1, 0, 2)).reshape(dims, group * rows)
+        )
     cols = target_pos.shape[1]
     cross = lax.dot_general(
         source_pos,
@@ -159,7 +177,7 @@
             pot_col, part_lse = sweep(scaled_cost, col_shift, log_mass_a, shrink, True, True, False)
         else:
             pot_col, weights = sweep(scaled_cost, col_shift, log_mass_a, shrink, True, False, True)
-    pot_src = pot_col[:, 0]
+    pot_src = pot_col.reshape(rows)
     final_handed = lax.all_gather(final_fates.astype(jnp.bfloat16), "tgt", axis=1, tiled=True)
     handed = jnp.where(is_last, final_handed, jnp.zeros(final_handed.shape, jnp.bfloat16))
     fate_maps = jnp.zeros((final_fates.shape[0], rows), jnp.float32)

time: 279 us -> 275 us (0.986)
  blocking collectives: 132 us -> 125 us
    all_gather x2 -> x1, blocking collectives: 18.1 us -> 9.83 us  [local(): pieces = lax.all_gather(piece, ('src', 'tgt'))]
    unnamed x21 -> x24, local copies, waits for them, and re-layouts: 31 us -> 31.4 us
  transfers between devices with their start and end apart: 4 -> 4, of which waited for: 2 -> 2; matrix products, arithmetic and copies ran while one was open for 2% -> 3% of each run, Pallas kernels for 0% -> 0%
where the time goes in v3:
time: 275 us; the launch traced here: 273 us
  blocking collectives  125 us (45%)
  Pallas kernels  63 us (23%)
  local copies, waits for them, and re-layouts  34.5 us (13%)
  matrix products  20.1 us (7%)
  other arithmetic  13.4 us (5%)
  waiting for transfers between devices  9.91 us (4%)
  starting transfers between devices  5.17 us (2%)
    all_gather x8, blocking collectives, local(): every = lax.all_gather(part_lse[0], ('src', 'tgt'))  69.8 us
    pallas_call x9, Pallas kernels, sweep(): pl.pallas_call(functools.partial(sweep_kernel, do_row, do_col, emit_w, sh...  63 us
    unnamed x24, local copies, waits for them, and re-layouts  31.4 us
    all_gather x3, blocking collectives, local(): fresh = lax.all_gather(passed, ('src', 'tgt'), axis=1, tiled=True)  27.3 us
    dot_general x4, matrix products, local(): lax.dot_general(handed, weights, (((1,), (1,)), ((), ())), preferred_elem...  12.7 us
    all_gather x1, blocking collectives, local(): pot_all = lax.all_gather(pot_src, 'tgt', axis=0, tiled=True)  10.1 us
    ppermute x4, waiting for transfers between devices, shifted(): return lax.ppermute(shard, axis, pairs)  9.91 us
    all_gather x1, blocking collectives, local(): pieces = lax.all_gather(piece, ('src', 'tgt'))  9.83 us
  transfers between devices with their start and end apart: 4, of which 2 were waited for; matrix products, arithmetic and copies ran while one was open for 3% of the time, Pallas kernels for 0%

profile of v3, /device:TPU:0, one launch (start us, length us, event | category | flops | bytes accessed | tf_op | source)
XLA Modules:
  0.0 273.4 jit_solution(752208404585688011)
XLA Ops:
  0.6 1.0 copy.38
  1.7 1.3 collective-permute-start
  4.5 1.3 fusion.34
  7.9 0.9 convert_element_type.18
  8.8 7.6 %all_gather.45 = bf16[40,4096]{1,0:T(8,128)(2,1)S(1)} all-gather(bf16[40,1024]{1,0:T(8,128)(2,1)S(1)} %convert_element_type.18), channel_id=1, replica_groups=mesh['pair'=4,'src'=2,'tgt'=4] {'tgt'}, dimensions={1}, use_global_device_ids=true | all-gather | bytes 409600 | tf_op jit(solution)/shard_map/all_gather | solution.py:181
  19.5 9.8 %all-gather.2 = f32[8,30,512]{2,1,0:T(8,128)S(1)} all-gather(f32[1,30,512]{2,1,0:T(8,128)S(1)} %select_bitcast_fusion.1), channel_id=2, replica_groups=mesh['pair'=4,'src'=2,'tgt'=4] {'src','tgt'}, dimensions={0}, use_global_device_ids=true | all-gather | bytes 552960 | tf_op jit(solution)/shard_map/all_gather | solution.py:130
  30.7 7.4 %subtract_multiply_fusion.c_ref = f32[512,4096]{1,0:T(8,128)S(1)} fusion(f32[30,4096]{1,0:T(8,128)S(1)} %bitcast.104, f32[4096]{0:T(1024)S(1)} %bitcast.107, f32[512]{0:T(512)S(1)} %fusion.23, f32[1,30,512]{2,0,1:T(1,128)S(1)} %constant_dynamic-slice_fusion), kind=kOutput, calls=%fused_computation.1 | convolution fusion | flops 763363328 | bytes 8960000 | tf_op jit(solution)/shard_map/dot_general | solution.py:145
  38.2 2.2 shard_map.77
  40.4 1.0 copy-done
  41.4 9.0 %all-gather.3 = f32[8,1,4096]{2,1,0:T(1,128)S(1)} all-gather(f32[1,1,4096]{2,1,0:T(1,128)S(1)} %bitcast.96), channel_id=1, replica_groups=mesh['pair'=4,'src'=2,'tgt'=4] {'src','tgt'}, dimensions={0}, use_global_device_ids=true | all-gather | bytes 147456 | tf_op jit(solution)/shard_map/all_gather | solution.py:171
  51.3 3.4 %copy-done.1 = f32[512,4096]{1,0:T(8,128)S(1)} copy-done((f32[512,4096]{1,0:T(8,128)S(1)}, f32[512,4096]{1,0:T(8,128)}, u32[]{:S(2)}) %copy-start.1) | copy-done | bytes 8388632
  54.7 7.9 %shard_map.78 = (f32[512,1]{1,0:T(8,128)}, f32[1,4096]{1,0:T(1,128)S(1)}) custom-call(f32[512,4096]{1,0:T(8,128)S(1)} %copy-done.1, f32[1,4096]{1,0:T(1,128)S(1)} %fusion.33.b_ref, f32[512,1]{1,0:T(8,128)S(1)} %fusion.4.la_ref), custom_call_target="tpu_custom_call" | custom-call | flops 33554432 | bytes 8388608 | tf_op jit(solution)/shard_map/pallas_call | solution.py:88
  62.6 8.5 %all-gather.4 = f32[8,1,4096]{2,1,0:T(1,128)S(1)} all-gather(f32[1,1,4096]{2,1,0:T(1,128)S(1)} %bitcast.97), channel_id=1, replica_groups=mesh['pair'=4,'src'=2,'tgt'=4] {'src','tgt'}, dimensions={0}, use_global_device_ids=true | all-gather | bytes 147456 | tf_op jit(solution)/shard_map/all_gather | solution.py:171
  72.1 3.4 %copy-done.2 = f32[512,4096]{1,0:T(8,128)S(1)} copy-done((f32[512,4096]{1,0:T(8,128)S(1)}, f32[512,4096]{1,0:T(8,128)}, u32[]{:S(2)}) %copy-start.2) | copy-done | bytes 8388632
  75.5 7.9 %shard_map.79 = (f32[512,1]{1,0:T(8,128)}, f32[1,4096]{1,0:T(1,128)S(1)}) custom-call(f32[512,4096]{1,0:T(8,128)S(1)} %copy-done.2, f32[1,4096]{1,0:T(1,128)S(1)} %fusion.32.b_ref, f32[512,1]{1,0:T(8,128)S(1)} %fusion.4.la_ref), custom_call_target="tpu_custom_call" | custom-call | flops 33554432 | bytes 8388608 | tf_op jit(solution)/shard_map/pallas_call | solution.py:88
  83.4 9.0 %all-gather.5 = f32[8,1,4096]{2,1,0:T(1,128)S(1)} all-gather(f32[1,1,4096]{2,1,0:T(1,128)S(1)} %bitcast.98), channel_id=1, replica_groups=mesh['pair'=4,'src'=2,'tgt'=4] {'src','tgt'}, dimensions={0}, use_global_device_ids=true | all-gather | bytes 147456 | tf_op jit(solution)/shard_map/all_gather | solution.py:171
  93.4 3.4 %copy-done.3 = f32[512,4096]{1,0:T(8,128)S(1)} copy-done((f32[512,4096]{1,0:T(8,128)S(1)}, f32[512,4096]{1,0:T(8,128)}, u32[]{:S(2)}) %copy-start.3) | copy-done | bytes 8388632
  96.8 7.9 %shard_map.80 = (f32[512,1]{1,0:T(8,128)}, f32[1,4096]{1,0:T(1,128)S(1)}) custom-call(f32[512,4096]{1,0:T(8,128)S(1)} %copy-done.3, f32[1,4096]{1,0:T(1,128)S(1)} %fusion.31.b_ref, f32[512,1]{1,0:T(8,128)S(1)} %fusion.4.la_ref), custom_call_target="tpu_custom_call" | custom-call | flops 33554432 | bytes 8388608 | tf_op jit(solution)/shard_map/pallas_call | solution.py:88
  104.7 8.4 %all-gather.6 = f32[8,1,4096]{2,1,0:T(1,128)S(1)} all-gather(f32[1,1,4096]{2,1,0:T(1,128)S(1)} %bitcast.99), channel_id=1, replica_groups=mesh['pair'=4,'src'=2,'tgt'=4] {'src','tgt'}, dimensions={0}, use_global_device_ids=true | all-gather | bytes 147456 | tf_op jit(solution)/shard_map/all_gather | solution.py:171
  114.0 3.4 %copy-done.4 = f32[512,4096]{1,0:T(8,128)S(1)} copy-done((f32[512,4096]{1,0:T(8,128)S(1)}, f32[512,4096]{1,0:T(8,128)}, u32[]{:S(2)}) %copy-start.4) | copy-done | bytes 8388632
  117.4 7.9 %shard_map.81 = (f32[512,1]{1,0:T(8,128)}, f32[1,4096]{1,0:T(1,128)S(1)}) custom-call(f32[512,4096]{1,0:T(8,128)S(1)} %copy-done.4, f32[1,4096]{1,0:T(1,128)S(1)} %fusion.30.b_ref, f32[512,1]{1,0:T(8,128)S(1)} %fusion.4.la_ref), custom_call_target="tpu_custom_call" | custom-call | flops 33554432 | bytes 8388608 | tf_op jit(solution)/shard_map/pallas_call | solution.py:88
  125.3 9.0 %all-gather.7 = f32[8,1,4096]{2,1,0:T(1,128)S(1)} all-gather(f32[1,1,4096]{2,1,0:T(1,128)S(1)} %bitcast.100), channel_id=1, replica_groups=mesh['pair'=4,'src'=2,'tgt'=4] {'src','tgt'}, dimensions={0}, use_global_device_ids=true | all-gather | bytes 147456 | tf_op jit(solution)/shard_map/all_gather | solution.py:171
  135.2 3.4 %copy-done.5 = f32[512,4096]{1,0:T(8,128)S(1)} copy-done((f32[512,4096]{1,0:T(8,128)S(1)}, f32[512,4096]{1,0:T(8,128)}, u32[]{:S(2)}) %copy-start.5) | copy-done | bytes 8388632
  138.6 7.9 %shard_map.82 = (f32[512,1]{1,0:T(8,128)}, f32[1,4096]{1,0:T(1,128)S(1)}) custom-call(f32[512,4096]{1,0:T(8,128)S(1)} %copy-done.5, f32[1,4096]{1,0:T(1,128)S(1)} %fusion.29.b_ref, f32[512,1]{1,0:T(8,128)S(1)} %fusion.4.la_ref), custom_call_target="tpu_custom_call" | custom-call | flops 33554432 | bytes 8388608 | tf_op jit(solution)/shard_map/pallas_call | solution.py:88
  146.5 8.4 %all-gather.8 = f32[8,1,4096]{2,1,0:T(1,128)S(1)} all-gather(f32[1,1,4096]{2,1,0:T(1,128)S(1)} %bitcast.101), channel_id=1, replica_groups=mesh['pair'=4,'src'=2,'tgt'=4] {'src','tgt'}, dimensions={0}, use_global_device_ids=true | all-gather | bytes 147456 | tf_op jit(solution)/shard_map/all_gather | solution.py:171
  155.8 3.4 %copy-done.6 = f32[512,4096]{1,0:T(8,128)S(1)} copy-done((f32[512,4096]{1,0:T(8,128)S(1)}, f32[512,4096]{1,0:T(8,128)}, u32[]{:S(2)}) %copy-start.6) | copy-done | bytes 8388632
  159.2 7.9 %shard_map.83 = (f32[512,1]{1,0:T(8,128)}, f32[1,4096]{1,0:T(1,128)S(1)}) custom-call(f32[512,4096]{1,0:T(8,128)S(1)} %copy-done.6, f32[1,4096]{1,0:T(1,128)S(1)} %fusion.28.b_ref, f32[512,1]{1,0:T(8,128)S(1)} %fusion.4.la_ref), custom_call_target="tpu_custom_call" | custom-call | flops 33554432 | bytes 8388608 | tf_op jit(solution)/shard_map/pallas_call | solution.py:88
  167.1 9.0 %all-gather.9 = f32[8,1,4096]{2,1,0:T(1,128)S(1)} all-gather(f32[1,1,4096]{2,1,0:T(1,128)S(1)} %bitcast.102), channel_id=1, replica_groups=mesh['pair'=4,'src'=2,'tgt'=4] {'src','tgt'}, dimensions={0}, use_global_device_ids=true | all-gather | bytes 147456 | tf_op jit(solution)/shard_map/all_gather | solution.py:171
  177.1 3.4 %copy-done.7 = f32[512,4096]{1,0:T(8,128)S(1)} copy-done((f32[512,4096]{1,0:T(8,128)S(1)}, f32[512,4096]{1,0:T(8,128)}, u32[]{:S(2)}) %copy-start.7) | copy-done | bytes 8388632
  180.5 7.9 %shard_map.84 = (f32[512,1]{1,0:T(8,128)}, f32[1,4096]{1,0:T(1,128)S(1)}) custom-call(f32[512,4096]{1,0:T(8,128)S(1)} %copy-done.7, f32[1,4096]{1,0:T(1,128)S(1)} %fusion.27.b_ref, f32[512,1]{1,0:T(8,128)S(1)} %fusion.4.la_ref), custom_call_target="tpu_custom_call" | custom-call | flops 33554432 | bytes 8388608 | tf_op jit(solution)/shard_map/pallas_call | solution.py:88
  188.4 8.4 %all-gather.10 = f32[8,1,4096]{2,1,0:T(1,128)S(1)} all-gather(f32[1,1,4096]{2,1,0:T(1,128)S(1)} %bitcast.103), channel_id=1, replica_groups=mesh['pair'=4,'src'=2,'tgt'=4] {'src','tgt'}, dimensions={0}, use_global_device_ids=true | all-gather | bytes 147456 | tf_op jit(solution)/shard_map/all_gather | solution.py:171
  197.7 3.4 %copy-done.8 = f32[512,4096]{1,0:T(8,128)S(1)} copy-done((f32[512,4096]{1,0:T(8,128)S(1)}, f32[512,4096]{1,0:T(8,128)}, u32[]{:S(2)}) %copy-start.8) | copy-done | bytes 8388632
  201.1 5.3 %shard_map.85 = (f32[512,1]{1,0:T(8,128)S(1)}, bf16[512,4096]{1,0:T(8,128)(2,1)S(1)}) custom-call(f32[512,4096]{1,0:T(8,128)S(1)} %copy-done.8, f32[1,4096]{1,0:T(1,128)S(1)} %fusion.26.b_ref, f32[512,1]{1,0:T(8,128)S(1)} %fusion.4.la_ref), custom_call_target="tpu_custom_call" | custom-call | flops 25165824 | bytes 12582912 | tf_op jit(solution)/shard_map/pallas_call | solution.py:88
  206.4 2.0 copy-done.9
  208.4 1.4 fusion.35
  209.8 1.3 collective-permute-start.1
  211.1 5.3 %collective-permute-done.1 = bf16[40,512]{1,0:T(8,128)(2,1)S(1)} collective-permute-done((bf16[40,512]{1,0:T(8,128)(2,1)S(1)}, bf16[40,512]{1,0:T(8,128)(2,1)S(1)}, u32[]{:S(2)}, u32[]{:S(2)}) %collective-permute-start.1) | collective-permute-done | bytes 40992 | tf_op jit(solution)/shard_map/ppermute | solution.py:106
  216.4 9.5 %all_gather.56 = bf16[40,4096]{1,0:T(8,128)(2,1)S(1)} all-gather(bf16[40,512]{1,0:T(8,128)(2,1)S(1)} %collective-permute-done.1), channel_id=1, replica_groups=mesh['pair'=4,'src'=2,'tgt'=4] {'src','tgt'}, dimensions={1}, use_global_device_ids=true | all-gather | bytes 368640 | tf_op jit(solution)/shard_map/all_gather | solution.py:193
  225.9 3.6 %fusion.36 = (bf16[40,512]{1,0:T(8,128)(2,1)S(1)}, f32[40,512]{1,0:T(8,128)S(1)}) fusion(bf16[40,4096]{1,0:T(8,128)(2,1)S(1)} %broadcast_select_fusion.1, bf16[512,4096]{1,0:T(8,128)(2,1)} %copy-done.9, pred[512]{0:T(512)(128)(4,1)S(1)} %add_compare_fusion.1), kind=kOutput, calls=%fused_computation.72 | convolution fusion | flops 167813120 | bytes 4645376 | tf_op jit(solution)/shard_map/dot_general | solution.py:186
  229.5 1.3 collective-permute-start.2
  230.8 4.6 %collective-permute-done.2 = bf16[40,512]{1,0:T(8,128)(2,1)S(1)} collective-permute-done((bf16[40,512]{1,0:T(8,128)(2,1)S(1)}, bf16[40,512]{1,0:T(8,128)(2,1)S(1)}, u32[]{:S(2)}, u32[]{:S(2)}) %collective-permute-start.2) | collective-permute-done | bytes 40992 | tf_op jit(solution)/shard_map/ppermute | solution.py:106
  235.4 8.6 %all_gather.57 = bf16[40,4096]{1,0:T(8,128)(2,1)S(1)} all-gather(bf16[40,512]{1,0:T(8,128)(2,1)S(1)} %collective-permute-done.2), channel_id=1, replica_groups=mesh['pair'=4,'src'=2,'tgt'=4] {'src','tgt'}, dimensions={1}, use_global_device_ids=true | all-gather | bytes 368640 | tf_op jit(solution)/shard_map/all_gather | solution.py:193
  244.0 3.6 %fusion.37 = (bf16[40,512]{1,0:T(8,128)(2,1)S(1)}, f32[40,512]{1,0:T(8,128)S(1)}) fusion(bf16[512,4096]{1,0:T(8,128)(2,1)} %copy-done.9, bf16[40,4096]{1,0:T(8,128)(2,1)S(1)} %all_gather.57, bf16[40,4096]{1,0:T(8,128)(2,1)S(1)} %broadcast_select_fusion.1, pred[]{:T(512)S(6)} %eq.19, pred[512]{0:T(512)(128)(4,1)S(1)} %add_compare_fusion.1), kind=kOutput, calls=%fused_computation.73 | convolution fusion | flops 167976960 | bytes 4973057 | tf_op jit(solution)/shard_map/dot_general | solution.py:186
  247.6 1.3 collective-permute-start.3
  248.9 10.1 %all-gather.1 = f32[2048,1]{1,0:T(8,128)S(1)} all-gather(f32[512,1]{1,0:T(8,128)S(1)} %get-tuple-element.19), channel_id=3, replica_groups=mesh['pair'=4,'src'=2,'tgt'=4] {'tgt'}, dimensions={0}, use_global_device_ids=true | all-gather | bytes 10240 | tf_op jit(solution)/shard_map/all_gather | solution.py:195
  259.0 0.9 reduce.9
  259.9 9.3 %all_gather.58 = bf16[40,4096]{1,0:T(8,128)(2,1)S(1)} all-gather(bf16[40,512]{1,0:T(8,128)(2,1)S(1)} %collective-permute-done.3), channel_id=1, replica_groups=mesh['pair'=4,'src'=2,'tgt'=4] {'src','tgt'}, dimensions={1}, use_global_device_ids=true | all-gather | bytes 368640 | tf_op jit(solution)/shard_map/all_gather | solution.py:193
  269.2 4.2 %fusion.1 = f32[1,40,512]{2,1,0:T(8,128)} fusion(bf16[512,4096]{1,0:T(8,128)(2,1)} %copy-done.9, bf16[40,4096]{1,0:T(8,128)(2,1)S(1)} %all_gather.58, pred[]{:T(512)S(6)} %eq.18, bf16[40,4096]{1,0:T(8,128)(2,1)S(1)} %all_gather.57, bf16[40,4096]{1,0:T(8,128)(2,1)S(1)} %broadcast_select_fusion.1, pred[]{:T(512)S(6)} %eq.19, ...), kind=kOutput, calls=%fused_computation.7 | convolution fusion | flops 168202240 | bytes 5505540 | tf_op jit(solution)/shard_map/dot_general | solution.py:186
  (60 shorter events, 13.8 us)
Async XLA Ops:
  1.7 17.0 %collective-permute-start = (f32[30,2048]{1,0:T(8,128)S(1)}, f32[30,2048]{1,0:T(8,128)S(1)}, u32[]{:S(2)}, u32[]{:S(2)}) collective-permute-start(f32[30,2048]{1,0:T(8,128)S(1)} %bitcast.106), channel_id=1, source_target_pairs={{8,0},{16,8},{24,16},{9,1},{17,9},{25,17},{10,2},{18,10},{26,18},{... | collective-permute-start | bytes 737288 | tf_op jit(solution)/shard_map/ppermute | solution.py:106
  38.2 3.2 %copy-start = (f32[512,4096]{1,0:T(8,128)}, f32[512,4096]{1,0:T(8,128)S(1)}, u32[]{:S(2)}) copy-start(f32[512,4096]{1,0:T(8,128)S(1)} %subtract_multiply_fusion.c_ref) | copy-start | bytes 25165828
  51.3 3.4 %copy-start.1 = (f32[512,4096]{1,0:T(8,128)S(1)}, f32[512,4096]{1,0:T(8,128)}, u32[]{:S(2)}) copy-start(f32[512,4096]{1,0:T(8,128)} %copy-done) | copy-start | bytes 25165828
  72.1 3.4 %copy-start.2 = (f32[512,4096]{1,0:T(8,128)S(1)}, f32[512,4096]{1,0:T(8,128)}, u32[]{:S(2)}) copy-start(f32[512,4096]{1,0:T(8,128)} %copy-done) | copy-start | bytes 25165828
  93.4 3.4 %copy-start.3 = (f32[512,4096]{1,0:T(8,128)S(1)}, f32[512,4096]{1,0:T(8,128)}, u32[]{:S(2)}) copy-start(f32[512,4096]{1,0:T(8,128)} %copy-done) | copy-start | bytes 25165828
  114.0 3.4 %copy-start.4 = (f32[512,4096]{1,0:T(8,128)S(1)}, f32[512,4096]{1,0:T(8,128)}, u32[]{:S(2)}) copy-start(f32[512,4096]{1,0:T(8,128)} %copy-done) | copy-start | bytes 25165828
  135.2 3.4 %copy-start.5 = (f32[512,4096]{1,0:T(8,128)S(1)}, f32[512,4096]{1,0:T(8,128)}, u32[]{:S(2)}) copy-start(f32[512,4096]{1,0:T(8,128)} %copy-done) | copy-start | bytes 25165828
  155.8 3.4 %copy-start.6 = (f32[512,4096]{1,0:T(8,128)S(1)}, f32[512,4096]{1,0:T(8,128)}, u32[]{:S(2)}) copy-start(f32[512,4096]{1,0:T(8,128)} %copy-done) | copy-start | bytes 25165828
  177.1 3.4 %copy-start.7 = (f32[512,4096]{1,0:T(8,128)S(1)}, f32[512,4096]{1,0:T(8,128)}, u32[]{:S(2)}) copy-start(f32[512,4096]{1,0:T(8,128)} %copy-done) | copy-start | bytes 25165828
  197.7 3.4 %copy-start.8 = (f32[512,4096]{1,0:T(8,128)S(1)}, f32[512,4096]{1,0:T(8,128)}, u32[]{:S(2)}) copy-start(f32[512,4096]{1,0:T(8,128)} %copy-done) | copy-start | bytes 25165828
  206.4 2.0 copy-start.9
  209.8 6.6 %collective-permute-start.1 = (bf16[40,512]{1,0:T(8,128)(2,1)S(1)}, bf16[40,512]{1,0:T(8,128)(2,1)S(1)}, u32[]{:S(2)}, u32[]{:S(2)}) collective-permute-start(bf16[40,512]{1,0:T(8,128)(2,1)S(1)} %get-tuple-element.24), channel_id=1, source_target_pairs={{8,0},{16,8},{24,16},{9,1},{17,9},{25,17},{10,2},{18,10},{26,18},{... | collective-permute-start | bytes 122888 | tf_op jit(solution)/shard_map/ppermute | solution.py:106
  229.5 5.9 %collective-permute-start.2 = (bf16[40,512]{1,0:T(8,128)(2,1)S(1)}, bf16[40,512]{1,0:T(8,128)(2,1)S(1)}, u32[]{:S(2)}, u32[]{:S(2)}) collective-permute-start(bf16[40,512]{1,0:T(8,128)(2,1)S(1)} %get-tuple-element.26), channel_id=1, source_target_pairs={{8,0},{16,8},{24,16},{9,1},{17,9},{25,17},{10,2},{18,10},{26,18},{... | collective-permute-start | bytes 122888 | tf_op jit(solution)/shard_map/ppermute | solution.py:106
  247.6 12.4 %collective-permute-start.3 = (bf16[40,512]{1,0:T(8,128)(2,1)S(1)}, bf16[40,512]{1,0:T(8,128)(2,1)S(1)}, u32[]{:S(2)}, u32[]{:S(2)}) collective-permute-start(bf16[40,512]{1,0:T(8,128)(2,1)S(1)} %get-tuple-element.28), channel_id=1, source_target_pairs={{8,0},{16,8},{24,16},{9,1},{17,9},{25,17},{10,2},{18,10},{26,18},{... | collective-permute-start | bytes 122888 | tf_op jit(solution)/shard_map/ppermute | solution.py:106

commit v4 on v3

--- a/solution.py
+++ b/solution.py
@@ -178,7 +178,11 @@
         else:
             pot_col, weights = sweep(scaled_cost, col_shift, log_mass_a, shrink, True, False, True)
     pot_src = pot_col.reshape(rows)
-    final_handed = lax.all_gather(final_fates.astype(jnp.bfloat16), "tgt", axis=1, tiled=True)
+    fin_fates = final_fates.astype(jnp.bfloat16)
+    spread = lax.dynamic_update_slice_in_dim(
+        jnp.zeros((fin_fates.shape[0], fin_width * tgt_count), jnp.bfloat16), fin_fates, tgt_rank * fin_width, 1
+    )
+    final_handed = lax.psum(spread, "tgt")
     handed = jnp.where(is_last, final_handed, jnp.zeros(final_handed.shape, jnp.bfloat16))
     fate_maps = jnp.zeros((final_fates.shape[0], rows), jnp.float32)
     for section_num in range(pair_count):
@@ -192,7 +196,8 @@
             passed = shifted(pulled.astype(jnp.bfloat16), "pair", -1)
             fresh = lax.all_gather(passed, ("src", "tgt"), axis=1, tiled=True)
             handed = jnp.where(pair_rank == active - 1, fresh, handed)
-    pot_all = lax.all_gather(pot_src, "tgt", axis=0, tiled=True)
+    pot_spread = lax.dynamic_update_slice_in_dim(jnp.zeros((src_width,), jnp.float32), pot_src, row_off, 0)
+    pot_all = lax.psum(pot_spread, "tgt")
     return (fate_maps[None], pot_all[None])
 
 

time: 275 us -> 281 us (1.022)
  between operations: 2.54 us -> 15.9 us
  blocking collectives: 125 us -> 115 us
    all_gather x2 -> x0, blocking collectives: 17.7 us -> none  [the longest x1 10.1 us: local(): pot_all = lax.all_gather(pot_src, 'tgt', axis=0, tiled=True)]
    psum x0 -> x1, blocking collectives: none -> 7.7 us  [local(): pot_all = lax.psum(pot_spread, 'tgt')]
    unnamed x24 -> x28, local copies, waits for them, and re-layouts: 31.4 us -> 32.1 us
  transfers between devices with their start and end apart: 4 -> 5, of which waited for: 2 -> 3; matrix products, arithmetic and copies ran while one was open for 3% -> 8% of each run, Pallas kernels for 0% -> 23%
where the time goes in v4:
time: 281 us; the launch traced here: 280 us
  blocking collectives  115 us (41%)
  Pallas kernels  63.1 us (22%)
  local copies, waits for them, and re-layouts  35.3 us (13%)
  matrix products  22.3 us (8%)
  between operations  15.9 us (6%)
  other arithmetic  12.7 us (5%)
  waiting for transfers between devices  10.4 us (4%)
  starting transfers between devices  5.21 us (2%)
    all_gather x8, blocking collectives, local(): every = lax.all_gather(part_lse[0], ('src', 'tgt'))  69.8 us
    pallas_call x9, Pallas kernels, sweep(): pl.pallas_call(functools.partial(sweep_kernel, do_row, do_col, emit_w, sh...  63.1 us
    unnamed x28, local copies, waits for them, and re-layouts  32.1 us
    all_gather x3, blocking collectives, local(): fresh = lax.all_gather(passed, ('src', 'tgt'), axis=1, tiled=True)  26.6 us
    dot_general x4, matrix products, local(): lax.dot_general(handed, weights, (((1,), (1,)), ((), ())), preferred_elem...  14.9 us
    all_gather x1, blocking collectives, local(): pieces = lax.all_gather(piece, ('src', 'tgt'))  10.9 us
    ppermute x4, waiting for transfers between devices, shifted(): return lax.ppermute(shard, axis, pairs)  10.4 us
    psum x1, blocking collectives, local(): pot_all = lax.psum(pot_spread, 'tgt')  7.7 us
  transfers between devices with their start and end apart: 5, of which 3 were waited for; matrix products, arithmetic and copies ran while one was open for 8% of the time, Pallas kernels for 23%

profile of v4, /device:TPU:0, one launch (start us, length us, event | category | flops | bytes accessed | tf_op | source)
XLA Modules:
  0.0 280.0 jit_solution(16458972010518440656)
XLA Ops:
  7.2 1.0 copy.38
  8.2 1.3 collective-permute-start
  9.6 0.9 convert_dynamic-update-slice_fusion
  12.8 1.3 fusion.34
  18.4 1.1 collective-permute-done
  19.5 0.9 select_bitcast_fusion.1
  20.4 10.9 %all-gather.1 = f32[8,30,512]{2,1,0:T(8,128)S(1)} all-gather(f32[1,30,512]{2,1,0:T(8,128)S(1)} %select_bitcast_fusion.1), channel_id=2, replica_groups=mesh['pair'=4,'src'=2,'tgt'=4] {'src','tgt'}, dimensions={0}, use_global_device_ids=true | all-gather | bytes 552960 | tf_op jit(solution)/shard_map/all_gather | solution.py:130
  32.7 7.4 %subtract_multiply_fusion.c_ref = f32[512,4096]{1,0:T(8,128)S(1)} fusion(f32[30,4096]{1,0:T(8,128)S(1)} %bitcast.104, f32[4096]{0:T(1024)S(1)} %bitcast.107, f32[512]{0:T(512)S(1)} %fusion.23, f32[1,30,512]{2,0,1:T(1,128)S(1)} %constant_dynamic-slice_fusion), kind=kOutput, calls=%fused_computation.1 | convolution fusion | flops 763363328 | bytes 8960000 | tf_op jit(solution)/shard_map/dot_general | solution.py:145
  40.1 2.2 shard_map.77
  42.3 1.0 copy-done
  43.3 9.3 %all-gather.2 = f32[8,1,4096]{2,1,0:T(1,128)S(1)} all-gather(f32[1,1,4096]{2,1,0:T(1,128)S(1)} %bitcast.96), channel_id=1, replica_groups=mesh['pair'=4,'src'=2,'tgt'=4] {'src','tgt'}, dimensions={0}, use_global_device_ids=true | all-gather | bytes 147456 | tf_op jit(solution)/shard_map/all_gather | solution.py:171
  53.6 3.4 %copy-done.1 = f32[512,4096]{1,0:T(8,128)S(1)} copy-done((f32[512,4096]{1,0:T(8,128)S(1)}, f32[512,4096]{1,0:T(8,128)}, u32[]{:S(2)}) %copy-start.1) | copy-done | bytes 8388632
  57.0 7.9 %shard_map.78 = (f32[512,1]{1,0:T(8,128)}, f32[1,4096]{1,0:T(1,128)S(1)}) custom-call(f32[512,4096]{1,0:T(8,128)S(1)} %copy-done.1, f32[1,4096]{1,0:T(1,128)S(1)} %fusion.33.b_ref, f32[512,1]{1,0:T(8,128)S(1)} %fusion.4.la_ref), custom_call_target="tpu_custom_call" | custom-call | flops 33554432 | bytes 8388608 | tf_op jit(solution)/shard_map/pallas_call | solution.py:88
  64.9 8.2 %all-gather.3 = f32[8,1,4096]{2,1,0:T(1,128)S(1)} all-gather(f32[1,1,4096]{2,1,0:T(1,128)S(1)} %bitcast.97), channel_id=1, replica_groups=mesh['pair'=4,'src'=2,'tgt'=4] {'src','tgt'}, dimensions={0}, use_global_device_ids=true | all-gather | bytes 147456 | tf_op jit(solution)/shard_map/all_gather | solution.py:171
  74.1 3.4 %copy-done.2 = f32[512,4096]{1,0:T(8,128)S(1)} copy-done((f32[512,4096]{1,0:T(8,128)S(1)}, f32[512,4096]{1,0:T(8,128)}, u32[]{:S(2)}) %copy-start.2) | copy-done | bytes 8388632
  77.4 7.9 %shard_map.79 = (f32[512,1]{1,0:T(8,128)}, f32[1,4096]{1,0:T(1,128)S(1)}) custom-call(f32[512,4096]{1,0:T(8,128)S(1)} %copy-done.2, f32[1,4096]{1,0:T(1,128)S(1)} %fusion.32.b_ref, f32[512,1]{1,0:T(8,128)S(1)} %fusion.4.la_ref), custom_call_target="tpu_custom_call" | custom-call | flops 33554432 | bytes 8388608 | tf_op jit(solution)/shard_map/pallas_call | solution.py:88
  85.4 9.3 %all-gather.4 = f32[8,1,4096]{2,1,0:T(1,128)S(1)} all-gather(f32[1,1,4096]{2,1,0:T(1,128)S(1)} %bitcast.98), channel_id=1, replica_groups=mesh['pair'=4,'src'=2,'tgt'=4] {'src','tgt'}, dimensions={0}, use_global_device_ids=true | all-gather | bytes 147456 | tf_op jit(solution)/shard_map/all_gather | solution.py:171
  95.7 3.4 %copy-done.3 = f32[512,4096]{1,0:T(8,128)S(1)} copy-done((f32[512,4096]{1,0:T(8,128)S(1)}, f32[512,4096]{1,0:T(8,128)}, u32[]{:S(2)}) %copy-start.3) | copy-done | bytes 8388632
  99.0 7.9 %shard_map.80 = (f32[512,1]{1,0:T(8,128)}, f32[1,4096]{1,0:T(1,128)S(1)}) custom-call(f32[512,4096]{1,0:T(8,128)S(1)} %copy-done.3, f32[1,4096]{1,0:T(1,128)S(1)} %fusion.31.b_ref, f32[512,1]{1,0:T(8,128)S(1)} %fusion.4.la_ref), custom_call_target="tpu_custom_call" | custom-call | flops 33554432 | bytes 8388608 | tf_op jit(solution)/shard_map/pallas_call | solution.py:88
  107.0 8.1 %all-gather.5 = f32[8,1,4096]{2,1,0:T(1,128)S(1)} all-gather(f32[1,1,4096]{2,1,0:T(1,128)S(1)} %bitcast.99), channel_id=1, replica_groups=mesh['pair'=4,'src'=2,'tgt'=4] {'src','tgt'}, dimensions={0}, use_global_device_ids=true | all-gather | bytes 147456 | tf_op jit(solution)/shard_map/all_gather | solution.py:171
  116.0 3.4 %copy-done.4 = f32[512,4096]{1,0:T(8,128)S(1)} copy-done((f32[512,4096]{1,0:T(8,128)S(1)}, f32[512,4096]{1,0:T(8,128)}, u32[]{:S(2)}) %copy-start.4) | copy-done | bytes 8388632
  119.3 7.9 %shard_map.81 = (f32[512,1]{1,0:T(8,128)}, f32[1,4096]{1,0:T(1,128)S(1)}) custom-call(f32[512,4096]{1,0:T(8,128)S(1)} %copy-done.4, f32[1,4096]{1,0:T(1,128)S(1)} %fusion.30.b_ref, f32[512,1]{1,0:T(8,128)S(1)} %fusion.4.la_ref), custom_call_target="tpu_custom_call" | custom-call | flops 33554432 | bytes 8388608 | tf_op jit(solution)/shard_map/pallas_call | solution.py:88
  127.3 9.3 %all-gather.6 = f32[8,1,4096]{2,1,0:T(1,128)S(1)} all-gather(f32[1,1,4096]{2,1,0:T(1,128)S(1)} %bitcast.100), channel_id=1, replica_groups=mesh['pair'=4,'src'=2,'tgt'=4] {'src','tgt'}, dimensions={0}, use_global_device_ids=true | all-gather | bytes 147456 | tf_op jit(solution)/shard_map/all_gather | solution.py:171
  137.5 3.4 %copy-done.5 = f32[512,4096]{1,0:T(8,128)S(1)} copy-done((f32[512,4096]{1,0:T(8,128)S(1)}, f32[512,4096]{1,0:T(8,128)}, u32[]{:S(2)}) %copy-start.5) | copy-done | bytes 8388632
  140.9 7.9 %shard_map.82 = (f32[512,1]{1,0:T(8,128)}, f32[1,4096]{1,0:T(1,128)S(1)}) custom-call(f32[512,4096]{1,0:T(8,128)S(1)} %copy-done.5, f32[1,4096]{1,0:T(1,128)S(1)} %fusion.29.b_ref, f32[512,1]{1,0:T(8,128)S(1)} %fusion.4.la_ref), custom_call_target="tpu_custom_call" | custom-call | flops 33554432 | bytes 8388608 | tf_op jit(solution)/shard_map/pallas_call | solution.py:88
  148.9 8.1 %all-gather.7 = f32[8,1,4096]{2,1,0:T(1,128)S(1)} all-gather(f32[1,1,4096]{2,1,0:T(1,128)S(1)} %bitcast.101), channel_id=1, replica_groups=mesh['pair'=4,'src'=2,'tgt'=4] {'src','tgt'}, dimensions={0}, use_global_device_ids=true | all-gather | bytes 147456 | tf_op jit(solution)/shard_map/all_gather | solution.py:171
  157.8 3.4 %copy-done.6 = f32[512,4096]{1,0:T(8,128)S(1)} copy-done((f32[512,4096]{1,0:T(8,128)S(1)}, f32[512,4096]{1,0:T(8,128)}, u32[]{:S(2)}) %copy-start.6) | copy-done | bytes 8388632
  161.2 7.9 %shard_map.83 = (f32[512,1]{1,0:T(8,128)}, f32[1,4096]{1,0:T(1,128)S(1)}) custom-call(f32[512,4096]{1,0:T(8,128)S(1)} %copy-done.6, f32[1,4096]{1,0:T(1,128)S(1)} %fusion.28.b_ref, f32[512,1]{1,0:T(8,128)S(1)} %fusion.4.la_ref), custom_call_target="tpu_custom_call" | custom-call | flops 33554432 | bytes 8388608 | tf_op jit(solution)/shard_map/pallas_call | solution.py:88
  169.2 9.3 %all-gather.8 = f32[8,1,4096]{2,1,0:T(1,128)S(1)} all-gather(f32[1,1,4096]{2,1,0:T(1,128)S(1)} %bitcast.102), channel_id=1, replica_groups=mesh['pair'=4,'src'=2,'tgt'=4] {'src','tgt'}, dimensions={0}, use_global_device_ids=true | all-gather | bytes 147456 | tf_op jit(solution)/shard_map/all_gather | solution.py:171
  179.4 3.4 %copy-done.7 = f32[512,4096]{1,0:T(8,128)S(1)} copy-done((f32[512,4096]{1,0:T(8,128)S(1)}, f32[512,4096]{1,0:T(8,128)}, u32[]{:S(2)}) %copy-start.7) | copy-done | bytes 8388632
  182.8 7.9 %shard_map.84 = (f32[512,1]{1,0:T(8,128)}, f32[1,4096]{1,0:T(1,128)S(1)}) custom-call(f32[512,4096]{1,0:T(8,128)S(1)} %copy-done.7, f32[1,4096]{1,0:T(1,128)S(1)} %fusion.27.b_ref, f32[512,1]{1,0:T(8,128)S(1)} %fusion.4.la_ref), custom_call_target="tpu_custom_call" | custom-call | flops 33554432 | bytes 8388608 | tf_op jit(solution)/shard_map/pallas_call | solution.py:88
  190.8 8.1 %all-gather.9 = f32[8,1,4096]{2,1,0:T(1,128)S(1)} all-gather(f32[1,1,4096]{2,1,0:T(1,128)S(1)} %bitcast.103), channel_id=1, replica_groups=mesh['pair'=4,'src'=2,'tgt'=4] {'src','tgt'}, dimensions={0}, use_global_device_ids=true | all-gather | bytes 147456 | tf_op jit(solution)/shard_map/all_gather | solution.py:171
  199.7 3.4 %copy-done.8 = f32[512,4096]{1,0:T(8,128)S(1)} copy-done((f32[512,4096]{1,0:T(8,128)S(1)}, f32[512,4096]{1,0:T(8,128)}, u32[]{:S(2)}) %copy-start.8) | copy-done | bytes 8388632
  203.1 5.3 %shard_map.85 = (f32[512,1]{1,0:T(8,128)S(1)}, bf16[512,4096]{1,0:T(8,128)(2,1)S(1)}) custom-call(f32[512,4096]{1,0:T(8,128)S(1)} %copy-done.8, f32[1,4096]{1,0:T(1,128)S(1)} %fusion.26.b_ref, f32[512,1]{1,0:T(8,128)S(1)} %fusion.4.la_ref), custom_call_target="tpu_custom_call" | custom-call | flops 25165824 | bytes 12582912 | tf_op jit(solution)/shard_map/pallas_call | solution.py:88
  208.5 2.0 copy-done.9
  210.4 3.6 %fusion.35 = (bf16[40,512]{1,0:T(8,128)(2,1)S(1)}, f32[40,512]{1,0:T(8,128)S(1)}) fusion(bf16[512,4096]{1,0:T(8,128)(2,1)} %copy-done.9, bf16[40,4096]{1,0:T(8,128)(2,1)} %all-reduce.2.cloned.1.call-done, pred[]{:T(512)S(6)} %eq.21, pred[512]{0:T(512)(128)(4,1)S(1)} %add_compare_fusion.1), kind=kOutput, calls=%fused_computation.73 | convolution fusion | flops 167976960 | bytes 4645377 | tf_op jit(solution)/shard_map/dot_general | solution.py:190
  214.0 1.3 collective-permute-start.1
  215.3 4.9 %collective-permute-done.1 = bf16[40,512]{1,0:T(8,128)(2,1)S(1)} collective-permute-done((bf16[40,512]{1,0:T(8,128)(2,1)S(1)}, bf16[40,512]{1,0:T(8,128)(2,1)S(1)}, u32[]{:S(2)}, u32[]{:S(2)}) %collective-permute-start.1) | collective-permute-done | bytes 40992 | tf_op jit(solution)/shard_map/ppermute | solution.py:106
  220.2 9.5 %all_gather.49 = bf16[40,4096]{1,0:T(8,128)(2,1)S(1)} all-gather(bf16[40,512]{1,0:T(8,128)(2,1)S(1)} %collective-permute-done.1), channel_id=1, replica_groups=mesh['pair'=4,'src'=2,'tgt'=4] {'src','tgt'}, dimensions={1}, use_global_device_ids=true | all-gather | bytes 368640 | tf_op jit(solution)/shard_map/all_gather | solution.py:197
  229.8 3.6 %fusion.36 = (bf16[40,512]{1,0:T(8,128)(2,1)S(1)}, f32[40,512]{1,0:T(8,128)S(1)}) fusion(bf16[40,4096]{1,0:T(8,128)(2,1)S(1)} %broadcast_select_fusion.1, bf16[512,4096]{1,0:T(8,128)(2,1)} %copy-done.9, pred[512]{0:T(512)(128)(4,1)S(1)} %add_compare_fusion.1), kind=kOutput, calls=%fused_computation.74 | convolution fusion | flops 167813120 | bytes 4645376 | tf_op jit(solution)/shard_map/dot_general | solution.py:190
  233.4 1.3 collective-permute-start.2
  234.8 4.4 %collective-permute-done.2 = bf16[40,512]{1,0:T(8,128)(2,1)S(1)} collective-permute-done((bf16[40,512]{1,0:T(8,128)(2,1)S(1)}, bf16[40,512]{1,0:T(8,128)(2,1)S(1)}, u32[]{:S(2)}, u32[]{:S(2)}) %collective-permute-start.2) | collective-permute-done | bytes 40992 | tf_op jit(solution)/shard_map/ppermute | solution.py:106
  239.3 8.5 %all_gather.50 = bf16[40,4096]{1,0:T(8,128)(2,1)S(1)} all-gather(bf16[40,512]{1,0:T(8,128)(2,1)S(1)} %collective-permute-done.2), channel_id=1, replica_groups=mesh['pair'=4,'src'=2,'tgt'=4] {'src','tgt'}, dimensions={1}, use_global_device_ids=true | all-gather | bytes 368640 | tf_op jit(solution)/shard_map/all_gather | solution.py:197
  247.8 3.6 %fusion.37 = (bf16[40,512]{1,0:T(8,128)(2,1)S(1)}, f32[40,512]{1,0:T(8,128)S(1)}) fusion(bf16[512,4096]{1,0:T(8,128)(2,1)} %copy-done.9, bf16[40,4096]{1,0:T(8,128)(2,1)S(1)} %all_gather.50, bf16[40,4096]{1,0:T(8,128)(2,1)S(1)} %broadcast_select_fusion.1, pred[]{:T(512)S(6)} %eq.19, pred[512]{0:T(512)(128)(4,1)S(1)} %add_compare_fusion.1), kind=kOutput, calls=%fused_computation.75 | convolution fusion | flops 167976960 | bytes 4973057 | tf_op jit(solution)/shard_map/dot_general | solution.py:190
  251.4 1.3 collective-permute-start.3
  252.7 7.7 %psum.15 = f32[1,2048]{1,0:T(1,128)} all-reduce(f32[1,2048]{1,0:T(1,128)S(1)} %constant_dynamic-update-slice_fusion), channel_id=1, replica_groups=mesh['pair'=4,'src'=2,'tgt'=4] {'tgt'}, use_global_device_ids=true, to_apply=%region_19.20 | all-reduce | flops 2048 | bytes 16384 | tf_op jit(solution)/shard_map/psum | solution.py:200
  260.4 8.5 %all_gather.51 = bf16[40,4096]{1,0:T(8,128)(2,1)S(1)} all-gather(bf16[40,512]{1,0:T(8,128)(2,1)S(1)} %collective-permute-done.3), channel_id=1, replica_groups=mesh['pair'=4,'src'=2,'tgt'=4] {'src','tgt'}, dimensions={1}, use_global_device_ids=true | all-gather | bytes 368640 | tf_op jit(solution)/shard_map/all_gather | solution.py:197
  268.9 4.2 %fusion.1 = f32[1,40,512]{2,1,0:T(8,128)} fusion(bf16[512,4096]{1,0:T(8,128)(2,1)} %copy-done.9, bf16[40,4096]{1,0:T(8,128)(2,1)S(1)} %all_gather.51, pred[]{:T(512)S(6)} %eq.18, bf16[40,4096]{1,0:T(8,128)(2,1)S(1)} %all_gather.50, bf16[40,4096]{1,0:T(8,128)(2,1)S(1)} %broadcast_select_fusion.1, pred[]{:T(512)S(6)} %eq.19, ...), kind=kOutput, calls=%fused_computation.7 | convolution fusion | flops 168202240 | bytes 5505540 | tf_op jit(solution)/shard_map/dot_general | solution.py:190
  (69 shorter events, 13.9 us)
Async XLA Ops:
  7.2 203.3 %all-reduce.2.cloned.1.call-start = ((), (), s32[]{:S(2)}) async-start(), calls=%async_computation | async-start | bytes 655360 | tf_op jit(solution)/shard_map/psum | solution.py:185
  8.2 11.3 %collective-permute-start = (f32[30,2048]{1,0:T(8,128)S(1)}, f32[30,2048]{1,0:T(8,128)S(1)}, u32[]{:S(2)}, u32[]{:S(2)}) collective-permute-start(f32[30,2048]{1,0:T(8,128)S(1)} %bitcast.106), channel_id=1, source_target_pairs={{8,0},{16,8},{24,16},{9,1},{17,9},{25,17},{10,2},{18,10},{26,18},{... | collective-permute-start | bytes 737288 | tf_op jit(solution)/shard_map/ppermute | solution.py:106
  10.5 0.7 copy-start.11
  40.1 3.2 %copy-start = (f32[512,4096]{1,0:T(8,128)}, f32[512,4096]{1,0:T(8,128)S(1)}, u32[]{:S(2)}) copy-start(f32[512,4096]{1,0:T(8,128)S(1)} %subtract_multiply_fusion.c_ref) | copy-start | bytes 25165828
  53.6 3.4 %copy-start.1 = (f32[512,4096]{1,0:T(8,128)S(1)}, f32[512,4096]{1,0:T(8,128)}, u32[]{:S(2)}) copy-start(f32[512,4096]{1,0:T(8,128)} %copy-done) | copy-start | bytes 25165828
  74.1 3.4 %copy-start.2 = (f32[512,4096]{1,0:T(8,128)S(1)}, f32[512,4096]{1,0:T(8,128)}, u32[]{:S(2)}) copy-start(f32[512,4096]{1,0:T(8,128)} %copy-done) | copy-start | bytes 25165828
  95.6 3.4 %copy-start.3 = (f32[512,4096]{1,0:T(8,128)S(1)}, f32[512,4096]{1,0:T(8,128)}, u32[]{:S(2)}) copy-start(f32[512,4096]{1,0:T(8,128)} %copy-done) | copy-start | bytes 25165828
  115.9 3.4 %copy-start.4 = (f32[512,4096]{1,0:T(8,128)S(1)}, f32[512,4096]{1,0:T(8,128)}, u32[]{:S(2)}) copy-start(f32[512,4096]{1,0:T(8,128)} %copy-done) | copy-start | bytes 25165828
  137.5 3.4 %copy-start.5 = (f32[512,4096]{1,0:T(8,128)S(1)}, f32[512,4096]{1,0:T(8,128)}, u32[]{:S(2)}) copy-start(f32[512,4096]{1,0:T(8,128)} %copy-done) | copy-start | bytes 25165828
  157.8 3.4 %copy-start.6 = (f32[512,4096]{1,0:T(8,128)S(1)}, f32[512,4096]{1,0:T(8,128)}, u32[]{:S(2)}) copy-start(f32[512,4096]{1,0:T(8,128)} %copy-done) | copy-start | bytes 25165828
  179.4 3.4 %copy-start.7 = (f32[512,4096]{1,0:T(8,128)S(1)}, f32[512,4096]{1,0:T(8,128)}, u32[]{:S(2)}) copy-start(f32[512,4096]{1,0:T(8,128)} %copy-done) | copy-start | bytes 25165828
  199.7 3.4 %copy-start.8 = (f32[512,4096]{1,0:T(8,128)S(1)}, f32[512,4096]{1,0:T(8,128)}, u32[]{:S(2)}) copy-start(f32[512,4096]{1,0:T(8,128)} %copy-done) | copy-start | bytes 25165828
  208.4 2.0 copy-start.9
  210.4 19.3 %copy-start.10 = (bf16[40,4096]{1,0:T(8,128)(2,1)S(1)}, bf16[40,4096]{1,0:T(8,128)(2,1)}, u32[]{:S(2)}) copy-start(bf16[40,4096]{1,0:T(8,128)(2,1)} %all-reduce.2.cloned.1.call-done) | copy-start | bytes 983044
  214.0 6.2 %collective-permute-start.1 = (bf16[40,512]{1,0:T(8,128)(2,1)S(1)}, bf16[40,512]{1,0:T(8,128)(2,1)S(1)}, u32[]{:S(2)}, u32[]{:S(2)}) collective-permute-start(bf16[40,512]{1,0:T(8,128)(2,1)S(1)} %get-tuple-element.24), channel_id=1, source_target_pairs={{8,0},{16,8},{24,16},{9,1},{17,9},{25,17},{10,2},{18,10},{26,18},{... | collective-permute-start | bytes 122888 | tf_op jit(solution)/shard_map/ppermute | solution.py:106
  233.4 5.9 %collective-permute-start.2 = (bf16[40,512]{1,0:T(8,128)(2,1)S(1)}, bf16[40,512]{1,0:T(8,128)(2,1)S(1)}, u32[]{:S(2)}, u32[]{:S(2)}) collective-permute-start(bf16[40,512]{1,0:T(8,128)(2,1)S(1)} %get-tuple-element.26), channel_id=1, source_target_pairs={{8,0},{16,8},{24,16},{9,1},{17,9},{25,17},{10,2},{18,10},{26,18},{... | collective-permute-start | bytes 122888 | tf_op jit(solution)/shard_map/ppermute | solution.py:106
  251.4 9.0 %collective-permute-start.3 = (bf16[40,512]{1,0:T(8,128)(2,1)S(1)}, bf16[40,512]{1,0:T(8,128)(2,1)S(1)}, u32[]{:S(2)}, u32[]{:S(2)}) collective-permute-start(bf16[40,512]{1,0:T(8,128)(2,1)S(1)} %get-tuple-element.28), channel_id=1, source_target_pairs={{8,0},{16,8},{24,16},{9,1},{17,9},{25,17},{10,2},{18,10},{26,18},{... | collective-permute-start | bytes 122888 | tf_op jit(solution)/shard_map/ppermute | solution.py:106
Sparse Core Ops, SparseCore 0:
  11.4 36.5 all-reduce.1

commit v5 on v3

--- a/solution.py
+++ b/solution.py
@@ -15,7 +15,7 @@
 
 
 GROUP = 16
-ROW_GROUP = 32
+ROW_GROUP = 128
 WIDTH = 512
 
 
@@ -30,7 +30,9 @@
     chunks = cols // WIDTH
 
     if do_row:
-        rg = ROW_GROUP if rows % ROW_GROUP == 0 else GROUP
+        rg = ROW_GROUP
+        while rows % rg:
+            rg //= 2
 
         def row_group(r, carry):
             rs = pl.ds(pl.multiple_of(r * rg, rg), rg)
@@ -192,7 +194,8 @@
             passed = shifted(pulled.astype(jnp.bfloat16), "pair", -1)
             fresh = lax.all_gather(passed, ("src", "tgt"), axis=1, tiled=True)
             handed = jnp.where(pair_rank == active - 1, fresh, handed)
-    pot_all = lax.all_gather(pot_src, "tgt", axis=0, tiled=True)
+    pot_spread = lax.dynamic_update_slice_in_dim(jnp.zeros((src_width,), jnp.float32), pot_src, row_off, 0)
+    pot_all = lax.psum(pot_spread, "tgt")
     return (fate_maps[None], pot_all[None])
 
 

time: 275 us -> 248 us (0.902)
  Pallas kernels: 63 us -> 40.4 us
  blocking collectives: 125 us -> 122 us
    pallas_call x9, Pallas kernels: 63 us -> 40.4 us  [sweep(): pl.pallas_call(functools.partial(sweep_kernel, do_row, do_col, emit_w, sh...]
    all_gather x1 -> x0, blocking collectives: 10.1 us -> none  [local(): pot_all = lax.all_gather(pot_src, 'tgt', axis=0, tiled=True)]
    psum x0 -> x1, blocking collectives: none -> 7.64 us  [local(): pot_all = lax.psum(pot_spread, 'tgt')]
where the time goes in v5:
time: 248 us; the launch traced here: 247 us
  blocking collectives  122 us (49%)
  Pallas kernels  40.4 us (16%)
  local copies, waits for them, and re-layouts  34.5 us (14%)
  matrix products  20.1 us (8%)
  other arithmetic  12.6 us (5%)
  waiting for transfers between devices  9.77 us (4%)
  starting transfers between devices  5.17 us (2%)
  between operations  2.54 us (1%)
    all_gather x8, blocking collectives, local(): every = lax.all_gather(part_lse[0], ('src', 'tgt'))  70 us
    pallas_call x9, Pallas kernels, sweep(): pl.pallas_call(functools.partial(sweep_kernel, do_row, do_col, emit_w, sh...  40.4 us
    unnamed x24, local copies, waits for them, and re-layouts  31.3 us
    all_gather x3, blocking collectives, local(): fresh = lax.all_gather(passed, ('src', 'tgt'), axis=1, tiled=True)  26.4 us
    dot_general x4, matrix products, local(): lax.dot_general(handed, weights, (((1,), (1,)), ((), ())), preferred_elem...  12.7 us
    all_gather x1, blocking collectives, local(): pieces = lax.all_gather(piece, ('src', 'tgt'))  9.83 us
    ppermute x4, waiting for transfers between devices, shifted(): return lax.ppermute(shard, axis, pairs)  9.77 us
    psum x1, blocking collectives, local(): pot_all = lax.psum(pot_spread, 'tgt')  7.64 us
  transfers between devices with their start and end apart: 4, of which 2 were waited for; matrix products, arithmetic and copies ran while one was open for 3% of the time, Pallas kernels for 0%

profile of v5, /device:TPU:0, one launch (start us, length us, event | category | flops | bytes accessed | tf_op | source)
XLA Modules:
  0.0 246.7 jit_solution(1372798913091404144)
XLA Ops:
  0.6 1.0 copy.38
  1.7 1.3 collective-permute-start
  4.5 1.3 fusion.34
  7.9 0.9 convert_element_type.18
  8.8 7.6 %all_gather.42 = bf16[40,4096]{1,0:T(8,128)(2,1)S(1)} all-gather(bf16[40,1024]{1,0:T(8,128)(2,1)S(1)} %convert_element_type.18), channel_id=1, replica_groups=mesh['pair'=4,'src'=2,'tgt'=4] {'tgt'}, dimensions={1}, use_global_device_ids=true | all-gather | bytes 409600 | tf_op jit(solution)/shard_map/all_gather | solution.py:183
  18.6 0.9 select_bitcast_fusion.1
  19.5 9.8 %all-gather.1 = f32[8,30,512]{2,1,0:T(8,128)S(1)} all-gather(f32[1,30,512]{2,1,0:T(8,128)S(1)} %select_bitcast_fusion.1), channel_id=2, replica_groups=mesh['pair'=4,'src'=2,'tgt'=4] {'src','tgt'}, dimensions={0}, use_global_device_ids=true | all-gather | bytes 552960 | tf_op jit(solution)/shard_map/all_gather | solution.py:132
  30.7 7.4 %subtract_multiply_fusion.c_ref = f32[512,4096]{1,0:T(8,128)S(1)} fusion(f32[30,4096]{1,0:T(8,128)S(1)} %bitcast.104, f32[4096]{0:T(1024)S(1)} %bitcast.107, f32[512]{0:T(512)S(1)} %fusion.23, f32[1,30,512]{2,0,1:T(1,128)S(1)} %constant_dynamic-slice_fusion), kind=kOutput, calls=%fused_computation.1 | convolution fusion | flops 763363328 | bytes 8960000 | tf_op jit(solution)/shard_map/dot_general | solution.py:147
  38.2 2.2 shard_map.77
  40.4 1.0 copy-done
  41.4 9.0 %all-gather.2 = f32[8,1,4096]{2,1,0:T(1,128)S(1)} all-gather(f32[1,1,4096]{2,1,0:T(1,128)S(1)} %bitcast.96), channel_id=1, replica_groups=mesh['pair'=4,'src'=2,'tgt'=4] {'src','tgt'}, dimensions={0}, use_global_device_ids=true | all-gather | bytes 147456 | tf_op jit(solution)/shard_map/all_gather | solution.py:173
  51.3 3.4 %copy-done.1 = f32[512,4096]{1,0:T(8,128)S(1)} copy-done((f32[512,4096]{1,0:T(8,128)S(1)}, f32[512,4096]{1,0:T(8,128)}, u32[]{:S(2)}) %copy-start.1) | copy-done | bytes 8388632
  54.7 5.0 %shard_map.78 = (f32[512,1]{1,0:T(8,128)}, f32[1,4096]{1,0:T(1,128)S(1)}) custom-call(f32[512,4096]{1,0:T(8,128)S(1)} %copy-done.1, f32[1,4096]{1,0:T(1,128)S(1)} %fusion.33.b_ref, f32[512,1]{1,0:T(8,128)S(1)} %fusion.4.la_ref), custom_call_target="tpu_custom_call" | custom-call | flops 33554432 | bytes 8388608 | tf_op jit(solution)/shard_map/pallas_call | solution.py:90
  59.7 8.5 %all-gather.3 = f32[8,1,4096]{2,1,0:T(1,128)S(1)} all-gather(f32[1,1,4096]{2,1,0:T(1,128)S(1)} %bitcast.97), channel_id=1, replica_groups=mesh['pair'=4,'src'=2,'tgt'=4] {'src','tgt'}, dimensions={0}, use_global_device_ids=true | all-gather | bytes 147456 | tf_op jit(solution)/shard_map/all_gather | solution.py:173
  69.1 3.4 %copy-done.2 = f32[512,4096]{1,0:T(8,128)S(1)} copy-done((f32[512,4096]{1,0:T(8,128)S(1)}, f32[512,4096]{1,0:T(8,128)}, u32[]{:S(2)}) %copy-start.2) | copy-done | bytes 8388632
  72.5 5.0 %shard_map.79 = (f32[512,1]{1,0:T(8,128)}, f32[1,4096]{1,0:T(1,128)S(1)}) custom-call(f32[512,4096]{1,0:T(8,128)S(1)} %copy-done.2, f32[1,4096]{1,0:T(1,128)S(1)} %fusion.32.b_ref, f32[512,1]{1,0:T(8,128)S(1)} %fusion.4.la_ref), custom_call_target="tpu_custom_call" | custom-call | flops 33554432 | bytes 8388608 | tf_op jit(solution)/shard_map/pallas_call | solution.py:90
  77.5 9.0 %all-gather.4 = f32[8,1,4096]{2,1,0:T(1,128)S(1)} all-gather(f32[1,1,4096]{2,1,0:T(1,128)S(1)} %bitcast.98), channel_id=1, replica_groups=mesh['pair'=4,'src'=2,'tgt'=4] {'src','tgt'}, dimensions={0}, use_global_device_ids=true | all-gather | bytes 147456 | tf_op jit(solution)/shard_map/all_gather | solution.py:173
  87.4 3.4 %copy-done.3 = f32[512,4096]{1,0:T(8,128)S(1)} copy-done((f32[512,4096]{1,0:T(8,128)S(1)}, f32[512,4096]{1,0:T(8,128)}, u32[]{:S(2)}) %copy-start.3) | copy-done | bytes 8388632
  90.8 5.0 %shard_map.80 = (f32[512,1]{1,0:T(8,128)}, f32[1,4096]{1,0:T(1,128)S(1)}) custom-call(f32[512,4096]{1,0:T(8,128)S(1)} %copy-done.3, f32[1,4096]{1,0:T(1,128)S(1)} %fusion.31.b_ref, f32[512,1]{1,0:T(8,128)S(1)} %fusion.4.la_ref), custom_call_target="tpu_custom_call" | custom-call | flops 33554432 | bytes 8388608 | tf_op jit(solution)/shard_map/pallas_call | solution.py:90
  95.7 8.4 %all-gather.5 = f32[8,1,4096]{2,1,0:T(1,128)S(1)} all-gather(f32[1,1,4096]{2,1,0:T(1,128)S(1)} %bitcast.99), channel_id=1, replica_groups=mesh['pair'=4,'src'=2,'tgt'=4] {'src','tgt'}, dimensions={0}, use_global_device_ids=true | all-gather | bytes 147456 | tf_op jit(solution)/shard_map/all_gather | solution.py:173
  105.0 3.4 %copy-done.4 = f32[512,4096]{1,0:T(8,128)S(1)} copy-done((f32[512,4096]{1,0:T(8,128)S(1)}, f32[512,4096]{1,0:T(8,128)}, u32[]{:S(2)}) %copy-start.4) | copy-done | bytes 8388632
  108.4 5.0 %shard_map.81 = (f32[512,1]{1,0:T(8,128)}, f32[1,4096]{1,0:T(1,128)S(1)}) custom-call(f32[512,4096]{1,0:T(8,128)S(1)} %copy-done.4, f32[1,4096]{1,0:T(1,128)S(1)} %fusion.30.b_ref, f32[512,1]{1,0:T(8,128)S(1)} %fusion.4.la_ref), custom_call_target="tpu_custom_call" | custom-call | flops 33554432 | bytes 8388608 | tf_op jit(solution)/shard_map/pallas_call | solution.py:90
  113.4 9.0 %all-gather.6 = f32[8,1,4096]{2,1,0:T(1,128)S(1)} all-gather(f32[1,1,4096]{2,1,0:T(1,128)S(1)} %bitcast.100), channel_id=1, replica_groups=mesh['pair'=4,'src'=2,'tgt'=4] {'src','tgt'}, dimensions={0}, use_global_device_ids=true | all-gather | bytes 147456 | tf_op jit(solution)/shard_map/all_gather | solution.py:173
  123.3 3.4 %copy-done.5 = f32[512,4096]{1,0:T(8,128)S(1)} copy-done((f32[512,4096]{1,0:T(8,128)S(1)}, f32[512,4096]{1,0:T(8,128)}, u32[]{:S(2)}) %copy-start.5) | copy-done | bytes 8388632
  126.7 5.0 %shard_map.82 = (f32[512,1]{1,0:T(8,128)}, f32[1,4096]{1,0:T(1,128)S(1)}) custom-call(f32[512,4096]{1,0:T(8,128)S(1)} %copy-done.5, f32[1,4096]{1,0:T(1,128)S(1)} %fusion.29.b_ref, f32[512,1]{1,0:T(8,128)S(1)} %fusion.4.la_ref), custom_call_target="tpu_custom_call" | custom-call | flops 33554432 | bytes 8388608 | tf_op jit(solution)/shard_map/pallas_call | solution.py:90
  131.7 8.4 %all-gather.7 = f32[8,1,4096]{2,1,0:T(1,128)S(1)} all-gather(f32[1,1,4096]{2,1,0:T(1,128)S(1)} %bitcast.101), channel_id=1, replica_groups=mesh['pair'=4,'src'=2,'tgt'=4] {'src','tgt'}, dimensions={0}, use_global_device_ids=true | all-gather | bytes 147456 | tf_op jit(solution)/shard_map/all_gather | solution.py:173
  140.9 3.4 %copy-done.6 = f32[512,4096]{1,0:T(8,128)S(1)} copy-done((f32[512,4096]{1,0:T(8,128)S(1)}, f32[512,4096]{1,0:T(8,128)}, u32[]{:S(2)}) %copy-start.6) | copy-done | bytes 8388632
  144.3 5.0 %shard_map.83 = (f32[512,1]{1,0:T(8,128)}, f32[1,4096]{1,0:T(1,128)S(1)}) custom-call(f32[512,4096]{1,0:T(8,128)S(1)} %copy-done.6, f32[1,4096]{1,0:T(1,128)S(1)} %fusion.28.b_ref, f32[512,1]{1,0:T(8,128)S(1)} %fusion.4.la_ref), custom_call_target="tpu_custom_call" | custom-call | flops 33554432 | bytes 8388608 | tf_op jit(solution)/shard_map/pallas_call | solution.py:90
  149.3 9.0 %all-gather.8 = f32[8,1,4096]{2,1,0:T(1,128)S(1)} all-gather(f32[1,1,4096]{2,1,0:T(1,128)S(1)} %bitcast.102), channel_id=1, replica_groups=mesh['pair'=4,'src'=2,'tgt'=4] {'src','tgt'}, dimensions={0}, use_global_device_ids=true | all-gather | bytes 147456 | tf_op jit(solution)/shard_map/all_gather | solution.py:173
  159.2 3.4 %copy-done.7 = f32[512,4096]{1,0:T(8,128)S(1)} copy-done((f32[512,4096]{1,0:T(8,128)S(1)}, f32[512,4096]{1,0:T(8,128)}, u32[]{:S(2)}) %copy-start.7) | copy-done | bytes 8388632
  162.6 5.0 %shard_map.84 = (f32[512,1]{1,0:T(8,128)}, f32[1,4096]{1,0:T(1,128)S(1)}) custom-call(f32[512,4096]{1,0:T(8,128)S(1)} %copy-done.7, f32[1,4096]{1,0:T(1,128)S(1)} %fusion.27.b_ref, f32[512,1]{1,0:T(8,128)S(1)} %fusion.4.la_ref), custom_call_target="tpu_custom_call" | custom-call | flops 33554432 | bytes 8388608 | tf_op jit(solution)/shard_map/pallas_call | solution.py:90
  167.6 8.6 %all-gather.9 = f32[8,1,4096]{2,1,0:T(1,128)S(1)} all-gather(f32[1,1,4096]{2,1,0:T(1,128)S(1)} %bitcast.103), channel_id=1, replica_groups=mesh['pair'=4,'src'=2,'tgt'=4] {'src','tgt'}, dimensions={0}, use_global_device_ids=true | all-gather | bytes 147456 | tf_op jit(solution)/shard_map/all_gather | solution.py:173
  177.1 3.4 %copy-done.8 = f32[512,4096]{1,0:T(8,128)S(1)} copy-done((f32[512,4096]{1,0:T(8,128)S(1)}, f32[512,4096]{1,0:T(8,128)}, u32[]{:S(2)}) %copy-start.8) | copy-done | bytes 8388632
  180.4 3.6 %shard_map.85 = (f32[512,1]{1,0:T(8,128)S(1)}, bf16[512,4096]{1,0:T(8,128)(2,1)S(1)}) custom-call(f32[512,4096]{1,0:T(8,128)S(1)} %copy-done.8, f32[1,4096]{1,0:T(1,128)S(1)} %fusion.26.b_ref, f32[512,1]{1,0:T(8,128)S(1)} %fusion.4.la_ref), custom_call_target="tpu_custom_call" | custom-call | flops 25165824 | bytes 12582912 | tf_op jit(solution)/shard_map/pallas_call | solution.py:90
  184.1 1.9 copy-done.9
  186.0 1.4 fusion.35
  187.3 1.3 collective-permute-start.1
  188.7 5.3 %collective-permute-done.1 = bf16[40,512]{1,0:T(8,128)(2,1)S(1)} collective-permute-done((bf16[40,512]{1,0:T(8,128)(2,1)S(1)}, bf16[40,512]{1,0:T(8,128)(2,1)S(1)}, u32[]{:S(2)}, u32[]{:S(2)}) %collective-permute-start.1) | collective-permute-done | bytes 40992 | tf_op jit(solution)/shard_map/ppermute | solution.py:108
  194.0 9.3 %all_gather.53 = bf16[40,4096]{1,0:T(8,128)(2,1)S(1)} all-gather(bf16[40,512]{1,0:T(8,128)(2,1)S(1)} %collective-permute-done.1), channel_id=1, replica_groups=mesh['pair'=4,'src'=2,'tgt'=4] {'src','tgt'}, dimensions={1}, use_global_device_ids=true | all-gather | bytes 368640 | tf_op jit(solution)/shard_map/all_gather | solution.py:195
  203.3 3.6 %fusion.36 = (bf16[40,512]{1,0:T(8,128)(2,1)S(1)}, f32[40,512]{1,0:T(8,128)S(1)}) fusion(bf16[40,4096]{1,0:T(8,128)(2,1)S(1)} %broadcast_select_fusion.1, bf16[512,4096]{1,0:T(8,128)(2,1)} %copy-done.9, pred[512]{0:T(512)(128)(4,1)S(1)} %add_compare_fusion.1), kind=kOutput, calls=%fused_computation.73 | convolution fusion | flops 167813120 | bytes 4645376 | tf_op jit(solution)/shard_map/dot_general | solution.py:188
  206.8 1.3 collective-permute-start.2
  208.3 4.4 %collective-permute-done.2 = bf16[40,512]{1,0:T(8,128)(2,1)S(1)} collective-permute-done((bf16[40,512]{1,0:T(8,128)(2,1)S(1)}, bf16[40,512]{1,0:T(8,128)(2,1)S(1)}, u32[]{:S(2)}, u32[]{:S(2)}) %collective-permute-start.2) | collective-permute-done | bytes 40992 | tf_op jit(solution)/shard_map/ppermute | solution.py:108
  212.7 8.6 %all_gather.54 = bf16[40,4096]{1,0:T(8,128)(2,1)S(1)} all-gather(bf16[40,512]{1,0:T(8,128)(2,1)S(1)} %collective-permute-done.2), channel_id=1, replica_groups=mesh['pair'=4,'src'=2,'tgt'=4] {'src','tgt'}, dimensions={1}, use_global_device_ids=true | all-gather | bytes 368640 | tf_op jit(solution)/shard_map/all_gather | solution.py:195
  221.3 3.6 %fusion.37 = (bf16[40,512]{1,0:T(8,128)(2,1)S(1)}, f32[40,512]{1,0:T(8,128)S(1)}) fusion(bf16[512,4096]{1,0:T(8,128)(2,1)} %copy-done.9, bf16[40,4096]{1,0:T(8,128)(2,1)S(1)} %all_gather.54, bf16[40,4096]{1,0:T(8,128)(2,1)S(1)} %broadcast_select_fusion.1, pred[]{:T(512)S(6)} %eq.19, pred[512]{0:T(512)(128)(4,1)S(1)} %add_compare_fusion.1), kind=kOutput, calls=%fused_computation.74 | convolution fusion | flops 167976960 | bytes 4973057 | tf_op jit(solution)/shard_map/dot_general | solution.py:188
  224.9 1.3 collective-permute-start.3
  226.2 7.6 %psum.7 = f32[1,2048]{1,0:T(1,128)} all-reduce(f32[1,2048]{1,0:T(1,128)S(1)} %constant_dynamic-update-slice_fusion), channel_id=1, replica_groups=mesh['pair'=4,'src'=2,'tgt'=4] {'tgt'}, use_global_device_ids=true, to_apply=%region_18.19 | all-reduce | flops 2048 | bytes 16384 | tf_op jit(solution)/shard_map/psum | solution.py:198
  233.9 8.6 %all_gather.55 = bf16[40,4096]{1,0:T(8,128)(2,1)S(1)} all-gather(bf16[40,512]{1,0:T(8,128)(2,1)S(1)} %collective-permute-done.3), channel_id=1, replica_groups=mesh['pair'=4,'src'=2,'tgt'=4] {'src','tgt'}, dimensions={1}, use_global_device_ids=true | all-gather | bytes 368640 | tf_op jit(solution)/shard_map/all_gather | solution.py:195
  242.5 4.2 %fusion.1 = f32[1,40,512]{2,1,0:T(8,128)} fusion(bf16[512,4096]{1,0:T(8,128)(2,1)} %copy-done.9, bf16[40,4096]{1,0:T(8,128)(2,1)S(1)} %all_gather.55, pred[]{:T(512)S(6)} %eq.18, bf16[40,4096]{1,0:T(8,128)(2,1)S(1)} %all_gather.54, bf16[40,4096]{1,0:T(8,128)(2,1)S(1)} %broadcast_select_fusion.1, pred[]{:T(512)S(6)} %eq.19, ...), kind=kOutput, calls=%fused_computation.7 | convolution fusion | flops 168202240 | bytes 5505540 | tf_op jit(solution)/shard_map/dot_general | solution.py:188
  (62 shorter events, 13.1 us)
Async XLA Ops:
  1.7 17.0 %collective-permute-start = (f32[30,2048]{1,0:T(8,128)S(1)}, f32[30,2048]{1,0:T(8,128)S(1)}, u32[]{:S(2)}, u32[]{:S(2)}) collective-permute-start(f32[30,2048]{1,0:T(8,128)S(1)} %bitcast.106), channel_id=1, source_target_pairs={{8,0},{16,8},{24,16},{9,1},{17,9},{25,17},{10,2},{18,10},{26,18},{... | collective-permute-start | bytes 737288 | tf_op jit(solution)/shard_map/ppermute | solution.py:108
  38.2 3.2 %copy-start = (f32[512,4096]{1,0:T(8,128)}, f32[512,4096]{1,0:T(8,128)S(1)}, u32[]{:S(2)}) copy-start(f32[512,4096]{1,0:T(8,128)S(1)} %subtract_multiply_fusion.c_ref) | copy-start | bytes 25165828
  51.3 3.4 %copy-start.1 = (f32[512,4096]{1,0:T(8,128)S(1)}, f32[512,4096]{1,0:T(8,128)}, u32[]{:S(2)}) copy-start(f32[512,4096]{1,0:T(8,128)} %copy-done) | copy-start | bytes 25165828
  69.1 3.4 %copy-start.2 = (f32[512,4096]{1,0:T(8,128)S(1)}, f32[512,4096]{1,0:T(8,128)}, u32[]{:S(2)}) copy-start(f32[512,4096]{1,0:T(8,128)} %copy-done) | copy-start | bytes 25165828
  87.4 3.4 %copy-start.3 = (f32[512,4096]{1,0:T(8,128)S(1)}, f32[512,4096]{1,0:T(8,128)}, u32[]{:S(2)}) copy-start(f32[512,4096]{1,0:T(8,128)} %copy-done) | copy-start | bytes 25165828
  105.0 3.4 %copy-start.4 = (f32[512,4096]{1,0:T(8,128)S(1)}, f32[512,4096]{1,0:T(8,128)}, u32[]{:S(2)}) copy-start(f32[512,4096]{1,0:T(8,128)} %copy-done) | copy-start | bytes 25165828
  123.3 3.4 %copy-start.5 = (f32[512,4096]{1,0:T(8,128)S(1)}, f32[512,4096]{1,0:T(8,128)}, u32[]{:S(2)}) copy-start(f32[512,4096]{1,0:T(8,128)} %copy-done) | copy-start | bytes 25165828
  140.9 3.4 %copy-start.6 = (f32[512,4096]{1,0:T(8,128)S(1)}, f32[512,4096]{1,0:T(8,128)}, u32[]{:S(2)}) copy-start(f32[512,4096]{1,0:T(8,128)} %copy-done) | copy-start | bytes 25165828
  159.2 3.4 %copy-start.7 = (f32[512,4096]{1,0:T(8,128)S(1)}, f32[512,4096]{1,0:T(8,128)}, u32[]{:S(2)}) copy-start(f32[512,4096]{1,0:T(8,128)} %copy-done) | copy-start | bytes 25165828
  177.1 3.4 %copy-start.8 = (f32[512,4096]{1,0:T(8,128)S(1)}, f32[512,4096]{1,0:T(8,128)}, u32[]{:S(2)}) copy-start(f32[512,4096]{1,0:T(8,128)} %copy-done) | copy-start | bytes 25165828
  184.0 1.9 copy-start.9
  187.3 6.6 %collective-permute-start.1 = (bf16[40,512]{1,0:T(8,128)(2,1)S(1)}, bf16[40,512]{1,0:T(8,128)(2,1)S(1)}, u32[]{:S(2)}, u32[]{:S(2)}) collective-permute-start(bf16[40,512]{1,0:T(8,128)(2,1)S(1)} %get-tuple-element.24), channel_id=1, source_target_pairs={{8,0},{16,8},{24,16},{9,1},{17,9},{25,17},{10,2},{18,10},{26,18},{... | collective-permute-start | bytes 122888 | tf_op jit(solution)/shard_map/ppermute | solution.py:108
  206.8 5.9 %collective-permute-start.2 = (bf16[40,512]{1,0:T(8,128)(2,1)S(1)}, bf16[40,512]{1,0:T(8,128)(2,1)S(1)}, u32[]{:S(2)}, u32[]{:S(2)}) collective-permute-start(bf16[40,512]{1,0:T(8,128)(2,1)S(1)} %get-tuple-element.26), channel_id=1, source_target_pairs={{8,0},{16,8},{24,16},{9,1},{17,9},{25,17},{10,2},{18,10},{26,18},{... | collective-permute-start | bytes 122888 | tf_op jit(solution)/shard_map/ppermute | solution.py:108
  224.9 9.0 %collective-permute-start.3 = (bf16[40,512]{1,0:T(8,128)(2,1)S(1)}, bf16[40,512]{1,0:T(8,128)(2,1)S(1)}, u32[]{:S(2)}, u32[]{:S(2)}) collective-permute-start(bf16[40,512]{1,0:T(8,128)(2,1)S(1)} %get-tuple-element.28), channel_id=1, source_target_pairs={{8,0},{16,8},{24,16},{9,1},{17,9},{25,17},{10,2},{18,10},{26,18},{... | collective-permute-start | bytes 122888 | tf_op jit(solution)/shard_map/ppermute | solution.py:108

commit v6 on v5

--- a/solution.py
+++ b/solution.py
@@ -19,17 +19,23 @@
 WIDTH = 512
 
 
-def sweep_kernel(do_row, do_col, emit_w, shrink, c_ref, b_ref, la_ref, *rest):
+def sweep_kernel(do_row, do_col, emit_w, shrink, c_ref, every_ref, lb_ref, la_ref, *rest):
     rest = list(rest)
     f_ref = rest.pop(0) if do_row else None
     lse_ref = rest.pop(0) if do_col else None
     w_ref = rest.pop(0) if emit_w else None
-    a_ref = rest.pop(0)
+    a_ref, b_ref = rest
     rows, cols = c_ref.shape
     groups = rows // GROUP
     chunks = cols // WIDTH
 
     if do_row:
+        for j in range(chunks):
+            cs = slice(j * WIDTH, (j + 1) * WIDTH)
+            ev = every_ref[:, cs]
+            top = jnp.max(ev, axis=0, keepdims=True)
+            col_lse = top + jnp.log(jnp.sum(jnp.exp(ev - top), axis=0, keepdims=True))
+            b_ref[:, cs] = (-shrink * EPS * col_lse) * (1.0 / EPS) + lb_ref[:, cs]
         rg = ROW_GROUP
         while rows % rg:
             rg //= 2
@@ -76,7 +82,7 @@
         lax.fori_loop(0, chunks, col_chunk, 0)
 
 
-def sweep(scaled_cost, col_shift, log_a, shrink, do_row, do_col, emit_w):
+def sweep(scaled_cost, every, log_b, log_a, shrink, do_row, do_col, emit_w):
     rows, cols = scaled_cost.shape
     outs = []
     if do_row:
@@ -90,16 +96,16 @@
     return pl.pallas_call(
         functools.partial(sweep_kernel, do_row, do_col, emit_w, shrink),
         out_shape=tuple(outs),
-        in_specs=[vmem] * 3,
+        in_specs=[vmem] * 4,
         out_specs=tuple([vmem] * len(outs)),
-        scratch_shapes=[pltpu.VMEM((rows, 128), jnp.float32)],
+        scratch_shapes=[pltpu.VMEM((rows, 128), jnp.float32), pltpu.VMEM((1, cols), jnp.float32)],
         compiler_params=pltpu.CompilerParams(vmem_limit_bytes=24 * 1024 * 1024),
         cost_estimate=pl.CostEstimate(
             flops=4 * passes * rows * cols,
             transcendentals=passes * rows * cols // 2,
             bytes_accessed=4 * rows * cols + (2 * rows * cols if emit_w else 0),
         ),
-    )(scaled_cost, col_shift[None, :], log_a[:, None])
+    )(scaled_cost, every, log_b[None, :], log_a[:, None])
 
 
 def shifted(shard, axis, by):
@@ -168,17 +174,13 @@
         live_tgt, -jnp.log(live_next.astype(jnp.float32)) * jnp.ones((cols,), jnp.float32), NEG
     )
     scaled_cost = cost_tile * (1.0 / EPS)
-    (part_lse,) = sweep(scaled_cost, log_mass_b, log_mass_a, shrink, False, True, False)
+    (part_lse,) = sweep(scaled_cost, log_mass_b[None, :], log_mass_b, log_mass_a, shrink, False, True, False)
     for step_num in range(ITERS):
         every = lax.all_gather(part_lse[0], ("src", "tgt"))
-        every_peak = jnp.max(every, axis=0)
-        col_lse = every_peak + jnp.log(jnp.sum(jnp.exp(every - every_peak[None, :]), axis=0))
-        pot_tgt = -shrink * EPS * col_lse
-        col_shift = pot_tgt * (1.0 / EPS) + log_mass_b
         if step_num + 1 < ITERS:
-            pot_col, part_lse = sweep(scaled_cost, col_shift, log_mass_a, shrink, True, True, False)
+            pot_col, part_lse = sweep(scaled_cost, every, log_mass_b, log_mass_a, shrink, True, True, False)
         else:
-            pot_col, weights = sweep(scaled_cost, col_shift, log_mass_a, shrink, True, False, True)
+            pot_col, weights = sweep(scaled_cost, every, log_mass_b, log_mass_a, shrink, True, False, True)
     pot_src = pot_col.reshape(rows)
     final_handed = lax.all_gather(final_fates.astype(jnp.bfloat16), "tgt", axis=1, tiled=True)
     handed = jnp.where(is_last, final_handed, jnp.zeros(final_handed.shape, jnp.bfloat16))
@@ -186,8 +188,8 @@
     for section_num in range(pair_count):
         active = pair_count - 1 - section_num
         pulled = lax.dot_general(
-            handed, weights, (((1,), (1,)), ((), ())), preferred_element_type=jnp.float32
-        )
+            weights, handed, (((1,), (1,)), ((), ())), preferred_element_type=jnp.float32
+        ).T
         pulled = jnp.where(live_src[None, :], pulled, 0.0)
         fate_maps = jnp.where(pair_rank == active, pulled, fate_maps)
         if section_num + 1 < pair_count:

time: 248 us -> 215 us (0.87)
  local copies, waits for them, and re-layouts: 34.5 us -> 7.15 us
  other arithmetic: 12.6 us -> 5.5 us
    unnamed x24 -> x14, local copies, waits for them, and re-layouts: 31.3 us -> 3.96 us
    add x8 -> x0, other arithmetic: 5.36 us -> none  [local(): col_shift = pot_tgt * (1.0 / EPS) + log_mass_b]
where the time goes in v6:
time: 215 us; the launch traced here: 214 us
  blocking collectives  122 us (57%)
  Pallas kernels  42.8 us (20%)
  matrix products  20.1 us (9%)
  waiting for transfers between devices  9.77 us (5%)
  local copies, waits for them, and re-layouts  7.15 us (3%)
  other arithmetic  5.5 us (3%)
  starting transfers between devices  5.17 us (2%)
  between operations  2.28 us (1%)
    all_gather x8, blocking collectives, local(): every = lax.all_gather(part_lse[0], ('src', 'tgt'))  70 us
    pallas_call x9, Pallas kernels, sweep(): pl.pallas_call(functools.partial(sweep_kernel, do_row, do_col, emit_w, sh...  42.8 us
    all_gather x3, blocking collectives, local(): fresh = lax.all_gather(passed, ('src', 'tgt'), axis=1, tiled=True)  26.4 us
    dot_general x4, matrix products, local(): lax.dot_general(weights, handed, (((1,), (1,)), ((), ())), preferred_elem...  12.7 us
    all_gather x1, blocking collectives, local(): pieces = lax.all_gather(piece, ('src', 'tgt'))  9.83 us
    ppermute x4, waiting for transfers between devices, shifted(): return lax.ppermute(shard, axis, pairs)  9.77 us
    psum x1, blocking collectives, local(): pot_all = lax.psum(pot_spread, 'tgt')  7.64 us
    all_gather x1, blocking collectives, local(): lax.all_gather(final_fates.astype(jnp.bfloat16), 'tgt', axis=1, tiled=True)  7.61 us
  transfers between devices with their start and end apart: 4, of which 2 were waited for; matrix products, arithmetic and copies ran while one was open for 3% of the time, Pallas kernels for 0%

profile of v6, /device:TPU:0, one launch (start us, length us, event | category | flops | bytes accessed | tf_op | source)
XLA Modules:
  0.0 214.3 jit_solution(2564678997645670009)
XLA Ops:
  0.6 1.0 copy.38
  1.7 1.3 collective-permute-start
  3.0 0.7 pad_clamp_fusion
  3.6 0.8 constant_dynamic-slice_fusion
  4.5 1.3 fusion.10
  7.2 0.7 compare_select_fusion.every_ref.lb_ref
  7.9 0.9 convert_element_type.18
  8.8 7.6 %all_gather.42 = bf16[40,4096]{1,0:T(8,128)(2,1)S(1)} all-gather(bf16[40,1024]{1,0:T(8,128)(2,1)S(1)} %convert_element_type.18), channel_id=1, replica_groups=mesh['pair'=4,'src'=2,'tgt'=4] {'tgt'}, dimensions={1}, use_global_device_ids=true | all-gather | bytes 409600 | tf_op jit(solution)/shard_map/all_gather | solution.py:185
  16.4 0.7 subtract_bitcast_fusion
  17.1 0.7 add_compare_fusion.1
  17.9 0.7 fusion.4.la_ref
  18.6 0.9 select_bitcast_fusion.1
  19.5 9.8 %all-gather.1 = f32[8,30,512]{2,1,0:T(8,128)S(1)} all-gather(f32[1,30,512]{2,1,0:T(8,128)S(1)} %select_bitcast_fusion.1), channel_id=2, replica_groups=mesh['pair'=4,'src'=2,'tgt'=4] {'src','tgt'}, dimensions={0}, use_global_device_ids=true | all-gather | bytes 552960 | tf_op jit(solution)/shard_map/all_gather | solution.py:138
  29.3 0.6 gather_fusion
  30.1 0.3 copy.10
  30.4 0.3 copy.23
  30.7 7.4 %subtract_multiply_fusion.c_ref = f32[512,4096]{1,0:T(8,128)S(1)} fusion(f32[30,4096]{1,0:T(8,128)S(1)} %bitcast.80, f32[4096]{0:T(1024)S(1)} %bitcast.83, f32[512]{0:T(512)S(1)} %fusion.7, f32[1,30,512]{2,0,1:T(1,128)S(1)} %constant_dynamic-slice_fusion), kind=kOutput, calls=%fused_computation.1 | convolution fusion | flops 763363328 | bytes 8960000 | tf_op jit(solution)/shard_map/dot_general | solution.py:153
  38.2 2.2 %shard_map.77 = f32[1,4096]{1,0:T(1,128)S(1)} custom-call(f32[512,4096]{1,0:T(8,128)S(1)} %subtract_multiply_fusion.c_ref, f32[1,4096]{1,0:T(1,128)S(1)} %compare_select_fusion.every_ref.lb_ref, f32[1,4096]{1,0:T(1,128)S(1)} %compare_select_fusion.every_ref.lb_ref, f32[512,1]{1,0:T(8,128)S(1)} %fusion.4.la_ref), custom_call_target="tpu_custom_call" | custom-call | flops 16777216 | bytes 8388608 | tf_op jit(solution)/shard_map/pallas_call | solution.py:96
  40.4 9.1 %all-gather.2 = f32[8,1,4096]{2,1,0:T(1,128)S(1)} all-gather(f32[1,1,4096]{2,1,0:T(1,128)S(1)} %bitcast.72), channel_id=1, replica_groups=mesh['pair'=4,'src'=2,'tgt'=4] {'src','tgt'}, dimensions={0}, use_global_device_ids=true | all-gather | bytes 147456 | tf_op jit(solution)/shard_map/all_gather | solution.py:179
  49.5 5.2 %shard_map.78 = (f32[512,1]{1,0:T(8,128)}, f32[1,4096]{1,0:T(1,128)S(1)}) custom-call(f32[512,4096]{1,0:T(8,128)S(1)} %subtract_multiply_fusion.c_ref, f32[8,4096]{1,0:T(8,128)S(1)} %bitcast.65, f32[1,4096]{1,0:T(1,128)S(1)} %compare_select_fusion.every_ref.lb_ref, f32[512,1]{1,0:T(8,128)S(1)} %fusion.4.la_ref), custom_call_target="tpu_custom_call" | custom-call | flops 33554432 | bytes 8388608 | tf_op jit(solution)/shard_map/pallas_call | solution.py:96
  54.7 8.5 %all-gather.3 = f32[8,1,4096]{2,1,0:T(1,128)S(1)} all-gather(f32[1,1,4096]{2,1,0:T(1,128)S(1)} %bitcast.73), channel_id=1, replica_groups=mesh['pair'=4,'src'=2,'tgt'=4] {'src','tgt'}, dimensions={0}, use_global_device_ids=true | all-gather | bytes 147456 | tf_op jit(solution)/shard_map/all_gather | solution.py:179
  63.4 5.2 %shard_map.79 = (f32[512,1]{1,0:T(8,128)}, f32[1,4096]{1,0:T(1,128)S(1)}) custom-call(f32[512,4096]{1,0:T(8,128)S(1)} %subtract_multiply_fusion.c_ref, f32[8,4096]{1,0:T(8,128)S(1)} %bitcast.66, f32[1,4096]{1,0:T(1,128)S(1)} %compare_select_fusion.every_ref.lb_ref, f32[512,1]{1,0:T(8,128)S(1)} %fusion.4.la_ref), custom_call_target="tpu_custom_call" | custom-call | flops 33554432 | bytes 8388608 | tf_op jit(solution)/shard_map/pallas_call | solution.py:96
  68.6 9.0 %all-gather.4 = f32[8,1,4096]{2,1,0:T(1,128)S(1)} all-gather(f32[1,1,4096]{2,1,0:T(1,128)S(1)} %bitcast.74), channel_id=1, replica_groups=mesh['pair'=4,'src'=2,'tgt'=4] {'src','tgt'}, dimensions={0}, use_global_device_ids=true | all-gather | bytes 147456 | tf_op jit(solution)/shard_map/all_gather | solution.py:179
  77.7 5.2 %shard_map.80 = (f32[512,1]{1,0:T(8,128)}, f32[1,4096]{1,0:T(1,128)S(1)}) custom-call(f32[512,4096]{1,0:T(8,128)S(1)} %subtract_multiply_fusion.c_ref, f32[8,4096]{1,0:T(8,128)S(1)} %bitcast.67, f32[1,4096]{1,0:T(1,128)S(1)} %compare_select_fusion.every_ref.lb_ref, f32[512,1]{1,0:T(8,128)S(1)} %fusion.4.la_ref), custom_call_target="tpu_custom_call" | custom-call | flops 33554432 | bytes 8388608 | tf_op jit(solution)/shard_map/pallas_call | solution.py:96
  83.0 8.4 %all-gather.5 = f32[8,1,4096]{2,1,0:T(1,128)S(1)} all-gather(f32[1,1,4096]{2,1,0:T(1,128)S(1)} %bitcast.75), channel_id=1, replica_groups=mesh['pair'=4,'src'=2,'tgt'=4] {'src','tgt'}, dimensions={0}, use_global_device_ids=true | all-gather | bytes 147456 | tf_op jit(solution)/shard_map/all_gather | solution.py:179
  91.4 5.2 %shard_map.81 = (f32[512,1]{1,0:T(8,128)}, f32[1,4096]{1,0:T(1,128)S(1)}) custom-call(f32[512,4096]{1,0:T(8,128)S(1)} %subtract_multiply_fusion.c_ref, f32[8,4096]{1,0:T(8,128)S(1)} %bitcast.68, f32[1,4096]{1,0:T(1,128)S(1)} %compare_select_fusion.every_ref.lb_ref, f32[512,1]{1,0:T(8,128)S(1)} %fusion.4.la_ref), custom_call_target="tpu_custom_call" | custom-call | flops 33554432 | bytes 8388608 | tf_op jit(solution)/shard_map/pallas_call | solution.py:96
  96.7 9.0 %all-gather.6 = f32[8,1,4096]{2,1,0:T(1,128)S(1)} all-gather(f32[1,1,4096]{2,1,0:T(1,128)S(1)} %bitcast.76), channel_id=1, replica_groups=mesh['pair'=4,'src'=2,'tgt'=4] {'src','tgt'}, dimensions={0}, use_global_device_ids=true | all-gather | bytes 147456 | tf_op jit(solution)/shard_map/all_gather | solution.py:179
  105.8 5.2 %shard_map.82 = (f32[512,1]{1,0:T(8,128)}, f32[1,4096]{1,0:T(1,128)S(1)}) custom-call(f32[512,4096]{1,0:T(8,128)S(1)} %subtract_multiply_fusion.c_ref, f32[8,4096]{1,0:T(8,128)S(1)} %bitcast.69, f32[1,4096]{1,0:T(1,128)S(1)} %compare_select_fusion.every_ref.lb_ref, f32[512,1]{1,0:T(8,128)S(1)} %fusion.4.la_ref), custom_call_target="tpu_custom_call" | custom-call | flops 33554432 | bytes 8388608 | tf_op jit(solution)/shard_map/pallas_call | solution.py:96
  111.0 8.4 %all-gather.7 = f32[8,1,4096]{2,1,0:T(1,128)S(1)} all-gather(f32[1,1,4096]{2,1,0:T(1,128)S(1)} %bitcast.77), channel_id=1, replica_groups=mesh['pair'=4,'src'=2,'tgt'=4] {'src','tgt'}, dimensions={0}, use_global_device_ids=true | all-gather | bytes 147456 | tf_op jit(solution)/shard_map/all_gather | solution.py:179
  119.5 5.2 %shard_map.83 = (f32[512,1]{1,0:T(8,128)}, f32[1,4096]{1,0:T(1,128)S(1)}) custom-call(f32[512,4096]{1,0:T(8,128)S(1)} %subtract_multiply_fusion.c_ref, f32[8,4096]{1,0:T(8,128)S(1)} %bitcast.70, f32[1,4096]{1,0:T(1,128)S(1)} %compare_select_fusion.every_ref.lb_ref, f32[512,1]{1,0:T(8,128)S(1)} %fusion.4.la_ref), custom_call_target="tpu_custom_call" | custom-call | flops 33554432 | bytes 8388608 | tf_op jit(solution)/shard_map/pallas_call | solution.py:96
  124.7 9.0 %all-gather.8 = f32[8,1,4096]{2,1,0:T(1,128)S(1)} all-gather(f32[1,1,4096]{2,1,0:T(1,128)S(1)} %bitcast.78), channel_id=1, replica_groups=mesh['pair'=4,'src'=2,'tgt'=4] {'src','tgt'}, dimensions={0}, use_global_device_ids=true | all-gather | bytes 147456 | tf_op jit(solution)/shard_map/all_gather | solution.py:179
  133.9 5.2 %shard_map.84 = (f32[512,1]{1,0:T(8,128)}, f32[1,4096]{1,0:T(1,128)S(1)}) custom-call(f32[512,4096]{1,0:T(8,128)S(1)} %subtract_multiply_fusion.c_ref, f32[8,4096]{1,0:T(8,128)S(1)} %bitcast.71, f32[1,4096]{1,0:T(1,128)S(1)} %compare_select_fusion.every_ref.lb_ref, f32[512,1]{1,0:T(8,128)S(1)} %fusion.4.la_ref), custom_call_target="tpu_custom_call" | custom-call | flops 33554432 | bytes 8388608 | tf_op jit(solution)/shard_map/pallas_call | solution.py:96
  139.1 8.6 %all-gather.9 = f32[8,1,4096]{2,1,0:T(1,128)S(1)} all-gather(f32[1,1,4096]{2,1,0:T(1,128)S(1)} %bitcast.79), channel_id=1, replica_groups=mesh['pair'=4,'src'=2,'tgt'=4] {'src','tgt'}, dimensions={0}, use_global_device_ids=true | all-gather | bytes 147456 | tf_op jit(solution)/shard_map/all_gather | solution.py:179
  147.8 3.9 %shard_map.85 = (f32[512,1]{1,0:T(8,128)S(1)}, bf16[512,4096]{1,0:T(8,128)(2,1)S(1)}) custom-call(f32[512,4096]{1,0:T(8,128)S(1)} %subtract_multiply_fusion.c_ref, f32[8,4096]{1,0:T(8,128)S(1)} %bitcast.64, f32[1,4096]{1,0:T(1,128)S(1)} %compare_select_fusion.every_ref.lb_ref, f32[512,1]{1,0:T(8,128)S(1)} %fusion.4.la_ref), custom_call_target="tpu_custom_call" | custom-call | flops 25165824 | bytes 12582912 | tf_op jit(solution)/shard_map/pallas_call | solution.py:96
  151.7 1.9 copy-done
  153.6 1.4 fusion.11
  155.0 1.3 collective-permute-start.1
  156.3 5.3 %collective-permute-done.1 = bf16[40,512]{1,0:T(8,128)(2,1)S(1)} collective-permute-done((bf16[40,512]{1,0:T(8,128)(2,1)S(1)}, bf16[40,512]{1,0:T(8,128)(2,1)S(1)}, u32[]{:S(2)}, u32[]{:S(2)}) %collective-permute-start.1) | collective-permute-done | bytes 40992 | tf_op jit(solution)/shard_map/ppermute | solution.py:114
  161.6 9.3 %all_gather.53 = bf16[40,4096]{1,0:T(8,128)(2,1)S(1)} all-gather(bf16[40,512]{1,0:T(8,128)(2,1)S(1)} %collective-permute-done.1), channel_id=1, replica_groups=mesh['pair'=4,'src'=2,'tgt'=4] {'src','tgt'}, dimensions={1}, use_global_device_ids=true | all-gather | bytes 368640 | tf_op jit(solution)/shard_map/all_gather | solution.py:197
  170.9 3.6 %fusion.12 = (bf16[40,512]{1,0:T(8,128)(2,1)S(1)}, f32[40,512]{1,0:T(8,128)S(1)}) fusion(bf16[40,4096]{1,0:T(8,128)(2,1)S(1)} %broadcast_select_fusion.1, bf16[512,4096]{1,0:T(8,128)(2,1)} %copy-done, pred[512]{0:T(512)(128)(4,1)S(1)} %add_compare_fusion.1), kind=kOutput, calls=%fused_computation.41 | convolution fusion | flops 167813120 | bytes 4645376 | tf_op jit(solution)/shard_map/dot_general | solution.py:190
  174.5 1.3 collective-permute-start.2
  175.9 4.4 %collective-permute-done.2 = bf16[40,512]{1,0:T(8,128)(2,1)S(1)} collective-permute-done((bf16[40,512]{1,0:T(8,128)(2,1)S(1)}, bf16[40,512]{1,0:T(8,128)(2,1)S(1)}, u32[]{:S(2)}, u32[]{:S(2)}) %collective-permute-start.2) | collective-permute-done | bytes 40992 | tf_op jit(solution)/shard_map/ppermute | solution.py:114
  180.4 8.6 %all_gather.54 = bf16[40,4096]{1,0:T(8,128)(2,1)S(1)} all-gather(bf16[40,512]{1,0:T(8,128)(2,1)S(1)} %collective-permute-done.2), channel_id=1, replica_groups=mesh['pair'=4,'src'=2,'tgt'=4] {'src','tgt'}, dimensions={1}, use_global_device_ids=true | all-gather | bytes 368640 | tf_op jit(solution)/shard_map/all_gather | solution.py:197
  189.0 3.6 %fusion.13 = (bf16[40,512]{1,0:T(8,128)(2,1)S(1)}, f32[40,512]{1,0:T(8,128)S(1)}) fusion(bf16[512,4096]{1,0:T(8,128)(2,1)} %copy-done, bf16[40,4096]{1,0:T(8,128)(2,1)S(1)} %all_gather.54, bf16[40,4096]{1,0:T(8,128)(2,1)S(1)} %broadcast_select_fusion.1, pred[]{:T(512)S(6)} %eq.19, pred[512]{0:T(512)(128)(4,1)S(1)} %add_compare_fusion.1), kind=kOutput, calls=%fused_computation.42 | convolution fusion | flops 167976960 | bytes 4973057 | tf_op jit(solution)/shard_map/dot_general | solution.py:190
  192.6 1.3 collective-permute-start.3
  193.9 7.6 %psum.7 = f32[1,2048]{1,0:T(1,128)} all-reduce(f32[1,2048]{1,0:T(1,128)S(1)} %constant_dynamic-update-slice_fusion), channel_id=1, replica_groups=mesh['pair'=4,'src'=2,'tgt'=4] {'tgt'}, use_global_device_ids=true, to_apply=%region_2.3 | all-reduce | flops 2048 | bytes 16384 | tf_op jit(solution)/shard_map/psum | solution.py:200
  201.5 8.6 %all_gather.55 = bf16[40,4096]{1,0:T(8,128)(2,1)S(1)} all-gather(bf16[40,512]{1,0:T(8,128)(2,1)S(1)} %collective-permute-done.3), channel_id=1, replica_groups=mesh['pair'=4,'src'=2,'tgt'=4] {'src','tgt'}, dimensions={1}, use_global_device_ids=true | all-gather | bytes 368640 | tf_op jit(solution)/shard_map/all_gather | solution.py:197
  210.1 4.2 %fusion.1 = f32[1,40,512]{2,1,0:T(8,128)} fusion(bf16[512,4096]{1,0:T(8,128)(2,1)} %copy-done, bf16[40,4096]{1,0:T(8,128)(2,1)S(1)} %all_gather.55, pred[]{:T(512)S(6)} %eq.18, bf16[40,4096]{1,0:T(8,128)(2,1)S(1)} %all_gather.54, bf16[40,4096]{1,0:T(8,128)(2,1)S(1)} %broadcast_select_fusion.1, pred[]{:T(512)S(6)} %eq.19, ...), kind=kOutput, calls=%fused_computation.7 | convolution fusion | flops 168202240 | bytes 5505540 | tf_op jit(solution)/shard_map/dot_general | solution.py:190
  (20 shorter events, 1.2 us)
Async XLA Ops:
  1.7 17.0 %collective-permute-start = (f32[30,2048]{1,0:T(8,128)S(1)}, f32[30,2048]{1,0:T(8,128)S(1)}, u32[]{:S(2)}, u32[]{:S(2)}) collective-permute-start(f32[30,2048]{1,0:T(8,128)S(1)} %bitcast.82), channel_id=1, source_target_pairs={{8,0},{16,8},{24,16},{9,1},{17,9},{25,17},{10,2},{18,10},{26,18},{... | collective-permute-start | bytes 737288 | tf_op jit(solution)/shard_map/ppermute | solution.py:114
  151.7 1.9 copy-start
  155.0 6.6 %collective-permute-start.1 = (bf16[40,512]{1,0:T(8,128)(2,1)S(1)}, bf16[40,512]{1,0:T(8,128)(2,1)S(1)}, u32[]{:S(2)}, u32[]{:S(2)}) collective-permute-start(bf16[40,512]{1,0:T(8,128)(2,1)S(1)} %get-tuple-element.24), channel_id=1, source_target_pairs={{8,0},{16,8},{24,16},{9,1},{17,9},{25,17},{10,2},{18,10},{26,18},{... | collective-permute-start | bytes 122888 | tf_op jit(solution)/shard_map/ppermute | solution.py:114
  174.5 5.9 %collective-permute-start.2 = (bf16[40,512]{1,0:T(8,128)(2,1)S(1)}, bf16[40,512]{1,0:T(8,128)(2,1)S(1)}, u32[]{:S(2)}, u32[]{:S(2)}) collective-permute-start(bf16[40,512]{1,0:T(8,128)(2,1)S(1)} %get-tuple-element.26), channel_id=1, source_target_pairs={{8,0},{16,8},{24,16},{9,1},{17,9},{25,17},{10,2},{18,10},{26,18},{... | collective-permute-start | bytes 122888 | tf_op jit(solution)/shard_map/ppermute | solution.py:114
  192.6 9.0 %collective-permute-start.3 = (bf16[40,512]{1,0:T(8,128)(2,1)S(1)}, bf16[40,512]{1,0:T(8,128)(2,1)S(1)}, u32[]{:S(2)}, u32[]{:S(2)}) collective-permute-start(bf16[40,512]{1,0:T(8,128)(2,1)S(1)} %get-tuple-element.28), channel_id=1, source_target_pairs={{8,0},{16,8},{24,16},{9,1},{17,9},{25,17},{10,2},{18,10},{26,18},{... | collective-permute-start | bytes 122888 | tf_op jit(solution)/shard_map/ppermute | solution.py:114

commit v7 on v6

--- a/solution.py
+++ b/solution.py
@@ -135,20 +135,28 @@
     fin_width = final_cells.shape[1]
     mine_final = lax.dynamic_slice_in_dim(final_cells, (src_rank * rows) % fin_width, rows, 1)
     piece = jnp.where(is_last, mine_final, mine_next)
-    pieces = lax.all_gather(piece, ("src", "tgt"))
+    fates_count = final_fates.shape[0]
     per_fin = fin_width // rows
-    final_order = [
-        (b % per_fin) * tgt_count + b // per_fin if per_fin == src_count else b for b in range(group)
-    ]
+    final_order = [(b % per_fin) * tgt_count + b // per_fin for b in range(group)]
     if per_fin == src_count:
+        fate_piece = lax.dynamic_slice_in_dim(final_fates, src_rank * rows, rows, 1)
+        fate_piece = fate_piece.astype(jnp.bfloat16).astype(jnp.float32)
+        pieces = lax.all_gather(jnp.concatenate([piece, fate_piece], axis=0), ("src", "tgt"))
         final_pieces = pieces[jnp.array(final_order, dtype=jnp.int32)]
-        pieces = jnp.where(is_last, final_pieces, pieces)
-        target_pos = jnp.transpose(pieces, (1, 0, 2)).reshape(dims, group * rows)
+        cell_pieces = jnp.where(is_last, final_pieces[:, :dims], pieces[:, :dims])
+        target_pos = jnp.transpose(cell_pieces, (1, 0, 2)).reshape(dims, group * rows)
+        final_handed = (
+            jnp.transpose(final_pieces[:, dims:], (1, 0, 2))
+            .reshape(fates_count, group * rows)
+            .astype(jnp.bfloat16)
+        )
     else:
+        pieces = lax.all_gather(piece, ("src", "tgt"))
         final_all = lax.all_gather(final_cells, "tgt", axis=1, tiled=True)
         target_pos = jnp.where(
             is_last, final_all, jnp.transpose(pieces, (1, 0, 2)).reshape(dims, group * rows)
         )
+        final_handed = lax.all_gather(final_fates.astype(jnp.bfloat16), "tgt", axis=1, tiled=True)
     cols = target_pos.shape[1]
     cross = lax.dot_general(
         source_pos,
@@ -182,7 +190,6 @@
         else:
             pot_col, weights = sweep(scaled_cost, every, log_mass_b, log_mass_a, shrink, True, False, True)
     pot_src = pot_col.reshape(rows)
-    final_handed = lax.all_gather(final_fates.astype(jnp.bfloat16), "tgt", axis=1, tiled=True)
     handed = jnp.where(is_last, final_handed, jnp.zeros(final_handed.shape, jnp.bfloat16))
     fate_maps = jnp.zeros((final_fates.shape[0], rows), jnp.float32)
     for section_num in range(pair_count):

time: 215 us -> 240 us (1.12)
  waiting for transfers between devices: 9.77 us -> 35.4 us
  blocking collectives: 122 us -> 104 us
  between operations: 2.28 us -> 15.7 us
    all_gather x2 -> x0, blocking collectives: 17.4 us -> none  [the longest x1 9.83 us: local(): pieces = lax.all_gather(piece, ('src', 'tgt'))]
    all_gather x0 -> x1, waiting for transfers between devices: none -> 17.3 us  [local(): lax.all_gather(jnp.concatenate([piece, fate_piece], axis=0), ('src', 'tgt'))]
    ppermute x4, waiting for transfers between devices: 9.77 us -> 18.1 us  [shifted(): return lax.ppermute(shard, axis, pairs)]
  transfers between devices with their start and end apart: 4 -> 5, of which waited for: 2 -> 4; matrix products, arithmetic and copies ran while one was open for 3% -> 3% of each run, Pallas kernels for 0% -> 0%
where the time goes in v7:
time: 240 us; the launch traced here: 239 us
  blocking collectives  104 us (43%)
  Pallas kernels  42.8 us (18%)
  waiting for transfers between devices  35.4 us (15%)
  matrix products  20.1 us (8%)
  between operations  15.7 us (7%)
  local copies, waits for them, and re-layouts  8.51 us (4%)
  other arithmetic  7.24 us (3%)
  starting transfers between devices  5.21 us (2%)
    all_gather x8, blocking collectives, local(): every = lax.all_gather(part_lse[0], ('src', 'tgt'))  70 us
    pallas_call x9, Pallas kernels, sweep(): pl.pallas_call(functools.partial(sweep_kernel, do_row, do_col, emit_w, sh...  42.8 us
    all_gather x3, blocking collectives, local(): fresh = lax.all_gather(passed, ('src', 'tgt'), axis=1, tiled=True)  26.3 us
    ppermute x4, waiting for transfers between devices, shifted(): return lax.ppermute(shard, axis, pairs)  18.1 us
    all_gather x1, waiting for transfers between devices, local(): lax.all_gather(jnp.concatenate([piece, fate_piece], axis=0), ('src', 'tgt'))  17.3 us
    dot_general x4, matrix products, local(): lax.dot_general(weights, handed, (((1,), (1,)), ((), ())), preferred_elem...  12.7 us
    psum x1, blocking collectives, local(): pot_all = lax.psum(pot_spread, 'tgt')  7.76 us
    dot_general x1, matrix products, local(): lax.dot_general(source_pos, target_pos, (((0,), (0,)), ((), ())), precisi...  7.41 us
  transfers between devices with their start and end apart: 5, of which 4 were waited for; matrix products, arithmetic and copies ran while one was open for 3% of the time, Pallas kernels for 0%

profile of v7, /device:TPU:0, one launch (start us, length us, event | category | flops | bytes accessed | tf_op | source)
XLA Modules:
  0.0 239.0 jit_solution(3778560841155790136)
XLA Ops:
  7.2 1.0 copy.42
  8.2 1.3 collective-permute-start
  9.6 0.9 fusion.11
  10.5 9.0 %collective-permute-done = f32[30,2048]{1,0:T(8,128)S(1)} collective-permute-done((f32[30,2048]{1,0:T(8,128)S(1)}, f32[30,2048]{1,0:T(8,128)S(1)}, u32[]{:S(2)}, u32[]{:S(2)}) %collective-permute-start) | collective-permute-done | bytes 245792 | tf_op jit(solution)/shard_map/ppermute | solution.py:114
  19.5 0.8 dynamic-slice_select_fusion
  20.3 0.7 maximum_bitcast_fusion
  21.1 1.3 fusion.13
  23.8 0.7 subtract_bitcast_fusion
  24.6 0.7 add_compare_fusion.1
  25.3 0.7 pad_clamp_fusion
  26.0 0.8 constant_dynamic-slice_fusion
  26.8 0.7 fusion.7.la_ref
  27.5 0.7 compare_select_fusion.every_ref.lb_ref
  28.2 17.3 %all-gather.12.cloned.1.call-done = f32[8,70,512]{2,1,0:T(8,128)} async-done(((f32[1,70,512]{2,1,0:T(8,128)}), f32[8,70,512]{2,1,0:T(8,128)}) %all-gather.12.cloned.1.call-update) | async-done | bytes 1146896 | tf_op jit(solution)/shard_map/all_gather | solution.py:144
  45.5 1.9 gather_fusion
  47.5 1.2 multiply_reduce_fusion
  49.4 7.4 %subtract_multiply_fusion.c_ref = f32[512,4096]{1,0:T(8,128)S(1)} fusion(f32[30,4096]{1,0:T(8,128)S(1)} %bitcast.87, f32[4096]{0:T(1024)S(1)} %bitcast.90, f32[512]{0:T(512)S(1)} %fusion.9, f32[1,30,512]{2,0,1:T(1,128)S(1)} %constant_dynamic-slice_fusion), kind=kOutput, calls=%fused_computation.1 | convolution fusion | flops 763363328 | bytes 8960000 | tf_op jit(solution)/shard_map/dot_general | solution.py:161
  56.8 2.2 shard_map.77
  59.0 9.2 %all-gather.2 = f32[8,1,4096]{2,1,0:T(1,128)S(1)} all-gather(f32[1,1,4096]{2,1,0:T(1,128)S(1)} %bitcast.77), channel_id=1, replica_groups=mesh['pair'=4,'src'=2,'tgt'=4] {'src','tgt'}, dimensions={0}, use_global_device_ids=true | all-gather | bytes 147456 | tf_op jit(solution)/shard_map/all_gather | solution.py:187
  68.2 5.2 %shard_map.78 = (f32[512,1]{1,0:T(8,128)}, f32[1,4096]{1,0:T(1,128)S(1)}) custom-call(f32[512,4096]{1,0:T(8,128)S(1)} %subtract_multiply_fusion.c_ref, f32[8,4096]{1,0:T(8,128)S(1)} %bitcast.70, f32[1,4096]{1,0:T(1,128)S(1)} %compare_select_fusion.every_ref.lb_ref, f32[512,1]{1,0:T(8,128)S(1)} %fusion.7.la_ref), custom_call_target="tpu_custom_call" | custom-call | flops 33554432 | bytes 8388608 | tf_op jit(solution)/shard_map/pallas_call | solution.py:96
  73.5 8.4 %all-gather.3 = f32[8,1,4096]{2,1,0:T(1,128)S(1)} all-gather(f32[1,1,4096]{2,1,0:T(1,128)S(1)} %bitcast.78), channel_id=1, replica_groups=mesh['pair'=4,'src'=2,'tgt'=4] {'src','tgt'}, dimensions={0}, use_global_device_ids=true | all-gather | bytes 147456 | tf_op jit(solution)/shard_map/all_gather | solution.py:187
  82.0 5.2 %shard_map.79 = (f32[512,1]{1,0:T(8,128)}, f32[1,4096]{1,0:T(1,128)S(1)}) custom-call(f32[512,4096]{1,0:T(8,128)S(1)} %subtract_multiply_fusion.c_ref, f32[8,4096]{1,0:T(8,128)S(1)} %bitcast.71, f32[1,4096]{1,0:T(1,128)S(1)} %compare_select_fusion.every_ref.lb_ref, f32[512,1]{1,0:T(8,128)S(1)} %fusion.7.la_ref), custom_call_target="tpu_custom_call" | custom-call | flops 33554432 | bytes 8388608 | tf_op jit(solution)/shard_map/pallas_call | solution.py:96
  87.2 9.1 %all-gather.4 = f32[8,1,4096]{2,1,0:T(1,128)S(1)} all-gather(f32[1,1,4096]{2,1,0:T(1,128)S(1)} %bitcast.79), channel_id=1, replica_groups=mesh['pair'=4,'src'=2,'tgt'=4] {'src','tgt'}, dimensions={0}, use_global_device_ids=true | all-gather | bytes 147456 | tf_op jit(solution)/shard_map/all_gather | solution.py:187
  96.5 5.2 %shard_map.80 = (f32[512,1]{1,0:T(8,128)}, f32[1,4096]{1,0:T(1,128)S(1)}) custom-call(f32[512,4096]{1,0:T(8,128)S(1)} %subtract_multiply_fusion.c_ref, f32[8,4096]{1,0:T(8,128)S(1)} %bitcast.72, f32[1,4096]{1,0:T(1,128)S(1)} %compare_select_fusion.every_ref.lb_ref, f32[512,1]{1,0:T(8,128)S(1)} %fusion.7.la_ref), custom_call_target="tpu_custom_call" | custom-call | flops 33554432 | bytes 8388608 | tf_op jit(solution)/shard_map/pallas_call | solution.py:96
  101.7 8.2 %all-gather.5 = f32[8,1,4096]{2,1,0:T(1,128)S(1)} all-gather(f32[1,1,4096]{2,1,0:T(1,128)S(1)} %bitcast.80), channel_id=1, replica_groups=mesh['pair'=4,'src'=2,'tgt'=4] {'src','tgt'}, dimensions={0}, use_global_device_ids=true | all-gather | bytes 147456 | tf_op jit(solution)/shard_map/all_gather | solution.py:187
  110.0 5.2 %shard_map.81 = (f32[512,1]{1,0:T(8,128)}, f32[1,4096]{1,0:T(1,128)S(1)}) custom-call(f32[512,4096]{1,0:T(8,128)S(1)} %subtract_multiply_fusion.c_ref, f32[8,4096]{1,0:T(8,128)S(1)} %bitcast.73, f32[1,4096]{1,0:T(1,128)S(1)} %compare_select_fusion.every_ref.lb_ref, f32[512,1]{1,0:T(8,128)S(1)} %fusion.7.la_ref), custom_call_target="tpu_custom_call" | custom-call | flops 33554432 | bytes 8388608 | tf_op jit(solution)/shard_map/pallas_call | solution.py:96
  115.3 9.1 %all-gather.6 = f32[8,1,4096]{2,1,0:T(1,128)S(1)} all-gather(f32[1,1,4096]{2,1,0:T(1,128)S(1)} %bitcast.81), channel_id=1, replica_groups=mesh['pair'=4,'src'=2,'tgt'=4] {'src','tgt'}, dimensions={0}, use_global_device_ids=true | all-gather | bytes 147456 | tf_op jit(solution)/shard_map/all_gather | solution.py:187
  124.5 5.2 %shard_map.82 = (f32[512,1]{1,0:T(8,128)}, f32[1,4096]{1,0:T(1,128)S(1)}) custom-call(f32[512,4096]{1,0:T(8,128)S(1)} %subtract_multiply_fusion.c_ref, f32[8,4096]{1,0:T(8,128)S(1)} %bitcast.74, f32[1,4096]{1,0:T(1,128)S(1)} %compare_select_fusion.every_ref.lb_ref, f32[512,1]{1,0:T(8,128)S(1)} %fusion.7.la_ref), custom_call_target="tpu_custom_call" | custom-call | flops 33554432 | bytes 8388608 | tf_op jit(solution)/shard_map/pallas_call | solution.py:96
  129.8 8.2 %all-gather.7 = f32[8,1,4096]{2,1,0:T(1,128)S(1)} all-gather(f32[1,1,4096]{2,1,0:T(1,128)S(1)} %bitcast.82), channel_id=1, replica_groups=mesh['pair'=4,'src'=2,'tgt'=4] {'src','tgt'}, dimensions={0}, use_global_device_ids=true | all-gather | bytes 147456 | tf_op jit(solution)/shard_map/all_gather | solution.py:187
  138.1 5.2 %shard_map.83 = (f32[512,1]{1,0:T(8,128)}, f32[1,4096]{1,0:T(1,128)S(1)}) custom-call(f32[512,4096]{1,0:T(8,128)S(1)} %subtract_multiply_fusion.c_ref, f32[8,4096]{1,0:T(8,128)S(1)} %bitcast.75, f32[1,4096]{1,0:T(1,128)S(1)} %compare_select_fusion.every_ref.lb_ref, f32[512,1]{1,0:T(8,128)S(1)} %fusion.7.la_ref), custom_call_target="tpu_custom_call" | custom-call | flops 33554432 | bytes 8388608 | tf_op jit(solution)/shard_map/pallas_call | solution.py:96
  143.3 9.1 %all-gather.8 = f32[8,1,4096]{2,1,0:T(1,128)S(1)} all-gather(f32[1,1,4096]{2,1,0:T(1,128)S(1)} %bitcast.83), channel_id=1, replica_groups=mesh['pair'=4,'src'=2,'tgt'=4] {'src','tgt'}, dimensions={0}, use_global_device_ids=true | all-gather | bytes 147456 | tf_op jit(solution)/shard_map/all_gather | solution.py:187
  152.6 5.2 %shard_map.84 = (f32[512,1]{1,0:T(8,128)}, f32[1,4096]{1,0:T(1,128)S(1)}) custom-call(f32[512,4096]{1,0:T(8,128)S(1)} %subtract_multiply_fusion.c_ref, f32[8,4096]{1,0:T(8,128)S(1)} %bitcast.76, f32[1,4096]{1,0:T(1,128)S(1)} %compare_select_fusion.every_ref.lb_ref, f32[512,1]{1,0:T(8,128)S(1)} %fusion.7.la_ref), custom_call_target="tpu_custom_call" | custom-call | flops 33554432 | bytes 8388608 | tf_op jit(solution)/shard_map/pallas_call | solution.py:96
  157.8 8.5 %all-gather.9 = f32[8,1,4096]{2,1,0:T(1,128)S(1)} all-gather(f32[1,1,4096]{2,1,0:T(1,128)S(1)} %bitcast.84), channel_id=1, replica_groups=mesh['pair'=4,'src'=2,'tgt'=4] {'src','tgt'}, dimensions={0}, use_global_device_ids=true | all-gather | bytes 147456 | tf_op jit(solution)/shard_map/all_gather | solution.py:187
  166.4 3.9 %shard_map.85 = (f32[512,1]{1,0:T(8,128)S(1)}, bf16[512,4096]{1,0:T(8,128)(2,1)S(1)}) custom-call(f32[512,4096]{1,0:T(8,128)S(1)} %subtract_multiply_fusion.c_ref, f32[8,4096]{1,0:T(8,128)S(1)} %bitcast.69, f32[1,4096]{1,0:T(1,128)S(1)} %compare_select_fusion.every_ref.lb_ref, f32[512,1]{1,0:T(8,128)S(1)} %fusion.7.la_ref), custom_call_target="tpu_custom_call" | custom-call | flops 25165824 | bytes 12582912 | tf_op jit(solution)/shard_map/pallas_call | solution.py:96
  170.3 1.9 copy-done
  172.2 1.4 fusion.14
  173.6 1.3 collective-permute-start.1
  174.9 4.6 %collective-permute-done.1 = bf16[40,512]{1,0:T(8,128)(2,1)S(1)} collective-permute-done((bf16[40,512]{1,0:T(8,128)(2,1)S(1)}, bf16[40,512]{1,0:T(8,128)(2,1)S(1)}, u32[]{:S(2)}, u32[]{:S(2)}) %collective-permute-start.1) | collective-permute-done | bytes 40992 | tf_op jit(solution)/shard_map/ppermute | solution.py:114
  179.5 9.4 %all_gather.49 = bf16[40,4096]{1,0:T(8,128)(2,1)S(1)} all-gather(bf16[40,512]{1,0:T(8,128)(2,1)S(1)} %collective-permute-done.1), channel_id=1, replica_groups=mesh['pair'=4,'src'=2,'tgt'=4] {'src','tgt'}, dimensions={1}, use_global_device_ids=true | all-gather | bytes 368640 | tf_op jit(solution)/shard_map/all_gather | solution.py:204
  188.9 3.6 %fusion.15 = (bf16[40,512]{1,0:T(8,128)(2,1)S(1)}, f32[40,512]{1,0:T(8,128)S(1)}) fusion(bf16[40,4096]{1,0:T(8,128)(2,1)S(1)} %broadcast_select_fusion, bf16[512,4096]{1,0:T(8,128)(2,1)} %copy-done, pred[512]{0:T(512)(128)(4,1)S(1)} %add_compare_fusion.1), kind=kOutput, calls=%fused_computation.45 | convolution fusion | flops 167813120 | bytes 4645376 | tf_op jit(solution)/shard_map/dot_general | solution.py:197
  192.5 1.3 collective-permute-start.2
  193.9 4.4 %collective-permute-done.2 = bf16[40,512]{1,0:T(8,128)(2,1)S(1)} collective-permute-done((bf16[40,512]{1,0:T(8,128)(2,1)S(1)}, bf16[40,512]{1,0:T(8,128)(2,1)S(1)}, u32[]{:S(2)}, u32[]{:S(2)}) %collective-permute-start.2) | collective-permute-done | bytes 40992 | tf_op jit(solution)/shard_map/ppermute | solution.py:114
  198.4 8.5 %all_gather.50 = bf16[40,4096]{1,0:T(8,128)(2,1)S(1)} all-gather(bf16[40,512]{1,0:T(8,128)(2,1)S(1)} %collective-permute-done.2), channel_id=1, replica_groups=mesh['pair'=4,'src'=2,'tgt'=4] {'src','tgt'}, dimensions={1}, use_global_device_ids=true | all-gather | bytes 368640 | tf_op jit(solution)/shard_map/all_gather | solution.py:204
  206.8 3.6 %fusion.16 = (bf16[40,512]{1,0:T(8,128)(2,1)S(1)}, f32[40,512]{1,0:T(8,128)S(1)}) fusion(bf16[512,4096]{1,0:T(8,128)(2,1)} %copy-done, bf16[40,4096]{1,0:T(8,128)(2,1)S(1)} %all_gather.50, bf16[40,4096]{1,0:T(8,128)(2,1)S(1)} %broadcast_select_fusion, pred[]{:T(512)S(6)} %eq.19, pred[512]{0:T(512)(128)(4,1)S(1)} %add_compare_fusion.1), kind=kOutput, calls=%fused_computation.46 | convolution fusion | flops 167976960 | bytes 4973057 | tf_op jit(solution)/shard_map/dot_general | solution.py:197
  210.4 1.3 collective-permute-start.3
  211.7 7.8 %psum.7 = f32[1,2048]{1,0:T(1,128)} all-reduce(f32[1,2048]{1,0:T(1,128)S(1)} %constant_dynamic-update-slice_fusion), channel_id=1, replica_groups=mesh['pair'=4,'src'=2,'tgt'=4] {'tgt'}, use_global_device_ids=true, to_apply=%region_2.3 | all-reduce | flops 2048 | bytes 16384 | tf_op jit(solution)/shard_map/psum | solution.py:207
  219.5 8.5 %all_gather.51 = bf16[40,4096]{1,0:T(8,128)(2,1)S(1)} all-gather(bf16[40,512]{1,0:T(8,128)(2,1)S(1)} %collective-permute-done.3), channel_id=1, replica_groups=mesh['pair'=4,'src'=2,'tgt'=4] {'src','tgt'}, dimensions={1}, use_global_device_ids=true | all-gather | bytes 368640 | tf_op jit(solution)/shard_map/all_gather | solution.py:204
  228.0 4.2 %fusion.1 = f32[1,40,512]{2,1,0:T(8,128)} fusion(bf16[512,4096]{1,0:T(8,128)(2,1)} %copy-done, bf16[40,4096]{1,0:T(8,128)(2,1)S(1)} %all_gather.51, pred[]{:T(512)S(6)} %eq.18, bf16[40,4096]{1,0:T(8,128)(2,1)S(1)} %all_gather.50, bf16[40,4096]{1,0:T(8,128)(2,1)S(1)} %broadcast_select_fusion, pred[]{:T(512)S(6)} %eq.19, f32[40,512]{1,0:T(8,128)S(1)} %get-tuple-element.29, ...), kind=kOutput, calls=%fused_computation.7 | convolution fusion | flops 168202240 | bytes 5505540 | tf_op jit(solution)/shard_map/dot_general | solution.py:197
  (24 shorter events, 1.8 us)
Async XLA Ops:
  7.2 38.4 %all-gather.12.cloned.1.call-start = ((), (), s32[]{:S(2)}) async-start(), calls=%async_computation | async-start | bytes 1327104 | tf_op jit(solution)/shard_map/all_gather | solution.py:144
  8.2 11.3 %collective-permute-start = (f32[30,2048]{1,0:T(8,128)S(1)}, f32[30,2048]{1,0:T(8,128)S(1)}, u32[]{:S(2)}, u32[]{:S(2)}) collective-permute-start(f32[30,2048]{1,0:T(8,128)S(1)} %bitcast.89), channel_id=1, source_target_pairs={{8,0},{16,8},{24,16},{9,1},{17,9},{25,17},{10,2},{18,10},{26,18},{... | collective-permute-start | bytes 737288 | tf_op jit(solution)/shard_map/ppermute | solution.py:114
  170.3 1.9 copy-start
  173.6 5.9 %collective-permute-start.1 = (bf16[40,512]{1,0:T(8,128)(2,1)S(1)}, bf16[40,512]{1,0:T(8,128)(2,1)S(1)}, u32[]{:S(2)}, u32[]{:S(2)}) collective-permute-start(bf16[40,512]{1,0:T(8,128)(2,1)S(1)} %get-tuple-element.24), channel_id=1, source_target_pairs={{8,0},{16,8},{24,16},{9,1},{17,9},{25,17},{10,2},{18,10},{26,18},{... | collective-permute-start | bytes 122888 | tf_op jit(solution)/shard_map/ppermute | solution.py:114
  192.5 5.9 %collective-permute-start.2 = (bf16[40,512]{1,0:T(8,128)(2,1)S(1)}, bf16[40,512]{1,0:T(8,128)(2,1)S(1)}, u32[]{:S(2)}, u32[]{:S(2)}) collective-permute-start(bf16[40,512]{1,0:T(8,128)(2,1)S(1)} %get-tuple-element.26), channel_id=1, source_target_pairs={{8,0},{16,8},{24,16},{9,1},{17,9},{25,17},{10,2},{18,10},{26,18},{... | collective-permute-start | bytes 122888 | tf_op jit(solution)/shard_map/ppermute | solution.py:114
  210.4 9.1 %collective-permute-start.3 = (bf16[40,512]{1,0:T(8,128)(2,1)S(1)}, bf16[40,512]{1,0:T(8,128)(2,1)S(1)}, u32[]{:S(2)}, u32[]{:S(2)}) collective-permute-start(bf16[40,512]{1,0:T(8,128)(2,1)S(1)} %get-tuple-element.28), channel_id=1, source_target_pairs={{8,0},{16,8},{24,16},{9,1},{17,9},{25,17},{10,2},{18,10},{26,18},{... | collective-permute-start | bytes 122888 | tf_op jit(solution)/shard_map/ppermute | solution.py:114
Sparse Core Ops, SparseCore 0:
  21.2 24.2 all-gather.11

commit v8 on v6

--- a/solution.py
+++ b/solution.py
@@ -21,9 +21,11 @@
 
 def sweep_kernel(do_row, do_col, emit_w, shrink, c_ref, every_ref, lb_ref, la_ref, *rest):
     rest = list(rest)
+    handed_ref = rest.pop(0) if emit_w else None
     f_ref = rest.pop(0) if do_row else None
     lse_ref = rest.pop(0) if do_col else None
     w_ref = rest.pop(0) if emit_w else None
+    p_ref = rest.pop(0) if emit_w else None
     a_ref, b_ref = rest
     rows, cols = c_ref.shape
     groups = rows // GROUP
@@ -60,6 +62,10 @@
                     cs = slice(j * WIDTH, (j + 1) * WIDTH)
                     e = jnp.exp(b_ref[:, cs] - c_ref[rs, cs] - peak)
                     w_ref[rs, cs] = (e / total).astype(w_ref.dtype)
+                p_ref[:, rs] = lax.dot_general(
+                    handed_ref[...], w_ref[rs, :], (((1,), (1,)), ((), ())),
+                    preferred_element_type=jnp.float32,
+                )
             return carry
         lax.fori_loop(0, rows // rg, row_group, 0)
     else:
@@ -82,7 +88,7 @@
         lax.fori_loop(0, chunks, col_chunk, 0)
 
 
-def sweep(scaled_cost, every, log_b, log_a, shrink, do_row, do_col, emit_w):
+def sweep(scaled_cost, every, log_b, log_a, shrink, do_row, do_col, emit_w, handed=None):
     rows, cols = scaled_cost.shape
     outs = []
     if do_row:
@@ -91,12 +97,13 @@
         outs.append(jax.ShapeDtypeStruct((1, cols), jnp.float32))
     if emit_w:
         outs.append(jax.ShapeDtypeStruct((rows, cols), jnp.bfloat16))
+        outs.append(jax.ShapeDtypeStruct((handed.shape[0], rows), jnp.float32))
     passes = (2 if do_row else 0) + (2 if do_col else 0) + (1 if emit_w else 0)
     vmem = pl.BlockSpec(memory_space=pltpu.VMEM)
     return pl.pallas_call(
         functools.partial(sweep_kernel, do_row, do_col, emit_w, shrink),
         out_shape=tuple(outs),
-        in_specs=[vmem] * 4,
+        in_specs=[vmem] * (5 if emit_w else 4),
         out_specs=tuple([vmem] * len(outs)),
         scratch_shapes=[pltpu.VMEM((rows, 128), jnp.float32), pltpu.VMEM((1, cols), jnp.float32)],
         compiler_params=pltpu.CompilerParams(vmem_limit_bytes=24 * 1024 * 1024),
@@ -105,7 +112,7 @@
             transcendentals=passes * rows * cols // 2,
             bytes_accessed=4 * rows * cols + (2 * rows * cols if emit_w else 0),
         ),
-    )(scaled_cost, every, log_b[None, :], log_a[:, None])
+    )(scaled_cost, every, log_b[None, :], log_a[:, None], *([handed] if emit_w else []))
 
 
 def shifted(shard, axis, by):
@@ -174,22 +181,32 @@
         live_tgt, -jnp.log(live_next.astype(jnp.float32)) * jnp.ones((cols,), jnp.float32), NEG
     )
     scaled_cost = cost_tile * (1.0 / EPS)
+    final_handed = lax.all_gather(final_fates.astype(jnp.bfloat16), "tgt", axis=1, tiled=True)
+    fates_count = final_handed.shape[0]
+    fates_pad = -fates_count % 16
+    handed_pad = jnp.concatenate(
+        [final_handed, jnp.zeros((fates_pad, final_handed.shape[1]), jnp.bfloat16)], axis=0
+    )
     (part_lse,) = sweep(scaled_cost, log_mass_b[None, :], log_mass_b, log_mass_a, shrink, False, True, False)
     for step_num in range(ITERS):
         every = lax.all_gather(part_lse[0], ("src", "tgt"))
         if step_num + 1 < ITERS:
             pot_col, part_lse = sweep(scaled_cost, every, log_mass_b, log_mass_a, shrink, True, True, False)
         else:
-            pot_col, weights = sweep(scaled_cost, every, log_mass_b, log_mass_a, shrink, True, False, True)
+            pot_col, weights, first_pull = sweep(
+                scaled_cost, every, log_mass_b, log_mass_a, shrink, True, False, True, handed_pad
+            )
     pot_src = pot_col.reshape(rows)
-    final_handed = lax.all_gather(final_fates.astype(jnp.bfloat16), "tgt", axis=1, tiled=True)
     handed = jnp.where(is_last, final_handed, jnp.zeros(final_handed.shape, jnp.bfloat16))
     fate_maps = jnp.zeros((final_fates.shape[0], rows), jnp.float32)
     for section_num in range(pair_count):
         active = pair_count - 1 - section_num
-        pulled = lax.dot_general(
-            weights, handed, (((1,), (1,)), ((), ())), preferred_element_type=jnp.float32
-        ).T
+        if section_num == 0:
+            pulled = first_pull[:fates_count]
+        else:
+            pulled = lax.dot_general(
+                weights, handed, (((1,), (1,)), ((), ())), preferred_element_type=jnp.float32
+            ).T
         pulled = jnp.where(live_src[None, :], pulled, 0.0)
         fate_maps = jnp.where(pair_rank == active, pulled, fate_maps)
         if section_num + 1 < pair_count:

time: 215 us -> 215 us (level)
    dot_general x4 -> x3, matrix products: 12.7 us -> 11.3 us  [local(): lax.dot_general(weights, handed, (((1,), (1,)), ((), ())), preferred_elem...]
where the time goes in v8:
time: 215 us; the launch traced here: 214 us
  blocking collectives  122 us (57%)
  Pallas kernels  43.5 us (20%)
  matrix products  18.7 us (9%)
  waiting for transfers between devices  9.78 us (5%)
  local copies, waits for them, and re-layouts  7.17 us (3%)
  other arithmetic  5.49 us (3%)
  starting transfers between devices  5.17 us (2%)
  between operations  2.28 us (1%)
    all_gather x8, blocking collectives, local(): every = lax.all_gather(part_lse[0], ('src', 'tgt'))  70 us
    pallas_call x9, Pallas kernels, sweep(): pl.pallas_call(functools.partial(sweep_kernel, do_row, do_col, emit_w, sh...  43.5 us
    all_gather x3, blocking collectives, local(): fresh = lax.all_gather(passed, ('src', 'tgt'), axis=1, tiled=True)  26.4 us
    dot_general x3, matrix products, local(): lax.dot_general(weights, handed, (((1,), (1,)), ((), ())), preferred_elem...  11.3 us
    all_gather x1, blocking collectives, local(): pieces = lax.all_gather(piece, ('src', 'tgt'))  9.83 us
    ppermute x4, waiting for transfers between devices, shifted(): return lax.ppermute(shard, axis, pairs)  9.78 us
    psum x1, blocking collectives, local(): pot_all = lax.psum(pot_spread, 'tgt')  7.65 us
    all_gather x1, blocking collectives, local(): lax.all_gather(final_fates.astype(jnp.bfloat16), 'tgt', axis=1, tiled=True)  7.61 us
  transfers between devices with their start and end apart: 4, of which 2 were waited for; matrix products, arithmetic and copies ran while one was open for 3% of the time, Pallas kernels for 0%

profile of v8, /device:TPU:0, one launch (start us, length us, event | category | flops | bytes accessed | tf_op | source)
XLA Modules:
  0.0 213.7 jit_solution(3594227585805068084)
XLA Ops:
  0.6 1.0 copy.38
  1.7 1.3 collective-permute-start
  3.0 0.7 pad_clamp_fusion
  3.6 0.8 constant_dynamic-slice_fusion
  4.5 1.3 fusion.9
  7.2 0.7 compare_select_fusion.every_ref.lb_ref
  7.9 0.9 convert_element_type.20
  8.8 7.6 %all_gather.52 = bf16[40,4096]{1,0:T(8,128)(2,1)S(1)} all-gather(bf16[40,1024]{1,0:T(8,128)(2,1)S(1)} %convert_element_type.20), channel_id=1, replica_groups=mesh['pair'=4,'src'=2,'tgt'=4] {'tgt'}, dimensions={1}, use_global_device_ids=true | all-gather | bytes 409600 | tf_op jit(solution)/shard_map/all_gather | solution.py:184
  16.4 0.7 subtract_bitcast_fusion
  17.1 0.7 add_compare_fusion.1
  17.8 0.1 copy.11
  18.0 0.7 fusion.4.la_ref
  18.7 0.9 select_bitcast_fusion.1
  19.5 9.8 %all-gather.1 = f32[8,30,512]{2,1,0:T(8,128)S(1)} all-gather(f32[1,30,512]{2,1,0:T(8,128)S(1)} %select_bitcast_fusion.1), channel_id=2, replica_groups=mesh['pair'=4,'src'=2,'tgt'=4] {'src','tgt'}, dimensions={0}, use_global_device_ids=true | all-gather | bytes 552960 | tf_op jit(solution)/shard_map/all_gather | solution.py:145
  29.4 0.6 gather_fusion
  30.1 0.3 copy.10
  30.4 0.3 copy.23
  30.8 7.4 %subtract_multiply_fusion.c_ref = f32[512,4096]{1,0:T(8,128)S(1)} fusion(f32[30,4096]{1,0:T(8,128)S(1)} %bitcast.79, f32[4096]{0:T(1024)S(1)} %bitcast.82, f32[512]{0:T(512)S(1)} %fusion.7, f32[1,30,512]{2,0,1:T(1,128)S(1)} %constant_dynamic-slice_fusion), kind=kOutput, calls=%fused_computation.1 | convolution fusion | flops 763363328 | bytes 8960000 | tf_op jit(solution)/shard_map/dot_general | solution.py:160
  38.2 2.2 %shard_map.77 = f32[1,4096]{1,0:T(1,128)S(1)} custom-call(f32[512,4096]{1,0:T(8,128)S(1)} %subtract_multiply_fusion.c_ref, f32[1,4096]{1,0:T(1,128)S(1)} %compare_select_fusion.every_ref.lb_ref, f32[1,4096]{1,0:T(1,128)S(1)} %compare_select_fusion.every_ref.lb_ref, f32[512,1]{1,0:T(8,128)S(1)} %fusion.4.la_ref), custom_call_target="tpu_custom_call" | custom-call | flops 16777216 | bytes 8388608 | tf_op jit(solution)/shard_map/pallas_call | solution.py:103
  40.4 9.1 %all-gather.2 = f32[8,1,4096]{2,1,0:T(1,128)S(1)} all-gather(f32[1,1,4096]{2,1,0:T(1,128)S(1)} %bitcast.71), channel_id=1, replica_groups=mesh['pair'=4,'src'=2,'tgt'=4] {'src','tgt'}, dimensions={0}, use_global_device_ids=true | all-gather | bytes 147456 | tf_op jit(solution)/shard_map/all_gather | solution.py:192
  49.5 5.2 %shard_map.78 = (f32[512,1]{1,0:T(8,128)}, f32[1,4096]{1,0:T(1,128)S(1)}) custom-call(f32[512,4096]{1,0:T(8,128)S(1)} %subtract_multiply_fusion.c_ref, f32[8,4096]{1,0:T(8,128)S(1)} %bitcast.64, f32[1,4096]{1,0:T(1,128)S(1)} %compare_select_fusion.every_ref.lb_ref, f32[512,1]{1,0:T(8,128)S(1)} %fusion.4.la_ref), custom_call_target="tpu_custom_call" | custom-call | flops 33554432 | bytes 8388608 | tf_op jit(solution)/shard_map/pallas_call | solution.py:103
  54.8 8.5 %all-gather.3 = f32[8,1,4096]{2,1,0:T(1,128)S(1)} all-gather(f32[1,1,4096]{2,1,0:T(1,128)S(1)} %bitcast.72), channel_id=1, replica_groups=mesh['pair'=4,'src'=2,'tgt'=4] {'src','tgt'}, dimensions={0}, use_global_device_ids=true | all-gather | bytes 147456 | tf_op jit(solution)/shard_map/all_gather | solution.py:192
  63.4 5.2 %shard_map.79 = (f32[512,1]{1,0:T(8,128)}, f32[1,4096]{1,0:T(1,128)S(1)}) custom-call(f32[512,4096]{1,0:T(8,128)S(1)} %subtract_multiply_fusion.c_ref, f32[8,4096]{1,0:T(8,128)S(1)} %bitcast.65, f32[1,4096]{1,0:T(1,128)S(1)} %compare_select_fusion.every_ref.lb_ref, f32[512,1]{1,0:T(8,128)S(1)} %fusion.4.la_ref), custom_call_target="tpu_custom_call" | custom-call | flops 33554432 | bytes 8388608 | tf_op jit(solution)/shard_map/pallas_call | solution.py:103
  68.6 9.0 %all-gather.4 = f32[8,1,4096]{2,1,0:T(1,128)S(1)} all-gather(f32[1,1,4096]{2,1,0:T(1,128)S(1)} %bitcast.73), channel_id=1, replica_groups=mesh['pair'=4,'src'=2,'tgt'=4] {'src','tgt'}, dimensions={0}, use_global_device_ids=true | all-gather | bytes 147456 | tf_op jit(solution)/shard_map/all_gather | solution.py:192
  77.7 5.2 %shard_map.80 = (f32[512,1]{1,0:T(8,128)}, f32[1,4096]{1,0:T(1,128)S(1)}) custom-call(f32[512,4096]{1,0:T(8,128)S(1)} %subtract_multiply_fusion.c_ref, f32[8,4096]{1,0:T(8,128)S(1)} %bitcast.66, f32[1,4096]{1,0:T(1,128)S(1)} %compare_select_fusion.every_ref.lb_ref, f32[512,1]{1,0:T(8,128)S(1)} %fusion.4.la_ref), custom_call_target="tpu_custom_call" | custom-call | flops 33554432 | bytes 8388608 | tf_op jit(solution)/shard_map/pallas_call | solution.py:103
  83.0 8.4 %all-gather.5 = f32[8,1,4096]{2,1,0:T(1,128)S(1)} all-gather(f32[1,1,4096]{2,1,0:T(1,128)S(1)} %bitcast.74), channel_id=1, replica_groups=mesh['pair'=4,'src'=2,'tgt'=4] {'src','tgt'}, dimensions={0}, use_global_device_ids=true | all-gather | bytes 147456 | tf_op jit(solution)/shard_map/all_gather | solution.py:192
  91.4 5.2 %shard_map.81 = (f32[512,1]{1,0:T(8,128)}, f32[1,4096]{1,0:T(1,128)S(1)}) custom-call(f32[512,4096]{1,0:T(8,128)S(1)} %subtract_multiply_fusion.c_ref, f32[8,4096]{1,0:T(8,128)S(1)} %bitcast.67, f32[1,4096]{1,0:T(1,128)S(1)} %compare_select_fusion.every_ref.lb_ref, f32[512,1]{1,0:T(8,128)S(1)} %fusion.4.la_ref), custom_call_target="tpu_custom_call" | custom-call | flops 33554432 | bytes 8388608 | tf_op jit(solution)/shard_map/pallas_call | solution.py:103
  96.7 9.0 %all-gather.6 = f32[8,1,4096]{2,1,0:T(1,128)S(1)} all-gather(f32[1,1,4096]{2,1,0:T(1,128)S(1)} %bitcast.75), channel_id=1, replica_groups=mesh['pair'=4,'src'=2,'tgt'=4] {'src','tgt'}, dimensions={0}, use_global_device_ids=true | all-gather | bytes 147456 | tf_op jit(solution)/shard_map/all_gather | solution.py:192
  105.8 5.2 %shard_map.82 = (f32[512,1]{1,0:T(8,128)}, f32[1,4096]{1,0:T(1,128)S(1)}) custom-call(f32[512,4096]{1,0:T(8,128)S(1)} %subtract_multiply_fusion.c_ref, f32[8,4096]{1,0:T(8,128)S(1)} %bitcast.68, f32[1,4096]{1,0:T(1,128)S(1)} %compare_select_fusion.every_ref.lb_ref, f32[512,1]{1,0:T(8,128)S(1)} %fusion.4.la_ref), custom_call_target="tpu_custom_call" | custom-call | flops 33554432 | bytes 8388608 | tf_op jit(solution)/shard_map/pallas_call | solution.py:103
  111.0 8.4 %all-gather.7 = f32[8,1,4096]{2,1,0:T(1,128)S(1)} all-gather(f32[1,1,4096]{2,1,0:T(1,128)S(1)} %bitcast.76), channel_id=1, replica_groups=mesh['pair'=4,'src'=2,'tgt'=4] {'src','tgt'}, dimensions={0}, use_global_device_ids=true | all-gather | bytes 147456 | tf_op jit(solution)/shard_map/all_gather | solution.py:192
  119.5 5.2 %shard_map.83 = (f32[512,1]{1,0:T(8,128)}, f32[1,4096]{1,0:T(1,128)S(1)}) custom-call(f32[512,4096]{1,0:T(8,128)S(1)} %subtract_multiply_fusion.c_ref, f32[8,4096]{1,0:T(8,128)S(1)} %bitcast.69, f32[1,4096]{1,0:T(1,128)S(1)} %compare_select_fusion.every_ref.lb_ref, f32[512,1]{1,0:T(8,128)S(1)} %fusion.4.la_ref), custom_call_target="tpu_custom_call" | custom-call | flops 33554432 | bytes 8388608 | tf_op jit(solution)/shard_map/pallas_call | solution.py:103
  124.7 9.0 %all-gather.8 = f32[8,1,4096]{2,1,0:T(1,128)S(1)} all-gather(f32[1,1,4096]{2,1,0:T(1,128)S(1)} %bitcast.77), channel_id=1, replica_groups=mesh['pair'=4,'src'=2,'tgt'=4] {'src','tgt'}, dimensions={0}, use_global_device_ids=true | all-gather | bytes 147456 | tf_op jit(solution)/shard_map/all_gather | solution.py:192
  133.8 5.2 %shard_map.84 = (f32[512,1]{1,0:T(8,128)}, f32[1,4096]{1,0:T(1,128)S(1)}) custom-call(f32[512,4096]{1,0:T(8,128)S(1)} %subtract_multiply_fusion.c_ref, f32[8,4096]{1,0:T(8,128)S(1)} %bitcast.70, f32[1,4096]{1,0:T(1,128)S(1)} %compare_select_fusion.every_ref.lb_ref, f32[512,1]{1,0:T(8,128)S(1)} %fusion.4.la_ref), custom_call_target="tpu_custom_call" | custom-call | flops 33554432 | bytes 8388608 | tf_op jit(solution)/shard_map/pallas_call | solution.py:103
  139.1 8.6 %all-gather.9 = f32[8,1,4096]{2,1,0:T(1,128)S(1)} all-gather(f32[1,1,4096]{2,1,0:T(1,128)S(1)} %bitcast.78), channel_id=1, replica_groups=mesh['pair'=4,'src'=2,'tgt'=4] {'src','tgt'}, dimensions={0}, use_global_device_ids=true | all-gather | bytes 147456 | tf_op jit(solution)/shard_map/all_gather | solution.py:192
  147.8 4.6 %shard_map.85 = (f32[512,1]{1,0:T(8,128)S(1)}, bf16[512,4096]{1,0:T(8,128)(2,1)S(1)}, f32[48,512]{1,0:T(8,128)S(1)}) custom-call(f32[512,4096]{1,0:T(8,128)S(1)} %subtract_multiply_fusion.c_ref, f32[8,4096]{1,0:T(8,128)S(1)} %bitcast.63, f32[1,4096]{1,0:T(1,128)S(1)} %compare_select_fusion.every_ref.lb_ref, f32[512,1]{1,0:T(8,128)S(1)} %fusion.4.la_ref, ...), custom_call_target="tpu_custom_call" | custom-call | flops 25165824 | bytes 12582912 | tf_op jit(solution)/shard_map/pallas_call | solution.py:103
  152.4 1.9 copy-done
  154.3 1.3 collective-permute-start.1
  155.6 5.3 %collective-permute-done.1 = bf16[40,512]{1,0:T(8,128)(2,1)S(1)} collective-permute-done((bf16[40,512]{1,0:T(8,128)(2,1)S(1)}, bf16[40,512]{1,0:T(8,128)(2,1)S(1)}, u32[]{:S(2)}, u32[]{:S(2)}) %collective-permute-start.1) | collective-permute-done | bytes 40992 | tf_op jit(solution)/shard_map/ppermute | solution.py:121
  161.0 9.3 %all_gather.53 = bf16[40,4096]{1,0:T(8,128)(2,1)S(1)} all-gather(bf16[40,512]{1,0:T(8,128)(2,1)S(1)} %collective-permute-done.1), channel_id=1, replica_groups=mesh['pair'=4,'src'=2,'tgt'=4] {'src','tgt'}, dimensions={1}, use_global_device_ids=true | all-gather | bytes 368640 | tf_op jit(solution)/shard_map/all_gather | solution.py:214
  170.3 3.6 %fusion.10 = (bf16[40,512]{1,0:T(8,128)(2,1)S(1)}, f32[40,512]{1,0:T(8,128)S(1)}) fusion(bf16[40,4096]{1,0:T(8,128)(2,1)S(1)} %select_select_fusion, bf16[512,4096]{1,0:T(8,128)(2,1)} %copy-done, pred[512]{0:T(512)(128)(4,1)S(1)} %add_compare_fusion.1), kind=kOutput, calls=%fused_computation.38 | convolution fusion | flops 167813120 | bytes 4645376 | tf_op jit(solution)/shard_map/dot_general | solution.py:207
  173.8 1.3 collective-permute-start.2
  175.3 4.4 %collective-permute-done.2 = bf16[40,512]{1,0:T(8,128)(2,1)S(1)} collective-permute-done((bf16[40,512]{1,0:T(8,128)(2,1)S(1)}, bf16[40,512]{1,0:T(8,128)(2,1)S(1)}, u32[]{:S(2)}, u32[]{:S(2)}) %collective-permute-start.2) | collective-permute-done | bytes 40992 | tf_op jit(solution)/shard_map/ppermute | solution.py:121
  179.7 8.6 %all_gather.54 = bf16[40,4096]{1,0:T(8,128)(2,1)S(1)} all-gather(bf16[40,512]{1,0:T(8,128)(2,1)S(1)} %collective-permute-done.2), channel_id=1, replica_groups=mesh['pair'=4,'src'=2,'tgt'=4] {'src','tgt'}, dimensions={1}, use_global_device_ids=true | all-gather | bytes 368640 | tf_op jit(solution)/shard_map/all_gather | solution.py:214
  188.3 3.6 %fusion.11 = (bf16[40,512]{1,0:T(8,128)(2,1)S(1)}, f32[40,512]{1,0:T(8,128)S(1)}) fusion(bf16[512,4096]{1,0:T(8,128)(2,1)} %copy-done, bf16[40,4096]{1,0:T(8,128)(2,1)S(1)} %all_gather.54, bf16[40,4096]{1,0:T(8,128)(2,1)S(1)} %select_select_fusion, pred[]{:T(512)S(6)} %eq.19, pred[512]{0:T(512)(128)(4,1)S(1)} %add_compare_fusion.1), kind=kOutput, calls=%fused_computation.39 | convolution fusion | flops 167976960 | bytes 4973057 | tf_op jit(solution)/shard_map/dot_general | solution.py:207
  191.9 1.3 collective-permute-start.3
  193.2 7.6 %psum.7 = f32[1,2048]{1,0:T(1,128)} all-reduce(f32[1,2048]{1,0:T(1,128)S(1)} %constant_dynamic-update-slice_fusion), channel_id=1, replica_groups=mesh['pair'=4,'src'=2,'tgt'=4] {'tgt'}, use_global_device_ids=true, to_apply=%region_2.3 | all-reduce | flops 2048 | bytes 16384 | tf_op jit(solution)/shard_map/psum | solution.py:217
  200.9 8.6 %all_gather.55 = bf16[40,4096]{1,0:T(8,128)(2,1)S(1)} all-gather(bf16[40,512]{1,0:T(8,128)(2,1)S(1)} %collective-permute-done.3), channel_id=1, replica_groups=mesh['pair'=4,'src'=2,'tgt'=4] {'src','tgt'}, dimensions={1}, use_global_device_ids=true | all-gather | bytes 368640 | tf_op jit(solution)/shard_map/all_gather | solution.py:214
  209.5 4.2 %fusion.1 = f32[1,40,512]{2,1,0:T(8,128)} fusion(bf16[512,4096]{1,0:T(8,128)(2,1)} %copy-done, bf16[40,4096]{1,0:T(8,128)(2,1)S(1)} %all_gather.55, pred[]{:T(512)S(6)} %eq.18, bf16[40,4096]{1,0:T(8,128)(2,1)S(1)} %all_gather.54, bf16[40,4096]{1,0:T(8,128)(2,1)S(1)} %select_select_fusion, pred[]{:T(512)S(6)} %eq.19, f32[40,512]{1,0:T(8,128)S(1)} %get-tuple-element.29, ...), kind=kOutput, calls=%fused_computation.6 | convolution fusion | flops 168222720 | bytes 5508608 | tf_op jit(solution)/shard_map/dot_general | solution.py:207
  (21 shorter events, 1.1 us)
Async XLA Ops:
  1.7 17.0 %collective-permute-start = (f32[30,2048]{1,0:T(8,128)S(1)}, f32[30,2048]{1,0:T(8,128)S(1)}, u32[]{:S(2)}, u32[]{:S(2)}) collective-permute-start(f32[30,2048]{1,0:T(8,128)S(1)} %bitcast.81), channel_id=1, source_target_pairs={{8,0},{16,8},{24,16},{9,1},{17,9},{25,17},{10,2},{18,10},{26,18},{... | collective-permute-start | bytes 737288 | tf_op jit(solution)/shard_map/ppermute | solution.py:121
  152.4 1.9 copy-start
  154.3 6.6 %collective-permute-start.1 = (bf16[40,512]{1,0:T(8,128)(2,1)S(1)}, bf16[40,512]{1,0:T(8,128)(2,1)S(1)}, u32[]{:S(2)}, u32[]{:S(2)}) collective-permute-start(bf16[40,512]{1,0:T(8,128)(2,1)S(1)} %fusion.5), channel_id=1, source_target_pairs={{8,0},{16,8},{24,16},{9,1},{17,9},{25,17},{10,2},{18,10},{26,18},{... | collective-permute-start | bytes 122888 | tf_op jit(solution)/shard_map/ppermute | solution.py:121
  173.8 5.9 %collective-permute-start.2 = (bf16[40,512]{1,0:T(8,128)(2,1)S(1)}, bf16[40,512]{1,0:T(8,128)(2,1)S(1)}, u32[]{:S(2)}, u32[]{:S(2)}) collective-permute-start(bf16[40,512]{1,0:T(8,128)(2,1)S(1)} %get-tuple-element.26), channel_id=1, source_target_pairs={{8,0},{16,8},{24,16},{9,1},{17,9},{25,17},{10,2},{18,10},{26,18},{... | collective-permute-start | bytes 122888 | tf_op jit(solution)/shard_map/ppermute | solution.py:121
  191.9 9.0 %collective-permute-start.3 = (bf16[40,512]{1,0:T(8,128)(2,1)S(1)}, bf16[40,512]{1,0:T(8,128)(2,1)S(1)}, u32[]{:S(2)}, u32[]{:S(2)}) collective-permute-start(bf16[40,512]{1,0:T(8,128)(2,1)S(1)} %get-tuple-element.28), channel_id=1, source_target_pairs={{8,0},{16,8},{24,16},{9,1},{17,9},{25,17},{10,2},{18,10},{26,18},{... | collective-permute-start | bytes 122888 | tf_op jit(solution)/shard_map/ppermute | solution.py:121

commit v9 on v8

--- a/solution.py
+++ b/solution.py
@@ -26,6 +26,7 @@
     lse_ref = rest.pop(0) if do_col else None
     w_ref = rest.pop(0) if emit_w else None
     p_ref = rest.pop(0) if emit_w else None
+    fl_ref = rest.pop(0) if emit_w else None
     a_ref, b_ref = rest
     rows, cols = c_ref.shape
     groups = rows // GROUP
@@ -62,6 +63,7 @@
                     cs = slice(j * WIDTH, (j + 1) * WIDTH)
                     e = jnp.exp(b_ref[:, cs] - c_ref[rs, cs] - peak)
                     w_ref[rs, cs] = (e / total).astype(w_ref.dtype)
+                fl_ref[:, rs] = jnp.transpose(jnp.broadcast_to(pot, (rg, 128)))[0:1, :]
                 p_ref[:, rs] = lax.dot_general(
                     handed_ref[...], w_ref[rs, :], (((1,), (1,)), ((), ())),
                     preferred_element_type=jnp.float32,
@@ -98,6 +100,7 @@
     if emit_w:
         outs.append(jax.ShapeDtypeStruct((rows, cols), jnp.bfloat16))
         outs.append(jax.ShapeDtypeStruct((handed.shape[0], rows), jnp.float32))
+        outs.append(jax.ShapeDtypeStruct((1, rows), jnp.float32))
     passes = (2 if do_row else 0) + (2 if do_col else 0) + (1 if emit_w else 0)
     vmem = pl.BlockSpec(memory_space=pltpu.VMEM)
     return pl.pallas_call(
@@ -193,7 +196,7 @@
         if step_num + 1 < ITERS:
             pot_col, part_lse = sweep(scaled_cost, every, log_mass_b, log_mass_a, shrink, True, True, False)
         else:
-            pot_col, weights, first_pull = sweep(
+            pot_col, weights, first_pull, pot_lanes = sweep(
                 scaled_cost, every, log_mass_b, log_mass_a, shrink, True, False, True, handed_pad
             )
     pot_src = pot_col.reshape(rows)
@@ -213,8 +216,7 @@
             passed = shifted(pulled.astype(jnp.bfloat16), "pair", -1)
             fresh = lax.all_gather(passed, ("src", "tgt"), axis=1, tiled=True)
             handed = jnp.where(pair_rank == active - 1, fresh, handed)
-    pot_spread = lax.dynamic_update_slice_in_dim(jnp.zeros((src_width,), jnp.float32), pot_src, row_off, 0)
-    pot_all = lax.psum(pot_spread, "tgt")
+    pot_all = lax.all_gather(pot_lanes.reshape(rows), "tgt", axis=0, tiled=True)
     return (fate_maps[None], pot_all[None])
 
 

time: 215 us -> 214 us (level)
    psum x1 -> x0, blocking collectives: 7.65 us -> none  [local(): pot_all = lax.psum(pot_spread, 'tgt')]
    all_gather x0 -> x1, blocking collectives: none -> 5.19 us  [local(): pot_all = lax.all_gather(pot_lanes.reshape(rows), 'tgt', axis=0, tiled=True)]
    unnamed x14 -> x15, local copies, waits for them, and re-layouts: 3.95 us -> 4.57 us
where the time goes in v9:
time: 214 us; the launch traced here: 213 us
  blocking collectives  120 us (56%)
  Pallas kernels  43.8 us (20%)
  matrix products  18.7 us (9%)
  waiting for transfers between devices  9.92 us (5%)
  local copies, waits for them, and re-layouts  7.78 us (4%)
  other arithmetic  5.35 us (2%)
  starting transfers between devices  5.17 us (2%)
  between operations  2.26 us (1%)
    all_gather x8, blocking collectives, local(): every = lax.all_gather(part_lse[0], ('src', 'tgt'))  70 us
    pallas_call x9, Pallas kernels, sweep(): pl.pallas_call(functools.partial(sweep_kernel, do_row, do_col, emit_w, sh...  43.8 us
    all_gather x3, blocking collectives, local(): fresh = lax.all_gather(passed, ('src', 'tgt'), axis=1, tiled=True)  27.1 us
    dot_general x3, matrix products, local(): lax.dot_general(weights, handed, (((1,), (1,)), ((), ())), preferred_elem...  11.3 us
    ppermute x4, waiting for transfers between devices, shifted(): return lax.ppermute(shard, axis, pairs)  9.92 us
    all_gather x1, blocking collectives, local(): pieces = lax.all_gather(piece, ('src', 'tgt'))  9.83 us
    all_gather x1, blocking collectives, local(): lax.all_gather(final_fates.astype(jnp.bfloat16), 'tgt', axis=1, tiled=True)  7.61 us
    dot_general x1, matrix products, local(): lax.dot_general(source_pos, target_pos, (((0,), (0,)), ((), ())), precisi...  7.4 us
  transfers between devices with their start and end apart: 4, of which 2 were waited for; matrix products, arithmetic and copies ran while one was open for 3% of the time, Pallas kernels for 0%

profile of v9, /device:TPU:0, one launch (start us, length us, event | category | flops | bytes accessed | tf_op | source)
XLA Modules:
  0.0 212.7 jit_solution(17782903287988604354)
XLA Ops:
  0.6 1.0 copy.38
  1.7 1.3 collective-permute-start
  3.0 0.7 pad_clamp_fusion
  3.6 0.8 constant_dynamic-slice_fusion
  4.5 1.3 fusion.9
  7.2 0.7 compare_select_fusion.every_ref.lb_ref
  7.9 0.9 convert_element_type.20
  8.8 7.6 %all_gather.55 = bf16[40,4096]{1,0:T(8,128)(2,1)S(1)} all-gather(bf16[40,1024]{1,0:T(8,128)(2,1)S(1)} %convert_element_type.20), channel_id=1, replica_groups=mesh['pair'=4,'src'=2,'tgt'=4] {'tgt'}, dimensions={1}, use_global_device_ids=true | all-gather | bytes 409600 | tf_op jit(solution)/shard_map/all_gather | solution.py:187
  16.4 0.7 subtract_bitcast_fusion
  17.1 0.7 add_compare_fusion.1
  18.0 0.7 fusion.4.la_ref
  18.7 0.9 select_bitcast_fusion.1
  19.5 9.8 %all-gather.2 = f32[8,30,512]{2,1,0:T(8,128)S(1)} all-gather(f32[1,30,512]{2,1,0:T(8,128)S(1)} %select_bitcast_fusion.1), channel_id=2, replica_groups=mesh['pair'=4,'src'=2,'tgt'=4] {'src','tgt'}, dimensions={0}, use_global_device_ids=true | all-gather | bytes 552960 | tf_op jit(solution)/shard_map/all_gather | solution.py:148
  29.4 0.6 gather_fusion
  30.1 0.3 copy.10
  30.4 0.3 copy.23
  30.8 7.4 %subtract_multiply_fusion.c_ref = f32[512,4096]{1,0:T(8,128)S(1)} fusion(f32[30,4096]{1,0:T(8,128)S(1)} %bitcast.78, f32[4096]{0:T(1024)S(1)} %bitcast.81, f32[512]{0:T(512)S(1)} %fusion.7, f32[1,30,512]{2,0,1:T(1,128)S(1)} %constant_dynamic-slice_fusion), kind=kOutput, calls=%fused_computation.1 | convolution fusion | flops 763363328 | bytes 8960000 | tf_op jit(solution)/shard_map/dot_general | solution.py:163
  38.2 2.2 %shard_map.77 = f32[1,4096]{1,0:T(1,128)S(1)} custom-call(f32[512,4096]{1,0:T(8,128)S(1)} %subtract_multiply_fusion.c_ref, f32[1,4096]{1,0:T(1,128)S(1)} %compare_select_fusion.every_ref.lb_ref, f32[1,4096]{1,0:T(1,128)S(1)} %compare_select_fusion.every_ref.lb_ref, f32[512,1]{1,0:T(8,128)S(1)} %fusion.4.la_ref), custom_call_target="tpu_custom_call" | custom-call | flops 16777216 | bytes 8388608 | tf_op jit(solution)/shard_map/pallas_call | solution.py:106
  40.4 9.1 %all-gather.3 = f32[8,1,4096]{2,1,0:T(1,128)S(1)} all-gather(f32[1,1,4096]{2,1,0:T(1,128)S(1)} %bitcast.70), channel_id=1, replica_groups=mesh['pair'=4,'src'=2,'tgt'=4] {'src','tgt'}, dimensions={0}, use_global_device_ids=true | all-gather | bytes 147456 | tf_op jit(solution)/shard_map/all_gather | solution.py:195
  49.5 5.3 %shard_map.78 = (f32[512,1]{1,0:T(8,128)}, f32[1,4096]{1,0:T(1,128)S(1)}) custom-call(f32[512,4096]{1,0:T(8,128)S(1)} %subtract_multiply_fusion.c_ref, f32[8,4096]{1,0:T(8,128)S(1)} %bitcast.63, f32[1,4096]{1,0:T(1,128)S(1)} %compare_select_fusion.every_ref.lb_ref, f32[512,1]{1,0:T(8,128)S(1)} %fusion.4.la_ref), custom_call_target="tpu_custom_call" | custom-call | flops 33554432 | bytes 8388608 | tf_op jit(solution)/shard_map/pallas_call | solution.py:106
  54.8 8.5 %all-gather.4 = f32[8,1,4096]{2,1,0:T(1,128)S(1)} all-gather(f32[1,1,4096]{2,1,0:T(1,128)S(1)} %bitcast.71), channel_id=1, replica_groups=mesh['pair'=4,'src'=2,'tgt'=4] {'src','tgt'}, dimensions={0}, use_global_device_ids=true | all-gather | bytes 147456 | tf_op jit(solution)/shard_map/all_gather | solution.py:195
  63.4 5.3 %shard_map.79 = (f32[512,1]{1,0:T(8,128)}, f32[1,4096]{1,0:T(1,128)S(1)}) custom-call(f32[512,4096]{1,0:T(8,128)S(1)} %subtract_multiply_fusion.c_ref, f32[8,4096]{1,0:T(8,128)S(1)} %bitcast.64, f32[1,4096]{1,0:T(1,128)S(1)} %compare_select_fusion.every_ref.lb_ref, f32[512,1]{1,0:T(8,128)S(1)} %fusion.4.la_ref), custom_call_target="tpu_custom_call" | custom-call | flops 33554432 | bytes 8388608 | tf_op jit(solution)/shard_map/pallas_call | solution.py:106
  68.6 9.0 %all-gather.5 = f32[8,1,4096]{2,1,0:T(1,128)S(1)} all-gather(f32[1,1,4096]{2,1,0:T(1,128)S(1)} %bitcast.72), channel_id=1, replica_groups=mesh['pair'=4,'src'=2,'tgt'=4] {'src','tgt'}, dimensions={0}, use_global_device_ids=true | all-gather | bytes 147456 | tf_op jit(solution)/shard_map/all_gather | solution.py:195
  77.8 5.3 %shard_map.80 = (f32[512,1]{1,0:T(8,128)}, f32[1,4096]{1,0:T(1,128)S(1)}) custom-call(f32[512,4096]{1,0:T(8,128)S(1)} %subtract_multiply_fusion.c_ref, f32[8,4096]{1,0:T(8,128)S(1)} %bitcast.65, f32[1,4096]{1,0:T(1,128)S(1)} %compare_select_fusion.every_ref.lb_ref, f32[512,1]{1,0:T(8,128)S(1)} %fusion.4.la_ref), custom_call_target="tpu_custom_call" | custom-call | flops 33554432 | bytes 8388608 | tf_op jit(solution)/shard_map/pallas_call | solution.py:106
  83.0 8.4 %all-gather.6 = f32[8,1,4096]{2,1,0:T(1,128)S(1)} all-gather(f32[1,1,4096]{2,1,0:T(1,128)S(1)} %bitcast.73), channel_id=1, replica_groups=mesh['pair'=4,'src'=2,'tgt'=4] {'src','tgt'}, dimensions={0}, use_global_device_ids=true | all-gather | bytes 147456 | tf_op jit(solution)/shard_map/all_gather | solution.py:195
  91.5 5.3 %shard_map.81 = (f32[512,1]{1,0:T(8,128)}, f32[1,4096]{1,0:T(1,128)S(1)}) custom-call(f32[512,4096]{1,0:T(8,128)S(1)} %subtract_multiply_fusion.c_ref, f32[8,4096]{1,0:T(8,128)S(1)} %bitcast.66, f32[1,4096]{1,0:T(1,128)S(1)} %compare_select_fusion.every_ref.lb_ref, f32[512,1]{1,0:T(8,128)S(1)} %fusion.4.la_ref), custom_call_target="tpu_custom_call" | custom-call | flops 33554432 | bytes 8388608 | tf_op jit(solution)/shard_map/pallas_call | solution.py:106
  96.7 9.0 %all-gather.7 = f32[8,1,4096]{2,1,0:T(1,128)S(1)} all-gather(f32[1,1,4096]{2,1,0:T(1,128)S(1)} %bitcast.74), channel_id=1, replica_groups=mesh['pair'=4,'src'=2,'tgt'=4] {'src','tgt'}, dimensions={0}, use_global_device_ids=true | all-gather | bytes 147456 | tf_op jit(solution)/shard_map/all_gather | solution.py:195
  105.8 5.3 %shard_map.82 = (f32[512,1]{1,0:T(8,128)}, f32[1,4096]{1,0:T(1,128)S(1)}) custom-call(f32[512,4096]{1,0:T(8,128)S(1)} %subtract_multiply_fusion.c_ref, f32[8,4096]{1,0:T(8,128)S(1)} %bitcast.67, f32[1,4096]{1,0:T(1,128)S(1)} %compare_select_fusion.every_ref.lb_ref, f32[512,1]{1,0:T(8,128)S(1)} %fusion.4.la_ref), custom_call_target="tpu_custom_call" | custom-call | flops 33554432 | bytes 8388608 | tf_op jit(solution)/shard_map/pallas_call | solution.py:106
  111.1 8.4 %all-gather.8 = f32[8,1,4096]{2,1,0:T(1,128)S(1)} all-gather(f32[1,1,4096]{2,1,0:T(1,128)S(1)} %bitcast.75), channel_id=1, replica_groups=mesh['pair'=4,'src'=2,'tgt'=4] {'src','tgt'}, dimensions={0}, use_global_device_ids=true | all-gather | bytes 147456 | tf_op jit(solution)/shard_map/all_gather | solution.py:195
  119.5 5.3 %shard_map.83 = (f32[512,1]{1,0:T(8,128)}, f32[1,4096]{1,0:T(1,128)S(1)}) custom-call(f32[512,4096]{1,0:T(8,128)S(1)} %subtract_multiply_fusion.c_ref, f32[8,4096]{1,0:T(8,128)S(1)} %bitcast.68, f32[1,4096]{1,0:T(1,128)S(1)} %compare_select_fusion.every_ref.lb_ref, f32[512,1]{1,0:T(8,128)S(1)} %fusion.4.la_ref), custom_call_target="tpu_custom_call" | custom-call | flops 33554432 | bytes 8388608 | tf_op jit(solution)/shard_map/pallas_call | solution.py:106
  124.8 9.0 %all-gather.9 = f32[8,1,4096]{2,1,0:T(1,128)S(1)} all-gather(f32[1,1,4096]{2,1,0:T(1,128)S(1)} %bitcast.76), channel_id=1, replica_groups=mesh['pair'=4,'src'=2,'tgt'=4] {'src','tgt'}, dimensions={0}, use_global_device_ids=true | all-gather | bytes 147456 | tf_op jit(solution)/shard_map/all_gather | solution.py:195
  133.9 5.3 %shard_map.84 = (f32[512,1]{1,0:T(8,128)}, f32[1,4096]{1,0:T(1,128)S(1)}) custom-call(f32[512,4096]{1,0:T(8,128)S(1)} %subtract_multiply_fusion.c_ref, f32[8,4096]{1,0:T(8,128)S(1)} %bitcast.69, f32[1,4096]{1,0:T(1,128)S(1)} %compare_select_fusion.every_ref.lb_ref, f32[512,1]{1,0:T(8,128)S(1)} %fusion.4.la_ref), custom_call_target="tpu_custom_call" | custom-call | flops 33554432 | bytes 8388608 | tf_op jit(solution)/shard_map/pallas_call | solution.py:106
  139.1 8.6 %all-gather.10 = f32[8,1,4096]{2,1,0:T(1,128)S(1)} all-gather(f32[1,1,4096]{2,1,0:T(1,128)S(1)} %bitcast.77), channel_id=1, replica_groups=mesh['pair'=4,'src'=2,'tgt'=4] {'src','tgt'}, dimensions={0}, use_global_device_ids=true | all-gather | bytes 147456 | tf_op jit(solution)/shard_map/all_gather | solution.py:195
  147.8 4.8 %shard_map.85 = (f32[512,1]{1,0:T(8,128)}, bf16[512,4096]{1,0:T(8,128)(2,1)S(1)}, f32[48,512]{1,0:T(8,128)S(1)}, f32[1,512]{1,0:T(1,128)S(1)}) custom-call(f32[512,4096]{1,0:T(8,128)S(1)} %subtract_multiply_fusion.c_ref, f32[8,4096]{1,0:T(8,128)S(1)} %bitcast.62, f32[1,4096]{1,0:T(1,128)S(1)} %compare_select_fusion.every_ref.lb_ref, ...), custom_call_target="tpu_custom_call" | custom-call | flops 25165824 | bytes 12582912 | tf_op jit(solution)/shard_map/pallas_call | solution.py:106
  152.6 2.0 copy-done
  154.6 1.3 collective-permute-start.1
  155.9 5.3 %collective-permute-done.1 = bf16[40,512]{1,0:T(8,128)(2,1)S(1)} collective-permute-done((bf16[40,512]{1,0:T(8,128)(2,1)S(1)}, bf16[40,512]{1,0:T(8,128)(2,1)S(1)}, u32[]{:S(2)}, u32[]{:S(2)}) %collective-permute-start.1) | collective-permute-done | bytes 40992 | tf_op jit(solution)/shard_map/ppermute | solution.py:124
  161.2 9.3 %all_gather.56 = bf16[40,4096]{1,0:T(8,128)(2,1)S(1)} all-gather(bf16[40,512]{1,0:T(8,128)(2,1)S(1)} %collective-permute-done.1), channel_id=1, replica_groups=mesh['pair'=4,'src'=2,'tgt'=4] {'src','tgt'}, dimensions={1}, use_global_device_ids=true | all-gather | bytes 368640 | tf_op jit(solution)/shard_map/all_gather | solution.py:217
  170.5 3.6 %fusion.10 = (bf16[40,512]{1,0:T(8,128)(2,1)S(1)}, f32[40,512]{1,0:T(8,128)S(1)}) fusion(bf16[40,4096]{1,0:T(8,128)(2,1)S(1)} %select_select_fusion, bf16[512,4096]{1,0:T(8,128)(2,1)} %copy-done, pred[512]{0:T(512)(128)(4,1)S(1)} %add_compare_fusion.1), kind=kOutput, calls=%fused_computation.37 | convolution fusion | flops 167813120 | bytes 4645376 | tf_op jit(solution)/shard_map/dot_general | solution.py:210
  174.1 1.3 collective-permute-start.2
  175.4 4.6 %collective-permute-done.2 = bf16[40,512]{1,0:T(8,128)(2,1)S(1)} collective-permute-done((bf16[40,512]{1,0:T(8,128)(2,1)S(1)}, bf16[40,512]{1,0:T(8,128)(2,1)S(1)}, u32[]{:S(2)}, u32[]{:S(2)}) %collective-permute-start.2) | collective-permute-done | bytes 40992 | tf_op jit(solution)/shard_map/ppermute | solution.py:124
  180.0 8.6 %all_gather.57 = bf16[40,4096]{1,0:T(8,128)(2,1)S(1)} all-gather(bf16[40,512]{1,0:T(8,128)(2,1)S(1)} %collective-permute-done.2), channel_id=1, replica_groups=mesh['pair'=4,'src'=2,'tgt'=4] {'src','tgt'}, dimensions={1}, use_global_device_ids=true | all-gather | bytes 368640 | tf_op jit(solution)/shard_map/all_gather | solution.py:217
  188.6 3.6 %fusion.11 = (bf16[40,512]{1,0:T(8,128)(2,1)S(1)}, f32[40,512]{1,0:T(8,128)S(1)}) fusion(bf16[512,4096]{1,0:T(8,128)(2,1)} %copy-done, bf16[40,4096]{1,0:T(8,128)(2,1)S(1)} %all_gather.57, bf16[40,4096]{1,0:T(8,128)(2,1)S(1)} %select_select_fusion, pred[]{:T(512)S(6)} %eq.19, pred[512]{0:T(512)(128)(4,1)S(1)} %add_compare_fusion.1), kind=kOutput, calls=%fused_computation.38 | convolution fusion | flops 167976960 | bytes 4973057 | tf_op jit(solution)/shard_map/dot_general | solution.py:210
  192.1 1.3 collective-permute-start.3
  193.5 5.2 %all-gather.1 = f32[1,2048]{1,0:T(1,128)S(1)} all-gather(f32[1,512]{1,0:T(1,128)S(1)} %get-tuple-element.21), channel_id=3, replica_groups=mesh['pair'=4,'src'=2,'tgt'=4] {'tgt'}, dimensions={1}, use_global_device_ids=true | all-gather | bytes 10240 | tf_op jit(solution)/shard_map/all_gather | solution.py:219
  198.7 9.3 %all_gather.58 = bf16[40,4096]{1,0:T(8,128)(2,1)S(1)} all-gather(bf16[40,512]{1,0:T(8,128)(2,1)S(1)} %collective-permute-done.3), channel_id=1, replica_groups=mesh['pair'=4,'src'=2,'tgt'=4] {'src','tgt'}, dimensions={1}, use_global_device_ids=true | all-gather | bytes 368640 | tf_op jit(solution)/shard_map/all_gather | solution.py:217
  207.9 4.2 %fusion.1 = f32[1,40,512]{2,1,0:T(8,128)} fusion(bf16[512,4096]{1,0:T(8,128)(2,1)} %copy-done, bf16[40,4096]{1,0:T(8,128)(2,1)S(1)} %all_gather.58, pred[]{:T(512)S(6)} %eq.18, bf16[40,4096]{1,0:T(8,128)(2,1)S(1)} %all_gather.57, bf16[40,4096]{1,0:T(8,128)(2,1)S(1)} %select_select_fusion, pred[]{:T(512)S(6)} %eq.19, f32[40,512]{1,0:T(8,128)S(1)} %get-tuple-element.29, ...), kind=kOutput, calls=%fused_computation.6 | convolution fusion | flops 168222720 | bytes 5508608 | tf_op jit(solution)/shard_map/dot_general | solution.py:210
  212.1 0.6 copy.48
  (19 shorter events, 1.1 us)
Async XLA Ops:
  1.7 17.0 %collective-permute-start = (f32[30,2048]{1,0:T(8,128)S(1)}, f32[30,2048]{1,0:T(8,128)S(1)}, u32[]{:S(2)}, u32[]{:S(2)}) collective-permute-start(f32[30,2048]{1,0:T(8,128)S(1)} %bitcast.80), channel_id=1, source_target_pairs={{8,0},{16,8},{24,16},{9,1},{17,9},{25,17},{10,2},{18,10},{26,18},{... | collective-permute-start | bytes 737288 | tf_op jit(solution)/shard_map/ppermute | solution.py:124
  152.6 2.0 copy-start
  154.6 6.6 %collective-permute-start.1 = (bf16[40,512]{1,0:T(8,128)(2,1)S(1)}, bf16[40,512]{1,0:T(8,128)(2,1)S(1)}, u32[]{:S(2)}, u32[]{:S(2)}) collective-permute-start(bf16[40,512]{1,0:T(8,128)(2,1)S(1)} %fusion.5), channel_id=1, source_target_pairs={{8,0},{16,8},{24,16},{9,1},{17,9},{25,17},{10,2},{18,10},{26,18},{... | collective-permute-start | bytes 122888 | tf_op jit(solution)/shard_map/ppermute | solution.py:124
  174.1 5.9 %collective-permute-start.2 = (bf16[40,512]{1,0:T(8,128)(2,1)S(1)}, bf16[40,512]{1,0:T(8,128)(2,1)S(1)}, u32[]{:S(2)}, u32[]{:S(2)}) collective-permute-start(bf16[40,512]{1,0:T(8,128)(2,1)S(1)} %get-tuple-element.26), channel_id=1, source_target_pairs={{8,0},{16,8},{24,16},{9,1},{17,9},{25,17},{10,2},{18,10},{26,18},{... | collective-permute-start | bytes 122888 | tf_op jit(solution)/shard_map/ppermute | solution.py:124
  192.1 6.5 %collective-permute-start.3 = (bf16[40,512]{1,0:T(8,128)(2,1)S(1)}, bf16[40,512]{1,0:T(8,128)(2,1)S(1)}, u32[]{:S(2)}, u32[]{:S(2)}) collective-permute-start(bf16[40,512]{1,0:T(8,128)(2,1)S(1)} %get-tuple-element.28), channel_id=1, source_target_pairs={{8,0},{16,8},{24,16},{9,1},{17,9},{25,17},{10,2},{18,10},{26,18},{... | collective-permute-start | bytes 122888 | tf_op jit(solution)/shard_map/ppermute | solution.py:124

commit v10 on v9

--- a/solution.py
+++ b/solution.py
@@ -116,6 +116,28 @@
             bytes_accessed=4 * rows * cols + (2 * rows * cols if emit_w else 0),
         ),
     )(scaled_cost, every, log_b[None, :], log_a[:, None], *([handed] if emit_w else []))
+
+
+def pull_kernel(handed_ref, w_ref, out_ref):
+    out_ref[...] = lax.dot_general(
+        handed_ref[...], w_ref[...], (((1,), (1,)), ((), ())), preferred_element_type=jnp.float32
+    )
+
+
+def pull(handed, weights):
+    vmem = pl.BlockSpec(memory_space=pltpu.VMEM)
+    fates, cols = handed.shape
+    rows = weights.shape[0]
+    return pl.pallas_call(
+        pull_kernel,
+        out_shape=jax.ShapeDtypeStruct((fates, rows), jnp.float32),
+        in_specs=[vmem, vmem],
+        out_specs=vmem,
+        compiler_params=pltpu.CompilerParams(vmem_limit_bytes=8 * 1024 * 1024),
+        cost_estimate=pl.CostEstimate(
+            flops=2 * fates * rows * cols, transcendentals=0, bytes_accessed=2 * (fates + rows) * cols
+        ),
+    )(handed, weights)
 
 
 def shifted(shard, axis, by):
@@ -207,9 +229,7 @@
         if section_num == 0:
             pulled = first_pull[:fates_count]
         else:
-            pulled = lax.dot_general(
-                weights, handed, (((1,), (1,)), ((), ())), preferred_element_type=jnp.float32
-            ).T
+            pulled = pull(handed, weights)
         pulled = jnp.where(live_src[None, :], pulled, 0.0)
         fate_maps = jnp.where(pair_rank == active, pulled, fate_maps)
         if section_num + 1 < pair_count:

time: 214 us -> 216 us (level)
  matrix products: 18.7 us -> 7.51 us
  local copies, waits for them, and re-layouts: 7.78 us -> 14.3 us
  Pallas kernels: 43.8 us -> 49.8 us
    dot_general x3 -> x0, matrix products: 11.3 us -> none  [local(): lax.dot_general(weights, handed, (((1,), (1,)), ((), ())), preferred_elem...]
    unnamed x15 -> x21, local copies, waits for them, and re-layouts: 4.57 us -> 11.1 us
    pallas_call x0 -> x3, Pallas kernels: none -> 4.07 us  [pull(): pl.pallas_call(pull_kernel, out_shape=jax.ShapeDtypeStruct((fates, rows),...]
where the time goes in v10:
time: 216 us; the launch traced here: 215 us
  blocking collectives  120 us (56%)
  Pallas kernels  49.8 us (23%)
  local copies, waits for them, and re-layouts  14.3 us (7%)
  waiting for transfers between devices  9.92 us (5%)
  matrix products  7.51 us (3%)
  other arithmetic  6.12 us (3%)
  starting transfers between devices  5.17 us (2%)
  between operations  2.31 us (1%)
    all_gather x8, blocking collectives, local(): every = lax.all_gather(part_lse[0], ('src', 'tgt'))  70 us
    pallas_call x9, Pallas kernels, sweep(): pl.pallas_call(functools.partial(sweep_kernel, do_row, do_col, emit_w, sh...  45.7 us
    all_gather x3, blocking collectives, local(): fresh = lax.all_gather(passed, ('src', 'tgt'), axis=1, tiled=True)  27.1 us
    unnamed x21, local copies, waits for them, and re-layouts  11.1 us
    ppermute x4, waiting for transfers between devices, shifted(): return lax.ppermute(shard, axis, pairs)  9.92 us
    all_gather x1, blocking collectives, local(): pieces = lax.all_gather(piece, ('src', 'tgt'))  9.83 us
    all_gather x1, blocking collectives, local(): lax.all_gather(final_fates.astype(jnp.bfloat16), 'tgt', axis=1, tiled=True)  7.61 us
    dot_general x1, matrix products, local(): lax.dot_general(source_pos, target_pos, (((0,), (0,)), ((), ())), precisi...  7.51 us
  transfers between devices with their start and end apart: 4, of which 2 were waited for; matrix products, arithmetic and copies ran while one was open for 3% of the time, Pallas kernels for 0%

profile of v10, /device:TPU:0, one launch (start us, length us, event | category | flops | bytes accessed | tf_op | source)
XLA Modules:
  0.0 214.9 jit_solution(11999490875265739949)
XLA Ops:
  0.6 1.0 copy.38
  1.7 1.3 collective-permute-start
  3.0 0.7 pad_clamp_fusion
  3.6 0.8 constant_dynamic-slice_fusion
  4.5 1.3 fusion.5
  7.2 0.7 compare_select_fusion.every_ref.lb_ref
  7.9 0.9 convert_element_type.20
  8.8 7.6 %all_gather.55 = bf16[40,4096]{1,0:T(8,128)(2,1)S(1)} all-gather(bf16[40,1024]{1,0:T(8,128)(2,1)S(1)} %convert_element_type.20), channel_id=1, replica_groups=mesh['pair'=4,'src'=2,'tgt'=4] {'tgt'}, dimensions={1}, use_global_device_ids=true | all-gather | bytes 409600 | tf_op jit(solution)/shard_map/all_gather | solution.py:209
  16.4 0.7 subtract_bitcast_fusion
  17.1 0.7 add_compare_fusion.1
  18.0 0.7 fusion.la_ref
  18.7 0.9 select_bitcast_fusion.2
  19.5 9.8 %all-gather.2 = f32[8,30,512]{2,1,0:T(8,128)S(1)} all-gather(f32[1,30,512]{2,1,0:T(8,128)S(1)} %select_bitcast_fusion.2), channel_id=2, replica_groups=mesh['pair'=4,'src'=2,'tgt'=4] {'src','tgt'}, dimensions={0}, use_global_device_ids=true | all-gather | bytes 552960 | tf_op jit(solution)/shard_map/all_gather | solution.py:170
  30.8 7.5 %subtract_multiply_fusion.c_ref = f32[512,4096]{1,0:T(8,128)S(1)} fusion(f32[30,4096]{1,0:T(8,128)S(1)} %bitcast.74, f32[4096]{0:T(1024)S(1)} %bitcast.77, f32[512]{0:T(512)S(1)} %fusion.3, f32[1,30,512]{2,0,1:T(1,128)S(1)} %constant_dynamic-slice_fusion), kind=kOutput, calls=%fused_computation.1 | convolution fusion | flops 763363328 | bytes 8960000 | tf_op jit(solution)/shard_map/dot_general | solution.py:185
  38.3 2.2 %shard_map.77 = f32[1,4096]{1,0:T(1,128)S(1)} custom-call(f32[512,4096]{1,0:T(8,128)S(1)} %subtract_multiply_fusion.c_ref, f32[1,4096]{1,0:T(1,128)S(1)} %compare_select_fusion.every_ref.lb_ref, f32[1,4096]{1,0:T(1,128)S(1)} %compare_select_fusion.every_ref.lb_ref, f32[512,1]{1,0:T(8,128)S(1)} %fusion.la_ref), custom_call_target="tpu_custom_call" | custom-call | flops 16777216 | bytes 8388608 | tf_op jit(solution)/shard_map/pallas_call | solution.py:106
  40.5 9.1 %all-gather.3 = f32[8,1,4096]{2,1,0:T(1,128)S(1)} all-gather(f32[1,1,4096]{2,1,0:T(1,128)S(1)} %bitcast.66), channel_id=1, replica_groups=mesh['pair'=4,'src'=2,'tgt'=4] {'src','tgt'}, dimensions={0}, use_global_device_ids=true | all-gather | bytes 147456 | tf_op jit(solution)/shard_map/all_gather | solution.py:217
  49.6 5.5 %shard_map.78 = (f32[512,1]{1,0:T(8,128)}, f32[1,4096]{1,0:T(1,128)S(1)}) custom-call(f32[512,4096]{1,0:T(8,128)S(1)} %subtract_multiply_fusion.c_ref, f32[8,4096]{1,0:T(8,128)S(1)} %bitcast.59, f32[1,4096]{1,0:T(1,128)S(1)} %compare_select_fusion.every_ref.lb_ref, f32[512,1]{1,0:T(8,128)S(1)} %fusion.la_ref), custom_call_target="tpu_custom_call" | custom-call | flops 33554432 | bytes 8388608 | tf_op jit(solution)/shard_map/pallas_call | solution.py:106
  55.1 8.5 %all-gather.4 = f32[8,1,4096]{2,1,0:T(1,128)S(1)} all-gather(f32[1,1,4096]{2,1,0:T(1,128)S(1)} %bitcast.67), channel_id=1, replica_groups=mesh['pair'=4,'src'=2,'tgt'=4] {'src','tgt'}, dimensions={0}, use_global_device_ids=true | all-gather | bytes 147456 | tf_op jit(solution)/shard_map/all_gather | solution.py:217
  63.7 5.5 %shard_map.79 = (f32[512,1]{1,0:T(8,128)}, f32[1,4096]{1,0:T(1,128)S(1)}) custom-call(f32[512,4096]{1,0:T(8,128)S(1)} %subtract_multiply_fusion.c_ref, f32[8,4096]{1,0:T(8,128)S(1)} %bitcast.60, f32[1,4096]{1,0:T(1,128)S(1)} %compare_select_fusion.every_ref.lb_ref, f32[512,1]{1,0:T(8,128)S(1)} %fusion.la_ref), custom_call_target="tpu_custom_call" | custom-call | flops 33554432 | bytes 8388608 | tf_op jit(solution)/shard_map/pallas_call | solution.py:106
  69.2 9.0 %all-gather.5 = f32[8,1,4096]{2,1,0:T(1,128)S(1)} all-gather(f32[1,1,4096]{2,1,0:T(1,128)S(1)} %bitcast.68), channel_id=1, replica_groups=mesh['pair'=4,'src'=2,'tgt'=4] {'src','tgt'}, dimensions={0}, use_global_device_ids=true | all-gather | bytes 147456 | tf_op jit(solution)/shard_map/all_gather | solution.py:217
  78.4 5.5 %shard_map.80 = (f32[512,1]{1,0:T(8,128)}, f32[1,4096]{1,0:T(1,128)S(1)}) custom-call(f32[512,4096]{1,0:T(8,128)S(1)} %subtract_multiply_fusion.c_ref, f32[8,4096]{1,0:T(8,128)S(1)} %bitcast.61, f32[1,4096]{1,0:T(1,128)S(1)} %compare_select_fusion.every_ref.lb_ref, f32[512,1]{1,0:T(8,128)S(1)} %fusion.la_ref), custom_call_target="tpu_custom_call" | custom-call | flops 33554432 | bytes 8388608 | tf_op jit(solution)/shard_map/pallas_call | solution.py:106
  83.8 8.4 %all-gather.6 = f32[8,1,4096]{2,1,0:T(1,128)S(1)} all-gather(f32[1,1,4096]{2,1,0:T(1,128)S(1)} %bitcast.69), channel_id=1, replica_groups=mesh['pair'=4,'src'=2,'tgt'=4] {'src','tgt'}, dimensions={0}, use_global_device_ids=true | all-gather | bytes 147456 | tf_op jit(solution)/shard_map/all_gather | solution.py:217
  92.3 5.5 %shard_map.81 = (f32[512,1]{1,0:T(8,128)}, f32[1,4096]{1,0:T(1,128)S(1)}) custom-call(f32[512,4096]{1,0:T(8,128)S(1)} %subtract_multiply_fusion.c_ref, f32[8,4096]{1,0:T(8,128)S(1)} %bitcast.62, f32[1,4096]{1,0:T(1,128)S(1)} %compare_select_fusion.every_ref.lb_ref, f32[512,1]{1,0:T(8,128)S(1)} %fusion.la_ref), custom_call_target="tpu_custom_call" | custom-call | flops 33554432 | bytes 8388608 | tf_op jit(solution)/shard_map/pallas_call | solution.py:106
  97.8 9.0 %all-gather.7 = f32[8,1,4096]{2,1,0:T(1,128)S(1)} all-gather(f32[1,1,4096]{2,1,0:T(1,128)S(1)} %bitcast.70), channel_id=1, replica_groups=mesh['pair'=4,'src'=2,'tgt'=4] {'src','tgt'}, dimensions={0}, use_global_device_ids=true | all-gather | bytes 147456 | tf_op jit(solution)/shard_map/all_gather | solution.py:217
  106.9 5.5 %shard_map.82 = (f32[512,1]{1,0:T(8,128)}, f32[1,4096]{1,0:T(1,128)S(1)}) custom-call(f32[512,4096]{1,0:T(8,128)S(1)} %subtract_multiply_fusion.c_ref, f32[8,4096]{1,0:T(8,128)S(1)} %bitcast.63, f32[1,4096]{1,0:T(1,128)S(1)} %compare_select_fusion.every_ref.lb_ref, f32[512,1]{1,0:T(8,128)S(1)} %fusion.la_ref), custom_call_target="tpu_custom_call" | custom-call | flops 33554432 | bytes 8388608 | tf_op jit(solution)/shard_map/pallas_call | solution.py:106
  112.4 8.4 %all-gather.8 = f32[8,1,4096]{2,1,0:T(1,128)S(1)} all-gather(f32[1,1,4096]{2,1,0:T(1,128)S(1)} %bitcast.71), channel_id=1, replica_groups=mesh['pair'=4,'src'=2,'tgt'=4] {'src','tgt'}, dimensions={0}, use_global_device_ids=true | all-gather | bytes 147456 | tf_op jit(solution)/shard_map/all_gather | solution.py:217
  120.8 5.5 %shard_map.83 = (f32[512,1]{1,0:T(8,128)}, f32[1,4096]{1,0:T(1,128)S(1)}) custom-call(f32[512,4096]{1,0:T(8,128)S(1)} %subtract_multiply_fusion.c_ref, f32[8,4096]{1,0:T(8,128)S(1)} %bitcast.64, f32[1,4096]{1,0:T(1,128)S(1)} %compare_select_fusion.every_ref.lb_ref, f32[512,1]{1,0:T(8,128)S(1)} %fusion.la_ref), custom_call_target="tpu_custom_call" | custom-call | flops 33554432 | bytes 8388608 | tf_op jit(solution)/shard_map/pallas_call | solution.py:106
  126.3 9.0 %all-gather.9 = f32[8,1,4096]{2,1,0:T(1,128)S(1)} all-gather(f32[1,1,4096]{2,1,0:T(1,128)S(1)} %bitcast.72), channel_id=1, replica_groups=mesh['pair'=4,'src'=2,'tgt'=4] {'src','tgt'}, dimensions={0}, use_global_device_ids=true | all-gather | bytes 147456 | tf_op jit(solution)/shard_map/all_gather | solution.py:217
  135.4 5.5 %shard_map.84 = (f32[512,1]{1,0:T(8,128)}, f32[1,4096]{1,0:T(1,128)S(1)}) custom-call(f32[512,4096]{1,0:T(8,128)S(1)} %subtract_multiply_fusion.c_ref, f32[8,4096]{1,0:T(8,128)S(1)} %bitcast.65, f32[1,4096]{1,0:T(1,128)S(1)} %compare_select_fusion.every_ref.lb_ref, f32[512,1]{1,0:T(8,128)S(1)} %fusion.la_ref), custom_call_target="tpu_custom_call" | custom-call | flops 33554432 | bytes 8388608 | tf_op jit(solution)/shard_map/pallas_call | solution.py:106
  140.9 8.6 %all-gather.10 = f32[8,1,4096]{2,1,0:T(1,128)S(1)} all-gather(f32[1,1,4096]{2,1,0:T(1,128)S(1)} %bitcast.73), channel_id=1, replica_groups=mesh['pair'=4,'src'=2,'tgt'=4] {'src','tgt'}, dimensions={0}, use_global_device_ids=true | all-gather | bytes 147456 | tf_op jit(solution)/shard_map/all_gather | solution.py:217
  149.6 5.1 %shard_map.85 = (f32[512,1]{1,0:T(8,128)}, bf16[512,4096]{1,0:T(8,128)(2,1)S(1)}, f32[48,512]{1,0:T(8,128)S(1)}, f32[1,512]{1,0:T(1,128)S(1)}) custom-call(f32[512,4096]{1,0:T(8,128)S(1)} %subtract_multiply_fusion.c_ref, f32[8,4096]{1,0:T(8,128)S(1)} %bitcast.58, f32[1,4096]{1,0:T(1,128)S(1)} %compare_select_fusion.every_ref.lb_ref, ...), custom_call_target="tpu_custom_call" | custom-call | flops 25165824 | bytes 12582912 | tf_op jit(solution)/shard_map/pallas_call | solution.py:106
  154.7 1.9 copy-done
  156.6 1.3 collective-permute-start.1
  157.9 5.3 %collective-permute-done.1 = bf16[40,512]{1,0:T(8,128)(2,1)S(1)} collective-permute-done((bf16[40,512]{1,0:T(8,128)(2,1)S(1)}, bf16[40,512]{1,0:T(8,128)(2,1)S(1)}, u32[]{:S(2)}, u32[]{:S(2)}) %collective-permute-start.1) | collective-permute-done | bytes 40992 | tf_op jit(solution)/shard_map/ppermute | solution.py:146
  163.2 9.3 %all_gather.56 = bf16[40,4096]{1,0:T(8,128)(2,1)S(1)} all-gather(bf16[40,512]{1,0:T(8,128)(2,1)S(1)} %collective-permute-done.1), channel_id=1, replica_groups=mesh['pair'=4,'src'=2,'tgt'=4] {'src','tgt'}, dimensions={1}, use_global_device_ids=true | all-gather | bytes 368640 | tf_op jit(solution)/shard_map/all_gather | solution.py:237
  172.6 2.2 %copy-done.1 = bf16[512,4096]{1,0:T(8,128)(2,1)S(1)} copy-done((bf16[512,4096]{1,0:T(8,128)(2,1)S(1)}, bf16[512,4096]{1,0:T(8,128)(2,1)}, u32[]{:S(2)}) %copy-start.1) | copy-done | bytes 4194328
  174.7 1.4 shard_map.86
  176.1 1.3 collective-permute-start.2
  177.4 4.6 %collective-permute-done.2 = bf16[40,512]{1,0:T(8,128)(2,1)S(1)} collective-permute-done((bf16[40,512]{1,0:T(8,128)(2,1)S(1)}, bf16[40,512]{1,0:T(8,128)(2,1)S(1)}, u32[]{:S(2)}, u32[]{:S(2)}) %collective-permute-start.2) | collective-permute-done | bytes 40992 | tf_op jit(solution)/shard_map/ppermute | solution.py:146
  182.0 8.6 %all_gather.57 = bf16[40,4096]{1,0:T(8,128)(2,1)S(1)} all-gather(bf16[40,512]{1,0:T(8,128)(2,1)S(1)} %collective-permute-done.2), channel_id=1, replica_groups=mesh['pair'=4,'src'=2,'tgt'=4] {'src','tgt'}, dimensions={1}, use_global_device_ids=true | all-gather | bytes 368640 | tf_op jit(solution)/shard_map/all_gather | solution.py:237
  190.7 2.2 %copy-done.2 = bf16[512,4096]{1,0:T(8,128)(2,1)S(1)} copy-done((bf16[512,4096]{1,0:T(8,128)(2,1)S(1)}, bf16[512,4096]{1,0:T(8,128)(2,1)}, u32[]{:S(2)}) %copy-start.2) | copy-done | bytes 4194328
  192.9 1.4 shard_map.87
  194.2 1.3 collective-permute-start.3
  195.5 5.2 %all-gather.1 = f32[1,2048]{1,0:T(1,128)S(1)} all-gather(f32[1,512]{1,0:T(1,128)S(1)} %get-tuple-element.21), channel_id=3, replica_groups=mesh['pair'=4,'src'=2,'tgt'=4] {'tgt'}, dimensions={1}, use_global_device_ids=true | all-gather | bytes 10240 | tf_op jit(solution)/shard_map/all_gather | solution.py:239
  200.7 9.3 %all_gather.58 = bf16[40,4096]{1,0:T(8,128)(2,1)S(1)} all-gather(bf16[40,512]{1,0:T(8,128)(2,1)S(1)} %collective-permute-done.3), channel_id=1, replica_groups=mesh['pair'=4,'src'=2,'tgt'=4] {'src','tgt'}, dimensions={1}, use_global_device_ids=true | all-gather | bytes 368640 | tf_op jit(solution)/shard_map/all_gather | solution.py:237
  210.0 2.2 %copy-done.3 = bf16[512,4096]{1,0:T(8,128)(2,1)S(1)} copy-done((bf16[512,4096]{1,0:T(8,128)(2,1)S(1)}, bf16[512,4096]{1,0:T(8,128)(2,1)}, u32[]{:S(2)}) %copy-start.3) | copy-done | bytes 4194328
  212.2 1.4 shard_map.88
  213.6 0.7 select_bitcast_fusion.1
  (30 shorter events, 3.0 us)
Async XLA Ops:
  1.7 17.0 %collective-permute-start = (f32[30,2048]{1,0:T(8,128)S(1)}, f32[30,2048]{1,0:T(8,128)S(1)}, u32[]{:S(2)}, u32[]{:S(2)}) collective-permute-start(f32[30,2048]{1,0:T(8,128)S(1)} %bitcast.76), channel_id=1, source_target_pairs={{8,0},{16,8},{24,16},{9,1},{17,9},{25,17},{10,2},{18,10},{26,18},{... | collective-permute-start | bytes 737288 | tf_op jit(solution)/shard_map/ppermute | solution.py:146
  154.7 2.0 copy-start
  156.6 6.6 %collective-permute-start.1 = (bf16[40,512]{1,0:T(8,128)(2,1)S(1)}, bf16[40,512]{1,0:T(8,128)(2,1)S(1)}, u32[]{:S(2)}, u32[]{:S(2)}) collective-permute-start(bf16[40,512]{1,0:T(8,128)(2,1)S(1)} %fusion.1), channel_id=1, source_target_pairs={{8,0},{16,8},{24,16},{9,1},{17,9},{25,17},{10,2},{18,10},{26,18},{... | collective-permute-start | bytes 122888 | tf_op jit(solution)/shard_map/ppermute | solution.py:146
  172.6 2.2 %copy-start.1 = (bf16[512,4096]{1,0:T(8,128)(2,1)S(1)}, bf16[512,4096]{1,0:T(8,128)(2,1)}, u32[]{:S(2)}) copy-start(bf16[512,4096]{1,0:T(8,128)(2,1)} %copy-done) | copy-start | bytes 12582916
  176.1 5.9 %collective-permute-start.2 = (bf16[40,512]{1,0:T(8,128)(2,1)S(1)}, bf16[40,512]{1,0:T(8,128)(2,1)S(1)}, u32[]{:S(2)}, u32[]{:S(2)}) collective-permute-start(bf16[40,512]{1,0:T(8,128)(2,1)S(1)} %select_convert_fusion.1), channel_id=1, source_target_pairs={{8,0},{16,8},{24,16},{9,1},{17,9},{25,17},{10,2},{18,10},{26,18},{... | collective-permute-start | bytes 122888 | tf_op jit(solution)/shard_map/ppermute | solution.py:146
  190.7 2.2 %copy-start.2 = (bf16[512,4096]{1,0:T(8,128)(2,1)S(1)}, bf16[512,4096]{1,0:T(8,128)(2,1)}, u32[]{:S(2)}) copy-start(bf16[512,4096]{1,0:T(8,128)(2,1)} %copy-done) | copy-start | bytes 12582916
  194.2 6.5 %collective-permute-start.3 = (bf16[40,512]{1,0:T(8,128)(2,1)S(1)}, bf16[40,512]{1,0:T(8,128)(2,1)S(1)}, u32[]{:S(2)}, u32[]{:S(2)}) collective-permute-start(bf16[40,512]{1,0:T(8,128)(2,1)S(1)} %select_convert_fusion), channel_id=1, source_target_pairs={{8,0},{16,8},{24,16},{9,1},{17,9},{25,17},{10,2},{18,10},{26,18},{... | collective-permute-start | bytes 122888 | tf_op jit(solution)/shard_map/ppermute | solution.py:146
  210.0 2.2 %copy-start.3 = (bf16[512,4096]{1,0:T(8,128)(2,1)S(1)}, bf16[512,4096]{1,0:T(8,128)(2,1)}, u32[]{:S(2)}) copy-start(bf16[512,4096]{1,0:T(8,128)(2,1)} %copy-done) | copy-start | bytes 12582916

commit v11 on v9

--- a/solution.py
+++ b/solution.py
@@ -14,7 +14,7 @@
 NEG = -1e30
 
 
-GROUP = 16
+GROUP = 32
 ROW_GROUP = 128
 WIDTH = 512
 

time: 214 us -> 214 us (level)
  no operation moved by 1% of the time
where the time goes in v11:
time: 214 us; the launch traced here: 213 us
  blocking collectives  120 us (56%)
  Pallas kernels  43.7 us (20%)
  matrix products  18.7 us (9%)
  waiting for transfers between devices  9.92 us (5%)
  local copies, waits for them, and re-layouts  7.78 us (4%)
  other arithmetic  5.35 us (2%)
  starting transfers between devices  5.17 us (2%)
  between operations  2.26 us (1%)
    all_gather x8, blocking collectives, local(): every = lax.all_gather(part_lse[0], ('src', 'tgt'))  70 us
    pallas_call x9, Pallas kernels, sweep(): pl.pallas_call(functools.partial(sweep_kernel, do_row, do_col, emit_w, sh...  43.7 us
    all_gather x3, blocking collectives, local(): fresh = lax.all_gather(passed, ('src', 'tgt'), axis=1, tiled=True)  27.1 us
    dot_general x3, matrix products, local(): lax.dot_general(weights, handed, (((1,), (1,)), ((), ())), preferred_elem...  11.3 us
    ppermute x4, waiting for transfers between devices, shifted(): return lax.ppermute(shard, axis, pairs)  9.92 us
    all_gather x1, blocking collectives, local(): pieces = lax.all_gather(piece, ('src', 'tgt'))  9.83 us
    all_gather x1, blocking collectives, local(): lax.all_gather(final_fates.astype(jnp.bfloat16), 'tgt', axis=1, tiled=True)  7.61 us
    dot_general x1, matrix products, local(): lax.dot_general(source_pos, target_pos, (((0,), (0,)), ((), ())), precisi...  7.4 us
  transfers between devices with their start and end apart: 4, of which 2 were waited for; matrix products, arithmetic and copies ran while one was open for 3% of the time, Pallas kernels for 0%

profile of v11, /device:TPU:0, one launch (start us, length us, event | category | flops | bytes accessed | tf_op | source)
XLA Modules:
  0.0 212.7 jit_solution(16533920557529456930)
XLA Ops:
  0.6 1.0 copy.38
  1.7 1.3 collective-permute-start
  3.0 0.7 pad_clamp_fusion
  3.6 0.8 constant_dynamic-slice_fusion
  4.5 1.3 fusion.9
  7.2 0.7 compare_select_fusion.every_ref.lb_ref
  7.9 0.9 convert_element_type.20
  8.8 7.6 %all_gather.55 = bf16[40,4096]{1,0:T(8,128)(2,1)S(1)} all-gather(bf16[40,1024]{1,0:T(8,128)(2,1)S(1)} %convert_element_type.20), channel_id=1, replica_groups=mesh['pair'=4,'src'=2,'tgt'=4] {'tgt'}, dimensions={1}, use_global_device_ids=true | all-gather | bytes 409600 | tf_op jit(solution)/shard_map/all_gather | solution.py:187
  16.4 0.7 subtract_bitcast_fusion
  17.1 0.7 add_compare_fusion.1
  18.0 0.7 fusion.4.la_ref
  18.7 0.9 select_bitcast_fusion.1
  19.5 9.8 %all-gather.2 = f32[8,30,512]{2,1,0:T(8,128)S(1)} all-gather(f32[1,30,512]{2,1,0:T(8,128)S(1)} %select_bitcast_fusion.1), channel_id=2, replica_groups=mesh['pair'=4,'src'=2,'tgt'=4] {'src','tgt'}, dimensions={0}, use_global_device_ids=true | all-gather | bytes 552960 | tf_op jit(solution)/shard_map/all_gather | solution.py:148
  29.4 0.6 gather_fusion
  30.1 0.3 copy.10
  30.4 0.3 copy.23
  30.8 7.4 %subtract_multiply_fusion.c_ref = f32[512,4096]{1,0:T(8,128)S(1)} fusion(f32[30,4096]{1,0:T(8,128)S(1)} %bitcast.78, f32[4096]{0:T(1024)S(1)} %bitcast.81, f32[512]{0:T(512)S(1)} %fusion.7, f32[1,30,512]{2,0,1:T(1,128)S(1)} %constant_dynamic-slice_fusion), kind=kOutput, calls=%fused_computation.1 | convolution fusion | flops 763363328 | bytes 8960000 | tf_op jit(solution)/shard_map/dot_general | solution.py:163
  38.2 2.2 %shard_map.77 = f32[1,4096]{1,0:T(1,128)S(1)} custom-call(f32[512,4096]{1,0:T(8,128)S(1)} %subtract_multiply_fusion.c_ref, f32[1,4096]{1,0:T(1,128)S(1)} %compare_select_fusion.every_ref.lb_ref, f32[1,4096]{1,0:T(1,128)S(1)} %compare_select_fusion.every_ref.lb_ref, f32[512,1]{1,0:T(8,128)S(1)} %fusion.4.la_ref), custom_call_target="tpu_custom_call" | custom-call | flops 16777216 | bytes 8388608 | tf_op jit(solution)/shard_map/pallas_call | solution.py:106
  40.4 9.1 %all-gather.3 = f32[8,1,4096]{2,1,0:T(1,128)S(1)} all-gather(f32[1,1,4096]{2,1,0:T(1,128)S(1)} %bitcast.70), channel_id=1, replica_groups=mesh['pair'=4,'src'=2,'tgt'=4] {'src','tgt'}, dimensions={0}, use_global_device_ids=true | all-gather | bytes 147456 | tf_op jit(solution)/shard_map/all_gather | solution.py:195
  49.5 5.2 %shard_map.78 = (f32[512,1]{1,0:T(8,128)}, f32[1,4096]{1,0:T(1,128)S(1)}) custom-call(f32[512,4096]{1,0:T(8,128)S(1)} %subtract_multiply_fusion.c_ref, f32[8,4096]{1,0:T(8,128)S(1)} %bitcast.63, f32[1,4096]{1,0:T(1,128)S(1)} %compare_select_fusion.every_ref.lb_ref, f32[512,1]{1,0:T(8,128)S(1)} %fusion.4.la_ref), custom_call_target="tpu_custom_call" | custom-call | flops 33554432 | bytes 8388608 | tf_op jit(solution)/shard_map/pallas_call | solution.py:106
  54.7 8.5 %all-gather.4 = f32[8,1,4096]{2,1,0:T(1,128)S(1)} all-gather(f32[1,1,4096]{2,1,0:T(1,128)S(1)} %bitcast.71), channel_id=1, replica_groups=mesh['pair'=4,'src'=2,'tgt'=4] {'src','tgt'}, dimensions={0}, use_global_device_ids=true | all-gather | bytes 147456 | tf_op jit(solution)/shard_map/all_gather | solution.py:195
  63.4 5.2 %shard_map.79 = (f32[512,1]{1,0:T(8,128)}, f32[1,4096]{1,0:T(1,128)S(1)}) custom-call(f32[512,4096]{1,0:T(8,128)S(1)} %subtract_multiply_fusion.c_ref, f32[8,4096]{1,0:T(8,128)S(1)} %bitcast.64, f32[1,4096]{1,0:T(1,128)S(1)} %compare_select_fusion.every_ref.lb_ref, f32[512,1]{1,0:T(8,128)S(1)} %fusion.4.la_ref), custom_call_target="tpu_custom_call" | custom-call | flops 33554432 | bytes 8388608 | tf_op jit(solution)/shard_map/pallas_call | solution.py:106
  68.6 9.0 %all-gather.5 = f32[8,1,4096]{2,1,0:T(1,128)S(1)} all-gather(f32[1,1,4096]{2,1,0:T(1,128)S(1)} %bitcast.72), channel_id=1, replica_groups=mesh['pair'=4,'src'=2,'tgt'=4] {'src','tgt'}, dimensions={0}, use_global_device_ids=true | all-gather | bytes 147456 | tf_op jit(solution)/shard_map/all_gather | solution.py:195
  77.7 5.2 %shard_map.80 = (f32[512,1]{1,0:T(8,128)}, f32[1,4096]{1,0:T(1,128)S(1)}) custom-call(f32[512,4096]{1,0:T(8,128)S(1)} %subtract_multiply_fusion.c_ref, f32[8,4096]{1,0:T(8,128)S(1)} %bitcast.65, f32[1,4096]{1,0:T(1,128)S(1)} %compare_select_fusion.every_ref.lb_ref, f32[512,1]{1,0:T(8,128)S(1)} %fusion.4.la_ref), custom_call_target="tpu_custom_call" | custom-call | flops 33554432 | bytes 8388608 | tf_op jit(solution)/shard_map/pallas_call | solution.py:106
  83.0 8.4 %all-gather.6 = f32[8,1,4096]{2,1,0:T(1,128)S(1)} all-gather(f32[1,1,4096]{2,1,0:T(1,128)S(1)} %bitcast.73), channel_id=1, replica_groups=mesh['pair'=4,'src'=2,'tgt'=4] {'src','tgt'}, dimensions={0}, use_global_device_ids=true | all-gather | bytes 147456 | tf_op jit(solution)/shard_map/all_gather | solution.py:195
  91.4 5.2 %shard_map.81 = (f32[512,1]{1,0:T(8,128)}, f32[1,4096]{1,0:T(1,128)S(1)}) custom-call(f32[512,4096]{1,0:T(8,128)S(1)} %subtract_multiply_fusion.c_ref, f32[8,4096]{1,0:T(8,128)S(1)} %bitcast.66, f32[1,4096]{1,0:T(1,128)S(1)} %compare_select_fusion.every_ref.lb_ref, f32[512,1]{1,0:T(8,128)S(1)} %fusion.4.la_ref), custom_call_target="tpu_custom_call" | custom-call | flops 33554432 | bytes 8388608 | tf_op jit(solution)/shard_map/pallas_call | solution.py:106
  96.7 9.0 %all-gather.7 = f32[8,1,4096]{2,1,0:T(1,128)S(1)} all-gather(f32[1,1,4096]{2,1,0:T(1,128)S(1)} %bitcast.74), channel_id=1, replica_groups=mesh['pair'=4,'src'=2,'tgt'=4] {'src','tgt'}, dimensions={0}, use_global_device_ids=true | all-gather | bytes 147456 | tf_op jit(solution)/shard_map/all_gather | solution.py:195
  105.8 5.2 %shard_map.82 = (f32[512,1]{1,0:T(8,128)}, f32[1,4096]{1,0:T(1,128)S(1)}) custom-call(f32[512,4096]{1,0:T(8,128)S(1)} %subtract_multiply_fusion.c_ref, f32[8,4096]{1,0:T(8,128)S(1)} %bitcast.67, f32[1,4096]{1,0:T(1,128)S(1)} %compare_select_fusion.every_ref.lb_ref, f32[512,1]{1,0:T(8,128)S(1)} %fusion.4.la_ref), custom_call_target="tpu_custom_call" | custom-call | flops 33554432 | bytes 8388608 | tf_op jit(solution)/shard_map/pallas_call | solution.py:106
  111.0 8.4 %all-gather.8 = f32[8,1,4096]{2,1,0:T(1,128)S(1)} all-gather(f32[1,1,4096]{2,1,0:T(1,128)S(1)} %bitcast.75), channel_id=1, replica_groups=mesh['pair'=4,'src'=2,'tgt'=4] {'src','tgt'}, dimensions={0}, use_global_device_ids=true | all-gather | bytes 147456 | tf_op jit(solution)/shard_map/all_gather | solution.py:195
  119.5 5.2 %shard_map.83 = (f32[512,1]{1,0:T(8,128)}, f32[1,4096]{1,0:T(1,128)S(1)}) custom-call(f32[512,4096]{1,0:T(8,128)S(1)} %subtract_multiply_fusion.c_ref, f32[8,4096]{1,0:T(8,128)S(1)} %bitcast.68, f32[1,4096]{1,0:T(1,128)S(1)} %compare_select_fusion.every_ref.lb_ref, f32[512,1]{1,0:T(8,128)S(1)} %fusion.4.la_ref), custom_call_target="tpu_custom_call" | custom-call | flops 33554432 | bytes 8388608 | tf_op jit(solution)/shard_map/pallas_call | solution.py:106
  124.7 9.0 %all-gather.9 = f32[8,1,4096]{2,1,0:T(1,128)S(1)} all-gather(f32[1,1,4096]{2,1,0:T(1,128)S(1)} %bitcast.76), channel_id=1, replica_groups=mesh['pair'=4,'src'=2,'tgt'=4] {'src','tgt'}, dimensions={0}, use_global_device_ids=true | all-gather | bytes 147456 | tf_op jit(solution)/shard_map/all_gather | solution.py:195
  133.8 5.2 %shard_map.84 = (f32[512,1]{1,0:T(8,128)}, f32[1,4096]{1,0:T(1,128)S(1)}) custom-call(f32[512,4096]{1,0:T(8,128)S(1)} %subtract_multiply_fusion.c_ref, f32[8,4096]{1,0:T(8,128)S(1)} %bitcast.69, f32[1,4096]{1,0:T(1,128)S(1)} %compare_select_fusion.every_ref.lb_ref, f32[512,1]{1,0:T(8,128)S(1)} %fusion.4.la_ref), custom_call_target="tpu_custom_call" | custom-call | flops 33554432 | bytes 8388608 | tf_op jit(solution)/shard_map/pallas_call | solution.py:106
  139.1 8.6 %all-gather.10 = f32[8,1,4096]{2,1,0:T(1,128)S(1)} all-gather(f32[1,1,4096]{2,1,0:T(1,128)S(1)} %bitcast.77), channel_id=1, replica_groups=mesh['pair'=4,'src'=2,'tgt'=4] {'src','tgt'}, dimensions={0}, use_global_device_ids=true | all-gather | bytes 147456 | tf_op jit(solution)/shard_map/all_gather | solution.py:195
  147.7 4.8 %shard_map.85 = (f32[512,1]{1,0:T(8,128)}, bf16[512,4096]{1,0:T(8,128)(2,1)S(1)}, f32[48,512]{1,0:T(8,128)S(1)}, f32[1,512]{1,0:T(1,128)S(1)}) custom-call(f32[512,4096]{1,0:T(8,128)S(1)} %subtract_multiply_fusion.c_ref, f32[8,4096]{1,0:T(8,128)S(1)} %bitcast.62, f32[1,4096]{1,0:T(1,128)S(1)} %compare_select_fusion.every_ref.lb_ref, ...), custom_call_target="tpu_custom_call" | custom-call | flops 25165824 | bytes 12582912 | tf_op jit(solution)/shard_map/pallas_call | solution.py:106
  152.6 2.0 copy-done
  154.5 1.3 collective-permute-start.1
  155.8 5.3 %collective-permute-done.1 = bf16[40,512]{1,0:T(8,128)(2,1)S(1)} collective-permute-done((bf16[40,512]{1,0:T(8,128)(2,1)S(1)}, bf16[40,512]{1,0:T(8,128)(2,1)S(1)}, u32[]{:S(2)}, u32[]{:S(2)}) %collective-permute-start.1) | collective-permute-done | bytes 40992 | tf_op jit(solution)/shard_map/ppermute | solution.py:124
  161.2 9.3 %all_gather.56 = bf16[40,4096]{1,0:T(8,128)(2,1)S(1)} all-gather(bf16[40,512]{1,0:T(8,128)(2,1)S(1)} %collective-permute-done.1), channel_id=1, replica_groups=mesh['pair'=4,'src'=2,'tgt'=4] {'src','tgt'}, dimensions={1}, use_global_device_ids=true | all-gather | bytes 368640 | tf_op jit(solution)/shard_map/all_gather | solution.py:217
  170.5 3.6 %fusion.10 = (bf16[40,512]{1,0:T(8,128)(2,1)S(1)}, f32[40,512]{1,0:T(8,128)S(1)}) fusion(bf16[40,4096]{1,0:T(8,128)(2,1)S(1)} %select_select_fusion, bf16[512,4096]{1,0:T(8,128)(2,1)} %copy-done, pred[512]{0:T(512)(128)(4,1)S(1)} %add_compare_fusion.1), kind=kOutput, calls=%fused_computation.37 | convolution fusion | flops 167813120 | bytes 4645376 | tf_op jit(solution)/shard_map/dot_general | solution.py:210
  174.0 1.3 collective-permute-start.2
  175.3 4.6 %collective-permute-done.2 = bf16[40,512]{1,0:T(8,128)(2,1)S(1)} collective-permute-done((bf16[40,512]{1,0:T(8,128)(2,1)S(1)}, bf16[40,512]{1,0:T(8,128)(2,1)S(1)}, u32[]{:S(2)}, u32[]{:S(2)}) %collective-permute-start.2) | collective-permute-done | bytes 40992 | tf_op jit(solution)/shard_map/ppermute | solution.py:124
  179.9 8.6 %all_gather.57 = bf16[40,4096]{1,0:T(8,128)(2,1)S(1)} all-gather(bf16[40,512]{1,0:T(8,128)(2,1)S(1)} %collective-permute-done.2), channel_id=1, replica_groups=mesh['pair'=4,'src'=2,'tgt'=4] {'src','tgt'}, dimensions={1}, use_global_device_ids=true | all-gather | bytes 368640 | tf_op jit(solution)/shard_map/all_gather | solution.py:217
  188.5 3.6 %fusion.11 = (bf16[40,512]{1,0:T(8,128)(2,1)S(1)}, f32[40,512]{1,0:T(8,128)S(1)}) fusion(bf16[512,4096]{1,0:T(8,128)(2,1)} %copy-done, bf16[40,4096]{1,0:T(8,128)(2,1)S(1)} %all_gather.57, bf16[40,4096]{1,0:T(8,128)(2,1)S(1)} %select_select_fusion, pred[]{:T(512)S(6)} %eq.19, pred[512]{0:T(512)(128)(4,1)S(1)} %add_compare_fusion.1), kind=kOutput, calls=%fused_computation.38 | convolution fusion | flops 167976960 | bytes 4973057 | tf_op jit(solution)/shard_map/dot_general | solution.py:210
  192.1 1.3 collective-permute-start.3
  193.4 5.2 %all-gather.1 = f32[1,2048]{1,0:T(1,128)S(1)} all-gather(f32[1,512]{1,0:T(1,128)S(1)} %get-tuple-element.21), channel_id=3, replica_groups=mesh['pair'=4,'src'=2,'tgt'=4] {'tgt'}, dimensions={1}, use_global_device_ids=true | all-gather | bytes 10240 | tf_op jit(solution)/shard_map/all_gather | solution.py:219
  198.6 9.3 %all_gather.58 = bf16[40,4096]{1,0:T(8,128)(2,1)S(1)} all-gather(bf16[40,512]{1,0:T(8,128)(2,1)S(1)} %collective-permute-done.3), channel_id=1, replica_groups=mesh['pair'=4,'src'=2,'tgt'=4] {'src','tgt'}, dimensions={1}, use_global_device_ids=true | all-gather | bytes 368640 | tf_op jit(solution)/shard_map/all_gather | solution.py:217
  207.8 4.2 %fusion.1 = f32[1,40,512]{2,1,0:T(8,128)} fusion(bf16[512,4096]{1,0:T(8,128)(2,1)} %copy-done, bf16[40,4096]{1,0:T(8,128)(2,1)S(1)} %all_gather.58, pred[]{:T(512)S(6)} %eq.18, bf16[40,4096]{1,0:T(8,128)(2,1)S(1)} %all_gather.57, bf16[40,4096]{1,0:T(8,128)(2,1)S(1)} %select_select_fusion, pred[]{:T(512)S(6)} %eq.19, f32[40,512]{1,0:T(8,128)S(1)} %get-tuple-element.29, ...), kind=kOutput, calls=%fused_computation.6 | convolution fusion | flops 168222720 | bytes 5508608 | tf_op jit(solution)/shard_map/dot_general | solution.py:210
  212.1 0.6 copy.48
  (19 shorter events, 1.1 us)
Async XLA Ops:
  1.7 17.0 %collective-permute-start = (f32[30,2048]{1,0:T(8,128)S(1)}, f32[30,2048]{1,0:T(8,128)S(1)}, u32[]{:S(2)}, u32[]{:S(2)}) collective-permute-start(f32[30,2048]{1,0:T(8,128)S(1)} %bitcast.80), channel_id=1, source_target_pairs={{8,0},{16,8},{24,16},{9,1},{17,9},{25,17},{10,2},{18,10},{26,18},{... | collective-permute-start | bytes 737288 | tf_op jit(solution)/shard_map/ppermute | solution.py:124
  152.6 2.0 copy-start
  154.5 6.6 %collective-permute-start.1 = (bf16[40,512]{1,0:T(8,128)(2,1)S(1)}, bf16[40,512]{1,0:T(8,128)(2,1)S(1)}, u32[]{:S(2)}, u32[]{:S(2)}) collective-permute-start(bf16[40,512]{1,0:T(8,128)(2,1)S(1)} %fusion.5), channel_id=1, source_target_pairs={{8,0},{16,8},{24,16},{9,1},{17,9},{25,17},{10,2},{18,10},{26,18},{... | collective-permute-start | bytes 122888 | tf_op jit(solution)/shard_map/ppermute | solution.py:124
  174.0 5.9 %collective-permute-start.2 = (bf16[40,512]{1,0:T(8,128)(2,1)S(1)}, bf16[40,512]{1,0:T(8,128)(2,1)S(1)}, u32[]{:S(2)}, u32[]{:S(2)}) collective-permute-start(bf16[40,512]{1,0:T(8,128)(2,1)S(1)} %get-tuple-element.26), channel_id=1, source_target_pairs={{8,0},{16,8},{24,16},{9,1},{17,9},{25,17},{10,2},{18,10},{26,18},{... | collective-permute-start | bytes 122888 | tf_op jit(solution)/shard_map/ppermute | solution.py:124
  192.1 6.5 %collective-permute-start.3 = (bf16[40,512]{1,0:T(8,128)(2,1)S(1)}, bf16[40,512]{1,0:T(8,128)(2,1)S(1)}, u32[]{:S(2)}, u32[]{:S(2)}) collective-permute-start(bf16[40,512]{1,0:T(8,128)(2,1)S(1)} %get-tuple-element.28), channel_id=1, source_target_pairs={{8,0},{16,8},{24,16},{9,1},{17,9},{25,17},{10,2},{18,10},{26,18},{... | collective-permute-start | bytes 122888 | tf_op jit(solution)/shard_map/ppermute | solution.py:124

commit v12 on v11

--- a/solution.py
+++ b/solution.py
@@ -184,7 +184,17 @@
         live_tgt, -jnp.log(live_next.astype(jnp.float32)) * jnp.ones((cols,), jnp.float32), NEG
     )
     scaled_cost = cost_tile * (1.0 / EPS)
-    final_handed = lax.all_gather(final_fates.astype(jnp.bfloat16), "tgt", axis=1, tiled=True)
+    fin_fates = final_fates.astype(jnp.bfloat16)
+    if tgt_count <= 4:
+        got = [fin_fates] + [
+            lax.ppermute(fin_fates, "tgt", [(i, (i + k) % tgt_count) for i in range(tgt_count)])
+            for k in range(1, tgt_count)
+        ]
+        order = (tgt_rank - jnp.arange(tgt_count, dtype=jnp.int32)) % tgt_count
+        got = jnp.take(jnp.stack(got), order, axis=0)
+        final_handed = jnp.transpose(got, (1, 0, 2)).reshape(fin_fates.shape[0], tgt_count * fin_width)
+    else:
+        final_handed = lax.all_gather(fin_fates, "tgt", axis=1, tiled=True)
     fates_count = final_handed.shape[0]
     fates_pad = -fates_count % 16
     handed_pad = jnp.concatenate(

time: 214 us -> 212 us (level)
  blocking collectives: 120 us -> 111 us
  starting transfers between devices: 5.17 us -> 9.68 us
    all_gather x1 -> x0, blocking collectives: 7.61 us -> none  [local(): lax.all_gather(final_fates.astype(jnp.bfloat16), 'tgt', axis=1, tiled=True)]
    ppermute x0 -> x3, starting transfers between devices: none -> 4.51 us  [local(): lax.ppermute(fin_fates, 'tgt', [(i, (i + k) % tgt_count) for i in range(t...]
  transfers between devices with their start and end apart: 4 -> 7, of which waited for: 2 -> 2; matrix products, arithmetic and copies ran while one was open for 3% -> 4% of each run, Pallas kernels for 0% -> 0%
where the time goes in v12:
time: 212 us; the launch traced here: 211 us
  blocking collectives  111 us (52%)
  Pallas kernels  43.7 us (21%)
  matrix products  18.7 us (9%)
  waiting for transfers between devices  9.92 us (5%)
  starting transfers between devices  9.68 us (5%)
  local copies, waits for them, and re-layouts  8.36 us (4%)
  other arithmetic  6.46 us (3%)
  between operations  2.33 us (1%)
    all_gather x8, blocking collectives, local(): every = lax.all_gather(part_lse[0], ('src', 'tgt'))  70 us
    pallas_call x9, Pallas kernels, sweep(): pl.pallas_call(functools.partial(sweep_kernel, do_row, do_col, emit_w, sh...  43.7 us
    all_gather x3, blocking collectives, local(): fresh = lax.all_gather(passed, ('src', 'tgt'), axis=1, tiled=True)  26.3 us
    dot_general x3, matrix products, local(): lax.dot_general(weights, handed, (((1,), (1,)), ((), ())), preferred_elem...  11.3 us
    ppermute x4, waiting for transfers between devices, shifted(): return lax.ppermute(shard, axis, pairs)  9.91 us
    all_gather x1, blocking collectives, local(): pieces = lax.all_gather(piece, ('src', 'tgt'))  9.83 us
    dot_general x1, matrix products, local(): lax.dot_general(source_pos, target_pos, (((0,), (0,)), ((), ())), precisi...  7.41 us
    all_gather x1, blocking collectives, local(): pot_all = lax.all_gather(pot_lanes.reshape(rows), 'tgt', axis=0, tiled=True)  5.19 us
  transfers between devices with their start and end apart: 7, of which 2 were waited for; matrix products, arithmetic and copies ran while one was open for 4% of the time, Pallas kernels for 0%

profile of v12, /device:TPU:0, one launch (start us, length us, event | category | flops | bytes accessed | tf_op | source)
XLA Modules:
  0.0 210.5 jit_solution(13928170726233290615)
XLA Ops:
  0.6 0.9 convert_element_type.20
  2.1 2.6 %collective-permute-start.2 = (bf16[40,1024]{1,0:T(8,128)(2,1)S(1)}, bf16[40,1024]{1,0:T(8,128)(2,1)S(1)}, u32[]{:S(2)}, u32[]{:S(2)}) collective-permute-start(bf16[40,1024]{1,0:T(8,128)(2,1)S(1)} %convert_element_type.20), channel_id=1, source_target_pairs={{0,2},{1,3},{2,0},{3,1},{4,6},{5,7},{6,4},{7,5},{8,10},{9,11},{10,... | collective-permute-start | bytes 245768 | tf_op jit(solution)/shard_map/ppermute | solution.py:190
  4.7 1.4 collective-permute-start.3
  6.1 1.0 copy.42
  7.1 1.3 collective-permute-start
  8.4 0.9 convert_bitcast_fusion
  9.4 0.7 pad_clamp_fusion.1
  10.1 0.8 constant_dynamic-slice_fusion
  10.9 1.3 fusion.12
  12.9 0.7 subtract_bitcast_fusion
  14.5 0.7 compare_select_fusion.every_ref.lb_ref
  15.2 0.7 fusion.4.la_ref
  15.9 0.7 add_compare_fusion.1
  17.4 0.9 select_bitcast_fusion.2
  18.2 9.8 %all-gather.2 = f32[8,30,512]{2,1,0:T(8,128)S(1)} all-gather(f32[1,30,512]{2,1,0:T(8,128)S(1)} %select_bitcast_fusion.2), channel_id=2, replica_groups=mesh['pair'=4,'src'=2,'tgt'=4] {'src','tgt'}, dimensions={0}, use_global_device_ids=true | all-gather | bytes 552960 | tf_op jit(solution)/shard_map/all_gather | solution.py:148
  28.1 0.6 gather_fusion
  29.5 7.4 %subtract_multiply_fusion.c_ref = f32[512,4096]{1,0:T(8,128)S(1)} fusion(f32[30,4096]{1,0:T(8,128)S(1)} %bitcast.91, f32[4096]{0:T(1024)S(1)} %bitcast.94, f32[512]{0:T(512)S(1)} %fusion.7, f32[1,30,512]{2,0,1:T(1,128)S(1)} %constant_dynamic-slice_fusion), kind=kOutput, calls=%fused_computation.2 | convolution fusion | flops 763363328 | bytes 8960000 | tf_op jit(solution)/shard_map/dot_general | solution.py:163
  36.9 2.2 %shard_map.77 = f32[1,4096]{1,0:T(1,128)S(1)} custom-call(f32[512,4096]{1,0:T(8,128)S(1)} %subtract_multiply_fusion.c_ref, f32[1,4096]{1,0:T(1,128)S(1)} %compare_select_fusion.every_ref.lb_ref, f32[1,4096]{1,0:T(1,128)S(1)} %compare_select_fusion.every_ref.lb_ref, f32[512,1]{1,0:T(8,128)S(1)} %fusion.4.la_ref), custom_call_target="tpu_custom_call" | custom-call | flops 16777216 | bytes 8388608 | tf_op jit(solution)/shard_map/pallas_call | solution.py:106
  39.1 8.4 %all-gather.3 = f32[8,1,4096]{2,1,0:T(1,128)S(1)} all-gather(f32[1,1,4096]{2,1,0:T(1,128)S(1)} %bitcast.81), channel_id=1, replica_groups=mesh['pair'=4,'src'=2,'tgt'=4] {'src','tgt'}, dimensions={0}, use_global_device_ids=true | all-gather | bytes 147456 | tf_op jit(solution)/shard_map/all_gather | solution.py:205
  47.6 5.2 %shard_map.78 = (f32[512,1]{1,0:T(8,128)}, f32[1,4096]{1,0:T(1,128)S(1)}) custom-call(f32[512,4096]{1,0:T(8,128)S(1)} %subtract_multiply_fusion.c_ref, f32[8,4096]{1,0:T(8,128)S(1)} %bitcast.74, f32[1,4096]{1,0:T(1,128)S(1)} %compare_select_fusion.every_ref.lb_ref, f32[512,1]{1,0:T(8,128)S(1)} %fusion.4.la_ref), custom_call_target="tpu_custom_call" | custom-call | flops 33554432 | bytes 8388608 | tf_op jit(solution)/shard_map/pallas_call | solution.py:106
  52.8 9.2 %all-gather.4 = f32[8,1,4096]{2,1,0:T(1,128)S(1)} all-gather(f32[1,1,4096]{2,1,0:T(1,128)S(1)} %bitcast.82), channel_id=1, replica_groups=mesh['pair'=4,'src'=2,'tgt'=4] {'src','tgt'}, dimensions={0}, use_global_device_ids=true | all-gather | bytes 147456 | tf_op jit(solution)/shard_map/all_gather | solution.py:205
  62.1 5.2 %shard_map.79 = (f32[512,1]{1,0:T(8,128)}, f32[1,4096]{1,0:T(1,128)S(1)}) custom-call(f32[512,4096]{1,0:T(8,128)S(1)} %subtract_multiply_fusion.c_ref, f32[8,4096]{1,0:T(8,128)S(1)} %bitcast.75, f32[1,4096]{1,0:T(1,128)S(1)} %compare_select_fusion.every_ref.lb_ref, f32[512,1]{1,0:T(8,128)S(1)} %fusion.4.la_ref), custom_call_target="tpu_custom_call" | custom-call | flops 33554432 | bytes 8388608 | tf_op jit(solution)/shard_map/pallas_call | solution.py:106
  67.3 8.2 %all-gather.5 = f32[8,1,4096]{2,1,0:T(1,128)S(1)} all-gather(f32[1,1,4096]{2,1,0:T(1,128)S(1)} %bitcast.83), channel_id=1, replica_groups=mesh['pair'=4,'src'=2,'tgt'=4] {'src','tgt'}, dimensions={0}, use_global_device_ids=true | all-gather | bytes 147456 | tf_op jit(solution)/shard_map/all_gather | solution.py:205
  75.6 5.2 %shard_map.80 = (f32[512,1]{1,0:T(8,128)}, f32[1,4096]{1,0:T(1,128)S(1)}) custom-call(f32[512,4096]{1,0:T(8,128)S(1)} %subtract_multiply_fusion.c_ref, f32[8,4096]{1,0:T(8,128)S(1)} %bitcast.76, f32[1,4096]{1,0:T(1,128)S(1)} %compare_select_fusion.every_ref.lb_ref, f32[512,1]{1,0:T(8,128)S(1)} %fusion.4.la_ref), custom_call_target="tpu_custom_call" | custom-call | flops 33554432 | bytes 8388608 | tf_op jit(solution)/shard_map/pallas_call | solution.py:106
  80.8 9.2 %all-gather.6 = f32[8,1,4096]{2,1,0:T(1,128)S(1)} all-gather(f32[1,1,4096]{2,1,0:T(1,128)S(1)} %bitcast.84), channel_id=1, replica_groups=mesh['pair'=4,'src'=2,'tgt'=4] {'src','tgt'}, dimensions={0}, use_global_device_ids=true | all-gather | bytes 147456 | tf_op jit(solution)/shard_map/all_gather | solution.py:205
  90.1 5.2 %shard_map.81 = (f32[512,1]{1,0:T(8,128)}, f32[1,4096]{1,0:T(1,128)S(1)}) custom-call(f32[512,4096]{1,0:T(8,128)S(1)} %subtract_multiply_fusion.c_ref, f32[8,4096]{1,0:T(8,128)S(1)} %bitcast.77, f32[1,4096]{1,0:T(1,128)S(1)} %compare_select_fusion.every_ref.lb_ref, f32[512,1]{1,0:T(8,128)S(1)} %fusion.4.la_ref), custom_call_target="tpu_custom_call" | custom-call | flops 33554432 | bytes 8388608 | tf_op jit(solution)/shard_map/pallas_call | solution.py:106
  95.4 8.2 %all-gather.7 = f32[8,1,4096]{2,1,0:T(1,128)S(1)} all-gather(f32[1,1,4096]{2,1,0:T(1,128)S(1)} %bitcast.85), channel_id=1, replica_groups=mesh['pair'=4,'src'=2,'tgt'=4] {'src','tgt'}, dimensions={0}, use_global_device_ids=true | all-gather | bytes 147456 | tf_op jit(solution)/shard_map/all_gather | solution.py:205
  103.7 5.2 %shard_map.82 = (f32[512,1]{1,0:T(8,128)}, f32[1,4096]{1,0:T(1,128)S(1)}) custom-call(f32[512,4096]{1,0:T(8,128)S(1)} %subtract_multiply_fusion.c_ref, f32[8,4096]{1,0:T(8,128)S(1)} %bitcast.78, f32[1,4096]{1,0:T(1,128)S(1)} %compare_select_fusion.every_ref.lb_ref, f32[512,1]{1,0:T(8,128)S(1)} %fusion.4.la_ref), custom_call_target="tpu_custom_call" | custom-call | flops 33554432 | bytes 8388608 | tf_op jit(solution)/shard_map/pallas_call | solution.py:106
  108.9 9.2 %all-gather.8 = f32[8,1,4096]{2,1,0:T(1,128)S(1)} all-gather(f32[1,1,4096]{2,1,0:T(1,128)S(1)} %bitcast.86), channel_id=1, replica_groups=mesh['pair'=4,'src'=2,'tgt'=4] {'src','tgt'}, dimensions={0}, use_global_device_ids=true | all-gather | bytes 147456 | tf_op jit(solution)/shard_map/all_gather | solution.py:205
  118.2 5.2 %shard_map.83 = (f32[512,1]{1,0:T(8,128)}, f32[1,4096]{1,0:T(1,128)S(1)}) custom-call(f32[512,4096]{1,0:T(8,128)S(1)} %subtract_multiply_fusion.c_ref, f32[8,4096]{1,0:T(8,128)S(1)} %bitcast.79, f32[1,4096]{1,0:T(1,128)S(1)} %compare_select_fusion.every_ref.lb_ref, f32[512,1]{1,0:T(8,128)S(1)} %fusion.4.la_ref), custom_call_target="tpu_custom_call" | custom-call | flops 33554432 | bytes 8388608 | tf_op jit(solution)/shard_map/pallas_call | solution.py:106
  123.4 8.4 %all-gather.9 = f32[8,1,4096]{2,1,0:T(1,128)S(1)} all-gather(f32[1,1,4096]{2,1,0:T(1,128)S(1)} %bitcast.87), channel_id=1, replica_groups=mesh['pair'=4,'src'=2,'tgt'=4] {'src','tgt'}, dimensions={0}, use_global_device_ids=true | all-gather | bytes 147456 | tf_op jit(solution)/shard_map/all_gather | solution.py:205
  131.9 5.2 %shard_map.84 = (f32[512,1]{1,0:T(8,128)}, f32[1,4096]{1,0:T(1,128)S(1)}) custom-call(f32[512,4096]{1,0:T(8,128)S(1)} %subtract_multiply_fusion.c_ref, f32[8,4096]{1,0:T(8,128)S(1)} %bitcast.80, f32[1,4096]{1,0:T(1,128)S(1)} %compare_select_fusion.every_ref.lb_ref, f32[512,1]{1,0:T(8,128)S(1)} %fusion.4.la_ref), custom_call_target="tpu_custom_call" | custom-call | flops 33554432 | bytes 8388608 | tf_op jit(solution)/shard_map/pallas_call | solution.py:106
  137.2 9.2 %all-gather.10 = f32[8,1,4096]{2,1,0:T(1,128)S(1)} all-gather(f32[1,1,4096]{2,1,0:T(1,128)S(1)} %bitcast.88), channel_id=1, replica_groups=mesh['pair'=4,'src'=2,'tgt'=4] {'src','tgt'}, dimensions={0}, use_global_device_ids=true | all-gather | bytes 147456 | tf_op jit(solution)/shard_map/all_gather | solution.py:205
  146.4 4.8 %shard_map.85 = (f32[512,1]{1,0:T(8,128)}, bf16[512,4096]{1,0:T(8,128)(2,1)S(1)}, f32[48,512]{1,0:T(8,128)S(1)}, f32[1,512]{1,0:T(1,128)S(1)}) custom-call(f32[512,4096]{1,0:T(8,128)S(1)} %subtract_multiply_fusion.c_ref, f32[8,4096]{1,0:T(8,128)S(1)} %bitcast.73, f32[1,4096]{1,0:T(1,128)S(1)} %compare_select_fusion.every_ref.lb_ref, ...), custom_call_target="tpu_custom_call" | custom-call | flops 25165824 | bytes 12582912 | tf_op jit(solution)/shard_map/pallas_call | solution.py:106
  151.2 1.9 copy-done
  153.2 1.3 collective-permute-start.4
  154.5 5.3 %collective-permute-done.4 = bf16[40,512]{1,0:T(8,128)(2,1)S(1)} collective-permute-done((bf16[40,512]{1,0:T(8,128)(2,1)S(1)}, bf16[40,512]{1,0:T(8,128)(2,1)S(1)}, u32[]{:S(2)}, u32[]{:S(2)}) %collective-permute-start.4) | collective-permute-done | bytes 40992 | tf_op jit(solution)/shard_map/ppermute | solution.py:124
  159.8 8.4 %all_gather.52 = bf16[40,4096]{1,0:T(8,128)(2,1)S(1)} all-gather(bf16[40,512]{1,0:T(8,128)(2,1)S(1)} %collective-permute-done.4), channel_id=1, replica_groups=mesh['pair'=4,'src'=2,'tgt'=4] {'src','tgt'}, dimensions={1}, use_global_device_ids=true | all-gather | bytes 368640 | tf_op jit(solution)/shard_map/all_gather | solution.py:227
  168.3 3.6 %fusion.13 = (bf16[40,512]{1,0:T(8,128)(2,1)S(1)}, f32[40,512]{1,0:T(8,128)S(1)}) fusion(bf16[40,4096]{1,0:T(8,128)(2,1)S(1)} %select_select_fusion, bf16[512,4096]{1,0:T(8,128)(2,1)} %copy-done, pred[512]{0:T(512)(128)(4,1)S(1)} %add_compare_fusion.1), kind=kOutput, calls=%fused_computation.53 | convolution fusion | flops 167813120 | bytes 4645376 | tf_op jit(solution)/shard_map/dot_general | solution.py:220
  171.9 1.3 collective-permute-start.5
  173.2 4.6 %collective-permute-done.5 = bf16[40,512]{1,0:T(8,128)(2,1)S(1)} collective-permute-done((bf16[40,512]{1,0:T(8,128)(2,1)S(1)}, bf16[40,512]{1,0:T(8,128)(2,1)S(1)}, u32[]{:S(2)}, u32[]{:S(2)}) %collective-permute-start.5) | collective-permute-done | bytes 40992 | tf_op jit(solution)/shard_map/ppermute | solution.py:124
  177.8 9.4 %all_gather.53 = bf16[40,4096]{1,0:T(8,128)(2,1)S(1)} all-gather(bf16[40,512]{1,0:T(8,128)(2,1)S(1)} %collective-permute-done.5), channel_id=1, replica_groups=mesh['pair'=4,'src'=2,'tgt'=4] {'src','tgt'}, dimensions={1}, use_global_device_ids=true | all-gather | bytes 368640 | tf_op jit(solution)/shard_map/all_gather | solution.py:227
  187.2 3.6 %fusion.14 = (bf16[40,512]{1,0:T(8,128)(2,1)S(1)}, f32[40,512]{1,0:T(8,128)S(1)}) fusion(bf16[512,4096]{1,0:T(8,128)(2,1)} %copy-done, bf16[40,4096]{1,0:T(8,128)(2,1)S(1)} %all_gather.53, bf16[40,4096]{1,0:T(8,128)(2,1)S(1)} %select_select_fusion, pred[]{:T(512)S(6)} %eq.21, pred[512]{0:T(512)(128)(4,1)S(1)} %add_compare_fusion.1), kind=kOutput, calls=%fused_computation.54 | convolution fusion | flops 167976960 | bytes 4973057 | tf_op jit(solution)/shard_map/dot_general | solution.py:220
  190.8 1.3 collective-permute-start.6
  192.1 5.2 %all-gather.1 = f32[1,2048]{1,0:T(1,128)S(1)} all-gather(f32[1,512]{1,0:T(1,128)S(1)} %get-tuple-element.21), channel_id=3, replica_groups=mesh['pair'=4,'src'=2,'tgt'=4] {'tgt'}, dimensions={1}, use_global_device_ids=true | all-gather | bytes 10240 | tf_op jit(solution)/shard_map/all_gather | solution.py:229
  197.3 8.4 %all_gather.54 = bf16[40,4096]{1,0:T(8,128)(2,1)S(1)} all-gather(bf16[40,512]{1,0:T(8,128)(2,1)S(1)} %collective-permute-done.6), channel_id=1, replica_groups=mesh['pair'=4,'src'=2,'tgt'=4] {'src','tgt'}, dimensions={1}, use_global_device_ids=true | all-gather | bytes 368640 | tf_op jit(solution)/shard_map/all_gather | solution.py:227
  205.7 4.2 %fusion.1 = f32[1,40,512]{2,1,0:T(8,128)} fusion(bf16[512,4096]{1,0:T(8,128)(2,1)} %copy-done, bf16[40,4096]{1,0:T(8,128)(2,1)S(1)} %all_gather.54, pred[]{:T(512)S(6)} %eq.20, bf16[40,4096]{1,0:T(8,128)(2,1)S(1)} %all_gather.53, bf16[40,4096]{1,0:T(8,128)(2,1)S(1)} %select_select_fusion, pred[]{:T(512)S(6)} %eq.21, f32[40,512]{1,0:T(8,128)S(1)} %get-tuple-element.29, ...), kind=kOutput, calls=%fused_computation.7 | convolution fusion | flops 168222720 | bytes 5508608 | tf_op jit(solution)/shard_map/dot_general | solution.py:220
  209.9 0.6 copy.52
  (32 shorter events, 3.0 us)
Async XLA Ops:
  1.6 15.0 %collective-permute-start.1 = (bf16[40,1024]{1,0:T(8,128)(2,1)S(1)}, bf16[40,1024]{1,0:T(8,128)(2,1)S(1)}, u32[]{:S(2)}, u32[]{:S(2)}) collective-permute-start(bf16[40,1024]{1,0:T(8,128)(2,1)S(1)} %convert_element_type.20), channel_id=1, source_target_pairs={{0,1},{1,2},{2,3},{3,0},{4,5},{5,6},{6,7},{7,4},{8,9},{9,10},{10,1... | collective-permute-start | bytes 245768 | tf_op jit(solution)/shard_map/ppermute | solution.py:190
  2.1 14.4 %collective-permute-start.2 = (bf16[40,1024]{1,0:T(8,128)(2,1)S(1)}, bf16[40,1024]{1,0:T(8,128)(2,1)S(1)}, u32[]{:S(2)}, u32[]{:S(2)}) collective-permute-start(bf16[40,1024]{1,0:T(8,128)(2,1)S(1)} %convert_element_type.20), channel_id=1, source_target_pairs={{0,2},{1,3},{2,0},{3,1},{4,6},{5,7},{6,4},{7,5},{8,10},{9,11},{10,... | collective-permute-start | bytes 245768 | tf_op jit(solution)/shard_map/ppermute | solution.py:190
  4.7 11.9 %collective-permute-start.3 = (bf16[40,1024]{1,0:T(8,128)(2,1)S(1)}, bf16[40,1024]{1,0:T(8,128)(2,1)S(1)}, u32[]{:S(2)}, u32[]{:S(2)}) collective-permute-start(bf16[40,1024]{1,0:T(8,128)(2,1)S(1)} %convert_element_type.20), channel_id=1, source_target_pairs={{0,3},{1,0},{2,1},{3,2},{4,7},{5,4},{6,5},{7,6},{8,11},{9,8},{10,9... | collective-permute-start | bytes 245768 | tf_op jit(solution)/shard_map/ppermute | solution.py:190
  7.1 10.3 %collective-permute-start = (f32[30,2048]{1,0:T(8,128)S(1)}, f32[30,2048]{1,0:T(8,128)S(1)}, u32[]{:S(2)}, u32[]{:S(2)}) collective-permute-start(f32[30,2048]{1,0:T(8,128)S(1)} %bitcast.93), channel_id=1, source_target_pairs={{8,0},{16,8},{24,16},{9,1},{17,9},{25,17},{10,2},{18,10},{26,18},{... | collective-permute-start | bytes 737288 | tf_op jit(solution)/shard_map/ppermute | solution.py:124
  151.2 1.9 copy-start
  153.2 6.6 %collective-permute-start.4 = (bf16[40,512]{1,0:T(8,128)(2,1)S(1)}, bf16[40,512]{1,0:T(8,128)(2,1)S(1)}, u32[]{:S(2)}, u32[]{:S(2)}) collective-permute-start(bf16[40,512]{1,0:T(8,128)(2,1)S(1)} %fusion.5), channel_id=1, source_target_pairs={{8,0},{16,8},{24,16},{9,1},{17,9},{25,17},{10,2},{18,10},{26,18},{... | collective-permute-start | bytes 122888 | tf_op jit(solution)/shard_map/ppermute | solution.py:124
  171.9 5.9 %collective-permute-start.5 = (bf16[40,512]{1,0:T(8,128)(2,1)S(1)}, bf16[40,512]{1,0:T(8,128)(2,1)S(1)}, u32[]{:S(2)}, u32[]{:S(2)}) collective-permute-start(bf16[40,512]{1,0:T(8,128)(2,1)S(1)} %get-tuple-element.26), channel_id=1, source_target_pairs={{8,0},{16,8},{24,16},{9,1},{17,9},{25,17},{10,2},{18,10},{26,18},{... | collective-permute-start | bytes 122888 | tf_op jit(solution)/shard_map/ppermute | solution.py:124
  190.8 6.5 %collective-permute-start.6 = (bf16[40,512]{1,0:T(8,128)(2,1)S(1)}, bf16[40,512]{1,0:T(8,128)(2,1)S(1)}, u32[]{:S(2)}, u32[]{:S(2)}) collective-permute-start(bf16[40,512]{1,0:T(8,128)(2,1)S(1)} %get-tuple-element.28), channel_id=1, source_target_pairs={{8,0},{16,8},{24,16},{9,1},{17,9},{25,17},{10,2},{18,10},{26,18},{... | collective-permute-start | bytes 122888 | tf_op jit(solution)/shard_map/ppermute | solution.py:124

commit v13 on v12

--- a/solution.py
+++ b/solution.py
@@ -226,7 +226,16 @@
             passed = shifted(pulled.astype(jnp.bfloat16), "pair", -1)
             fresh = lax.all_gather(passed, ("src", "tgt"), axis=1, tiled=True)
             handed = jnp.where(pair_rank == active - 1, fresh, handed)
-    pot_all = lax.all_gather(pot_lanes.reshape(rows), "tgt", axis=0, tiled=True)
+    pot_row = pot_lanes.reshape(rows)
+    if tgt_count <= 4:
+        got = [pot_row] + [
+            lax.ppermute(pot_row, "tgt", [(i, (i + k) % tgt_count) for i in range(tgt_count)])
+            for k in range(1, tgt_count)
+        ]
+        order = (tgt_rank - jnp.arange(tgt_count, dtype=jnp.int32)) % tgt_count
+        pot_all = jnp.take(jnp.stack(got), order, axis=0).reshape(tgt_count * rows)
+    else:
+        pot_all = lax.all_gather(pot_row, "tgt", axis=0, tiled=True)
     return (fate_maps[None], pot_all[None])
 
 

time: 212 us -> 210 us (level)
  blocking collectives: 111 us -> 106 us
    all_gather x1 -> x0, blocking collectives: 5.19 us -> none  [local(): pot_all = lax.all_gather(pot_lanes.reshape(rows), 'tgt', axis=0, tiled=True)]
  transfers between devices with their start and end apart: 7 -> 10, of which waited for: 2 -> 3; matrix products, arithmetic and copies ran while one was open for 4% -> 6% of each run, Pallas kernels for 0% -> 0%
where the time goes in v13:
time: 210 us; the launch traced here: 209 us
  blocking collectives  106 us (50%)
  Pallas kernels  43.6 us (21%)
  matrix products  18.7 us (9%)
  starting transfers between devices  11.7 us (6%)
  waiting for transfers between devices  11.2 us (5%)
  local copies, waits for them, and re-layouts  8.95 us (4%)
  other arithmetic  6.55 us (3%)
  between operations  2.36 us (1%)
    all_gather x8, blocking collectives, local(): every = lax.all_gather(part_lse[0], ('src', 'tgt'))  70 us
    pallas_call x9, Pallas kernels, sweep(): pl.pallas_call(functools.partial(sweep_kernel, do_row, do_col, emit_w, sh...  43.6 us
    all_gather x3, blocking collectives, local(): fresh = lax.all_gather(passed, ('src', 'tgt'), axis=1, tiled=True)  26.3 us
    dot_general x3, matrix products, local(): lax.dot_general(weights, handed, (((1,), (1,)), ((), ())), preferred_elem...  11.3 us
    ppermute x4, waiting for transfers between devices, shifted(): return lax.ppermute(shard, axis, pairs)  11.2 us
    all_gather x1, blocking collectives, local(): pieces = lax.all_gather(piece, ('src', 'tgt'))  9.83 us
    dot_general x1, matrix products, local(): lax.dot_general(source_pos, target_pos, (((0,), (0,)), ((), ())), precisi...  7.41 us
    ppermute x4, starting transfers between devices, shifted(): return lax.ppermute(shard, axis, pairs)  5.17 us
  transfers between devices with their start and end apart: 10, of which 3 were waited for; matrix products, arithmetic and copies ran while one was open for 6% of the time, Pallas kernels for 0%

profile of v13, /device:TPU:0, one launch (start us, length us, event | category | flops | bytes accessed | tf_op | source)
XLA Modules:
  0.0 209.2 jit_solution(5876916833905135001)
XLA Ops:
  0.6 0.9 convert_element_type.20
  2.1 2.6 %collective-permute-start.2 = (bf16[40,1024]{1,0:T(8,128)(2,1)S(1)}, bf16[40,1024]{1,0:T(8,128)(2,1)S(1)}, u32[]{:S(2)}, u32[]{:S(2)}) collective-permute-start(bf16[40,1024]{1,0:T(8,128)(2,1)S(1)} %convert_element_type.20), channel_id=1, source_target_pairs={{0,2},{1,3},{2,0},{3,1},{4,6},{5,7},{6,4},{7,5},{8,10},{9,11},{10,... | collective-permute-start | bytes 245768 | tf_op jit(solution)/shard_map/ppermute | solution.py:190
  4.7 1.4 collective-permute-start.3
  6.1 1.0 copy.43
  7.1 1.3 collective-permute-start
  8.4 0.9 convert_bitcast_fusion
  9.4 0.7 pad_clamp_fusion.1
  10.1 0.8 constant_dynamic-slice_fusion
  10.9 1.3 fusion.12
  12.9 0.7 subtract_bitcast_fusion
  14.5 0.7 compare_select_fusion.every_ref.lb_ref
  15.2 0.7 fusion.4.la_ref
  15.9 0.7 add_compare_fusion.1
  17.4 0.9 select_bitcast_fusion.2
  18.2 9.8 %all-gather.1 = f32[8,30,512]{2,1,0:T(8,128)S(1)} all-gather(f32[1,30,512]{2,1,0:T(8,128)S(1)} %select_bitcast_fusion.2), channel_id=2, replica_groups=mesh['pair'=4,'src'=2,'tgt'=4] {'src','tgt'}, dimensions={0}, use_global_device_ids=true | all-gather | bytes 552960 | tf_op jit(solution)/shard_map/all_gather | solution.py:148
  29.5 7.4 %subtract_multiply_fusion.c_ref = f32[512,4096]{1,0:T(8,128)S(1)} fusion(f32[30,4096]{1,0:T(8,128)S(1)} %bitcast.102, f32[4096]{0:T(1024)S(1)} %bitcast.105, f32[512]{0:T(512)S(1)} %fusion.7, f32[1,30,512]{2,0,1:T(1,128)S(1)} %constant_dynamic-slice_fusion), kind=kOutput, calls=%fused_computation.3 | convolution fusion | flops 763363328 | bytes 8960000 | tf_op jit(solution)/shard_map/dot_general | solution.py:163
  36.9 2.2 %shard_map.77 = f32[1,4096]{1,0:T(1,128)S(1)} custom-call(f32[512,4096]{1,0:T(8,128)S(1)} %subtract_multiply_fusion.c_ref, f32[1,4096]{1,0:T(1,128)S(1)} %compare_select_fusion.every_ref.lb_ref, f32[1,4096]{1,0:T(1,128)S(1)} %compare_select_fusion.every_ref.lb_ref, f32[512,1]{1,0:T(8,128)S(1)} %fusion.4.la_ref), custom_call_target="tpu_custom_call" | custom-call | flops 16777216 | bytes 8388608 | tf_op jit(solution)/shard_map/pallas_call | solution.py:106
  39.1 8.4 %all-gather.2 = f32[8,1,4096]{2,1,0:T(1,128)S(1)} all-gather(f32[1,1,4096]{2,1,0:T(1,128)S(1)} %bitcast.89), channel_id=1, replica_groups=mesh['pair'=4,'src'=2,'tgt'=4] {'src','tgt'}, dimensions={0}, use_global_device_ids=true | all-gather | bytes 147456 | tf_op jit(solution)/shard_map/all_gather | solution.py:205
  47.6 5.2 %shard_map.78 = (f32[512,1]{1,0:T(8,128)}, f32[1,4096]{1,0:T(1,128)S(1)}) custom-call(f32[512,4096]{1,0:T(8,128)S(1)} %subtract_multiply_fusion.c_ref, f32[8,4096]{1,0:T(8,128)S(1)} %bitcast.82, f32[1,4096]{1,0:T(1,128)S(1)} %compare_select_fusion.every_ref.lb_ref, f32[512,1]{1,0:T(8,128)S(1)} %fusion.4.la_ref), custom_call_target="tpu_custom_call" | custom-call | flops 33554432 | bytes 8388608 | tf_op jit(solution)/shard_map/pallas_call | solution.py:106
  52.8 9.2 %all-gather.3 = f32[8,1,4096]{2,1,0:T(1,128)S(1)} all-gather(f32[1,1,4096]{2,1,0:T(1,128)S(1)} %bitcast.90), channel_id=1, replica_groups=mesh['pair'=4,'src'=2,'tgt'=4] {'src','tgt'}, dimensions={0}, use_global_device_ids=true | all-gather | bytes 147456 | tf_op jit(solution)/shard_map/all_gather | solution.py:205
  62.0 5.2 %shard_map.79 = (f32[512,1]{1,0:T(8,128)}, f32[1,4096]{1,0:T(1,128)S(1)}) custom-call(f32[512,4096]{1,0:T(8,128)S(1)} %subtract_multiply_fusion.c_ref, f32[8,4096]{1,0:T(8,128)S(1)} %bitcast.83, f32[1,4096]{1,0:T(1,128)S(1)} %compare_select_fusion.every_ref.lb_ref, f32[512,1]{1,0:T(8,128)S(1)} %fusion.4.la_ref), custom_call_target="tpu_custom_call" | custom-call | flops 33554432 | bytes 8388608 | tf_op jit(solution)/shard_map/pallas_call | solution.py:106
  67.3 8.2 %all-gather.4 = f32[8,1,4096]{2,1,0:T(1,128)S(1)} all-gather(f32[1,1,4096]{2,1,0:T(1,128)S(1)} %bitcast.91), channel_id=1, replica_groups=mesh['pair'=4,'src'=2,'tgt'=4] {'src','tgt'}, dimensions={0}, use_global_device_ids=true | all-gather | bytes 147456 | tf_op jit(solution)/shard_map/all_gather | solution.py:205
  75.6 5.2 %shard_map.80 = (f32[512,1]{1,0:T(8,128)}, f32[1,4096]{1,0:T(1,128)S(1)}) custom-call(f32[512,4096]{1,0:T(8,128)S(1)} %subtract_multiply_fusion.c_ref, f32[8,4096]{1,0:T(8,128)S(1)} %bitcast.84, f32[1,4096]{1,0:T(1,128)S(1)} %compare_select_fusion.every_ref.lb_ref, f32[512,1]{1,0:T(8,128)S(1)} %fusion.4.la_ref), custom_call_target="tpu_custom_call" | custom-call | flops 33554432 | bytes 8388608 | tf_op jit(solution)/shard_map/pallas_call | solution.py:106
  80.8 9.2 %all-gather.5 = f32[8,1,4096]{2,1,0:T(1,128)S(1)} all-gather(f32[1,1,4096]{2,1,0:T(1,128)S(1)} %bitcast.92), channel_id=1, replica_groups=mesh['pair'=4,'src'=2,'tgt'=4] {'src','tgt'}, dimensions={0}, use_global_device_ids=true | all-gather | bytes 147456 | tf_op jit(solution)/shard_map/all_gather | solution.py:205
  90.1 5.2 %shard_map.81 = (f32[512,1]{1,0:T(8,128)}, f32[1,4096]{1,0:T(1,128)S(1)}) custom-call(f32[512,4096]{1,0:T(8,128)S(1)} %subtract_multiply_fusion.c_ref, f32[8,4096]{1,0:T(8,128)S(1)} %bitcast.85, f32[1,4096]{1,0:T(1,128)S(1)} %compare_select_fusion.every_ref.lb_ref, f32[512,1]{1,0:T(8,128)S(1)} %fusion.4.la_ref), custom_call_target="tpu_custom_call" | custom-call | flops 33554432 | bytes 8388608 | tf_op jit(solution)/shard_map/pallas_call | solution.py:106
  95.3 8.2 %all-gather.6 = f32[8,1,4096]{2,1,0:T(1,128)S(1)} all-gather(f32[1,1,4096]{2,1,0:T(1,128)S(1)} %bitcast.93), channel_id=1, replica_groups=mesh['pair'=4,'src'=2,'tgt'=4] {'src','tgt'}, dimensions={0}, use_global_device_ids=true | all-gather | bytes 147456 | tf_op jit(solution)/shard_map/all_gather | solution.py:205
  103.6 5.2 %shard_map.82 = (f32[512,1]{1,0:T(8,128)}, f32[1,4096]{1,0:T(1,128)S(1)}) custom-call(f32[512,4096]{1,0:T(8,128)S(1)} %subtract_multiply_fusion.c_ref, f32[8,4096]{1,0:T(8,128)S(1)} %bitcast.86, f32[1,4096]{1,0:T(1,128)S(1)} %compare_select_fusion.every_ref.lb_ref, f32[512,1]{1,0:T(8,128)S(1)} %fusion.4.la_ref), custom_call_target="tpu_custom_call" | custom-call | flops 33554432 | bytes 8388608 | tf_op jit(solution)/shard_map/pallas_call | solution.py:106
  108.8 9.2 %all-gather.7 = f32[8,1,4096]{2,1,0:T(1,128)S(1)} all-gather(f32[1,1,4096]{2,1,0:T(1,128)S(1)} %bitcast.94), channel_id=1, replica_groups=mesh['pair'=4,'src'=2,'tgt'=4] {'src','tgt'}, dimensions={0}, use_global_device_ids=true | all-gather | bytes 147456 | tf_op jit(solution)/shard_map/all_gather | solution.py:205
  118.1 5.2 %shard_map.83 = (f32[512,1]{1,0:T(8,128)}, f32[1,4096]{1,0:T(1,128)S(1)}) custom-call(f32[512,4096]{1,0:T(8,128)S(1)} %subtract_multiply_fusion.c_ref, f32[8,4096]{1,0:T(8,128)S(1)} %bitcast.87, f32[1,4096]{1,0:T(1,128)S(1)} %compare_select_fusion.every_ref.lb_ref, f32[512,1]{1,0:T(8,128)S(1)} %fusion.4.la_ref), custom_call_target="tpu_custom_call" | custom-call | flops 33554432 | bytes 8388608 | tf_op jit(solution)/shard_map/pallas_call | solution.py:106
  123.3 8.4 %all-gather.8 = f32[8,1,4096]{2,1,0:T(1,128)S(1)} all-gather(f32[1,1,4096]{2,1,0:T(1,128)S(1)} %bitcast.95), channel_id=1, replica_groups=mesh['pair'=4,'src'=2,'tgt'=4] {'src','tgt'}, dimensions={0}, use_global_device_ids=true | all-gather | bytes 147456 | tf_op jit(solution)/shard_map/all_gather | solution.py:205
  131.8 5.2 %shard_map.84 = (f32[512,1]{1,0:T(8,128)}, f32[1,4096]{1,0:T(1,128)S(1)}) custom-call(f32[512,4096]{1,0:T(8,128)S(1)} %subtract_multiply_fusion.c_ref, f32[8,4096]{1,0:T(8,128)S(1)} %bitcast.88, f32[1,4096]{1,0:T(1,128)S(1)} %compare_select_fusion.every_ref.lb_ref, f32[512,1]{1,0:T(8,128)S(1)} %fusion.4.la_ref), custom_call_target="tpu_custom_call" | custom-call | flops 33554432 | bytes 8388608 | tf_op jit(solution)/shard_map/pallas_call | solution.py:106
  137.1 9.2 %all-gather.9 = f32[8,1,4096]{2,1,0:T(1,128)S(1)} all-gather(f32[1,1,4096]{2,1,0:T(1,128)S(1)} %bitcast.96), channel_id=1, replica_groups=mesh['pair'=4,'src'=2,'tgt'=4] {'src','tgt'}, dimensions={0}, use_global_device_ids=true | all-gather | bytes 147456 | tf_op jit(solution)/shard_map/all_gather | solution.py:205
  146.3 4.8 %shard_map.85 = (f32[512,1]{1,0:T(8,128)}, bf16[512,4096]{1,0:T(8,128)(2,1)S(1)}, f32[48,512]{1,0:T(8,128)S(1)}, f32[1,512]{1,0:T(1,128)S(1)}) custom-call(f32[512,4096]{1,0:T(8,128)S(1)} %subtract_multiply_fusion.c_ref, f32[8,4096]{1,0:T(8,128)S(1)} %bitcast.81, f32[1,4096]{1,0:T(1,128)S(1)} %compare_select_fusion.every_ref.lb_ref, ...), custom_call_target="tpu_custom_call" | custom-call | flops 25165824 | bytes 12582912 | tf_op jit(solution)/shard_map/pallas_call | solution.py:106
  151.1 2.0 copy-done
  153.1 1.3 collective-permute-start.4
  155.3 1.1 collective-permute-start.9
  156.5 3.3 %collective-permute-done.4 = bf16[40,512]{1,0:T(8,128)(2,1)S(1)} collective-permute-done((bf16[40,512]{1,0:T(8,128)(2,1)S(1)}, bf16[40,512]{1,0:T(8,128)(2,1)S(1)}, u32[]{:S(2)}, u32[]{:S(2)}) %collective-permute-start.4) | collective-permute-done | bytes 40992 | tf_op jit(solution)/shard_map/ppermute | solution.py:124
  159.7 8.4 %all_gather.49 = bf16[40,4096]{1,0:T(8,128)(2,1)S(1)} all-gather(bf16[40,512]{1,0:T(8,128)(2,1)S(1)} %collective-permute-done.4), channel_id=1, replica_groups=mesh['pair'=4,'src'=2,'tgt'=4] {'src','tgt'}, dimensions={1}, use_global_device_ids=true | all-gather | bytes 368640 | tf_op jit(solution)/shard_map/all_gather | solution.py:227
  168.2 3.6 %fusion.13 = (bf16[40,512]{1,0:T(8,128)(2,1)S(1)}, f32[40,512]{1,0:T(8,128)S(1)}) fusion(bf16[40,4096]{1,0:T(8,128)(2,1)S(1)} %select_select_fusion, bf16[512,4096]{1,0:T(8,128)(2,1)} %copy-done, pred[512]{0:T(512)(128)(4,1)S(1)} %add_compare_fusion.1), kind=kOutput, calls=%fused_computation.56 | convolution fusion | flops 167813120 | bytes 4645376 | tf_op jit(solution)/shard_map/dot_general | solution.py:220
  171.8 1.3 collective-permute-start.5
  173.7 4.0 %collective-permute-done.5 = bf16[40,512]{1,0:T(8,128)(2,1)S(1)} collective-permute-done((bf16[40,512]{1,0:T(8,128)(2,1)S(1)}, bf16[40,512]{1,0:T(8,128)(2,1)S(1)}, u32[]{:S(2)}, u32[]{:S(2)}) %collective-permute-start.5) | collective-permute-done | bytes 40992 | tf_op jit(solution)/shard_map/ppermute | solution.py:124
  177.7 9.4 %all_gather.50 = bf16[40,4096]{1,0:T(8,128)(2,1)S(1)} all-gather(bf16[40,512]{1,0:T(8,128)(2,1)S(1)} %collective-permute-done.5), channel_id=1, replica_groups=mesh['pair'=4,'src'=2,'tgt'=4] {'src','tgt'}, dimensions={1}, use_global_device_ids=true | all-gather | bytes 368640 | tf_op jit(solution)/shard_map/all_gather | solution.py:227
  187.1 3.6 %fusion.14 = (bf16[40,512]{1,0:T(8,128)(2,1)S(1)}, f32[40,512]{1,0:T(8,128)S(1)}) fusion(bf16[512,4096]{1,0:T(8,128)(2,1)} %copy-done, bf16[40,4096]{1,0:T(8,128)(2,1)S(1)} %all_gather.50, bf16[40,4096]{1,0:T(8,128)(2,1)S(1)} %select_select_fusion, pred[]{:T(512)S(6)} %eq.22, pred[512]{0:T(512)(128)(4,1)S(1)} %add_compare_fusion.1), kind=kOutput, calls=%fused_computation.57 | convolution fusion | flops 167976960 | bytes 4973057 | tf_op jit(solution)/shard_map/dot_general | solution.py:220
  190.6 1.3 collective-permute-start.6
  192.0 0.6 copy.28
  192.6 3.9 %collective-permute-done.6 = bf16[40,512]{1,0:T(8,128)(2,1)S(1)} collective-permute-done((bf16[40,512]{1,0:T(8,128)(2,1)S(1)}, bf16[40,512]{1,0:T(8,128)(2,1)S(1)}, u32[]{:S(2)}, u32[]{:S(2)}) %collective-permute-start.6) | collective-permute-done | bytes 40992 | tf_op jit(solution)/shard_map/ppermute | solution.py:124
  196.5 8.4 %all_gather.51 = bf16[40,4096]{1,0:T(8,128)(2,1)S(1)} all-gather(bf16[40,512]{1,0:T(8,128)(2,1)S(1)} %collective-permute-done.6), channel_id=1, replica_groups=mesh['pair'=4,'src'=2,'tgt'=4] {'src','tgt'}, dimensions={1}, use_global_device_ids=true | all-gather | bytes 368640 | tf_op jit(solution)/shard_map/all_gather | solution.py:227
  205.0 4.2 %fusion.1 = f32[1,40,512]{2,1,0:T(8,128)} fusion(bf16[512,4096]{1,0:T(8,128)(2,1)} %copy-done, bf16[40,4096]{1,0:T(8,128)(2,1)S(1)} %all_gather.51, pred[]{:T(512)S(6)} %eq.21, bf16[40,4096]{1,0:T(8,128)(2,1)S(1)} %all_gather.50, bf16[40,4096]{1,0:T(8,128)(2,1)S(1)} %select_select_fusion, pred[]{:T(512)S(6)} %eq.22, f32[40,512]{1,0:T(8,128)S(1)} %get-tuple-element.29, ...), kind=kOutput, calls=%fused_computation.8 | convolution fusion | flops 168222720 | bytes 5508608 | tf_op jit(solution)/shard_map/dot_general | solution.py:220
  (40 shorter events, 5.2 us)
Async XLA Ops:
  1.6 15.0 %collective-permute-start.1 = (bf16[40,1024]{1,0:T(8,128)(2,1)S(1)}, bf16[40,1024]{1,0:T(8,128)(2,1)S(1)}, u32[]{:S(2)}, u32[]{:S(2)}) collective-permute-start(bf16[40,1024]{1,0:T(8,128)(2,1)S(1)} %convert_element_type.20), channel_id=1, source_target_pairs={{0,1},{1,2},{2,3},{3,0},{4,5},{5,6},{6,7},{7,4},{8,9},{9,10},{10,1... | collective-permute-start | bytes 245768 | tf_op jit(solution)/shard_map/ppermute | solution.py:190
  2.1 14.4 %collective-permute-start.2 = (bf16[40,1024]{1,0:T(8,128)(2,1)S(1)}, bf16[40,1024]{1,0:T(8,128)(2,1)S(1)}, u32[]{:S(2)}, u32[]{:S(2)}) collective-permute-start(bf16[40,1024]{1,0:T(8,128)(2,1)S(1)} %convert_element_type.20), channel_id=1, source_target_pairs={{0,2},{1,3},{2,0},{3,1},{4,6},{5,7},{6,4},{7,5},{8,10},{9,11},{10,... | collective-permute-start | bytes 245768 | tf_op jit(solution)/shard_map/ppermute | solution.py:190
  4.7 11.9 %collective-permute-start.3 = (bf16[40,1024]{1,0:T(8,128)(2,1)S(1)}, bf16[40,1024]{1,0:T(8,128)(2,1)S(1)}, u32[]{:S(2)}, u32[]{:S(2)}) collective-permute-start(bf16[40,1024]{1,0:T(8,128)(2,1)S(1)} %convert_element_type.20), channel_id=1, source_target_pairs={{0,3},{1,0},{2,1},{3,2},{4,7},{5,4},{6,5},{7,6},{8,11},{9,8},{10,9... | collective-permute-start | bytes 245768 | tf_op jit(solution)/shard_map/ppermute | solution.py:190
  7.1 10.3 %collective-permute-start = (f32[30,2048]{1,0:T(8,128)S(1)}, f32[30,2048]{1,0:T(8,128)S(1)}, u32[]{:S(2)}, u32[]{:S(2)}) collective-permute-start(f32[30,2048]{1,0:T(8,128)S(1)} %bitcast.104), channel_id=1, source_target_pairs={{8,0},{16,8},{24,16},{9,1},{17,9},{25,17},{10,2},{18,10},{26,18},{... | collective-permute-start | bytes 737288 | tf_op jit(solution)/shard_map/ppermute | solution.py:124
  151.1 2.0 copy-start
  153.1 6.6 %collective-permute-start.4 = (bf16[40,512]{1,0:T(8,128)(2,1)S(1)}, bf16[40,512]{1,0:T(8,128)(2,1)S(1)}, u32[]{:S(2)}, u32[]{:S(2)}) collective-permute-start(bf16[40,512]{1,0:T(8,128)(2,1)S(1)} %fusion.5), channel_id=1, source_target_pairs={{8,0},{16,8},{24,16},{9,1},{17,9},{25,17},{10,2},{18,10},{26,18},{... | collective-permute-start | bytes 122888 | tf_op jit(solution)/shard_map/ppermute | solution.py:124
  154.4 18.7 %collective-permute-start.7 = (f32[512]{0:T(512)S(1)}, f32[512]{0:T(512)S(1)}, u32[]{:S(2)}, u32[]{:S(2)}) collective-permute-start(f32[512]{0:T(512)S(1)} %bitcast.97), channel_id=1, source_target_pairs={{0,1},{1,2},{2,3},{3,0},{4,5},{5,6},{6,7},{7,4},{8,9},{9,10},{10,1... | collective-permute-start | bytes 6152 | tf_op jit(solution)/shard_map/ppermute | solution.py:232
  154.8 18.3 %collective-permute-start.8 = (f32[512]{0:T(512)S(1)}, f32[512]{0:T(512)S(1)}, u32[]{:S(2)}, u32[]{:S(2)}) collective-permute-start(f32[512]{0:T(512)S(1)} %bitcast.98), channel_id=1, source_target_pairs={{0,2},{1,3},{2,0},{3,1},{4,6},{5,7},{6,4},{7,5},{8,10},{9,11},{10,... | collective-permute-start | bytes 6152 | tf_op jit(solution)/shard_map/ppermute | solution.py:232
  155.3 17.8 %collective-permute-start.9 = (f32[512]{0:T(512)S(1)}, f32[512]{0:T(512)S(1)}, u32[]{:S(2)}, u32[]{:S(2)}) collective-permute-start(f32[512]{0:T(512)S(1)} %bitcast.99), channel_id=1, source_target_pairs={{0,3},{1,0},{2,1},{3,2},{4,7},{5,4},{6,5},{7,6},{8,11},{9,8},{10,9... | collective-permute-start | bytes 6152 | tf_op jit(solution)/shard_map/ppermute | solution.py:232
  171.8 5.9 %collective-permute-start.5 = (bf16[40,512]{1,0:T(8,128)(2,1)S(1)}, bf16[40,512]{1,0:T(8,128)(2,1)S(1)}, u32[]{:S(2)}, u32[]{:S(2)}) collective-permute-start(bf16[40,512]{1,0:T(8,128)(2,1)S(1)} %get-tuple-element.26), channel_id=1, source_target_pairs={{8,0},{16,8},{24,16},{9,1},{17,9},{25,17},{10,2},{18,10},{26,18},{... | collective-permute-start | bytes 122888 | tf_op jit(solution)/shard_map/ppermute | solution.py:124
  190.6 5.9 %collective-permute-start.6 = (bf16[40,512]{1,0:T(8,128)(2,1)S(1)}, bf16[40,512]{1,0:T(8,128)(2,1)S(1)}, u32[]{:S(2)}, u32[]{:S(2)}) collective-permute-start(bf16[40,512]{1,0:T(8,128)(2,1)S(1)} %get-tuple-element.28), channel_id=1, source_target_pairs={{8,0},{16,8},{24,16},{9,1},{17,9},{25,17},{10,2},{18,10},{26,18},{... | collective-permute-start | bytes 122888 | tf_op jit(solution)/shard_map/ppermute | solution.py:124

commit v14 on v13

--- a/solution.py
+++ b/solution.py
@@ -140,8 +140,7 @@
     source_pos = lax.dynamic_slice_in_dim(source_all, row_off, rows, 1)
     group = lax.axis_size("src") * tgt_count
     src_count = lax.axis_size("src")
-    arrived = shifted(source_all, "pair", -1)
-    mine_next = lax.dynamic_slice_in_dim(arrived, row_off, rows, 1)
+    mine_next = shifted(source_pos, "pair", -1)
     fin_width = final_cells.shape[1]
     mine_final = lax.dynamic_slice_in_dim(final_cells, (src_rank * rows) % fin_width, rows, 1)
     piece = jnp.where(is_last, mine_final, mine_next)

time: 210 us -> 212 us (level)
    unnamed x15 -> x21, local copies, waits for them, and re-layouts: 4.59 us -> 6.95 us
  transfers between devices with their start and end apart: 10 -> 10, of which waited for: 3 -> 3; matrix products, arithmetic and copies ran while one was open for 6% -> 10% of each run, Pallas kernels for 0% -> 18%
where the time goes in v14:
time: 212 us; the launch traced here: 211 us
  blocking collectives  106 us (50%)
  Pallas kernels  43.7 us (21%)
  matrix products  18.8 us (9%)
  starting transfers between devices  11.7 us (6%)
  waiting for transfers between devices  11.2 us (5%)
  local copies, waits for them, and re-layouts  10.5 us (5%)
  other arithmetic  6.59 us (3%)
  between operations  2.4 us (1%)
    all_gather x8, blocking collectives, local(): every = lax.all_gather(part_lse[0], ('src', 'tgt'))  70 us
    pallas_call x9, Pallas kernels, sweep(): pl.pallas_call(functools.partial(sweep_kernel, do_row, do_col, emit_w, sh...  43.7 us
    all_gather x3, blocking collectives, local(): fresh = lax.all_gather(passed, ('src', 'tgt'), axis=1, tiled=True)  26.3 us
    dot_general x3, matrix products, local(): lax.dot_general(weights, handed, (((1,), (1,)), ((), ())), preferred_elem...  11.3 us
    ppermute x4, waiting for transfers between devices, shifted(): return lax.ppermute(shard, axis, pairs)  11.2 us
    all_gather x1, blocking collectives, local(): pieces = lax.all_gather(piece, ('src', 'tgt'))  9.83 us
    dot_general x1, matrix products, local(): lax.dot_general(source_pos, target_pos, (((0,), (0,)), ((), ())), precisi...  7.41 us
    unnamed x21, local copies, waits for them, and re-layouts  6.95 us
  transfers between devices with their start and end apart: 10, of which 3 were waited for; matrix products, arithmetic and copies ran while one was open for 10% of the time, Pallas kernels for 18%

profile of v14, /device:TPU:0, one launch (start us, length us, event | category | flops | bytes accessed | tf_op | source)
XLA Modules:
  0.0 211.0 jit_solution(9635095751833099383)
XLA Ops:
  0.6 1.0 convert_element_type.20
  2.2 2.6 %collective-permute-start.2 = (bf16[40,1024]{1,0:T(8,128)(2,1)S(1)}, bf16[40,1024]{1,0:T(8,128)(2,1)S(1)}, u32[]{:S(2)}, u32[]{:S(2)}) collective-permute-start(bf16[40,1024]{1,0:T(8,128)(2,1)S(1)} %convert_element_type.20), channel_id=1, source_target_pairs={{0,2},{1,3},{2,0},{3,1},{4,6},{5,7},{6,4},{7,5},{8,10},{9,11},{10,... | collective-permute-start | bytes 245768 | tf_op jit(solution)/shard_map/ppermute | solution.py:189
  4.7 1.4 collective-permute-start.3
  6.2 1.3 collective-permute-start
  7.5 0.9 convert_bitcast_fusion
  8.5 0.7 pad_clamp_fusion.1
  9.1 1.3 fusion.9
  11.2 0.7 subtract_bitcast_fusion
  12.7 0.7 compare_select_fusion.every_ref.lb_ref
  13.4 0.7 fusion.4.la_ref
  14.1 0.7 add_compare_fusion.1
  14.8 0.9 select_bitcast_fusion.2
  15.6 9.8 %all-gather.1 = f32[8,30,512]{2,1,0:T(8,128)S(1)} all-gather(f32[1,30,512]{2,1,0:T(8,128)S(1)} %select_bitcast_fusion.2), channel_id=2, replica_groups=mesh['pair'=4,'src'=2,'tgt'=4] {'src','tgt'}, dimensions={0}, use_global_device_ids=true | all-gather | bytes 552960 | tf_op jit(solution)/shard_map/all_gather | solution.py:147
  25.5 0.6 gather_fusion
  26.9 7.4 %subtract_multiply_fusion.c_ref = f32[512,4096]{1,0:T(8,128)S(1)} fusion(f32[30,4096]{1,0:T(8,128)S(1)} %bitcast.99, f32[4096]{0:T(1024)S(1)} %bitcast.101, f32[512]{0:T(512)S(1)} %multiply_reduce_fusion.1, f32[1,30,512]{2,0,1:T(1,128)S(1)} %constant_dynamic-slice_fusion), kind=kOutput, calls=%fused_computation.3 | convolution fusion | flops 763363328 | bytes 8960000 | tf_op jit(solution)/shard_map/dot_general | solution.py:162
  34.3 2.2 %shard_map.77 = f32[1,4096]{1,0:T(1,128)S(1)} custom-call(f32[512,4096]{1,0:T(8,128)S(1)} %subtract_multiply_fusion.c_ref, f32[1,4096]{1,0:T(1,128)S(1)} %compare_select_fusion.every_ref.lb_ref, f32[1,4096]{1,0:T(1,128)S(1)} %compare_select_fusion.every_ref.lb_ref, f32[512,1]{1,0:T(8,128)S(1)} %fusion.4.la_ref), custom_call_target="tpu_custom_call" | custom-call | flops 16777216 | bytes 8388608 | tf_op jit(solution)/shard_map/pallas_call | solution.py:106
  36.5 8.2 %all-gather.2 = f32[8,1,4096]{2,1,0:T(1,128)S(1)} all-gather(f32[1,1,4096]{2,1,0:T(1,128)S(1)} %bitcast.86), channel_id=1, replica_groups=mesh['pair'=4,'src'=2,'tgt'=4] {'src','tgt'}, dimensions={0}, use_global_device_ids=true | all-gather | bytes 147456 | tf_op jit(solution)/shard_map/all_gather | solution.py:204
  44.8 5.3 %shard_map.78 = (f32[512,1]{1,0:T(8,128)}, f32[1,4096]{1,0:T(1,128)S(1)}) custom-call(f32[512,4096]{1,0:T(8,128)S(1)} %subtract_multiply_fusion.c_ref, f32[8,4096]{1,0:T(8,128)S(1)} %bitcast.79, f32[1,4096]{1,0:T(1,128)S(1)} %compare_select_fusion.every_ref.lb_ref, f32[512,1]{1,0:T(8,128)S(1)} %fusion.4.la_ref), custom_call_target="tpu_custom_call" | custom-call | flops 33554432 | bytes 8388608 | tf_op jit(solution)/shard_map/pallas_call | solution.py:106
  50.0 9.4 %all-gather.3 = f32[8,1,4096]{2,1,0:T(1,128)S(1)} all-gather(f32[1,1,4096]{2,1,0:T(1,128)S(1)} %bitcast.87), channel_id=1, replica_groups=mesh['pair'=4,'src'=2,'tgt'=4] {'src','tgt'}, dimensions={0}, use_global_device_ids=true | all-gather | bytes 147456 | tf_op jit(solution)/shard_map/all_gather | solution.py:204
  59.5 5.3 %shard_map.79 = (f32[512,1]{1,0:T(8,128)}, f32[1,4096]{1,0:T(1,128)S(1)}) custom-call(f32[512,4096]{1,0:T(8,128)S(1)} %subtract_multiply_fusion.c_ref, f32[8,4096]{1,0:T(8,128)S(1)} %bitcast.80, f32[1,4096]{1,0:T(1,128)S(1)} %compare_select_fusion.every_ref.lb_ref, f32[512,1]{1,0:T(8,128)S(1)} %fusion.4.la_ref), custom_call_target="tpu_custom_call" | custom-call | flops 33554432 | bytes 8388608 | tf_op jit(solution)/shard_map/pallas_call | solution.py:106
  64.7 8.2 %all-gather.4 = f32[8,1,4096]{2,1,0:T(1,128)S(1)} all-gather(f32[1,1,4096]{2,1,0:T(1,128)S(1)} %bitcast.88), channel_id=1, replica_groups=mesh['pair'=4,'src'=2,'tgt'=4] {'src','tgt'}, dimensions={0}, use_global_device_ids=true | all-gather | bytes 147456 | tf_op jit(solution)/shard_map/all_gather | solution.py:204
  73.0 5.3 %shard_map.80 = (f32[512,1]{1,0:T(8,128)}, f32[1,4096]{1,0:T(1,128)S(1)}) custom-call(f32[512,4096]{1,0:T(8,128)S(1)} %subtract_multiply_fusion.c_ref, f32[8,4096]{1,0:T(8,128)S(1)} %bitcast.81, f32[1,4096]{1,0:T(1,128)S(1)} %compare_select_fusion.every_ref.lb_ref, f32[512,1]{1,0:T(8,128)S(1)} %fusion.4.la_ref), custom_call_target="tpu_custom_call" | custom-call | flops 33554432 | bytes 8388608 | tf_op jit(solution)/shard_map/pallas_call | solution.py:106
  78.3 9.2 %all-gather.5 = f32[8,1,4096]{2,1,0:T(1,128)S(1)} all-gather(f32[1,1,4096]{2,1,0:T(1,128)S(1)} %bitcast.89), channel_id=1, replica_groups=mesh['pair'=4,'src'=2,'tgt'=4] {'src','tgt'}, dimensions={0}, use_global_device_ids=true | all-gather | bytes 147456 | tf_op jit(solution)/shard_map/all_gather | solution.py:204
  87.5 5.3 %shard_map.81 = (f32[512,1]{1,0:T(8,128)}, f32[1,4096]{1,0:T(1,128)S(1)}) custom-call(f32[512,4096]{1,0:T(8,128)S(1)} %subtract_multiply_fusion.c_ref, f32[8,4096]{1,0:T(8,128)S(1)} %bitcast.82, f32[1,4096]{1,0:T(1,128)S(1)} %compare_select_fusion.every_ref.lb_ref, f32[512,1]{1,0:T(8,128)S(1)} %fusion.4.la_ref), custom_call_target="tpu_custom_call" | custom-call | flops 33554432 | bytes 8388608 | tf_op jit(solution)/shard_map/pallas_call | solution.py:106
  92.8 8.2 %all-gather.6 = f32[8,1,4096]{2,1,0:T(1,128)S(1)} all-gather(f32[1,1,4096]{2,1,0:T(1,128)S(1)} %bitcast.90), channel_id=1, replica_groups=mesh['pair'=4,'src'=2,'tgt'=4] {'src','tgt'}, dimensions={0}, use_global_device_ids=true | all-gather | bytes 147456 | tf_op jit(solution)/shard_map/all_gather | solution.py:204
  101.1 5.3 %shard_map.82 = (f32[512,1]{1,0:T(8,128)}, f32[1,4096]{1,0:T(1,128)S(1)}) custom-call(f32[512,4096]{1,0:T(8,128)S(1)} %subtract_multiply_fusion.c_ref, f32[8,4096]{1,0:T(8,128)S(1)} %bitcast.83, f32[1,4096]{1,0:T(1,128)S(1)} %compare_select_fusion.every_ref.lb_ref, f32[512,1]{1,0:T(8,128)S(1)} %fusion.4.la_ref), custom_call_target="tpu_custom_call" | custom-call | flops 33554432 | bytes 8388608 | tf_op jit(solution)/shard_map/pallas_call | solution.py:106
  106.3 9.2 %all-gather.7 = f32[8,1,4096]{2,1,0:T(1,128)S(1)} all-gather(f32[1,1,4096]{2,1,0:T(1,128)S(1)} %bitcast.91), channel_id=1, replica_groups=mesh['pair'=4,'src'=2,'tgt'=4] {'src','tgt'}, dimensions={0}, use_global_device_ids=true | all-gather | bytes 147456 | tf_op jit(solution)/shard_map/all_gather | solution.py:204
  115.6 5.3 %shard_map.83 = (f32[512,1]{1,0:T(8,128)}, f32[1,4096]{1,0:T(1,128)S(1)}) custom-call(f32[512,4096]{1,0:T(8,128)S(1)} %subtract_multiply_fusion.c_ref, f32[8,4096]{1,0:T(8,128)S(1)} %bitcast.84, f32[1,4096]{1,0:T(1,128)S(1)} %compare_select_fusion.every_ref.lb_ref, f32[512,1]{1,0:T(8,128)S(1)} %fusion.4.la_ref), custom_call_target="tpu_custom_call" | custom-call | flops 33554432 | bytes 8388608 | tf_op jit(solution)/shard_map/pallas_call | solution.py:106
  120.9 8.2 %all-gather.8 = f32[8,1,4096]{2,1,0:T(1,128)S(1)} all-gather(f32[1,1,4096]{2,1,0:T(1,128)S(1)} %bitcast.92), channel_id=1, replica_groups=mesh['pair'=4,'src'=2,'tgt'=4] {'src','tgt'}, dimensions={0}, use_global_device_ids=true | all-gather | bytes 147456 | tf_op jit(solution)/shard_map/all_gather | solution.py:204
  129.2 5.3 %shard_map.84 = (f32[512,1]{1,0:T(8,128)}, f32[1,4096]{1,0:T(1,128)S(1)}) custom-call(f32[512,4096]{1,0:T(8,128)S(1)} %subtract_multiply_fusion.c_ref, f32[8,4096]{1,0:T(8,128)S(1)} %bitcast.85, f32[1,4096]{1,0:T(1,128)S(1)} %compare_select_fusion.every_ref.lb_ref, f32[512,1]{1,0:T(8,128)S(1)} %fusion.4.la_ref), custom_call_target="tpu_custom_call" | custom-call | flops 33554432 | bytes 8388608 | tf_op jit(solution)/shard_map/pallas_call | solution.py:106
  134.4 9.4 %all-gather.9 = f32[8,1,4096]{2,1,0:T(1,128)S(1)} all-gather(f32[1,1,4096]{2,1,0:T(1,128)S(1)} %bitcast.93), channel_id=1, replica_groups=mesh['pair'=4,'src'=2,'tgt'=4] {'src','tgt'}, dimensions={0}, use_global_device_ids=true | all-gather | bytes 147456 | tf_op jit(solution)/shard_map/all_gather | solution.py:204
  144.7 3.4 %copy-done.2 = f32[512,4096]{1,0:T(8,128)S(1)} copy-done((f32[512,4096]{1,0:T(8,128)S(1)}, f32[512,4096]{1,0:T(8,128)}, u32[]{:S(2)}) %copy-start.2) | copy-done | bytes 8388632
  148.1 4.8 %shard_map.85 = (f32[512,1]{1,0:T(8,128)}, bf16[512,4096]{1,0:T(8,128)(2,1)S(1)}, f32[48,512]{1,0:T(8,128)S(1)}, f32[1,512]{1,0:T(1,128)S(1)}) custom-call(f32[512,4096]{1,0:T(8,128)S(1)} %copy-done.2, f32[8,4096]{1,0:T(8,128)S(1)} %bitcast.78, f32[1,4096]{1,0:T(1,128)S(1)} %compare_select_fusion.every_ref.lb_ref, f32[512,1]{1,0:T(8,128)S(1)} %fusion.4.la_ref, ...), custom_call_target="tpu_custom_call" | custom-call | flops 25165824 | bytes 12582912 | tf_op jit(solution)/shard_map/pallas_call | solution.py:106
  152.9 1.9 copy-done.3
  154.9 1.3 collective-permute-start.4
  157.1 1.1 collective-permute-start.9
  158.2 3.3 %collective-permute-done.4 = bf16[40,512]{1,0:T(8,128)(2,1)S(1)} collective-permute-done((bf16[40,512]{1,0:T(8,128)(2,1)S(1)}, bf16[40,512]{1,0:T(8,128)(2,1)S(1)}, u32[]{:S(2)}, u32[]{:S(2)}) %collective-permute-start.4) | collective-permute-done | bytes 40992 | tf_op jit(solution)/shard_map/ppermute | solution.py:124
  161.5 8.4 %all_gather.49 = bf16[40,4096]{1,0:T(8,128)(2,1)S(1)} all-gather(bf16[40,512]{1,0:T(8,128)(2,1)S(1)} %collective-permute-done.4), channel_id=1, replica_groups=mesh['pair'=4,'src'=2,'tgt'=4] {'src','tgt'}, dimensions={1}, use_global_device_ids=true | all-gather | bytes 368640 | tf_op jit(solution)/shard_map/all_gather | solution.py:226
  170.0 3.6 %fusion.10 = (bf16[40,512]{1,0:T(8,128)(2,1)S(1)}, f32[40,512]{1,0:T(8,128)S(1)}) fusion(bf16[40,4096]{1,0:T(8,128)(2,1)S(1)} %select_select_fusion, bf16[512,4096]{1,0:T(8,128)(2,1)} %copy-done.3, pred[512]{0:T(512)(128)(4,1)S(1)} %add_compare_fusion.1), kind=kOutput, calls=%fused_computation.53 | convolution fusion | flops 167813120 | bytes 4645376 | tf_op jit(solution)/shard_map/dot_general | solution.py:219
  173.5 1.3 collective-permute-start.5
  175.5 4.0 %collective-permute-done.5 = bf16[40,512]{1,0:T(8,128)(2,1)S(1)} collective-permute-done((bf16[40,512]{1,0:T(8,128)(2,1)S(1)}, bf16[40,512]{1,0:T(8,128)(2,1)S(1)}, u32[]{:S(2)}, u32[]{:S(2)}) %collective-permute-start.5) | collective-permute-done | bytes 40992 | tf_op jit(solution)/shard_map/ppermute | solution.py:124
  179.4 9.4 %all_gather.50 = bf16[40,4096]{1,0:T(8,128)(2,1)S(1)} all-gather(bf16[40,512]{1,0:T(8,128)(2,1)S(1)} %collective-permute-done.5), channel_id=1, replica_groups=mesh['pair'=4,'src'=2,'tgt'=4] {'src','tgt'}, dimensions={1}, use_global_device_ids=true | all-gather | bytes 368640 | tf_op jit(solution)/shard_map/all_gather | solution.py:226
  188.8 3.6 %fusion.11 = (bf16[40,512]{1,0:T(8,128)(2,1)S(1)}, f32[40,512]{1,0:T(8,128)S(1)}) fusion(bf16[512,4096]{1,0:T(8,128)(2,1)} %copy-done.3, bf16[40,4096]{1,0:T(8,128)(2,1)S(1)} %all_gather.50, bf16[40,4096]{1,0:T(8,128)(2,1)S(1)} %select_select_fusion, pred[]{:T(512)S(6)} %eq.22, pred[512]{0:T(512)(128)(4,1)S(1)} %add_compare_fusion.1), kind=kOutput, calls=%fused_computation.54 | convolution fusion | flops 167976960 | bytes 4973057 | tf_op jit(solution)/shard_map/dot_general | solution.py:219
  192.4 1.3 collective-permute-start.6
  193.8 0.6 copy.27
  194.4 3.9 %collective-permute-done.6 = bf16[40,512]{1,0:T(8,128)(2,1)S(1)} collective-permute-done((bf16[40,512]{1,0:T(8,128)(2,1)S(1)}, bf16[40,512]{1,0:T(8,128)(2,1)S(1)}, u32[]{:S(2)}, u32[]{:S(2)}) %collective-permute-start.6) | collective-permute-done | bytes 40992 | tf_op jit(solution)/shard_map/ppermute | solution.py:124
  198.3 8.4 %all_gather.51 = bf16[40,4096]{1,0:T(8,128)(2,1)S(1)} all-gather(bf16[40,512]{1,0:T(8,128)(2,1)S(1)} %collective-permute-done.6), channel_id=1, replica_groups=mesh['pair'=4,'src'=2,'tgt'=4] {'src','tgt'}, dimensions={1}, use_global_device_ids=true | all-gather | bytes 368640 | tf_op jit(solution)/shard_map/all_gather | solution.py:226
  206.8 4.2 %fusion.1 = f32[1,40,512]{2,1,0:T(8,128)} fusion(bf16[512,4096]{1,0:T(8,128)(2,1)} %copy-done.3, bf16[40,4096]{1,0:T(8,128)(2,1)S(1)} %all_gather.51, pred[]{:T(512)S(6)} %eq.21, bf16[40,4096]{1,0:T(8,128)(2,1)S(1)} %all_gather.50, bf16[40,4096]{1,0:T(8,128)(2,1)S(1)} %select_select_fusion, pred[]{:T(512)S(6)} %eq.22, f32[40,512]{1,0:T(8,128)S(1)} %get-tuple-element.29, ...), kind=kOutput, calls=%fused_computation.8 | convolution fusion | flops 168222720 | bytes 5508608 | tf_op jit(solution)/shard_map/dot_general | solution.py:219
  (46 shorter events, 4.6 us)
Async XLA Ops:
  0.6 5.5 %copy-start = (f32[1,30,2048]{2,0,1:T(1,128)S(1)}, f32[1,30,2048]{2,0,1:T(1,128)}, u32[]{:S(2)}) copy-start(f32[1,30,2048]{2,0,1:T(1,128)} %param.6) | copy-start | bytes 737284
  1.6 142.3 %collective-permute-start.1 = (bf16[40,1024]{1,0:T(8,128)(2,1)S(1)}, bf16[40,1024]{1,0:T(8,128)(2,1)S(1)}, u32[]{:S(2)}, u32[]{:S(2)}) collective-permute-start(bf16[40,1024]{1,0:T(8,128)(2,1)S(1)} %convert_element_type.20), channel_id=1, source_target_pairs={{0,1},{1,2},{2,3},{3,0},{4,5},{5,6},{6,7},{7,4},{8,9},{9,10},{10,1... | collective-permute-start | bytes 245768 | tf_op jit(solution)/shard_map/ppermute | solution.py:189
  2.2 141.7 %collective-permute-start.2 = (bf16[40,1024]{1,0:T(8,128)(2,1)S(1)}, bf16[40,1024]{1,0:T(8,128)(2,1)S(1)}, u32[]{:S(2)}, u32[]{:S(2)}) collective-permute-start(bf16[40,1024]{1,0:T(8,128)(2,1)S(1)} %convert_element_type.20), channel_id=1, source_target_pairs={{0,2},{1,3},{2,0},{3,1},{4,6},{5,7},{6,4},{7,5},{8,10},{9,11},{10,... | collective-permute-start | bytes 245768 | tf_op jit(solution)/shard_map/ppermute | solution.py:189
  4.7 139.2 %collective-permute-start.3 = (bf16[40,1024]{1,0:T(8,128)(2,1)S(1)}, bf16[40,1024]{1,0:T(8,128)(2,1)S(1)}, u32[]{:S(2)}, u32[]{:S(2)}) collective-permute-start(bf16[40,1024]{1,0:T(8,128)(2,1)S(1)} %convert_element_type.20), channel_id=1, source_target_pairs={{0,3},{1,0},{2,1},{3,2},{4,7},{5,4},{6,5},{7,6},{8,11},{9,8},{10,9... | collective-permute-start | bytes 245768 | tf_op jit(solution)/shard_map/ppermute | solution.py:189
  6.2 8.6 %collective-permute-start = (f32[30,512]{1,0:T(8,128)S(1)}, f32[30,512]{1,0:T(8,128)S(1)}, u32[]{:S(2)}, u32[]{:S(2)}) collective-permute-start(f32[30,512]{1,0:T(8,128)S(1)} %bitcast.106), channel_id=1, source_target_pairs={{8,0},{16,8},{24,16},{9,1},{17,9},{25,17},{10,2},{18,10},{26,18},{... | collective-permute-start | bytes 184328 | tf_op jit(solution)/shard_map/ppermute | solution.py:124
  34.3 94.9 %copy-start.1 = (f32[512,4096]{1,0:T(8,128)}, f32[512,4096]{1,0:T(8,128)S(1)}, u32[]{:S(2)}) copy-start(f32[512,4096]{1,0:T(8,128)S(1)} %subtract_multiply_fusion.c_ref) | copy-start | bytes 25165828
  144.7 3.4 %copy-start.2 = (f32[512,4096]{1,0:T(8,128)S(1)}, f32[512,4096]{1,0:T(8,128)}, u32[]{:S(2)}) copy-start(f32[512,4096]{1,0:T(8,128)} %copy-done.1) | copy-start | bytes 25165828
  152.9 1.9 copy-start.3
  154.9 6.6 %collective-permute-start.4 = (bf16[40,512]{1,0:T(8,128)(2,1)S(1)}, bf16[40,512]{1,0:T(8,128)(2,1)S(1)}, u32[]{:S(2)}, u32[]{:S(2)}) collective-permute-start(bf16[40,512]{1,0:T(8,128)(2,1)S(1)} %fusion.5), channel_id=1, source_target_pairs={{8,0},{16,8},{24,16},{9,1},{17,9},{25,17},{10,2},{18,10},{26,18},{... | collective-permute-start | bytes 122888 | tf_op jit(solution)/shard_map/ppermute | solution.py:124
  156.2 18.7 %collective-permute-start.7 = (f32[512]{0:T(512)S(1)}, f32[512]{0:T(512)S(1)}, u32[]{:S(2)}, u32[]{:S(2)}) collective-permute-start(f32[512]{0:T(512)S(1)} %bitcast.94), channel_id=1, source_target_pairs={{0,1},{1,2},{2,3},{3,0},{4,5},{5,6},{6,7},{7,4},{8,9},{9,10},{10,1... | collective-permute-start | bytes 6152 | tf_op jit(solution)/shard_map/ppermute | solution.py:231
  156.6 18.3 %collective-permute-start.8 = (f32[512]{0:T(512)S(1)}, f32[512]{0:T(512)S(1)}, u32[]{:S(2)}, u32[]{:S(2)}) collective-permute-start(f32[512]{0:T(512)S(1)} %bitcast.95), channel_id=1, source_target_pairs={{0,2},{1,3},{2,0},{3,1},{4,6},{5,7},{6,4},{7,5},{8,10},{9,11},{10,... | collective-permute-start | bytes 6152 | tf_op jit(solution)/shard_map/ppermute | solution.py:231
  157.1 17.7 %collective-permute-start.9 = (f32[512]{0:T(512)S(1)}, f32[512]{0:T(512)S(1)}, u32[]{:S(2)}, u32[]{:S(2)}) collective-permute-start(f32[512]{0:T(512)S(1)} %bitcast.96), channel_id=1, source_target_pairs={{0,3},{1,0},{2,1},{3,2},{4,7},{5,4},{6,5},{7,6},{8,11},{9,8},{10,9... | collective-permute-start | bytes 6152 | tf_op jit(solution)/shard_map/ppermute | solution.py:231
  173.5 5.9 %collective-permute-start.5 = (bf16[40,512]{1,0:T(8,128)(2,1)S(1)}, bf16[40,512]{1,0:T(8,128)(2,1)S(1)}, u32[]{:S(2)}, u32[]{:S(2)}) collective-permute-start(bf16[40,512]{1,0:T(8,128)(2,1)S(1)} %get-tuple-element.26), channel_id=1, source_target_pairs={{8,0},{16,8},{24,16},{9,1},{17,9},{25,17},{10,2},{18,10},{26,18},{... | collective-permute-start | bytes 122888 | tf_op jit(solution)/shard_map/ppermute | solution.py:124
  192.4 5.9 %collective-permute-start.6 = (bf16[40,512]{1,0:T(8,128)(2,1)S(1)}, bf16[40,512]{1,0:T(8,128)(2,1)S(1)}, u32[]{:S(2)}, u32[]{:S(2)}) collective-permute-start(bf16[40,512]{1,0:T(8,128)(2,1)S(1)} %get-tuple-element.28), channel_id=1, source_target_pairs={{8,0},{16,8},{24,16},{9,1},{17,9},{25,17},{10,2},{18,10},{26,18},{... | collective-permute-start | bytes 122888 | tf_op jit(solution)/shard_map/ppermute | solution.py:124
